TPU v7x, 32 devices: a whole 2x2x4 slice. The times are simulated.
32 devices in a mesh: dom: 8 (over z, y), band: 4 (over x, core).
Axes of the slice: x: 2, y: 2, z: 4, core: 2. Of those that a mesh axis runs over, the one named last changes fastest.
Arguments:
- wavefunctions: float32 [3072, 1024], P('dom', 'band'), may hold values from -6 to 6
- cell_matrix: float32 [16, 512, 512], P('dom'), may hold values from -0.25 to 0.25
- connectivity: int32 [16, 512], P('dom'), may hold values from 0 to 639, as said below
- projector: float32 [32, 16, 512], P('dom', None, 'band'), may hold values from -0.25 to 0.25
- coupling: float32 [32, 16], P('dom'), may hold values from 0.5 to 4
- atom_start: int32 [32], P('dom'), may hold values from 0 to 128
- atom_count: int32 [8], P('dom'), may hold values from 1 to 4, as said below
Outputs:
- filtered: float32 [3072, 1024], P('dom', 'band')
Inputs may be any that keep to these rules, and one draw needn't show every extreme that they name: `connectivity`: row c holds 512 distinct rows of its partition's extended block (the 128 rows before the partition's own, its 384 own rows, the 128 rows after), all within 0 to 639, both ends included. `atom_count`: at least one partition has all 4 slots live.
All inputs are finite; a program needn't handle non-finite values.
Results may differ from a plain program's by a relative error of at most 0.0003.
Values sent between devices are 32-bit elements; how exact they have to be, the bound alone decides.
No kernel may reach another device: no remote copies, remote signals or barrier semaphores. Data moves between devices by JAX's collectives and lax.ppermute only.
A program may use at most 64 MiB of HBM per device.

v0:
```python
import jax
import jax.numpy as jnp
from jax import lax
from jax.sharding import PartitionSpec as P

GHOST = 128


filter_center = 0.25
filter_half = 2.0
highest = lax.Precision.HIGHEST


def from_left(x, axis):
    count = lax.axis_size(axis)
    return lax.ppermute(x, axis, [(i, i + 1) for i in range(count - 1)])


def from_right(x, axis):
    count = lax.axis_size(axis)
    return lax.ppermute(x, axis, [(i + 1, i) for i in range(count - 1)])


def gather_band(piece):
    count = lax.axis_size("band")
    me = lax.axis_index("band")
    pieces = [piece]
    for k in range(1, count):
        pieces.append(
            lax.ppermute(piece, "band", [(i, (i + k) % count) for i in range(count)])
        )
    stacked = jnp.stack(pieces)
    order = (me - jnp.arange(count)) % count
    ordered = jnp.take(stacked, order, axis=0)
    slots, channels, width = piece.shape
    return ordered.transpose(1, 2, 0, 3).reshape(slots, channels, count * width)


def local_operator(cell_matrix, connectivity, projector_full, coupling, atom_start, atom_count, ext):
    rows = jnp.arange(ext, dtype=connectivity.dtype)
    onehot = (connectivity[:, :, None] == rows[None, None, :]).astype(jnp.float32)
    moved = jnp.einsum("cij,cjq->ciq", cell_matrix, onehot, precision=highest)
    cells = jnp.einsum("cip,ciq->pq", onehot, moved, precision=highest)
    slots, channels, support = projector_full.shape
    live = (jnp.arange(slots) < atom_count[0]).astype(jnp.float32)
    weights = (coupling * live[:, None]).reshape(slots * channels)
    placed = []
    for slot_index in range(slots):
        placed.append(
            lax.dynamic_update_slice(
                jnp.zeros((channels, ext), jnp.float32),
                projector_full[slot_index],
                (0, atom_start[slot_index]),
            )
        )
    placed = jnp.concatenate(placed, axis=0)
    atoms = jnp.dot((placed * weights[:, None]).T, placed, precision=highest)
    return cells + atoms


def on_device(
    wavefunctions, cell_matrix, connectivity, projector, coupling, atom_start, atom_count
):
    own = wavefunctions.shape[0]
    g = GHOST
    ext = own + 2 * g
    count = lax.axis_size("dom")
    me = lax.axis_index("dom")

    low = from_left(wavefunctions[own - g :], "dom")
    high = from_right(wavefunctions[:g], "dom")
    extended = jnp.concatenate([low, wavefunctions, high], axis=0)

    projector_full = gather_band(projector)
    operator = local_operator(
        cell_matrix, connectivity, projector_full, coupling, atom_start, atom_count, ext
    )

    first = jnp.dot(operator, extended, precision=highest)
    left_sums = from_left(first[ext - 2 * g :], "dom")
    right_sums = from_right(first[: 2 * g], "dom")
    zeros_side = jnp.zeros((ext - 2 * g, first.shape[1]), jnp.float32)
    first_image = (
        first
        + jnp.concatenate([left_sums, zeros_side], axis=0)
        + jnp.concatenate([zeros_side, right_sums], axis=0)
    )
    step_ext = (first_image - filter_center * extended) / filter_half
    row = lax.broadcasted_iota(jnp.int32, (ext, 1), 0)
    keep = jnp.logical_and(
        jnp.logical_or(row >= g, me > 0), jnp.logical_or(row < ext - g, me < count - 1)
    )
    step_ext = jnp.where(keep, step_ext, 0.0)
    step_one = step_ext[g : g + own]

    second = jnp.dot(operator, step_ext, precision=highest)
    from_before = from_left(second[ext - g :], "dom")
    from_after = from_right(second[:g], "dom")
    owned = second[g : g + own]
    zeros_own = jnp.zeros((own - g, owned.shape[1]), jnp.float32)
    second_image = (
        owned
        + jnp.concatenate([from_before, zeros_own], axis=0)
        + jnp.concatenate([zeros_own, from_after], axis=0)
    )
    filtered = 2.0 * (second_image - filter_center * step_one) / filter_half - wavefunctions
    return filtered


def solution(mesh):
    return jax.shard_map(
        on_device,
        mesh=mesh,
        in_specs=(
            P("dom", "band"),
            P("dom", None, None),
            P("dom", None),
            P("dom", None, "band"),
            P("dom", None),
            P("dom"),
            P("dom"),
        ),
        out_specs=P("dom", "band"),
        check_vma=False,
    )
```

profile of v0, /device:TPU:0, one launch (start us, length us, event | category | flops | bytes accessed | tf_op | source)
XLA Modules:
  0.0 69.5 jit_solution(18253950918985105372)
XLA Ops:
  0.0 0.0 copy-start
  0.0 0.5 collective-permute-start
  0.5 2.6 %collective-permute-start.1 = (f32[4,16,128]{2,1,0:T(8,128)}, f32[4,16,128]{2,1,0:T(8,128)S(1)}, u32[]{:S(2)}, u32[]{:S(2)}) collective-permute-start(f32[4,16,128]{2,1,0:T(8,128)} %param.10), channel_id=1, source_target_pairs={{0,2},{1,3},{2,0},{3,1},{4,6},{5,7},{6,4},{7,5},{8,10},{9,11},{10,... | collective-permute-start | bytes 98312 | tf_op jit(solution)/shard_map/ppermute | solution.py:30
  3.0 1.4 %collective-permute-start.2 = (f32[4,16,128]{2,1,0:T(8,128)}, f32[4,16,128]{2,1,0:T(8,128)S(1)}, u32[]{:S(2)}, u32[]{:S(2)}) collective-permute-start(f32[4,16,128]{2,1,0:T(8,128)} %param.10), channel_id=1, source_target_pairs={{0,3},{1,0},{2,1},{3,2},{4,7},{5,4},{6,5},{7,6},{8,11},{9,8},{10,9... | collective-permute-start | bytes 98312 | tf_op jit(solution)/shard_map/ppermute | solution.py:30
  4.4 1.0 %fusion.29 = (f32[128,256]{1,0:T(8,128)S(1)}, f32[128,256]{1,0:T(8,128)S(1)}) fusion(f32[384,256]{1,0:T(8,128)} %param.7), kind=kLoop, calls=%fused_computation.56 | loop fusion | bytes 524288 | tf_op jit(solution)/shard_map/slice | solution.py:71
  5.4 3.4 %collective-permute-start.3 = (f32[128,256]{1,0:T(8,128)S(1)}, f32[128,256]{1,0:T(8,128)S(1)}, u32[]{:S(2)}, u32[]{:S(2)}) collective-permute-start(f32[128,256]{1,0:T(8,128)S(1)} %get-tuple-element.10), channel_id=1, source_target_pairs={{0,4},{4,8},{8,12},{12,16},{16,20},{20,24},{24,28},{1,5},{5,9},{9,... | collective-permute-start | bytes 393224 | tf_op jit(solution)/shard_map/ppermute | solution.py:16
  8.8 1.3 %collective-permute-start.4 = (f32[128,256]{1,0:T(8,128)S(1)}, f32[128,256]{1,0:T(8,128)S(1)}, u32[]{:S(2)}, u32[]{:S(2)}) collective-permute-start(f32[128,256]{1,0:T(8,128)S(1)} %get-tuple-element.9), channel_id=1, source_target_pairs={{4,0},{8,4},{12,8},{16,12},{20,16},{24,20},{28,24},{5,1},{9,5},{13... | collective-permute-start | bytes 393224 | tf_op jit(solution)/shard_map/ppermute | solution.py:21
  10.1 1.4 %fusion.31 = (s32[1]{0:T(128)}, s32[1]{0:T(128)}, s32[1]{0:T(128)}, s32[1]{0:T(128)}) fusion(s32[4]{0:T(128)} %param.12), kind=kLoop, calls=%fused_computation.58 | loop fusion | bytes 32 | tf_op jit(solution)/shard_map/slice | solution.py:53
  12.2 0.8 %broadcast_multiply_fusion = f32[4,16]{1,0:T(4,128)S(1)} fusion(f32[4,16]{1,0:T(4,128)} %param.11, f32[4]{0:T(128)S(1)} %compare_convert_fusion), kind=kLoop, calls=%fused_computation.49 | loop fusion | flops 64 | bytes 528 | tf_op jit(solution)/shard_map/mul | solution.py:46
  13.0 0.0 copy-done
  13.0 5.0 %fusion.2 = f32[2,640,512]{1,2,0:T(8,128)} fusion(f32[2,512,512]{2,1,0:T(8,128)S(1)} %copy-done, s32[2,512]{1,0:T(2,128)} %param.9), kind=kOutput, calls=%fused_computation.4 | convolution fusion | flops 4027187200 | bytes 4722688 | tf_op jit(solution)/shard_map/cij,cjq->ciq/dot_general | solution.py:42
  22.9 0.1 mul.33
  25.4 0.0 collective-permute-done
  25.4 0.0 collective-permute-done.1
  25.4 0.0 collective-permute-done.2
  25.4 0.0 copy-done.5
  25.5 0.6 gather_fusion
  26.0 0.1 select_bitcast_fusion
  26.3 0.5 dynamic_update_slice.12
  26.8 0.5 dynamic_update_slice.13
  27.4 0.5 dynamic_update_slice.14
  27.9 0.5 dynamic_update_slice.15
  28.5 1.6 %fusion.10 = f32[640,640]{1,0:T(8,128)S(1)} fusion(f32[16,640]{1,0:T(8,128)S(1)} %dynamic_update_slice.15, f32[16,640]{1,0:T(8,128)S(1)} %dynamic_update_slice.14, f32[16,640]{1,0:T(8,128)S(1)} %dynamic_update_slice.13, f32[16,640]{1,0:T(8,128)S(1)} %dynamic_update_slice.12, f32[64]{0:T(128)S(1)} %mul.33), kind=kOutput, calls=%fused_computation.14 | convolution fusion | flops 314859520 | bytes 1802496 | tf_op jit(solution)/shard_map/dot_general | solution.py:57
  30.1 0.0 copy-done.6
  30.1 0.0 copy-start.3
  30.1 5.2 %bitcast_add_fusion = f32[640,640]{1,0:T(8,128)S(1)} fusion(f32[640,640]{1,0:T(8,128)S(1)} %fusion.10, f32[2,640,512]{1,2,0:T(8,128)} %fusion.2, s32[2,512]{1,0:T(2,128)S(1)} %copy-done.6), kind=kOutput, calls=%fused_computation.5 | convolution fusion | flops 5034229760 | bytes 5902336 | tf_op jit(solution)/shard_map/cip,ciq->pq/dot_general | solution.py:43
  35.3 0.0 copy-start.1
  35.3 0.0 collective-permute-done.3
  35.4 0.0 copy-done.3
  35.4 0.0 collective-permute-done.4
  35.4 1.7 %fusion.32 = f32[640,256]{1,0:T(8,128)S(1)} fusion(f32[640,640]{1,0:T(8,128)S(1)} %bitcast_add_fusion, f32[640,256]{1,0:T(8,128)S(1)} %constant_dynamic-update-slice_fusion), kind=kOutput, calls=%fused_computation.59 | convolution fusion | flops 1258291200 | bytes 2949120 | tf_op jit(solution)/shard_map/dot_general | solution.py:79
  37.2 0.0 copy-done.1
  37.2 0.8 %fusion.28 = (f32[256,256]{1,0:T(8,128)}, f32[256,256]{1,0:T(8,128)}) fusion(f32[640,256]{1,0:T(8,128)S(1)} %fusion.32), kind=kLoop, calls=%fused_computation.55 | loop fusion | bytes 1048576 | tf_op jit(solution)/shard_map/slice | solution.py:80
  38.0 5.2 %collective-permute-start.5 = (f32[256,256]{1,0:T(8,128)}, f32[256,256]{1,0:T(8,128)}, u32[]{:S(2)}, u32[]{:S(2)}) collective-permute-start(f32[256,256]{1,0:T(8,128)} %get-tuple-element.7), channel_id=1, source_target_pairs={{0,4},{4,8},{8,12},{12,16},{16,20},{20,24},{24,28},{1,5},{5,9},{9,... | collective-permute-start | bytes 786440 | tf_op jit(solution)/shard_map/ppermute | solution.py:16
  43.2 1.3 %collective-permute-start.6 = (f32[256,256]{1,0:T(8,128)}, f32[256,256]{1,0:T(8,128)}, u32[]{:S(2)}, u32[]{:S(2)}) collective-permute-start(f32[256,256]{1,0:T(8,128)} %get-tuple-element.8), channel_id=1, source_target_pairs={{4,0},{8,4},{12,8},{16,12},{20,16},{24,20},{28,24},{5,1},{9,5},{13... | collective-permute-start | bytes 786440 | tf_op jit(solution)/shard_map/ppermute | solution.py:21
  44.5 0.0 copy-start.2
  44.6 8.2 %collective-permute-done.5 = f32[256,256]{1,0:T(8,128)} collective-permute-done((f32[256,256]{1,0:T(8,128)}, f32[256,256]{1,0:T(8,128)}, u32[]{:S(2)}, u32[]{:S(2)}) %collective-permute-start.5) | collective-permute-done | bytes 262176 | tf_op jit(solution)/shard_map/ppermute | solution.py:16
  52.8 0.0 collective-permute-done.6
  52.8 1.2 %multiply_select_fusion = f32[640,256]{1,0:T(8,128)S(1)} fusion(f32[640,256]{1,0:T(8,128)S(1)} %constant_dynamic-update-slice_fusion, f32[256,256]{1,0:T(8,128)} %collective-permute-done.6, f32[640,256]{1,0:T(8,128)S(1)} %fusion.32, f32[256,256]{1,0:T(8,128)} %collective-permute-done.5, pred[640]{0:T(1024)(128)(4,1)S(1)} %fusion.21), kind=kLoop, calls=%fused_computation.8 | loop fusion | flops 983040 | bytes 2491008 | tf_op jit(solution)/shard_map/jit(_where)/select_n | solution.py:93
  54.0 0.0 copy-done.2
  54.0 0.0 copy-start.4
  54.0 1.7 %fusion.33 = f32[640,256]{1,0:T(8,128)S(1)} fusion(f32[640,640]{1,0:T(8,128)S(1)} %copy-done.2, f32[640,256]{1,0:T(8,128)S(1)} %multiply_select_fusion), kind=kOutput, calls=%fused_computation.60 | convolution fusion | flops 1258291200 | bytes 2949120 | tf_op jit(solution)/shard_map/dot_general | solution.py:96
  55.7 4.4 %collective-permute-start.7 = (f32[128,256]{1,0:T(8,128)S(1)}, f32[128,256]{1,0:T(8,128)S(1)}, u32[]{:S(2)}, u32[]{:S(2)}) collective-permute-start(f32[128,256]{1,0:T(8,128)S(1)} %get-tuple-element.5), channel_id=1, source_target_pairs={{0,4},{4,8},{8,12},{12,16},{16,20},{20,24},{24,28},{1,5},{5,9},{9,... | collective-permute-start | bytes 393224 | tf_op jit(solution)/shard_map/ppermute | solution.py:16
  60.1 1.3 %collective-permute-start.8 = (f32[128,256]{1,0:T(8,128)S(1)}, f32[128,256]{1,0:T(8,128)S(1)}, u32[]{:S(2)}, u32[]{:S(2)}) collective-permute-start(f32[128,256]{1,0:T(8,128)S(1)} %get-tuple-element.6), channel_id=1, source_target_pairs={{4,0},{8,4},{12,8},{16,12},{20,16},{24,20},{28,24},{5,1},{9,5},{13... | collective-permute-start | bytes 393224 | tf_op jit(solution)/shard_map/ppermute | solution.py:21
  61.4 1.2 %collective-permute-done.7 = f32[128,256]{1,0:T(8,128)S(1)} collective-permute-done((f32[128,256]{1,0:T(8,128)S(1)}, f32[128,256]{1,0:T(8,128)S(1)}, u32[]{:S(2)}, u32[]{:S(2)}) %collective-permute-start.7) | collective-permute-done | bytes 131104 | tf_op jit(solution)/shard_map/ppermute | solution.py:16
  62.6 6.1 %collective-permute-done.8 = f32[128,256]{1,0:T(8,128)S(1)} collective-permute-done((f32[128,256]{1,0:T(8,128)S(1)}, f32[128,256]{1,0:T(8,128)S(1)}, u32[]{:S(2)}, u32[]{:S(2)}) %collective-permute-start.8) | collective-permute-done | bytes 131104 | tf_op jit(solution)/shard_map/ppermute | solution.py:21
  68.7 0.0 copy-done.4
  68.7 0.8 %fusion.8 = f32[384,256]{1,0:T(8,128)} fusion(f32[384,256]{1,0:T(8,128)S(1)} %copy-done.4, f32[640,256]{1,0:T(8,128)S(1)} %multiply_select_fusion, f32[640,256]{1,0:T(8,128)S(1)} %fusion.33, f32[128,256]{1,0:T(8,128)S(1)} %collective-permute-done.8, f32[128,256]{1,0:T(8,128)S(1)} %collective-permute-done.7), kind=kLoop, calls=%fused_computation.11 | loop fusion | flops 491520 | bytes 1835008 | tf_op jit(solution)/shard_map/sub | solution.py:106
  (25 shorter events, 0.2 us)
Async XLA Ops:
  0.0 13.0 %copy-start = (f32[2,512,512]{2,1,0:T(8,128)S(1)}, f32[2,512,512]{2,1,0:T(8,128)}, u32[]{:S(2)}) copy-start(f32[2,512,512]{2,1,0:T(8,128)} %param.8) | copy-start | bytes 6291460
  0.0 25.4 %collective-permute-start = (f32[4,16,128]{2,1,0:T(8,128)}, f32[4,16,128]{2,1,0:T(8,128)S(1)}, u32[]{:S(2)}, u32[]{:S(2)}) collective-permute-start(f32[4,16,128]{2,1,0:T(8,128)} %param.10), channel_id=1, source_target_pairs={{0,1},{1,2},{2,3},{3,0},{4,5},{5,6},{6,7},{7,4},{8,9},{9,10},{10,1... | collective-permute-start | bytes 98312 | tf_op jit(solution)/shard_map/ppermute | solution.py:30
  0.5 25.0 %collective-permute-start.1 = (f32[4,16,128]{2,1,0:T(8,128)}, f32[4,16,128]{2,1,0:T(8,128)S(1)}, u32[]{:S(2)}, u32[]{:S(2)}) collective-permute-start(f32[4,16,128]{2,1,0:T(8,128)} %param.10), channel_id=1, source_target_pairs={{0,2},{1,3},{2,0},{3,1},{4,6},{5,7},{6,4},{7,5},{8,10},{9,11},{10,... | collective-permute-start | bytes 98312 | tf_op jit(solution)/shard_map/ppermute | solution.py:30
  3.0 22.4 %collective-permute-start.2 = (f32[4,16,128]{2,1,0:T(8,128)}, f32[4,16,128]{2,1,0:T(8,128)S(1)}, u32[]{:S(2)}, u32[]{:S(2)}) collective-permute-start(f32[4,16,128]{2,1,0:T(8,128)} %param.10), channel_id=1, source_target_pairs={{0,3},{1,0},{2,1},{3,2},{4,7},{5,4},{6,5},{7,6},{8,11},{9,8},{10,9... | collective-permute-start | bytes 98312 | tf_op jit(solution)/shard_map/ppermute | solution.py:30
  5.4 29.9 %collective-permute-start.3 = (f32[128,256]{1,0:T(8,128)S(1)}, f32[128,256]{1,0:T(8,128)S(1)}, u32[]{:S(2)}, u32[]{:S(2)}) collective-permute-start(f32[128,256]{1,0:T(8,128)S(1)} %get-tuple-element.10), channel_id=1, source_target_pairs={{0,4},{4,8},{8,12},{12,16},{16,20},{20,24},{24,28},{1,5},{5,9},{9,... | collective-permute-start | bytes 393224 | tf_op jit(solution)/shard_map/ppermute | solution.py:16
  8.8 26.6 %collective-permute-start.4 = (f32[128,256]{1,0:T(8,128)S(1)}, f32[128,256]{1,0:T(8,128)S(1)}, u32[]{:S(2)}, u32[]{:S(2)}) collective-permute-start(f32[128,256]{1,0:T(8,128)S(1)} %get-tuple-element.9), channel_id=1, source_target_pairs={{4,0},{8,4},{12,8},{16,12},{20,16},{24,20},{28,24},{5,1},{9,5},{13... | collective-permute-start | bytes 393224 | tf_op jit(solution)/shard_map/ppermute | solution.py:21
  13.0 12.5 %copy-start.5 = (f32[4,16,128]{2,1,0:T(8,128)S(1)}, f32[4,16,128]{2,1,0:T(8,128)}, u32[]{:S(2)}) copy-start(f32[4,16,128]{2,1,0:T(8,128)} %param.10) | copy-start | bytes 98308
  18.0 12.1 %copy-start.6 = (s32[2,512]{1,0:T(2,128)S(1)}, s32[2,512]{1,0:T(2,128)}, u32[]{:S(2)}) copy-start(s32[2,512]{1,0:T(2,128)} %param.9) | copy-start | bytes 12292
  30.1 5.3 %copy-start.3 = (f32[384,256]{1,0:T(8,128)S(1)}, f32[384,256]{1,0:T(8,128)}, u32[]{:S(2)}) copy-start(f32[384,256]{1,0:T(8,128)} %param.7) | copy-start | bytes 1179652
  35.3 1.9 %copy-start.1 = (f32[640,640]{1,0:T(8,128)}, f32[640,640]{1,0:T(8,128)S(1)}, u32[]{:S(2)}) copy-start(f32[640,640]{1,0:T(8,128)S(1)} %bitcast_add_fusion) | copy-start | bytes 4915204
  38.0 14.8 %collective-permute-start.5 = (f32[256,256]{1,0:T(8,128)}, f32[256,256]{1,0:T(8,128)}, u32[]{:S(2)}, u32[]{:S(2)}) collective-permute-start(f32[256,256]{1,0:T(8,128)} %get-tuple-element.7), channel_id=1, source_target_pairs={{0,4},{4,8},{8,12},{12,16},{16,20},{20,24},{24,28},{1,5},{5,9},{9,... | collective-permute-start | bytes 786440 | tf_op jit(solution)/shard_map/ppermute | solution.py:16
  43.2 9.5 %collective-permute-start.6 = (f32[256,256]{1,0:T(8,128)}, f32[256,256]{1,0:T(8,128)}, u32[]{:S(2)}, u32[]{:S(2)}) collective-permute-start(f32[256,256]{1,0:T(8,128)} %get-tuple-element.8), channel_id=1, source_target_pairs={{4,0},{8,4},{12,8},{16,12},{20,16},{24,20},{28,24},{5,1},{9,5},{13... | collective-permute-start | bytes 786440 | tf_op jit(solution)/shard_map/ppermute | solution.py:21
  44.5 9.4 %copy-start.2 = (f32[640,640]{1,0:T(8,128)S(1)}, f32[640,640]{1,0:T(8,128)}, u32[]{:S(2)}) copy-start(f32[640,640]{1,0:T(8,128)} %copy-done.1) | copy-start | bytes 4915204
  54.0 14.7 %copy-start.4 = (f32[384,256]{1,0:T(8,128)S(1)}, f32[384,256]{1,0:T(8,128)}, u32[]{:S(2)}) copy-start(f32[384,256]{1,0:T(8,128)} %param.7) | copy-start | bytes 1179652
  55.7 6.9 %collective-permute-start.7 = (f32[128,256]{1,0:T(8,128)S(1)}, f32[128,256]{1,0:T(8,128)S(1)}, u32[]{:S(2)}, u32[]{:S(2)}) collective-permute-start(f32[128,256]{1,0:T(8,128)S(1)} %get-tuple-element.5), channel_id=1, source_target_pairs={{0,4},{4,8},{8,12},{12,16},{16,20},{20,24},{24,28},{1,5},{5,9},{9,... | collective-permute-start | bytes 393224 | tf_op jit(solution)/shard_map/ppermute | solution.py:16
  60.1 8.6 %collective-permute-start.8 = (f32[128,256]{1,0:T(8,128)S(1)}, f32[128,256]{1,0:T(8,128)S(1)}, u32[]{:S(2)}, u32[]{:S(2)}) collective-permute-start(f32[128,256]{1,0:T(8,128)S(1)} %get-tuple-element.6), channel_id=1, source_target_pairs={{4,0},{8,4},{12,8},{16,12},{20,16},{24,20},{28,24},{5,1},{9,5},{13... | collective-permute-start | bytes 393224 | tf_op jit(solution)/shard_map/ppermute | solution.py:21
where the time goes:
time: 70 us; the launch traced here: 69.5 us
  starting transfers between devices  21.3 us (30%)
  waiting for transfers between devices  15.5 us (22%)
  matrix products  15.2 us (22%)
  between operations  8.41 us (12%)
  local copies, waits for them, and re-layouts  6.2 us (9%)
  other arithmetic  2.91 us (4%)
    ppermute x3, starting transfers between devices, from_left(): return lax.ppermute(x, axis, [(i, i + 1) for i in range(count - 1)])  13 us
    ppermute x3, waiting for transfers between devices, from_left(): return lax.ppermute(x, axis, [(i, i + 1) for i in range(count - 1)])  9.41 us
    ppermute x3, waiting for transfers between devices, from_right(): return lax.ppermute(x, axis, [(i + 1, i) for i in range(count - 1)])  6.11 us
    dot_general x1, matrix products, local_operator(): cells = jnp.einsum('cip,ciq->pq', onehot, moved, precision=highest)  5.23 us
    dot_general x1, matrix products, local_operator(): moved = jnp.einsum('cij,cjq->ciq', cell_matrix, onehot, precision=highest)  4.96 us
    ppermute x3, starting transfers between devices, gather_band(): lax.ppermute(piece, 'band', [(i, (i + k) % count) for i in range(count)])  4.4 us
    ppermute x3, starting transfers between devices, from_right(): return lax.ppermute(x, axis, [(i + 1, i) for i in range(count - 1)])  3.86 us
    dynamic_update_slice x4, local copies, waits for them, and re-layouts, local_operator(): lax.dynamic_update_slice(jnp.zeros((channels, ext), jnp.float32), project...  2.11 us
  transfers between devices with their start and end apart: 9, of which 3 were waited for; matrix products, arithmetic and copies ran while one was open for 26% of the time, Pallas kernels for 0%

commit v1 on v0

--- a/solution.py
+++ b/solution.py
@@ -23,39 +23,42 @@
 
 def gather_band(piece):
     count = lax.axis_size("band")
-    me = lax.axis_index("band")
-    pieces = [piece]
-    for k in range(1, count):
-        pieces.append(
-            lax.ppermute(piece, "band", [(i, (i + k) % count) for i in range(count)])
-        )
-    stacked = jnp.stack(pieces)
-    order = (me - jnp.arange(count)) % count
-    ordered = jnp.take(stacked, order, axis=0)
-    slots, channels, width = piece.shape
-    return ordered.transpose(1, 2, 0, 3).reshape(slots, channels, count * width)
+    copies = jnp.broadcast_to(piece[None], (count,) + piece.shape)
+    return lax.all_to_all(copies, "band", 0, 0, tiled=True)
 
 
-def local_operator(cell_matrix, connectivity, projector_full, coupling, atom_start, atom_count, ext):
+def split_bf16(x):
+    hi = lax.reduce_precision(x, exponent_bits=8, mantissa_bits=7)
+    rest = x - hi
+    mid = lax.reduce_precision(rest, exponent_bits=8, mantissa_bits=7)
+    lo = rest - mid
+    return [part.astype(jnp.bfloat16) for part in (hi, mid, lo)]
+
+
+def cell_operator(cell_matrix, connectivity, ext):
+    cells = cell_matrix.shape[0]
     rows = jnp.arange(ext, dtype=connectivity.dtype)
-    onehot = (connectivity[:, :, None] == rows[None, None, :]).astype(jnp.float32)
-    moved = jnp.einsum("cij,cjq->ciq", cell_matrix, onehot, precision=highest)
-    cells = jnp.einsum("cip,ciq->pq", onehot, moved, precision=highest)
-    slots, channels, support = projector_full.shape
-    live = (jnp.arange(slots) < atom_count[0]).astype(jnp.float32)
-    weights = (coupling * live[:, None]).reshape(slots * channels)
-    placed = []
-    for slot_index in range(slots):
-        placed.append(
-            lax.dynamic_update_slice(
-                jnp.zeros((channels, ext), jnp.float32),
-                projector_full[slot_index],
-                (0, atom_start[slot_index]),
-            )
-        )
-    placed = jnp.concatenate(placed, axis=0)
-    atoms = jnp.dot((placed * weights[:, None]).T, placed, precision=highest)
-    return cells + atoms
+    onehot = (connectivity[:, :, None] == rows[None, None, :]).astype(jnp.bfloat16)
+    parts = jnp.concatenate(split_bf16(cell_matrix), axis=2)
+    moved = jnp.einsum("cip,cij->cpj", onehot, parts, preferred_element_type=jnp.float32)
+    moved = moved.astype(jnp.bfloat16)
+    nodes = connectivity.shape[1]
+    left = moved.reshape(cells, ext, 3, nodes).transpose(1, 0, 2, 3).reshape(ext, cells * 3 * nodes)
+    right = jnp.broadcast_to(onehot[:, None], (cells, 3, nodes, ext)).reshape(cells * 3 * nodes, ext)
+    return jnp.dot(left, right, preferred_element_type=jnp.float32)
+
+
+def atom_rows(pieces, coupling, atom_start, atom_count, ext):
+    count, slots, channels, width = pieces.shape
+    t = lax.broadcasted_iota(jnp.int32, (count, slots, width, ext), 2)
+    q = lax.broadcasted_iota(jnp.int32, (count, slots, width, ext), 3)
+    k = lax.broadcasted_iota(jnp.int32, (count, slots, width, ext), 0)
+    first = atom_start.astype(jnp.int32)[None, :, None, None]
+    shift = (q == first + k * width + t).astype(jnp.float32)
+    placed = jnp.einsum("kscj,ksjq->scq", pieces, shift, precision=highest)
+    live = (jnp.arange(slots, dtype=jnp.int32)[:, None] < atom_count.astype(jnp.int32)[None, :])
+    weights = coupling * live.astype(jnp.float32)
+    return placed.reshape(slots * channels, ext), weights.reshape(slots * channels)
 
 
 def on_device(
@@ -71,12 +74,14 @@
     high = from_right(wavefunctions[:g], "dom")
     extended = jnp.concatenate([low, wavefunctions, high], axis=0)
 
-    projector_full = gather_band(projector)
-    operator = local_operator(
-        cell_matrix, connectivity, projector_full, coupling, atom_start, atom_count, ext
+    cells = cell_operator(cell_matrix, connectivity, ext)
+    placed, weights = atom_rows(gather_band(projector), coupling, atom_start, atom_count, ext)
+    operator = cells + jnp.dot((placed * weights[:, None]).T, placed, precision=highest)
+
+    coefficients = jnp.dot(placed, extended, precision=highest) * weights[:, None]
+    first = jnp.dot(cells, extended, precision=highest) + jnp.dot(
+        placed.T, coefficients, precision=highest
     )
-
-    first = jnp.dot(operator, extended, precision=highest)
     left_sums = from_left(first[ext - 2 * g :], "dom")
     right_sums = from_right(first[: 2 * g], "dom")
     zeros_side = jnp.zeros((ext - 2 * g, first.shape[1]), jnp.float32)

time: 70 us -> 70.3 us (level)
  between operations: 8.41 us -> 0.91 us
  local copies, waits for them, and re-layouts: 6.2 us -> 10 us
  matrix products: 15.2 us -> 17.1 us
  other arithmetic: 2.91 us -> 4.35 us
    convert_element_type x0 -> x2, local copies, waits for them, and re-layouts: none -> 6.77 us  [the longest x1 6.06 us: cell_operator(): moved = moved.astype(jnp.bfloat16)]
    ppermute x3 -> x0, starting transfers between devices: 4.4 us -> none  [gather_band(): lax.ppermute(piece, 'band', [(i, (i + k) % count) for i in range(count)])]
    all_to_all x0 -> x1, starting transfers between devices: none -> 3.32 us  [gather_band(): return lax.all_to_all(copies, 'band', 0, 0, tiled=True)]
    convert_element_type x1 -> x3, other arithmetic: 0.01 us -> 2.56 us  [the longest x1 2.1 us: split_bf16(): return [part.astype(jnp.bfloat16) for part in (hi, mid, lo)]]
    dynamic_update_slice x4 -> x0, local copies, waits for them, and re-layouts: 2.11 us -> none  [local_operator(): lax.dynamic_update_slice(jnp.zeros((channels, ext), jnp.float32), project...]
    dot_general x4 -> x7, matrix products: 13.5 us -> 15.3 us  [the longest x1 5.38 us: cell_operator(): return jnp.dot(left, right, preferred_element_type=jnp.float32)]
    slice x6 -> x0, local copies, waits for them, and re-layouts: 1.49 us -> none  [the longest x1 1.42 us: local_operator(): atom_start[slot_index]]
    broadcast_in_dim x0 -> x1, local copies, waits for them, and re-layouts: none -> 1.41 us  [gather_band(): copies = jnp.broadcast_to(piece[None], (count,) + piece.shape)]
  transfers between devices with their start and end apart: 9 -> 7, of which waited for: 3 -> 3; matrix products, arithmetic and copies ran while one was open for 26% -> 35% of each run, Pallas kernels for 0% -> 0%
where the time goes in v1:
time: 70.3 us; the launch traced here: 69.7 us
  starting transfers between devices  21.2 us (30%)
  matrix products  17.1 us (24%)
  waiting for transfers between devices  16.1 us (23%)
  local copies, waits for them, and re-layouts  10 us (14%)
  other arithmetic  4.35 us (6%)
  between operations  0.91 us (1%)
    ppermute x3, starting transfers between devices, from_left(): return lax.ppermute(x, axis, [(i, i + 1) for i in range(count - 1)])  13.8 us
    ppermute x3, waiting for transfers between devices, from_left(): return lax.ppermute(x, axis, [(i, i + 1) for i in range(count - 1)])  10 us
    ppermute x3, waiting for transfers between devices, from_right(): return lax.ppermute(x, axis, [(i + 1, i) for i in range(count - 1)])  6.09 us
    convert_element_type x1, local copies, waits for them, and re-layouts, cell_operator(): moved = moved.astype(jnp.bfloat16)  6.06 us
    dot_general x1, matrix products, cell_operator(): return jnp.dot(left, right, preferred_element_type=jnp.float32)  5.38 us
    ppermute x3, starting transfers between devices, from_right(): return lax.ppermute(x, axis, [(i + 1, i) for i in range(count - 1)])  4.06 us
    dot_general x1, matrix products, cell_operator(): jnp.einsum('cip,cij->cpj', onehot, parts, preferred_element_type=jnp.floa...  3.66 us
    all_to_all x1, starting transfers between devices, gather_band(): return lax.all_to_all(copies, 'band', 0, 0, tiled=True)  3.32 us
  transfers between devices with their start and end apart: 7, of which 3 were waited for; matrix products, arithmetic and copies ran while one was open for 35% of the time, Pallas kernels for 0%

profile of v1, /device:TPU:0, one launch (start us, length us, event | category | flops | bytes accessed | tf_op | source)
XLA Modules:
  0.0 69.7 jit_solution(10477567024019530992)
XLA Ops:
  0.0 1.6 %fusion.34 = (f32[128,256]{1,0:T(8,128)S(1)}, f32[128,256]{1,0:T(8,128)}) fusion(f32[384,256]{1,0:T(8,128)} %param.7), kind=kLoop, calls=%fused_computation.52 | loop fusion | bytes 524288 | tf_op jit(solution)/shard_map/slice | solution.py:74
  1.6 4.9 %collective-permute-start = (f32[128,256]{1,0:T(8,128)}, f32[128,256]{1,0:T(8,128)S(1)}, u32[]{:S(2)}, u32[]{:S(2)}) collective-permute-start(f32[128,256]{1,0:T(8,128)} %get-tuple-element.13), channel_id=1, source_target_pairs={{0,4},{4,8},{8,12},{12,16},{16,20},{20,24},{24,28},{1,5},{5,9},{9,... | collective-permute-start | bytes 393224 | tf_op jit(solution)/shard_map/ppermute | solution.py:16
  6.5 1.3 %collective-permute-start.1 = (f32[128,256]{1,0:T(8,128)S(1)}, f32[128,256]{1,0:T(8,128)S(1)}, u32[]{:S(2)}, u32[]{:S(2)}) collective-permute-start(f32[128,256]{1,0:T(8,128)S(1)} %get-tuple-element.12), channel_id=1, source_target_pairs={{4,0},{8,4},{12,8},{16,12},{20,16},{24,20},{28,24},{5,1},{9,5},{13... | collective-permute-start | bytes 393224 | tf_op jit(solution)/shard_map/ppermute | solution.py:21
  7.8 1.4 %broadcast_in_dim.13 = f32[4,4,16,128]{3,2,1,0:T(8,128)} broadcast(f32[4,16,128]{2,1,0:T(8,128)} %param.10), dimensions={1,2,3} | broadcast | bytes 163840 | tf_op jit(solution)/shard_map/broadcast_in_dim | solution.py:26
  9.2 3.3 %all-to-all-start = ((f32[4,4,16,128]{3,2,1,0:T(8,128)}), f32[4,4,16,128]{3,2,1,0:T(8,128)S(1)}, u32[]{:S(2)}, u32[]{:S(2)}) async-start(f32[4,4,16,128]{3,2,1,0:T(8,128)} %broadcast_in_dim.13), calls=%async_computation | async-start | bytes 262144 | tf_op jit(solution)/shard_map/all_to_all | solution.py:27
  13.2 0.8 %broadcast_multiply_fusion = f32[4,16]{1,0:T(4,128)S(1)} fusion(f32[4,16]{1,0:T(4,128)} %param.11, f32[4]{0:T(128)S(1)} %compare_convert_fusion), kind=kLoop, calls=%fused_computation.47 | loop fusion | flops 64 | bytes 528 | tf_op jit(solution)/shard_map/mul | solution.py:60
  14.0 0.1 mul.53
  14.1 0.0 copy-start.1
  14.1 2.1 %reduce-precision_convert_fusion.1 = (bf16[2,512,512]{2,1,0:T(8,128)(2,1)S(1)}, bf16[2,512,512]{2,1,0:T(8,128)(2,1)S(1)}, bf16[2,512,512]{2,1,0:T(8,128)(2,1)S(1)}) fusion(f32[2,512,512]{2,1,0:T(8,128)} %param.8), kind=kLoop, calls=%fused_computation.11 | loop fusion | flops 3670016 | bytes 5242880 | tf_op jit(solution)/shard_map/convert_element_type | solution.py:35
  16.2 0.0 copy-done.1
  16.2 0.5 fusion.8
  16.6 3.7 %convolution_convert_fusion = bf16[2,640,1536]{2,1,0:T(8,128)(2,1)} fusion(bf16[2,512,512]{2,1,0:T(8,128)(2,1)S(1)} %get-tuple-element.6, bf16[2,512,512]{2,1,0:T(8,128)(2,1)S(1)} %get-tuple-element.7, bf16[2,512,512]{2,1,0:T(8,128)(2,1)S(1)} %get-tuple-element.5, s32[2,512]{1,0:T(2,128)S(1)} %copy-done.1), kind=kOutput, calls=%fused_computation.2 | convolution fusion | flops 2025324544 | bytes 7081984 | tf_op jit(solution)/shard_map/cip,cij->cpj/dot_general | solution.py:43
  20.3 6.1 %copy.13 = bf16[2,640,1536]{1,2,0:T(8,128)(2,1)} copy(bf16[2,640,1536]{2,1,0:T(8,128)(2,1)} %convolution_convert_fusion) | data formatting | bytes 7864320 | tf_op jit(solution)/shard_map/convert_element_type | solution.py:44
  26.4 0.7 %copy.14 = bf16[2,512,640]{2,1,0:T(8,128)(2,1)S(1)} copy(bf16[2,512,640]{1,2,0:T(8,128)(2,1)S(1)} %fusion.8) | data formatting | bytes 2621440 | tf_op jit(solution)/shard_map/convert_element_type | solution.py:41
  27.1 0.0 copy-start.2
  27.1 5.4 %fusion.10 = f32[640,640,1,1]{1,0,3,2:T(8,128)S(1)} fusion(bf16[640,2,3,512]{0,3,2,1:T(8,128)(2,1)} %bitcast.36, bf16[2,512,640]{2,1,0:T(8,128)(2,1)S(1)} %copy.14), kind=kOutput, calls=%fused_computation.17 | convolution fusion | flops 2516582400 | bytes 6881280 | tf_op jit(solution)/shard_map/dot_general | solution.py:48
  32.5 0.0 copy-start
  32.5 0.0 all-to-all-done
  32.5 0.0 copy-done.2
  32.5 1.8 %fusion = f32[4,640,16,1]{1,2,3,0:T(8,128)S(1)} fusion(s32[4]{0:T(128)S(1)} %iota_multiply_fusion, s32[4]{0:T(128)S(1)} %copy-done.2, f32[4,4,16,128]{3,2,1,0:T(8,128)S(1)} %all-to-all-done), kind=kOutput, calls=%fused_computation.1 | convolution fusion | flops 255590400 | bytes 294944 | tf_op jit(solution)/shard_map/kscj,ksjq->scq/dot_general | solution.py:58
  34.4 0.0 collective-permute-done
  34.4 0.0 copy-done
  34.5 0.0 collective-permute-done.1
  34.5 0.4 convolution_multiply_fusion
  35.0 0.7 %fusion.35 = f32[640,256]{1,0:T(8,128)S(1)} fusion(f32[64,640]{1,0:T(8,128)S(1)} %bitcast.38, f32[64,256]{1,0:T(8,128)S(1)} %convolution_multiply_fusion), kind=kOutput, calls=%fused_computation.53 | convolution fusion | flops 125829120 | bytes 884736 | tf_op jit(solution)/shard_map/dot_general | solution.py:82
  35.7 1.7 %fusion.17 = f32[640,256]{1,0:T(8,128)S(1)} fusion(f32[640,256]{1,0:T(8,128)S(1)} %fusion.35, f32[640,256]{1,0:T(8,128)S(1)} %constant_dynamic-update-slice_fusion, f32[640,640,1,1]{1,0,3,2:T(8,128)S(1)} %fusion.10), kind=kOutput, calls=%fused_computation.25 | convolution fusion | flops 1258455040 | bytes 3604480 | tf_op jit(solution)/shard_map/dot_general | solution.py:82
  37.4 4.6 %collective-permute-start.2 = (f32[256,256]{1,0:T(8,128)S(1)}, f32[256,256]{1,0:T(8,128)S(1)}, u32[]{:S(2)}, u32[]{:S(2)}) collective-permute-start(f32[256,256]{1,0:T(8,128)S(1)} %get-tuple-element.10), channel_id=1, source_target_pairs={{0,4},{4,8},{8,12},{12,16},{16,20},{20,24},{24,28},{1,5},{5,9},{9,... | collective-permute-start | bytes 786440 | tf_op jit(solution)/shard_map/ppermute | solution.py:16
  42.0 1.5 %collective-permute-start.3 = (f32[256,256]{1,0:T(8,128)S(1)}, f32[256,256]{1,0:T(8,128)S(1)}, u32[]{:S(2)}, u32[]{:S(2)}) collective-permute-start(f32[256,256]{1,0:T(8,128)S(1)} %get-tuple-element.11), channel_id=1, source_target_pairs={{4,0},{8,4},{12,8},{16,12},{20,16},{24,20},{28,24},{5,1},{9,5},{13... | collective-permute-start | bytes 786440 | tf_op jit(solution)/shard_map/ppermute | solution.py:21
  43.5 1.6 %fusion.23 = f32[640,640,1]{1,0,2:T(8,128)S(1)} fusion(f32[4,640,16,1]{1,2,3,0:T(8,128)S(1)} %fusion, f32[4,16]{1,0:T(4,128)S(1)} %broadcast_multiply_fusion), kind=kOutput, calls=%fused_computation.33 | convolution fusion | flops 314613760 | bytes 1802496 | tf_op jit(solution)/shard_map/dot_general | solution.py:79
  45.1 8.8 %collective-permute-done.2 = f32[256,256]{1,0:T(8,128)S(1)} collective-permute-done((f32[256,256]{1,0:T(8,128)S(1)}, f32[256,256]{1,0:T(8,128)S(1)}, u32[]{:S(2)}, u32[]{:S(2)}) %collective-permute-start.2) | collective-permute-done | bytes 262176 | tf_op jit(solution)/shard_map/ppermute | solution.py:16
  53.8 0.0 collective-permute-done.3
  53.8 0.2 multiply_select_fusion
  54.0 1.8 %fusion.14 = f32[640,256]{1,0:T(8,128)S(1)} fusion(f32[640,256]{1,0:T(8,128)S(1)} %multiply_select_fusion, f32[640,640,1,1]{1,0,3,2:T(8,128)S(1)} %fusion.10, f32[640,640,1]{1,0,2:T(8,128)S(1)} %fusion.23), kind=kOutput, calls=%fused_computation.22 | convolution fusion | flops 1258700800 | bytes 4587520 | tf_op jit(solution)/shard_map/dot_general | solution.py:101
  55.8 4.4 %collective-permute-start.4 = (f32[128,256]{1,0:T(8,128)S(1)}, f32[128,256]{1,0:T(8,128)S(1)}, u32[]{:S(2)}, u32[]{:S(2)}) collective-permute-start(f32[128,256]{1,0:T(8,128)S(1)} %get-tuple-element.8), channel_id=1, source_target_pairs={{0,4},{4,8},{8,12},{12,16},{16,20},{20,24},{24,28},{1,5},{5,9},{9,... | collective-permute-start | bytes 393224 | tf_op jit(solution)/shard_map/ppermute | solution.py:16
  60.2 1.3 %collective-permute-start.5 = (f32[128,256]{1,0:T(8,128)S(1)}, f32[128,256]{1,0:T(8,128)S(1)}, u32[]{:S(2)}, u32[]{:S(2)}) collective-permute-start(f32[128,256]{1,0:T(8,128)S(1)} %get-tuple-element.9), channel_id=1, source_target_pairs={{4,0},{8,4},{12,8},{16,12},{20,16},{24,20},{28,24},{5,1},{9,5},{13... | collective-permute-start | bytes 393224 | tf_op jit(solution)/shard_map/ppermute | solution.py:21
  61.5 1.3 %collective-permute-done.4 = f32[128,256]{1,0:T(8,128)S(1)} collective-permute-done((f32[128,256]{1,0:T(8,128)S(1)}, f32[128,256]{1,0:T(8,128)S(1)}, u32[]{:S(2)}, u32[]{:S(2)}) %collective-permute-start.4) | collective-permute-done | bytes 131104 | tf_op jit(solution)/shard_map/ppermute | solution.py:16
  62.8 6.1 %collective-permute-done.5 = f32[128,256]{1,0:T(8,128)S(1)} collective-permute-done((f32[128,256]{1,0:T(8,128)S(1)}, f32[128,256]{1,0:T(8,128)S(1)}, u32[]{:S(2)}, u32[]{:S(2)}) %collective-permute-start.5) | collective-permute-done | bytes 131104 | tf_op jit(solution)/shard_map/ppermute | solution.py:21
  68.8 0.8 %fusion.21 = f32[384,256]{1,0:T(8,128)} fusion(f32[384,256]{1,0:T(8,128)S(1)} %copy-done, f32[640,256]{1,0:T(8,128)S(1)} %multiply_select_fusion, f32[640,256]{1,0:T(8,128)S(1)} %fusion.14, f32[128,256]{1,0:T(8,128)S(1)} %collective-permute-done.5, f32[128,256]{1,0:T(8,128)S(1)} %collective-permute-done.4), kind=kLoop, calls=%fused_computation.30 | loop fusion | flops 491520 | bytes 1835008 | tf_op jit(solution)/shard_map/sub | solution.py:111
  (8 shorter events, 0.1 us)
Async XLA Ops:
  1.6 32.8 %collective-permute-start = (f32[128,256]{1,0:T(8,128)}, f32[128,256]{1,0:T(8,128)S(1)}, u32[]{:S(2)}, u32[]{:S(2)}) collective-permute-start(f32[128,256]{1,0:T(8,128)} %get-tuple-element.13), channel_id=1, source_target_pairs={{0,4},{4,8},{8,12},{12,16},{16,20},{20,24},{24,28},{1,5},{5,9},{9,... | collective-permute-start | bytes 393224 | tf_op jit(solution)/shard_map/ppermute | solution.py:16
  6.5 28.0 %collective-permute-start.1 = (f32[128,256]{1,0:T(8,128)S(1)}, f32[128,256]{1,0:T(8,128)S(1)}, u32[]{:S(2)}, u32[]{:S(2)}) collective-permute-start(f32[128,256]{1,0:T(8,128)S(1)} %get-tuple-element.12), channel_id=1, source_target_pairs={{4,0},{8,4},{12,8},{16,12},{20,16},{24,20},{28,24},{5,1},{9,5},{13... | collective-permute-start | bytes 393224 | tf_op jit(solution)/shard_map/ppermute | solution.py:21
  9.2 23.3 %all-to-all-start = ((f32[4,4,16,128]{3,2,1,0:T(8,128)}), f32[4,4,16,128]{3,2,1,0:T(8,128)S(1)}, u32[]{:S(2)}, u32[]{:S(2)}) async-start(f32[4,4,16,128]{3,2,1,0:T(8,128)} %broadcast_in_dim.13), calls=%async_computation | async-start | bytes 262144 | tf_op jit(solution)/shard_map/all_to_all | solution.py:27
  14.1 2.1 %copy-start.1 = (s32[2,512]{1,0:T(2,128)S(1)}, s32[2,512]{1,0:T(2,128)}, u32[]{:S(2)}) copy-start(s32[2,512]{1,0:T(2,128)} %param.9) | copy-start | bytes 12292
  27.1 5.4 %copy-start.2 = (s32[4]{0:T(128)S(1)}, s32[4]{0:T(128)}, u32[]{:S(2)}) copy-start(s32[4]{0:T(128)} %param.12) | copy-start | bytes 52
  32.5 1.9 %copy-start = (f32[384,256]{1,0:T(8,128)S(1)}, f32[384,256]{1,0:T(8,128)}, u32[]{:S(2)}) copy-start(f32[384,256]{1,0:T(8,128)} %param.7) | copy-start | bytes 1179652
  37.4 16.4 %collective-permute-start.2 = (f32[256,256]{1,0:T(8,128)S(1)}, f32[256,256]{1,0:T(8,128)S(1)}, u32[]{:S(2)}, u32[]{:S(2)}) collective-permute-start(f32[256,256]{1,0:T(8,128)S(1)} %get-tuple-element.10), channel_id=1, source_target_pairs={{0,4},{4,8},{8,12},{12,16},{16,20},{20,24},{24,28},{1,5},{5,9},{9,... | collective-permute-start | bytes 786440 | tf_op jit(solution)/shard_map/ppermute | solution.py:16
  42.0 11.8 %collective-permute-start.3 = (f32[256,256]{1,0:T(8,128)S(1)}, f32[256,256]{1,0:T(8,128)S(1)}, u32[]{:S(2)}, u32[]{:S(2)}) collective-permute-start(f32[256,256]{1,0:T(8,128)S(1)} %get-tuple-element.11), channel_id=1, source_target_pairs={{4,0},{8,4},{12,8},{16,12},{20,16},{24,20},{28,24},{5,1},{9,5},{13... | collective-permute-start | bytes 786440 | tf_op jit(solution)/shard_map/ppermute | solution.py:21
  55.8 6.9 %collective-permute-start.4 = (f32[128,256]{1,0:T(8,128)S(1)}, f32[128,256]{1,0:T(8,128)S(1)}, u32[]{:S(2)}, u32[]{:S(2)}) collective-permute-start(f32[128,256]{1,0:T(8,128)S(1)} %get-tuple-element.8), channel_id=1, source_target_pairs={{0,4},{4,8},{8,12},{12,16},{16,20},{20,24},{24,28},{1,5},{5,9},{9,... | collective-permute-start | bytes 393224 | tf_op jit(solution)/shard_map/ppermute | solution.py:16
  60.2 8.7 %collective-permute-start.5 = (f32[128,256]{1,0:T(8,128)S(1)}, f32[128,256]{1,0:T(8,128)S(1)}, u32[]{:S(2)}, u32[]{:S(2)}) collective-permute-start(f32[128,256]{1,0:T(8,128)S(1)} %get-tuple-element.9), channel_id=1, source_target_pairs={{4,0},{8,4},{12,8},{16,12},{20,16},{24,20},{28,24},{5,1},{9,5},{13... | collective-permute-start | bytes 393224 | tf_op jit(solution)/shard_map/ppermute | solution.py:21

commit v2 on v1

--- a/solution.py
+++ b/solution.py
@@ -27,25 +27,16 @@
     return lax.all_to_all(copies, "band", 0, 0, tiled=True)
 
 
-def split_bf16(x):
+def split_parts(x):
     hi = lax.reduce_precision(x, exponent_bits=8, mantissa_bits=7)
     rest = x - hi
     mid = lax.reduce_precision(rest, exponent_bits=8, mantissa_bits=7)
     lo = rest - mid
-    return [part.astype(jnp.bfloat16) for part in (hi, mid, lo)]
+    return jnp.concatenate([hi, mid, lo], axis=0).astype(jnp.bfloat16)
 
 
-def cell_operator(cell_matrix, connectivity, ext):
-    cells = cell_matrix.shape[0]
-    rows = jnp.arange(ext, dtype=connectivity.dtype)
-    onehot = (connectivity[:, :, None] == rows[None, None, :]).astype(jnp.bfloat16)
-    parts = jnp.concatenate(split_bf16(cell_matrix), axis=2)
-    moved = jnp.einsum("cip,cij->cpj", onehot, parts, preferred_element_type=jnp.float32)
-    moved = moved.astype(jnp.bfloat16)
-    nodes = connectivity.shape[1]
-    left = moved.reshape(cells, ext, 3, nodes).transpose(1, 0, 2, 3).reshape(ext, cells * 3 * nodes)
-    right = jnp.broadcast_to(onehot[:, None], (cells, 3, nodes, ext)).reshape(cells * 3 * nodes, ext)
-    return jnp.dot(left, right, preferred_element_type=jnp.float32)
+def select_rows(tripled, x):
+    return jnp.dot(tripled, split_parts(x), preferred_element_type=jnp.float32)
 
 
 def atom_rows(pieces, coupling, atom_start, atom_count, ext):
@@ -56,9 +47,29 @@
     first = atom_start.astype(jnp.int32)[None, :, None, None]
     shift = (q == first + k * width + t).astype(jnp.float32)
     placed = jnp.einsum("kscj,ksjq->scq", pieces, shift, precision=highest)
-    live = (jnp.arange(slots, dtype=jnp.int32)[:, None] < atom_count.astype(jnp.int32)[None, :])
+    live = jnp.arange(slots, dtype=jnp.int32)[:, None] < atom_count.astype(jnp.int32)[None, :]
     weights = coupling * live.astype(jnp.float32)
     return placed.reshape(slots * channels, ext), weights.reshape(slots * channels)
+
+
+def make_operator(cell_matrix, connectivity, placed, weights, ext):
+    cells, nodes, _ = cell_matrix.shape
+    rows = jnp.arange(ext, dtype=connectivity.dtype)
+    onehot = (connectivity.reshape(cells * nodes)[:, None] == rows[None, :]).astype(jnp.bfloat16)
+    gather3 = jnp.concatenate([onehot] * 3, axis=1)
+    scatter3 = jnp.concatenate([onehot.T] * 3, axis=1)
+
+    def apply(x):
+        gathered = select_rows(gather3, x).reshape(cells, nodes, x.shape[1])
+        local = jnp.einsum(
+            "cij,cjb->cib", cell_matrix, gathered, precision=highest,
+            preferred_element_type=jnp.float32,
+        )
+        out = select_rows(scatter3, local.reshape(cells * nodes, x.shape[1]))
+        coefficients = jnp.dot(placed, x, precision=highest) * weights[:, None]
+        return out + jnp.dot(placed.T, coefficients, precision=highest)
+
+    return apply
 
 
 def on_device(
@@ -74,14 +85,10 @@
     high = from_right(wavefunctions[:g], "dom")
     extended = jnp.concatenate([low, wavefunctions, high], axis=0)
 
-    cells = cell_operator(cell_matrix, connectivity, ext)
     placed, weights = atom_rows(gather_band(projector), coupling, atom_start, atom_count, ext)
-    operator = cells + jnp.dot((placed * weights[:, None]).T, placed, precision=highest)
+    apply = make_operator(cell_matrix, connectivity, placed, weights, ext)
 
-    coefficients = jnp.dot(placed, extended, precision=highest) * weights[:, None]
-    first = jnp.dot(cells, extended, precision=highest) + jnp.dot(
-        placed.T, coefficients, precision=highest
-    )
+    first = apply(extended)
     left_sums = from_left(first[ext - 2 * g :], "dom")
     right_sums = from_right(first[: 2 * g], "dom")
     zeros_side = jnp.zeros((ext - 2 * g, first.shape[1]), jnp.float32)
@@ -98,7 +105,7 @@
     step_ext = jnp.where(keep, step_ext, 0.0)
     step_one = step_ext[g : g + own]
 
-    second = jnp.dot(operator, step_ext, precision=highest)
+    second = apply(step_ext)
     from_before = from_left(second[ext - g :], "dom")
     from_after = from_right(second[:g], "dom")
     owned = second[g : g + own]

time: 70.3 us -> 78.1 us (1.11)
  other arithmetic: 4.35 us -> 8.17 us
  local copies, waits for them, and re-layouts: 10 us -> 11.7 us
  matrix products: 17.1 us -> 18.3 us
    convert_element_type x2 -> x0, local copies, waits for them, and re-layouts: 6.77 us -> none  [the longest x1 6.06 us: cell_operator(): moved = moved.astype(jnp.bfloat16)]
    dot_general x0 -> x2, local copies, waits for them, and re-layouts: none -> 5.09 us  [apply(): jnp.einsum('cij,cjb->cib', cell_matrix, gathered, precision=highest, pref...]
    another operation x0 -> x5, other arithmetic: none -> 4.68 us
    unnamed x8 -> x31, local copies, waits for them, and re-layouts: 0.06 us -> 3.29 us
    eq x0 -> x2, other arithmetic: none -> 2.57 us  [make_operator(): connectivity.reshape(cells * nodes)[:, None] == rows[None, :]]
    convert_element_type x2 -> x0, other arithmetic: 2.56 us -> none  [the longest x1 2.1 us: split_bf16(): return [part.astype(jnp.bfloat16) for part in (hi, mid, lo)]]
    dot_general x7 -> x10, matrix products: 15.3 us -> 16.5 us  [the longest x2 9.24 us: apply(): jnp.einsum('cij,cjb->cib', cell_matrix, gathered, precision=highest, pref...]
    ppermute x3, waiting for transfers between devices: 6.09 us -> 4.89 us  [from_right(): return lax.ppermute(x, axis, [(i + 1, i) for i in range(count - 1)])]
  transfers between devices with their start and end apart: 7 -> 7, of which waited for: 3 -> 4; matrix products, arithmetic and copies ran while one was open for 35% -> 10% of each run, Pallas kernels for 0% -> 0%
where the time goes in v2:
time: 78.1 us; the launch traced here: 77.4 us
  starting transfers between devices  21.8 us (28%)
  matrix products  18.3 us (23%)
  waiting for transfers between devices  16.4 us (21%)
  local copies, waits for them, and re-layouts  11.7 us (15%)
  other arithmetic  8.17 us (10%)
  between operations  1.01 us (1%)
    ppermute x3, starting transfers between devices, from_left(): return lax.ppermute(x, axis, [(i, i + 1) for i in range(count - 1)])  14.5 us
    ppermute x3, waiting for transfers between devices, from_left(): return lax.ppermute(x, axis, [(i, i + 1) for i in range(count - 1)])  11 us
    dot_general x2, matrix products, apply(): jnp.einsum('cij,cjb->cib', cell_matrix, gathered, precision=highest, pref...  9.24 us
    dot_general x2, local copies, waits for them, and re-layouts, apply(): jnp.einsum('cij,cjb->cib', cell_matrix, gathered, precision=highest, pref...  5.09 us
    ppermute x3, waiting for transfers between devices, from_right(): return lax.ppermute(x, axis, [(i + 1, i) for i in range(count - 1)])  4.89 us
    dot_general x4, matrix products, select_rows(): return jnp.dot(tripled, split_parts(x), preferred_element_type=jnp.float32)  4.88 us
    another operation x5, other arithmetic  4.68 us
    ppermute x3, starting transfers between devices, from_right(): return lax.ppermute(x, axis, [(i + 1, i) for i in range(count - 1)])  4.04 us
  transfers between devices with their start and end apart: 7, of which 4 were waited for; matrix products, arithmetic and copies ran while one was open for 10% of the time, Pallas kernels for 0%

profile of v2, /device:TPU:0, one launch (start us, length us, event | category | flops | bytes accessed | tf_op | source)
XLA Modules:
  0.0 77.4 jit_solution(6536220098248923197)
XLA Ops:
  0.0 0.0 copy-start
  0.0 1.8 %fusion.48 = (f32[128,256]{1,0:T(8,128)}, f32[128,256]{1,0:T(8,128)S(1)}) fusion(f32[384,256]{1,0:T(8,128)} %param.7), kind=kLoop, calls=%fused_computation.86 | loop fusion | bytes 524288 | tf_op jit(solution)/shard_map/slice | solution.py:85
  1.8 5.5 %collective-permute-start = (f32[128,256]{1,0:T(8,128)S(1)}, f32[128,256]{1,0:T(8,128)}, u32[]{:S(2)}, u32[]{:S(2)}) collective-permute-start(f32[128,256]{1,0:T(8,128)S(1)} %get-tuple-element.23), channel_id=1, source_target_pairs={{0,4},{4,8},{8,12},{12,16},{16,20},{20,24},{24,28},{1,5},{5,9},{9,... | collective-permute-start | bytes 393224 | tf_op jit(solution)/shard_map/ppermute | solution.py:16
  7.3 1.3 %collective-permute-start.1 = (f32[128,256]{1,0:T(8,128)}, f32[128,256]{1,0:T(8,128)S(1)}, u32[]{:S(2)}, u32[]{:S(2)}) collective-permute-start(f32[128,256]{1,0:T(8,128)} %get-tuple-element.22), channel_id=1, source_target_pairs={{4,0},{8,4},{12,8},{16,12},{20,16},{24,20},{28,24},{5,1},{9,5},{13... | collective-permute-start | bytes 393224 | tf_op jit(solution)/shard_map/ppermute | solution.py:21
  8.6 1.4 %broadcast_in_dim.11 = f32[4,4,16,128]{3,2,1,0:T(8,128)} broadcast(f32[4,16,128]{2,1,0:T(8,128)} %param.10), dimensions={1,2,3} | broadcast | bytes 163840 | tf_op jit(solution)/shard_map/broadcast_in_dim | solution.py:26
  10.0 3.3 %all-to-all-start = ((f32[4,4,16,128]{3,2,1,0:T(8,128)}), f32[4,4,16,128]{3,2,1,0:T(8,128)S(1)}, u32[]{:S(2)}, u32[]{:S(2)}) async-start(f32[4,4,16,128]{3,2,1,0:T(8,128)} %broadcast_in_dim.11), calls=%async_computation | async-start | bytes 262144 | tf_op jit(solution)/shard_map/all_to_all | solution.py:27
  13.4 0.7 copy.22
  14.0 1.3 %iota_compare_fusion = pred[1024,640]{1,0:T(32,128)(4,1)} fusion(s32[1024]{0:T(1024)S(1)} %bitcast.48), kind=kLoop, calls=%fused_computation.6 | loop fusion | flops 655360 | bytes 659456 | tf_op jit(solution)/shard_map/eq | solution.py:58
  15.3 1.3 %iota_compare_fusion.1 = pred[640,1024]{1,0:T(32,128)(4,1)} fusion(s32[1024]{0:T(1024)S(1)} %bitcast.49), kind=kLoop, calls=%fused_computation.7 | loop fusion | flops 655360 | bytes 659456 | tf_op jit(solution)/shard_map/eq | solution.py:58
  17.3 0.1 broadcast_multiply_fusion
  17.4 0.1 mul.48
  17.4 0.5 all-to-all-done
  18.0 1.8 %fusion = f32[4,640,16,1]{1,2,3,0:T(8,128)S(1)} fusion(s32[4]{0:T(128)S(1)} %iota_multiply_fusion, s32[4]{0:T(128)S(1)} %copy-done.13, f32[4,4,16,128]{3,2,1,0:T(8,128)S(1)} %all-to-all-done), kind=kOutput, calls=%fused_computation.3 | convolution fusion | flops 255590400 | bytes 294944 | tf_op jit(solution)/shard_map/kscj,ksjq->scq/dot_general | solution.py:49
  19.8 0.0 collective-permute-done
  19.8 1.0 %constant_dynamic-update-slice_fusion.2 = f32[640,256]{1,0:T(8,128)S(1)} fusion(f32[128,256]{1,0:T(8,128)} %collective-permute-done), kind=kLoop, calls=%fused_computation.67 | loop fusion | bytes 262144
  20.9 0.0 collective-permute-done.1
  20.9 0.2 reduce-precision_convert_fusion.7
  21.1 1.3 %fusion.15 = f32[1024,256]{1,0:T(8,128)S(1)} fusion(pred[1024,640]{1,0:T(32,128)(4,1)S(1)} %copy-done.9, bf16[640,256]{1,0:T(8,128)(2,1)S(1)} %get-tuple-element.20, bf16[640,256]{1,0:T(8,128)(2,1)S(1)} %get-tuple-element.21, bf16[640,256]{1,0:T(8,128)(2,1)S(1)} %get-tuple-element.19), kind=kOutput, calls=%fused_computation.32 | convolution fusion | flops 1013514240 | bytes 2686976 | tf_op jit(solution)/shard_map/dot_general | solution.py:39
  22.3 4.6 %convolution_bitcast_fusion.1 = f32[2,512,256]{1,2,0:T(8,128)} fusion(f32[2,512,256]{2,1,0:T(8,128)S(1)} %bitcast.47, f32[2,512,512]{2,1,0:T(8,128)S(1)} %copy-done), kind=kOutput, calls=%fused_computation.29 | convolution fusion | flops 1610612736 | bytes 4194304 | tf_op jit(solution)/shard_map/cij,cjb->cib/dot_general | solution.py:64
  27.0 2.5 %copy.15 = f32[2,512,256]{2,1,0:T(8,128)} copy(f32[2,512,256]{1,2,0:T(8,128)} %convolution_bitcast_fusion.1) | data formatting | bytes 2097152 | tf_op jit(solution)/shard_map/cij,cjb->cib/dot_general | solution.py:64
  29.5 1.5 %reduce-precision_convert_fusion.3 = (bf16[1024,256]{1,0:T(8,128)(2,1)S(1)}, bf16[1024,256]{1,0:T(8,128)(2,1)S(1)}, bf16[1024,256]{1,0:T(8,128)(2,1)S(1)}) fusion(f32[2,512,256]{2,1,0:T(8,128)} %copy.15), kind=kLoop, calls=%fused_computation.27 | loop fusion | flops 1835008 | bytes 2621440 | tf_op jit(solution)/shard_map/convert.8
  31.0 0.4 convolution_multiply_fusion.1
  31.5 0.0 copy-done.7
  31.5 1.2 %fusion.3 = f32[640,256]{1,0:T(8,128)S(1)} fusion(bf16[1024,256]{1,0:T(8,128)(2,1)S(1)} %get-tuple-element.11, bf16[1024,256]{1,0:T(8,128)(2,1)S(1)} %get-tuple-element.12, bf16[1024,256]{1,0:T(8,128)(2,1)S(1)} %get-tuple-element.10, pred[640,1024]{1,0:T(32,128)(4,1)S(1)} %copy-done.7), kind=kOutput, calls=%fused_computation.8 | convolution fusion | flops 1015283712 | bytes 2883584 | tf_op jit(solution)/shard_map/dot_general | solution.py:39
  32.7 0.7 convolution_add_fusion.1
  33.4 0.8 %copy-done.1 = f32[640,256]{1,0:T(8,128)} copy-done((f32[640,256]{1,0:T(8,128)}, f32[640,256]{1,0:T(8,128)S(1)}, u32[]{:S(2)}) %copy-start.1) | copy-done | bytes 655384
  34.3 4.6 %collective-permute-start.2 = (f32[256,256]{1,0:T(8,128)S(1)}, f32[256,256]{1,0:T(8,128)S(1)}, u32[]{:S(2)}, u32[]{:S(2)}) collective-permute-start(f32[256,256]{1,0:T(8,128)S(1)} %get-tuple-element.17), channel_id=1, source_target_pairs={{0,4},{4,8},{8,12},{12,16},{16,20},{20,24},{24,28},{1,5},{5,9},{9,... | collective-permute-start | bytes 786440 | tf_op jit(solution)/shard_map/ppermute | solution.py:16
  38.9 1.5 %collective-permute-start.3 = (f32[256,256]{1,0:T(8,128)S(1)}, f32[256,256]{1,0:T(8,128)}, u32[]{:S(2)}, u32[]{:S(2)}) collective-permute-start(f32[256,256]{1,0:T(8,128)S(1)} %get-tuple-element.18), channel_id=1, source_target_pairs={{4,0},{8,4},{12,8},{16,12},{20,16},{24,20},{28,24},{5,1},{9,5},{13... | collective-permute-start | bytes 786440 | tf_op jit(solution)/shard_map/ppermute | solution.py:21
  40.4 9.8 %collective-permute-done.2 = f32[256,256]{1,0:T(8,128)S(1)} collective-permute-done((f32[256,256]{1,0:T(8,128)S(1)}, f32[256,256]{1,0:T(8,128)S(1)}, u32[]{:S(2)}, u32[]{:S(2)}) %collective-permute-start.2) | collective-permute-done | bytes 262176 | tf_op jit(solution)/shard_map/ppermute | solution.py:16
  50.2 0.7 copy-done.11
  50.9 0.0 collective-permute-done.3
  50.9 1.4 %reduce-precision_convert_fusion.5 = (bf16[640,256]{1,0:T(8,128)(2,1)S(1)}, f32[640,256]{1,0:T(8,128)S(1)}) fusion(f32[640,256]{1,0:T(8,128)S(1)} %constant_dynamic-update-slice_fusion, f32[256,256]{1,0:T(8,128)} %collective-permute-done.3, f32[640,256]{1,0:T(8,128)} %copy-done.1, f32[256,256]{1,0:T(8,128)} %copy-done.11, pred[640]{0:T(1024)(128)(4,1)S(1)} %fusion.36), kind=kLoop, calls=%fused_computation.51 | loop fusion | flops 1310720 | bytes 2818688 | tf_op jit(solution)/shard_map/convert.5
  52.3 0.1 reduce-precision_convert_fusion.4
  52.4 0.0 copy-done.5
  52.4 0.5 convolution_multiply_fusion
  52.9 1.3 %fusion.16 = f32[1024,256]{1,0:T(8,128)S(1)} fusion(pred[1024,640]{1,0:T(32,128)(4,1)S(1)} %copy-done.10, bf16[640,256]{1,0:T(8,128)(2,1)S(1)} %get-tuple-element.16, bf16[640,256]{1,0:T(8,128)(2,1)S(1)} %get-tuple-element.15, bf16[640,256]{1,0:T(8,128)(2,1)S(1)} %get-tuple-element.5), kind=kOutput, calls=%fused_computation.33 | convolution fusion | flops 1013514240 | bytes 2686976 | tf_op jit(solution)/shard_map/dot_general | solution.py:39
  54.1 4.6 %convolution_bitcast_fusion = f32[2,512,256]{1,2,0:T(8,128)} fusion(f32[2,512,256]{2,1,0:T(8,128)S(1)} %bitcast.46, f32[2,512,512]{2,1,0:T(8,128)S(1)} %copy-done), kind=kOutput, calls=%fused_computation.28 | convolution fusion | flops 1610612736 | bytes 4194304 | tf_op jit(solution)/shard_map/cij,cjb->cib/dot_general | solution.py:64
  58.8 2.6 %copy.18 = f32[2,512,256]{2,1,0:T(8,128)} copy(f32[2,512,256]{1,2,0:T(8,128)} %convolution_bitcast_fusion) | data formatting | bytes 2097152 | tf_op jit(solution)/shard_map/cij,cjb->cib/dot_general | solution.py:64
  61.3 1.5 %reduce-precision_convert_fusion.1 = (bf16[1024,256]{1,0:T(8,128)(2,1)S(1)}, bf16[1024,256]{1,0:T(8,128)(2,1)S(1)}, bf16[1024,256]{1,0:T(8,128)(2,1)S(1)}) fusion(f32[2,512,256]{2,1,0:T(8,128)} %copy.18), kind=kLoop, calls=%fused_computation.23 | loop fusion | flops 1835008 | bytes 2621440 | tf_op jit(solution)/shard_map/convert.2
  62.8 0.0 copy-done.8
  62.8 1.2 %fusion.9 = f32[640,256]{1,0:T(8,128)S(1)} fusion(bf16[1024,256]{1,0:T(8,128)(2,1)S(1)} %get-tuple-element.8, bf16[1024,256]{1,0:T(8,128)(2,1)S(1)} %get-tuple-element.9, bf16[1024,256]{1,0:T(8,128)(2,1)S(1)} %get-tuple-element.7, pred[640,1024]{1,0:T(32,128)(4,1)S(1)} %copy-done.8), kind=kOutput, calls=%fused_computation.14 | convolution fusion | flops 1015283712 | bytes 2883584 | tf_op jit(solution)/shard_map/dot_general | solution.py:39
  64.0 0.0 copy-start.3
  64.0 0.7 convolution_add_fusion
  64.8 4.4 %collective-permute-start.4 = (f32[128,256]{1,0:T(8,128)S(1)}, f32[128,256]{1,0:T(8,128)S(1)}, u32[]{:S(2)}, u32[]{:S(2)}) collective-permute-start(f32[128,256]{1,0:T(8,128)S(1)} %get-tuple-element.13), channel_id=1, source_target_pairs={{0,4},{4,8},{8,12},{12,16},{16,20},{20,24},{24,28},{1,5},{5,9},{9,... | collective-permute-start | bytes 393224 | tf_op jit(solution)/shard_map/ppermute | solution.py:16
  69.2 1.3 %collective-permute-start.5 = (f32[128,256]{1,0:T(8,128)S(1)}, f32[128,256]{1,0:T(8,128)S(1)}, u32[]{:S(2)}, u32[]{:S(2)}) collective-permute-start(f32[128,256]{1,0:T(8,128)S(1)} %get-tuple-element.14), channel_id=1, source_target_pairs={{4,0},{8,4},{12,8},{16,12},{20,16},{24,20},{28,24},{5,1},{9,5},{13... | collective-permute-start | bytes 393224 | tf_op jit(solution)/shard_map/ppermute | solution.py:21
  70.5 1.2 %collective-permute-done.4 = f32[128,256]{1,0:T(8,128)S(1)} collective-permute-done((f32[128,256]{1,0:T(8,128)S(1)}, f32[128,256]{1,0:T(8,128)S(1)}, u32[]{:S(2)}, u32[]{:S(2)}) %collective-permute-start.4) | collective-permute-done | bytes 131104 | tf_op jit(solution)/shard_map/ppermute | solution.py:16
  71.7 4.9 %collective-permute-done.5 = f32[128,256]{1,0:T(8,128)S(1)} collective-permute-done((f32[128,256]{1,0:T(8,128)S(1)}, f32[128,256]{1,0:T(8,128)S(1)}, u32[]{:S(2)}, u32[]{:S(2)}) %collective-permute-start.5) | collective-permute-done | bytes 131104 | tf_op jit(solution)/shard_map/ppermute | solution.py:21
  76.6 0.8 %fusion.32 = f32[384,256]{1,0:T(8,128)} fusion(f32[384,256]{1,0:T(8,128)S(1)} %copy-done.3, f32[640,256]{1,0:T(8,128)S(1)} %get-tuple-element.6, f32[640,256]{1,0:T(8,128)S(1)} %convolution_add_fusion, f32[128,256]{1,0:T(8,128)S(1)} %collective-permute-done.5, f32[128,256]{1,0:T(8,128)S(1)} %collective-permute-done.4), kind=kLoop, calls=%fused_computation.61 | loop fusion | flops 491520 | bytes 1835008 | tf_op jit(solution)/shard_map/sub | solution.py:118
  (28 shorter events, 0.1 us)
Async XLA Ops:
  0.0 22.3 %copy-start = (f32[2,512,512]{2,1,0:T(8,128)S(1)}, f32[2,512,512]{2,1,0:T(8,128)}, u32[]{:S(2)}) copy-start(f32[2,512,512]{2,1,0:T(8,128)} %param.8) | copy-start | bytes 6291460
  0.0 17.3 %copy-start.12 = (f32[4,16]{1,0:T(4,128)S(1)}, f32[4,16]{1,0:T(4,128)}, u32[]{:S(2)}) copy-start(f32[4,16]{1,0:T(4,128)} %param.11) | copy-start | bytes 772
  0.0 17.9 %copy-start.13 = (s32[4]{0:T(128)S(1)}, s32[4]{0:T(128)}, u32[]{:S(2)}) copy-start(s32[4]{0:T(128)} %param.12) | copy-start | bytes 52
  1.8 18.0 %collective-permute-start = (f32[128,256]{1,0:T(8,128)S(1)}, f32[128,256]{1,0:T(8,128)}, u32[]{:S(2)}, u32[]{:S(2)}) collective-permute-start(f32[128,256]{1,0:T(8,128)S(1)} %get-tuple-element.23), channel_id=1, source_target_pairs={{0,4},{4,8},{8,12},{12,16},{16,20},{20,24},{24,28},{1,5},{5,9},{9,... | collective-permute-start | bytes 393224 | tf_op jit(solution)/shard_map/ppermute | solution.py:16
  7.3 13.5 %collective-permute-start.1 = (f32[128,256]{1,0:T(8,128)}, f32[128,256]{1,0:T(8,128)S(1)}, u32[]{:S(2)}, u32[]{:S(2)}) collective-permute-start(f32[128,256]{1,0:T(8,128)} %get-tuple-element.22), channel_id=1, source_target_pairs={{4,0},{8,4},{12,8},{16,12},{20,16},{24,20},{28,24},{5,1},{9,5},{13... | collective-permute-start | bytes 393224 | tf_op jit(solution)/shard_map/ppermute | solution.py:21
  10.0 7.9 %all-to-all-start = ((f32[4,4,16,128]{3,2,1,0:T(8,128)}), f32[4,4,16,128]{3,2,1,0:T(8,128)S(1)}, u32[]{:S(2)}, u32[]{:S(2)}) async-start(f32[4,4,16,128]{3,2,1,0:T(8,128)} %broadcast_in_dim.11), calls=%async_computation | async-start | bytes 262144 | tf_op jit(solution)/shard_map/all_to_all | solution.py:27
  17.4 3.4 %copy-start.2 = (f32[384,256]{1,0:T(8,128)S(1)}, f32[384,256]{1,0:T(8,128)}, u32[]{:S(2)}) copy-start(f32[384,256]{1,0:T(8,128)} %param.7) | copy-start | bytes 1179652
  19.8 12.9 %copy-start.4 = (f32[4,640,16,1]{1,2,3,0:T(8,128)}, f32[4,640,16,1]{1,2,3,0:T(8,128)S(1)}, u32[]{:S(2)}) copy-start(f32[4,640,16,1]{1,2,3,0:T(8,128)S(1)} %fusion) | copy-start | bytes 491524
  19.8 1.3 %copy-start.9 = (pred[1024,640]{1,0:T(32,128)(4,1)S(1)}, pred[1024,640]{1,0:T(32,128)(4,1)}, u32[]{:S(2)}) copy-start(pred[1024,640]{1,0:T(32,128)(4,1)} %iota_compare_fusion) | copy-start | bytes 1966084
  29.5 2.0 %copy-start.7 = (pred[640,1024]{1,0:T(32,128)(4,1)S(1)}, pred[640,1024]{1,0:T(32,128)(4,1)}, u32[]{:S(2)}) copy-start(pred[640,1024]{1,0:T(32,128)(4,1)} %iota_compare_fusion.1) | copy-start | bytes 1966084
  33.4 0.8 %copy-start.1 = (f32[640,256]{1,0:T(8,128)}, f32[640,256]{1,0:T(8,128)S(1)}, u32[]{:S(2)}) copy-start(f32[640,256]{1,0:T(8,128)S(1)} %convolution_add_fusion.1) | copy-start | bytes 1966084
  34.3 15.9 %collective-permute-start.2 = (f32[256,256]{1,0:T(8,128)S(1)}, f32[256,256]{1,0:T(8,128)S(1)}, u32[]{:S(2)}, u32[]{:S(2)}) collective-permute-start(f32[256,256]{1,0:T(8,128)S(1)} %get-tuple-element.17), channel_id=1, source_target_pairs={{0,4},{4,8},{8,12},{12,16},{16,20},{20,24},{24,28},{1,5},{5,9},{9,... | collective-permute-start | bytes 786440 | tf_op jit(solution)/shard_map/ppermute | solution.py:16
  38.9 12.0 %collective-permute-start.3 = (f32[256,256]{1,0:T(8,128)S(1)}, f32[256,256]{1,0:T(8,128)}, u32[]{:S(2)}, u32[]{:S(2)}) collective-permute-start(f32[256,256]{1,0:T(8,128)S(1)} %get-tuple-element.18), channel_id=1, source_target_pairs={{4,0},{8,4},{12,8},{16,12},{20,16},{24,20},{28,24},{5,1},{9,5},{13... | collective-permute-start | bytes 786440 | tf_op jit(solution)/shard_map/ppermute | solution.py:21
  40.4 12.0 %copy-start.5 = (f32[4,640,16,1]{1,2,3,0:T(8,128)S(1)}, f32[4,640,16,1]{1,2,3,0:T(8,128)}, u32[]{:S(2)}) copy-start(f32[4,640,16,1]{1,2,3,0:T(8,128)} %copy-done.4) | copy-start | bytes 491524
  40.4 12.5 %copy-start.10 = (pred[1024,640]{1,0:T(32,128)(4,1)S(1)}, pred[1024,640]{1,0:T(32,128)(4,1)}, u32[]{:S(2)}) copy-start(pred[1024,640]{1,0:T(32,128)(4,1)} %iota_compare_fusion) | copy-start | bytes 1966084
  50.2 0.7 copy-start.11
  58.8 4.1 %copy-start.8 = (pred[640,1024]{1,0:T(32,128)(4,1)S(1)}, pred[640,1024]{1,0:T(32,128)(4,1)}, u32[]{:S(2)}) copy-start(pred[640,1024]{1,0:T(32,128)(4,1)} %iota_compare_fusion.1) | copy-start | bytes 1966084
  62.8 1.2 %copy-start.6 = (f32[4,640,16,1]{1,2,3,0:T(8,128)S(1)}, f32[4,640,16,1]{1,2,3,0:T(8,128)}, u32[]{:S(2)}) copy-start(f32[4,640,16,1]{1,2,3,0:T(8,128)} %copy-done.4) | copy-start | bytes 491524
  64.0 12.5 %copy-start.3 = (f32[384,256]{1,0:T(8,128)S(1)}, f32[384,256]{1,0:T(8,128)}, u32[]{:S(2)}) copy-start(f32[384,256]{1,0:T(8,128)} %param.7) | copy-start | bytes 1179652
  64.8 6.9 %collective-permute-start.4 = (f32[128,256]{1,0:T(8,128)S(1)}, f32[128,256]{1,0:T(8,128)S(1)}, u32[]{:S(2)}, u32[]{:S(2)}) collective-permute-start(f32[128,256]{1,0:T(8,128)S(1)} %get-tuple-element.13), channel_id=1, source_target_pairs={{0,4},{4,8},{8,12},{12,16},{16,20},{20,24},{24,28},{1,5},{5,9},{9,... | collective-permute-start | bytes 393224 | tf_op jit(solution)/shard_map/ppermute | solution.py:16
  69.2 7.4 %collective-permute-start.5 = (f32[128,256]{1,0:T(8,128)S(1)}, f32[128,256]{1,0:T(8,128)S(1)}, u32[]{:S(2)}, u32[]{:S(2)}) collective-permute-start(f32[128,256]{1,0:T(8,128)S(1)} %get-tuple-element.14), channel_id=1, source_target_pairs={{4,0},{8,4},{12,8},{16,12},{20,16},{24,20},{28,24},{5,1},{9,5},{13... | collective-permute-start | bytes 393224 | tf_op jit(solution)/shard_map/ppermute | solution.py:21

commit v3 on v1

--- a/solution.py
+++ b/solution.py
@@ -27,27 +27,6 @@
     return lax.all_to_all(copies, "band", 0, 0, tiled=True)
 
 
-def split_bf16(x):
-    hi = lax.reduce_precision(x, exponent_bits=8, mantissa_bits=7)
-    rest = x - hi
-    mid = lax.reduce_precision(rest, exponent_bits=8, mantissa_bits=7)
-    lo = rest - mid
-    return [part.astype(jnp.bfloat16) for part in (hi, mid, lo)]
-
-
-def cell_operator(cell_matrix, connectivity, ext):
-    cells = cell_matrix.shape[0]
-    rows = jnp.arange(ext, dtype=connectivity.dtype)
-    onehot = (connectivity[:, :, None] == rows[None, None, :]).astype(jnp.bfloat16)
-    parts = jnp.concatenate(split_bf16(cell_matrix), axis=2)
-    moved = jnp.einsum("cip,cij->cpj", onehot, parts, preferred_element_type=jnp.float32)
-    moved = moved.astype(jnp.bfloat16)
-    nodes = connectivity.shape[1]
-    left = moved.reshape(cells, ext, 3, nodes).transpose(1, 0, 2, 3).reshape(ext, cells * 3 * nodes)
-    right = jnp.broadcast_to(onehot[:, None], (cells, 3, nodes, ext)).reshape(cells * 3 * nodes, ext)
-    return jnp.dot(left, right, preferred_element_type=jnp.float32)
-
-
 def atom_rows(pieces, coupling, atom_start, atom_count, ext):
     count, slots, channels, width = pieces.shape
     t = lax.broadcasted_iota(jnp.int32, (count, slots, width, ext), 2)
@@ -56,9 +35,23 @@
     first = atom_start.astype(jnp.int32)[None, :, None, None]
     shift = (q == first + k * width + t).astype(jnp.float32)
     placed = jnp.einsum("kscj,ksjq->scq", pieces, shift, precision=highest)
-    live = (jnp.arange(slots, dtype=jnp.int32)[:, None] < atom_count.astype(jnp.int32)[None, :])
+    live = jnp.arange(slots, dtype=jnp.int32)[:, None] < atom_count.astype(jnp.int32)[None, :]
     weights = coupling * live.astype(jnp.float32)
     return placed.reshape(slots * channels, ext), weights.reshape(slots * channels)
+
+
+def cell_operator(cell_matrix, connectivity, ext):
+    cells, nodes, _ = cell_matrix.shape
+    rows = jnp.arange(ext, dtype=connectivity.dtype)
+    onehot = (connectivity[:, :, None] == rows[None, None, :]).astype(jnp.float32)
+    total = None
+    for c in range(cells):
+        moved = jnp.dot(cell_matrix[c], onehot[c], precision=lax.Precision.HIGH)
+        part = lax.dot_general(
+            onehot[c], moved, (((0,), (0,)), ((), ())), precision=lax.Precision.HIGH
+        )
+        total = part if total is None else total + part
+    return total
 
 
 def on_device(
@@ -74,8 +67,8 @@
     high = from_right(wavefunctions[:g], "dom")
     extended = jnp.concatenate([low, wavefunctions, high], axis=0)
 
+    placed, weights = atom_rows(gather_band(projector), coupling, atom_start, atom_count, ext)
     cells = cell_operator(cell_matrix, connectivity, ext)
-    placed, weights = atom_rows(gather_band(projector), coupling, atom_start, atom_count, ext)
     operator = cells + jnp.dot((placed * weights[:, None]).T, placed, precision=highest)
 
     coefficients = jnp.dot(placed, extended, precision=highest) * weights[:, None]

time: 70.3 us -> 63.2 us (0.90)
  local copies, waits for them, and re-layouts: 10 us -> 3.31 us
  other arithmetic: 4.35 us -> 2.38 us
  matrix products: 17.1 us -> 18.2 us
    convert_element_type x2 -> x0, local copies, waits for them, and re-layouts: 6.77 us -> none  [the longest x1 6.06 us: cell_operator(): moved = moved.astype(jnp.bfloat16)]
    convert_element_type x2 -> x0, other arithmetic: 2.56 us -> none  [the longest x1 2.1 us: split_bf16(): return [part.astype(jnp.bfloat16) for part in (hi, mid, lo)]]
    eq x0 -> x1, other arithmetic: none -> 1.27 us  [cell_operator(): connectivity[:, :, None] == rows[None, None, :]]
    dot_general x1, matrix products: 1.85 us -> 2.79 us  [atom_rows(): placed = jnp.einsum('kscj,ksjq->scq', pieces, shift, precision=highest)]
    dot_general x2 -> x4, matrix products: 9.04 us -> 9.16 us  [the longest x2 4.76 us: cell_operator(): moved = jnp.dot(cell_matrix[c], onehot[c], precision=lax.Precision.HIGH)]
  transfers between devices with their start and end apart: 7 -> 7, of which waited for: 3 -> 3; matrix products, arithmetic and copies ran while one was open for 35% -> 26% of each run, Pallas kernels for 0% -> 0%
where the time goes in v3:
time: 63.2 us; the launch traced here: 62.7 us
  starting transfers between devices  21.8 us (34%)
  matrix products  18.2 us (29%)
  waiting for transfers between devices  16.1 us (25%)
  local copies, waits for them, and re-layouts  3.31 us (5%)
  other arithmetic  2.38 us (4%)
  between operations  0.92 us (1%)
    ppermute x3, starting transfers between devices, from_left(): return lax.ppermute(x, axis, [(i, i + 1) for i in range(count - 1)])  13.8 us
    ppermute x3, waiting for transfers between devices, from_left(): return lax.ppermute(x, axis, [(i, i + 1) for i in range(count - 1)])  9.99 us
    ppermute x3, waiting for transfers between devices, from_right(): return lax.ppermute(x, axis, [(i + 1, i) for i in range(count - 1)])  6.1 us
    dot_general x2, matrix products, cell_operator(): moved = jnp.dot(cell_matrix[c], onehot[c], precision=lax.Precision.HIGH)  4.76 us
    dot_general x2, matrix products, cell_operator(): lax.dot_general(onehot[c], moved, (((0,), (0,)), ((), ())), precision=lax...  4.41 us
    ppermute x3, starting transfers between devices, from_right(): return lax.ppermute(x, axis, [(i + 1, i) for i in range(count - 1)])  4.06 us
    all_to_all x1, starting transfers between devices, gather_band(): return lax.all_to_all(copies, 'band', 0, 0, tiled=True)  3.94 us
    dot_general x1, matrix products, atom_rows(): placed = jnp.einsum('kscj,ksjq->scq', pieces, shift, precision=highest)  2.79 us
  transfers between devices with their start and end apart: 7, of which 3 were waited for; matrix products, arithmetic and copies ran while one was open for 26% of the time, Pallas kernels for 0%

profile of v3, /device:TPU:0, one launch (start us, length us, event | category | flops | bytes accessed | tf_op | source)
XLA Modules:
  0.0 62.7 jit_solution(7873716696142184122)
XLA Ops:
  0.0 1.7 %fusion.30 = (f32[128,256]{1,0:T(8,128)}, f32[128,256]{1,0:T(8,128)}) fusion(f32[384,256]{1,0:T(8,128)} %param.7), kind=kLoop, calls=%fused_computation.45 | loop fusion | bytes 524288 | tf_op jit(solution)/shard_map/slice | solution.py:67
  1.7 4.9 %collective-permute-start = (f32[128,256]{1,0:T(8,128)}, f32[128,256]{1,0:T(8,128)S(1)}, u32[]{:S(2)}, u32[]{:S(2)}) collective-permute-start(f32[128,256]{1,0:T(8,128)} %get-tuple-element.10), channel_id=1, source_target_pairs={{0,4},{4,8},{8,12},{12,16},{16,20},{20,24},{24,28},{1,5},{5,9},{9,... | collective-permute-start | bytes 393224 | tf_op jit(solution)/shard_map/ppermute | solution.py:16
  6.5 1.3 %collective-permute-start.1 = (f32[128,256]{1,0:T(8,128)}, f32[128,256]{1,0:T(8,128)S(1)}, u32[]{:S(2)}, u32[]{:S(2)}) collective-permute-start(f32[128,256]{1,0:T(8,128)} %get-tuple-element.9), channel_id=1, source_target_pairs={{4,0},{8,4},{12,8},{16,12},{20,16},{24,20},{28,24},{5,1},{9,5},{13... | collective-permute-start | bytes 393224 | tf_op jit(solution)/shard_map/ppermute | solution.py:21
  7.8 1.4 %broadcast_in_dim.10 = f32[4,4,16,128]{3,2,1,0:T(8,128)} broadcast(f32[4,16,128]{2,1,0:T(8,128)} %param.10), dimensions={1,2,3} | broadcast | bytes 163840 | tf_op jit(solution)/shard_map/broadcast_in_dim | solution.py:26
  9.3 3.9 %all-to-all-start = ((f32[4,4,16,128]{3,2,1,0:T(8,128)}), f32[4,4,16,128]{3,2,1,0:T(8,128)}, u32[]{:S(2)}, u32[]{:S(2)}) async-start(f32[4,4,16,128]{3,2,1,0:T(8,128)} %broadcast_in_dim.10), calls=%async_computation | async-start | bytes 262144 | tf_op jit(solution)/shard_map/all_to_all | solution.py:27
  13.2 0.0 copy-start.2
  13.2 1.3 %iota_compare_fusion = pred[2,512,640]{2,1,0:T(32,128)(4,1)S(1)} fusion(s32[2,512]{1,0:T(2,128)} %param.9), kind=kLoop, calls=%fused_computation.4 | loop fusion | flops 655360 | bytes 659456 | tf_op jit(solution)/shard_map/eq | solution.py:46
  14.5 0.0 copy-start
  14.5 2.5 %fusion.8 = f32[640,512]{1,0:T(8,128)S(1)} fusion(f32[2,512,512]{2,1,0:T(8,128)} %param.8, pred[2,512,640]{2,1,0:T(32,128)(4,1)S(1)} %iota_compare_fusion), kind=kOutput, calls=%fused_computation.16 | convolution fusion | flops 1006960640 | bytes 2686976 | tf_op jit(solution)/shard_map/dot_general | solution.py:49
  17.0 0.0 copy-done.2
  17.1 2.2 %fusion.6 = f32[640,512]{1,0:T(8,128)} fusion(f32[2,512,512]{2,1,0:T(8,128)S(1)} %copy-done.2, pred[2,512,640]{2,1,0:T(32,128)(4,1)S(1)} %iota_compare_fusion), kind=kOutput, calls=%fused_computation.14 | convolution fusion | flops 1006960640 | bytes 2686976 | tf_op jit(solution)/shard_map/dot_general | solution.py:49
  19.3 0.0 copy-done
  19.3 0.0 copy-start.3
  19.3 1.5 %fusion.13 = f32[640,640]{1,0:T(8,128)S(1)} fusion(f32[640,512]{1,0:T(8,128)S(1)} %fusion.8, pred[2,512,640]{2,1,0:T(32,128)(4,1)S(1)} %iota_compare_fusion), kind=kOutput, calls=%fused_computation.20 | convolution fusion | flops 1258618880 | bytes 3276800 | tf_op jit(solution)/shard_map/dot_general | solution.py:50
  21.4 0.0 copy-done.3
  21.5 0.1 broadcast_multiply_fusion
  21.5 0.1 mul.53
  21.6 0.0 copy-start.4
  21.6 2.9 %convolution_add_fusion = f32[640,640]{1,0:T(8,128)S(1)} fusion(f32[640,640]{1,0:T(8,128)S(1)} %fusion.13, f32[640,512]{1,0:T(8,128)} %fusion.6, pred[2,512,640]{2,1,0:T(32,128)(4,1)} %copy-done), kind=kOutput, calls=%fused_computation.7 | convolution fusion | flops 1259028480 | bytes 4915200 | tf_op jit(solution)/shard_map/dot_general | solution.py:50
  24.6 0.0 copy-start.1
  24.6 0.0 all-to-all-done
  24.6 0.0 copy-done.4
  24.6 2.8 %fusion = f32[4,640,16,1]{1,2,3,0:T(8,128)S(1)} fusion(s32[4]{0:T(128)S(1)} %iota_multiply_fusion, s32[4]{0:T(128)S(1)} %copy-done.4, f32[4,4,16,128]{3,2,1,0:T(8,128)} %all-to-all-done), kind=kOutput, calls=%fused_computation.1 | convolution fusion | flops 255590400 | bytes 294944 | tf_op jit(solution)/shard_map/kscj,ksjq->scq/dot_general | solution.py:37
  27.4 0.0 collective-permute-done
  27.4 0.0 copy-done.1
  27.5 0.0 collective-permute-done.1
  27.5 0.4 convolution_multiply_fusion
  27.9 0.7 %fusion.31 = f32[640,256]{1,0:T(8,128)S(1)} fusion(f32[64,640]{1,0:T(8,128)S(1)} %bitcast.43, f32[64,256]{1,0:T(8,128)S(1)} %convolution_multiply_fusion), kind=kOutput, calls=%fused_computation.46 | convolution fusion | flops 125829120 | bytes 884736 | tf_op jit(solution)/shard_map/dot_general | solution.py:75
  28.7 1.7 %convolution_add_fusion.1 = f32[640,256]{1,0:T(8,128)S(1)} fusion(f32[640,256]{1,0:T(8,128)S(1)} %fusion.31, f32[640,640]{1,0:T(8,128)S(1)} %convolution_add_fusion, f32[640,256]{1,0:T(8,128)S(1)} %constant_dynamic-update-slice_fusion), kind=kOutput, calls=%fused_computation.12 | convolution fusion | flops 1258455040 | bytes 3604480 | tf_op jit(solution)/shard_map/dot_general | solution.py:75
  30.4 4.6 %collective-permute-start.2 = (f32[256,256]{1,0:T(8,128)S(1)}, f32[256,256]{1,0:T(8,128)S(1)}, u32[]{:S(2)}, u32[]{:S(2)}) collective-permute-start(f32[256,256]{1,0:T(8,128)S(1)} %get-tuple-element.7), channel_id=1, source_target_pairs={{0,4},{4,8},{8,12},{12,16},{16,20},{20,24},{24,28},{1,5},{5,9},{9,... | collective-permute-start | bytes 786440 | tf_op jit(solution)/shard_map/ppermute | solution.py:16
  35.0 1.5 %collective-permute-start.3 = (f32[256,256]{1,0:T(8,128)S(1)}, f32[256,256]{1,0:T(8,128)S(1)}, u32[]{:S(2)}, u32[]{:S(2)}) collective-permute-start(f32[256,256]{1,0:T(8,128)S(1)} %get-tuple-element.8), channel_id=1, source_target_pairs={{4,0},{8,4},{12,8},{16,12},{20,16},{24,20},{28,24},{5,1},{9,5},{13... | collective-permute-start | bytes 786440 | tf_op jit(solution)/shard_map/ppermute | solution.py:21
  36.5 1.6 %fusion.20 = f32[640,640,1]{1,0,2:T(8,128)S(1)} fusion(f32[4,640,16,1]{1,2,3,0:T(8,128)S(1)} %fusion, f32[4,16]{1,0:T(4,128)S(1)} %broadcast_multiply_fusion), kind=kOutput, calls=%fused_computation.27 | convolution fusion | flops 314613760 | bytes 1802496 | tf_op jit(solution)/shard_map/dot_general | solution.py:72
  38.1 8.7 %collective-permute-done.2 = f32[256,256]{1,0:T(8,128)S(1)} collective-permute-done((f32[256,256]{1,0:T(8,128)S(1)}, f32[256,256]{1,0:T(8,128)S(1)}, u32[]{:S(2)}, u32[]{:S(2)}) %collective-permute-start.2) | collective-permute-done | bytes 262176 | tf_op jit(solution)/shard_map/ppermute | solution.py:16
  46.8 0.0 collective-permute-done.3
  46.8 0.2 multiply_select_fusion
  47.0 1.8 %fusion.3 = f32[640,256]{1,0:T(8,128)S(1)} fusion(f32[640,256]{1,0:T(8,128)S(1)} %multiply_select_fusion, f32[640,640]{1,0:T(8,128)S(1)} %convolution_add_fusion, f32[640,640,1]{1,0,2:T(8,128)S(1)} %fusion.20), kind=kOutput, calls=%fused_computation.6 | convolution fusion | flops 1258700800 | bytes 4587520 | tf_op jit(solution)/shard_map/dot_general | solution.py:94
  48.8 4.4 %collective-permute-start.4 = (f32[128,256]{1,0:T(8,128)S(1)}, f32[128,256]{1,0:T(8,128)S(1)}, u32[]{:S(2)}, u32[]{:S(2)}) collective-permute-start(f32[128,256]{1,0:T(8,128)S(1)} %get-tuple-element.5), channel_id=1, source_target_pairs={{0,4},{4,8},{8,12},{12,16},{16,20},{20,24},{24,28},{1,5},{5,9},{9,... | collective-permute-start | bytes 393224 | tf_op jit(solution)/shard_map/ppermute | solution.py:16
  53.2 1.3 %collective-permute-start.5 = (f32[128,256]{1,0:T(8,128)S(1)}, f32[128,256]{1,0:T(8,128)S(1)}, u32[]{:S(2)}, u32[]{:S(2)}) collective-permute-start(f32[128,256]{1,0:T(8,128)S(1)} %get-tuple-element.6), channel_id=1, source_target_pairs={{4,0},{8,4},{12,8},{16,12},{20,16},{24,20},{28,24},{5,1},{9,5},{13... | collective-permute-start | bytes 393224 | tf_op jit(solution)/shard_map/ppermute | solution.py:21
  54.5 1.3 %collective-permute-done.4 = f32[128,256]{1,0:T(8,128)S(1)} collective-permute-done((f32[128,256]{1,0:T(8,128)S(1)}, f32[128,256]{1,0:T(8,128)S(1)}, u32[]{:S(2)}, u32[]{:S(2)}) %collective-permute-start.4) | collective-permute-done | bytes 131104 | tf_op jit(solution)/shard_map/ppermute | solution.py:16
  55.7 6.1 %collective-permute-done.5 = f32[128,256]{1,0:T(8,128)S(1)} collective-permute-done((f32[128,256]{1,0:T(8,128)S(1)}, f32[128,256]{1,0:T(8,128)S(1)}, u32[]{:S(2)}, u32[]{:S(2)}) %collective-permute-start.5) | collective-permute-done | bytes 131104 | tf_op jit(solution)/shard_map/ppermute | solution.py:21
  61.8 0.8 %fusion.18 = f32[384,256]{1,0:T(8,128)} fusion(f32[384,256]{1,0:T(8,128)S(1)} %copy-done.1, f32[640,256]{1,0:T(8,128)S(1)} %multiply_select_fusion, f32[640,256]{1,0:T(8,128)S(1)} %fusion.3, f32[128,256]{1,0:T(8,128)S(1)} %collective-permute-done.5, f32[128,256]{1,0:T(8,128)S(1)} %collective-permute-done.4), kind=kLoop, calls=%fused_computation.24 | loop fusion | flops 491520 | bytes 1835008 | tf_op jit(solution)/shard_map/sub | solution.py:104
  (8 shorter events, 0.1 us)
Async XLA Ops:
  1.7 25.7 %collective-permute-start = (f32[128,256]{1,0:T(8,128)}, f32[128,256]{1,0:T(8,128)S(1)}, u32[]{:S(2)}, u32[]{:S(2)}) collective-permute-start(f32[128,256]{1,0:T(8,128)} %get-tuple-element.10), channel_id=1, source_target_pairs={{0,4},{4,8},{8,12},{12,16},{16,20},{20,24},{24,28},{1,5},{5,9},{9,... | collective-permute-start | bytes 393224 | tf_op jit(solution)/shard_map/ppermute | solution.py:16
  6.5 20.9 %collective-permute-start.1 = (f32[128,256]{1,0:T(8,128)}, f32[128,256]{1,0:T(8,128)S(1)}, u32[]{:S(2)}, u32[]{:S(2)}) collective-permute-start(f32[128,256]{1,0:T(8,128)} %get-tuple-element.9), channel_id=1, source_target_pairs={{4,0},{8,4},{12,8},{16,12},{20,16},{24,20},{28,24},{5,1},{9,5},{13... | collective-permute-start | bytes 393224 | tf_op jit(solution)/shard_map/ppermute | solution.py:21
  9.3 15.3 %all-to-all-start = ((f32[4,4,16,128]{3,2,1,0:T(8,128)}), f32[4,4,16,128]{3,2,1,0:T(8,128)}, u32[]{:S(2)}, u32[]{:S(2)}) async-start(f32[4,4,16,128]{3,2,1,0:T(8,128)} %broadcast_in_dim.10), calls=%async_computation | async-start | bytes 262144 | tf_op jit(solution)/shard_map/all_to_all | solution.py:27
  13.2 3.8 %copy-start.2 = (f32[2,512,512]{2,1,0:T(8,128)S(1)}, f32[2,512,512]{2,1,0:T(8,128)}, u32[]{:S(2)}) copy-start(f32[2,512,512]{2,1,0:T(8,128)} %param.8) | copy-start | bytes 6291460
  14.5 4.8 %copy-start = (pred[2,512,640]{2,1,0:T(32,128)(4,1)}, pred[2,512,640]{2,1,0:T(32,128)(4,1)S(1)}, u32[]{:S(2)}) copy-start(pred[2,512,640]{2,1,0:T(32,128)(4,1)S(1)} %iota_compare_fusion) | copy-start | bytes 1966084
  19.3 2.2 %copy-start.3 = (f32[4,16]{1,0:T(4,128)S(1)}, f32[4,16]{1,0:T(4,128)}, u32[]{:S(2)}) copy-start(f32[4,16]{1,0:T(4,128)} %param.11) | copy-start | bytes 772
  21.6 3.0 %copy-start.4 = (s32[4]{0:T(128)S(1)}, s32[4]{0:T(128)}, u32[]{:S(2)}) copy-start(s32[4]{0:T(128)} %param.12) | copy-start | bytes 52
  24.6 2.9 %copy-start.1 = (f32[384,256]{1,0:T(8,128)S(1)}, f32[384,256]{1,0:T(8,128)}, u32[]{:S(2)}) copy-start(f32[384,256]{1,0:T(8,128)} %param.7) | copy-start | bytes 1179652
  30.4 16.4 %collective-permute-start.2 = (f32[256,256]{1,0:T(8,128)S(1)}, f32[256,256]{1,0:T(8,128)S(1)}, u32[]{:S(2)}, u32[]{:S(2)}) collective-permute-start(f32[256,256]{1,0:T(8,128)S(1)} %get-tuple-element.7), channel_id=1, source_target_pairs={{0,4},{4,8},{8,12},{12,16},{16,20},{20,24},{24,28},{1,5},{5,9},{9,... | collective-permute-start | bytes 786440 | tf_op jit(solution)/shard_map/ppermute | solution.py:16
  35.0 11.8 %collective-permute-start.3 = (f32[256,256]{1,0:T(8,128)S(1)}, f32[256,256]{1,0:T(8,128)S(1)}, u32[]{:S(2)}, u32[]{:S(2)}) collective-permute-start(f32[256,256]{1,0:T(8,128)S(1)} %get-tuple-element.8), channel_id=1, source_target_pairs={{4,0},{8,4},{12,8},{16,12},{20,16},{24,20},{28,24},{5,1},{9,5},{13... | collective-permute-start | bytes 786440 | tf_op jit(solution)/shard_map/ppermute | solution.py:21
  48.8 6.9 %collective-permute-start.4 = (f32[128,256]{1,0:T(8,128)S(1)}, f32[128,256]{1,0:T(8,128)S(1)}, u32[]{:S(2)}, u32[]{:S(2)}) collective-permute-start(f32[128,256]{1,0:T(8,128)S(1)} %get-tuple-element.5), channel_id=1, source_target_pairs={{0,4},{4,8},{8,12},{12,16},{16,20},{20,24},{24,28},{1,5},{5,9},{9,... | collective-permute-start | bytes 393224 | tf_op jit(solution)/shard_map/ppermute | solution.py:16
  53.2 8.7 %collective-permute-start.5 = (f32[128,256]{1,0:T(8,128)S(1)}, f32[128,256]{1,0:T(8,128)S(1)}, u32[]{:S(2)}, u32[]{:S(2)}) collective-permute-start(f32[128,256]{1,0:T(8,128)S(1)} %get-tuple-element.6), channel_id=1, source_target_pairs={{4,0},{8,4},{12,8},{16,12},{20,16},{24,20},{28,24},{5,1},{9,5},{13... | collective-permute-start | bytes 393224 | tf_op jit(solution)/shard_map/ppermute | solution.py:21

commit v4 on v3

--- a/solution.py
+++ b/solution.py
@@ -23,35 +23,68 @@
 
 def gather_band(piece):
     count = lax.axis_size("band")
-    copies = jnp.broadcast_to(piece[None], (count,) + piece.shape)
-    return lax.all_to_all(copies, "band", 0, 0, tiled=True)
+    me = lax.axis_index("band")
+    pieces = [piece]
+    for k in range(1, count):
+        pieces.append(
+            lax.ppermute(piece, "band", [(i, (i + k) % count) for i in range(count)])
+        )
+    stacked = jnp.stack(pieces)
+    order = (me - jnp.arange(count)) % count
+    ordered = jnp.take(stacked, order, axis=0)
+    slots, channels, width = piece.shape
+    return ordered.transpose(1, 2, 0, 3).reshape(slots, channels, count * width)
 
 
-def atom_rows(pieces, coupling, atom_start, atom_count, ext):
-    count, slots, channels, width = pieces.shape
-    t = lax.broadcasted_iota(jnp.int32, (count, slots, width, ext), 2)
-    q = lax.broadcasted_iota(jnp.int32, (count, slots, width, ext), 3)
-    k = lax.broadcasted_iota(jnp.int32, (count, slots, width, ext), 0)
-    first = atom_start.astype(jnp.int32)[None, :, None, None]
-    shift = (q == first + k * width + t).astype(jnp.float32)
-    placed = jnp.einsum("kscj,ksjq->scq", pieces, shift, precision=highest)
+def shift_right(x, amount, bits):
+    for b in range(bits):
+        step = 1 << b
+        moved = jnp.concatenate(
+            [jnp.zeros(x.shape[:-1] + (step,), x.dtype), x[..., :-step]], axis=-1
+        )
+        x = jnp.where(((amount >> b) & 1)[:, None, None] == 1, moved, x)
+    return x
+
+
+def atom_rows(projector_full, coupling, atom_start, atom_count, ext):
+    slots, channels, support = projector_full.shape
+    first = jnp.clip(atom_start.astype(jnp.int32), 0, ext - support)
+    padded = jnp.concatenate(
+        [projector_full, jnp.zeros((slots, channels, ext - support), projector_full.dtype)], axis=-1
+    )
+    placed = shift_right(padded, first, (ext - support).bit_length())
     live = jnp.arange(slots, dtype=jnp.int32)[:, None] < atom_count.astype(jnp.int32)[None, :]
     weights = coupling * live.astype(jnp.float32)
     return placed.reshape(slots * channels, ext), weights.reshape(slots * channels)
 
 
+def split_parts(x, axis):
+    hi = lax.reduce_precision(x, exponent_bits=8, mantissa_bits=7)
+    rest = x - hi
+    mid = lax.reduce_precision(rest, exponent_bits=8, mantissa_bits=7)
+    lo = rest - mid
+    return jnp.concatenate([hi, mid, lo], axis=axis).astype(jnp.bfloat16)
+
+
 def cell_operator(cell_matrix, connectivity, ext):
     cells, nodes, _ = cell_matrix.shape
     rows = jnp.arange(ext, dtype=connectivity.dtype)
-    onehot = (connectivity[:, :, None] == rows[None, None, :]).astype(jnp.float32)
-    total = None
+    onehot = (connectivity[:, :, None] == rows[None, None, :]).astype(jnp.bfloat16)
+    onehot_t = (rows[None, :, None] == connectivity[:, None, :]).astype(jnp.bfloat16)
+    lefts, rights = [], []
     for c in range(cells):
-        moved = jnp.dot(cell_matrix[c], onehot[c], precision=lax.Precision.HIGH)
-        part = lax.dot_general(
-            onehot[c], moved, (((0,), (0,)), ((), ())), precision=lax.Precision.HIGH
+        moved = jnp.dot(
+            split_parts(cell_matrix[c], 1),
+            jnp.concatenate([onehot[c]] * 3, axis=0),
+            preferred_element_type=jnp.float32,
         )
-        total = part if total is None else total + part
-    return total
+        lefts += [onehot_t[c]] * 3
+        rights.append(split_parts(moved, 0))
+    return jnp.dot(
+        jnp.concatenate(lefts, axis=1),
+        jnp.concatenate(rights, axis=0),
+        preferred_element_type=jnp.float32,
+    )
 
 
 def on_device(
@@ -72,7 +105,7 @@
     operator = cells + jnp.dot((placed * weights[:, None]).T, placed, precision=highest)
 
     coefficients = jnp.dot(placed, extended, precision=highest) * weights[:, None]
-    first = jnp.dot(cells, extended, precision=highest) + jnp.dot(
+    first = jnp.dot(cells, extended, precision=lax.Precision.HIGH) + jnp.dot(
         placed.T, coefficients, precision=highest
     )
     left_sums = from_left(first[ext - 2 * g :], "dom")
@@ -91,7 +124,7 @@
     step_ext = jnp.where(keep, step_ext, 0.0)
     step_one = step_ext[g : g + own]
 
-    second = jnp.dot(operator, step_ext, precision=highest)
+    second = jnp.dot(operator, step_ext, precision=lax.Precision.HIGH)
     from_before = from_left(second[ext - g :], "dom")
     from_after = from_right(second[:g], "dom")
     owned = second[g : g + own]

time: 63.2 us -> 62 us (0.981)
  matrix products: 18.2 us -> 14 us
  other arithmetic: 2.38 us -> 5.73 us
  local copies, waits for them, and re-layouts: 3.31 us -> 5.79 us
  waiting for transfers between devices: 16.1 us -> 14.2 us
  starting transfers between devices: 21.8 us -> 20.8 us
    ppermute x0 -> x3, starting transfers between devices: none -> 4.4 us  [gather_band(): lax.ppermute(piece, 'band', [(i, (i + k) % count) for i in range(count)])]
    dot_general x7 -> x5, matrix products: 15.4 us -> 11.3 us  [the longest x1 6.52 us: cell_operator(): jnp.dot(jnp.concatenate(lefts, axis=1), jnp.concatenate(rights, axis=0),...]
    all_to_all x1 -> x0, starting transfers between devices: 3.94 us -> none  [gather_band(): return lax.all_to_all(copies, 'band', 0, 0, tiled=True)]
    unnamed x12 -> x21, local copies, waits for them, and re-layouts: 0.06 us -> 3.87 us
    convert_element_type x0 -> x2, other arithmetic: none -> 2.12 us  [the longest x1 1.15 us: cell_operator(): (rows[None, :, None] == connectivity[:, None, :]).astype(jnp.bfloat16)]
    ppermute x3, waiting for transfers between devices: 9.99 us -> 8.03 us  [from_left(): return lax.ppermute(x, axis, [(i, i + 1) for i in range(count - 1)])]
    ppermute x3, starting transfers between devices: 13.8 us -> 12.4 us  [from_left(): return lax.ppermute(x, axis, [(i, i + 1) for i in range(count - 1)])]
    broadcast_in_dim x1 -> x0, local copies, waits for them, and re-layouts: 1.42 us -> none  [gather_band(): copies = jnp.broadcast_to(piece[None], (count,) + piece.shape)]
  transfers between devices with their start and end apart: 7 -> 9, of which waited for: 3 -> 3; matrix products, arithmetic and copies ran while one was open for 26% -> 29% of each run, Pallas kernels for 0% -> 0%
where the time goes in v4:
time: 62 us; the launch traced here: 61.6 us
  starting transfers between devices  20.8 us (34%)
  waiting for transfers between devices  14.2 us (23%)
  matrix products  14 us (23%)
  local copies, waits for them, and re-layouts  5.79 us (9%)
  other arithmetic  5.73 us (9%)
  between operations  1.09 us (2%)
    ppermute x3, starting transfers between devices, from_left(): return lax.ppermute(x, axis, [(i, i + 1) for i in range(count - 1)])  12.4 us
    ppermute x3, waiting for transfers between devices, from_left(): return lax.ppermute(x, axis, [(i, i + 1) for i in range(count - 1)])  8.03 us
    dot_general x1, matrix products, cell_operator(): jnp.dot(jnp.concatenate(lefts, axis=1), jnp.concatenate(rights, axis=0),...  6.52 us
    ppermute x3, waiting for transfers between devices, from_right(): return lax.ppermute(x, axis, [(i + 1, i) for i in range(count - 1)])  6.11 us
    ppermute x3, starting transfers between devices, gather_band(): lax.ppermute(piece, 'band', [(i, (i + k) % count) for i in range(count)])  4.4 us
    ppermute x3, starting transfers between devices, from_right(): return lax.ppermute(x, axis, [(i + 1, i) for i in range(count - 1)])  4.06 us
    unnamed x21, local copies, waits for them, and re-layouts  3.87 us
    dot_general x2, matrix products, cell_operator(): jnp.dot(split_parts(cell_matrix[c], 1), jnp.concatenate([onehot[c]] * 3,...  2.82 us
  transfers between devices with their start and end apart: 9, of which 3 were waited for; matrix products, arithmetic and copies ran while one was open for 29% of the time, Pallas kernels for 0%

profile of v4, /device:TPU:0, one launch (start us, length us, event | category | flops | bytes accessed | tf_op | source)
XLA Modules:
  0.0 61.6 jit_solution(2400701737420056828)
XLA Ops:
  0.0 0.5 collective-permute-start
  0.5 2.5 %collective-permute-start.1 = (f32[4,16,128]{2,1,0:T(8,128)}, f32[4,16,128]{2,1,0:T(8,128)S(1)}, u32[]{:S(2)}, u32[]{:S(2)}) collective-permute-start(f32[4,16,128]{2,1,0:T(8,128)} %param.10), channel_id=1, source_target_pairs={{0,2},{1,3},{2,0},{3,1},{4,6},{5,7},{6,4},{7,5},{8,10},{9,11},{10,... | collective-permute-start | bytes 98312 | tf_op jit(solution)/shard_map/ppermute | solution.py:30
  3.0 1.4 %collective-permute-start.2 = (f32[4,16,128]{2,1,0:T(8,128)}, f32[4,16,128]{2,1,0:T(8,128)S(1)}, u32[]{:S(2)}, u32[]{:S(2)}) collective-permute-start(f32[4,16,128]{2,1,0:T(8,128)} %param.10), channel_id=1, source_target_pairs={{0,3},{1,0},{2,1},{3,2},{4,7},{5,4},{6,5},{7,6},{8,11},{9,8},{10,9... | collective-permute-start | bytes 98312 | tf_op jit(solution)/shard_map/ppermute | solution.py:30
  4.4 1.0 %fusion.57 = (f32[128,256]{1,0:T(8,128)S(1)}, f32[128,256]{1,0:T(8,128)S(1)}) fusion(f32[384,256]{1,0:T(8,128)} %param.7), kind=kLoop, calls=%fused_computation.124 | loop fusion | bytes 524288 | tf_op jit(solution)/shard_map/slice | solution.py:100
  5.4 3.4 %collective-permute-start.3 = (f32[128,256]{1,0:T(8,128)S(1)}, f32[128,256]{1,0:T(8,128)S(1)}, u32[]{:S(2)}, u32[]{:S(2)}) collective-permute-start(f32[128,256]{1,0:T(8,128)S(1)} %get-tuple-element.18), channel_id=1, source_target_pairs={{0,4},{4,8},{8,12},{12,16},{16,20},{20,24},{24,28},{1,5},{5,9},{9,... | collective-permute-start | bytes 393224 | tf_op jit(solution)/shard_map/ppermute | solution.py:16
  8.8 1.3 %collective-permute-start.4 = (f32[128,256]{1,0:T(8,128)S(1)}, f32[128,256]{1,0:T(8,128)S(1)}, u32[]{:S(2)}, u32[]{:S(2)}) collective-permute-start(f32[128,256]{1,0:T(8,128)S(1)} %get-tuple-element.17), channel_id=1, source_target_pairs={{4,0},{8,4},{12,8},{16,12},{20,16},{24,20},{28,24},{5,1},{9,5},{13... | collective-permute-start | bytes 393224 | tf_op jit(solution)/shard_map/ppermute | solution.py:21
  10.1 1.0 %fusion.1 = bf16[2,512,640]{2,1,0:T(8,128)(2,1)S(1)} fusion(s32[2,512]{1,0:T(2,128)} %param.9), kind=kLoop, calls=%fused_computation.4 | loop fusion | flops 1310720 | bytes 1314816 | tf_op jit(solution)/shard_map/convert_element_type | solution.py:72
  11.1 1.1 %fusion = bf16[2,640,512]{2,1,0:T(8,128)(2,1)S(1)} fusion(s32[2,512]{1,0:T(2,128)} %param.9), kind=kLoop, calls=%fused_computation.3 | loop fusion | flops 1310720 | bytes 1314816 | tf_op jit(solution)/shard_map/convert_element_type | solution.py:73
  12.3 0.5 reduce-precision_convert_fusion.5
  12.8 0.1 slice_bitcast_fusion
  12.9 1.4 %fusion.31 = (bf16[3072,640]{1,0:T(8,128)(2,1)S(1)}, f32[512,640]{1,0:T(8,128)S(1)}) fusion(bf16[512,640]{1,0:T(8,128)(2,1)S(1)} %get-tuple-element.12, bf16[512,512]{1,0:T(8,128)(2,1)S(1)} %get-tuple-element.7, bf16[512,512]{1,0:T(8,128)(2,1)S(1)} %get-tuple-element.8, bf16[512,512]{1,0:T(8,128)(2,1)S(1)} %get-tuple-element.10), kind=kOutput, calls=%fused_computation.53 | convolution fusion | flops 1017905152 | bytes 4194304 | tf_op jit(solution)/shard_map/dot_general | solution.py:76
  14.3 0.2 fusion.32
  14.5 0.3 fusion.30
  14.8 1.4 %fusion.33 = (bf16[3072,640]{1,0:T(8,128)(2,1)S(1)}, f32[512,640]{1,0:T(8,128)S(1)}) fusion(bf16[3072,640]{1,0:T(8,128)(2,1)S(1)} %fusion.30, bf16[512,640]{1,0:T(8,128)(2,1)S(1)} %get-tuple-element.11, bf16[512,512]{1,0:T(8,128)(2,1)S(1)} %get-tuple-element.6, bf16[512,512]{1,0:T(8,128)(2,1)S(1)} %get-tuple-element.9, ...), kind=kOutput, calls=%fused_computation.55 | convolution fusion | flops 1017905152 | bytes 4194304 | tf_op jit(solution)/shard_map/dot_general | solution.py:76
  16.3 0.2 fusion.34
  16.5 0.3 fusion.29
  16.8 0.1 fusion.36
  16.8 0.1 fusion.35
  16.9 0.1 fusion.37
  17.1 0.1 fusion.39
  17.1 1.5 %copy-done.6 = bf16[3072,640]{1,0:T(8,128)(2,1)} copy-done((bf16[3072,640]{1,0:T(8,128)(2,1)}, bf16[3072,640]{1,0:T(8,128)(2,1)S(1)}, u32[]{:S(2)}) %copy-start.6) | copy-done | bytes 3932184
  18.7 0.1 fusion.40
  18.8 1.9 %copy-done.2 = bf16[640,3072]{1,0:T(8,128)(2,1)} copy-done((bf16[640,3072]{1,0:T(8,128)(2,1)}, bf16[640,3072]{1,0:T(8,128)(2,1)S(1)}, u32[]{:S(2)}) %copy-start.2) | copy-done | bytes 3932184
  21.4 6.5 %fusion.58 = f32[640,640]{1,0:T(8,128)S(1)} fusion(bf16[640,3072]{1,0:T(8,128)(2,1)} %copy-done.2, bf16[3072,640]{1,0:T(8,128)(2,1)} %copy-done.6), kind=kOutput, calls=%fused_computation.125 | convolution fusion | flops 2516582400 | bytes 9502720 | tf_op jit(solution)/shard_map/dot_general | solution.py:83
  28.1 0.1 mul.44
  28.2 0.6 gather_fusion
  28.9 0.1 pad_select_fusion
  29.0 0.1 pad_select_fusion.7
  29.1 0.1 pad_select_fusion.6
  29.2 0.1 pad_select_fusion.5
  29.3 0.1 pad_select_fusion.4
  29.4 0.1 pad_select_fusion.3
  29.6 0.1 pad_select_fusion.2
  29.7 0.1 pad_select_fusion.1
  29.9 0.4 convolution_multiply_fusion
  30.4 0.7 %fusion.59 = f32[640,256]{1,0:T(8,128)S(1)} fusion(f32[64,640]{1,0:T(8,128)S(1)} %bitcast.69, f32[64,256]{1,0:T(8,128)S(1)} %convolution_multiply_fusion), kind=kOutput, calls=%fused_computation.126 | convolution fusion | flops 125829120 | bytes 884736 | tf_op jit(solution)/shard_map/dot_general | solution.py:108
  31.1 0.9 %convolution_add_fusion = f32[640,256]{1,0:T(8,128)S(1)} fusion(f32[640,256]{1,0:T(8,128)S(1)} %fusion.59, f32[640,640]{1,0:T(8,128)S(1)} %fusion.58, f32[640,256]{1,0:T(8,128)S(1)} %constant_dynamic-update-slice_fusion), kind=kOutput, calls=%fused_computation.47 | convolution fusion | flops 629309440 | bytes 3604480 | tf_op jit(solution)/shard_map/dot_general | solution.py:108
  32.1 4.6 %collective-permute-start.5 = (f32[256,256]{1,0:T(8,128)S(1)}, f32[256,256]{1,0:T(8,128)S(1)}, u32[]{:S(2)}, u32[]{:S(2)}) collective-permute-start(f32[256,256]{1,0:T(8,128)S(1)} %get-tuple-element.15), channel_id=1, source_target_pairs={{0,4},{4,8},{8,12},{12,16},{16,20},{20,24},{24,28},{1,5},{5,9},{9,... | collective-permute-start | bytes 786440 | tf_op jit(solution)/shard_map/ppermute | solution.py:16
  36.7 1.5 %collective-permute-start.6 = (f32[256,256]{1,0:T(8,128)S(1)}, f32[256,256]{1,0:T(8,128)S(1)}, u32[]{:S(2)}, u32[]{:S(2)}) collective-permute-start(f32[256,256]{1,0:T(8,128)S(1)} %get-tuple-element.16), channel_id=1, source_target_pairs={{4,0},{8,4},{12,8},{16,12},{20,16},{24,20},{28,24},{5,1},{9,5},{13... | collective-permute-start | bytes 786440 | tf_op jit(solution)/shard_map/ppermute | solution.py:21
  38.1 1.6 %fusion.44 = f32[640,640,1]{1,0,2:T(8,128)S(1)} fusion(f32[4,16,640]{2,1,0:T(8,128)S(1)} %pad_select_fusion.1, f32[4,16]{1,0:T(4,128)S(1)} %broadcast_multiply_fusion), kind=kOutput, calls=%fused_computation.73 | convolution fusion | flops 314613760 | bytes 1802496 | tf_op jit(solution)/shard_map/dot_general | solution.py:105
  39.7 6.8 %collective-permute-done.5 = f32[256,256]{1,0:T(8,128)S(1)} collective-permute-done((f32[256,256]{1,0:T(8,128)S(1)}, f32[256,256]{1,0:T(8,128)S(1)}, u32[]{:S(2)}, u32[]{:S(2)}) %collective-permute-start.5) | collective-permute-done | bytes 262176 | tf_op jit(solution)/shard_map/ppermute | solution.py:16
  46.6 0.2 multiply_select_fusion
  46.8 1.0 %fusion.14 = f32[640,256]{1,0:T(8,128)S(1)} fusion(f32[640,256]{1,0:T(8,128)S(1)} %multiply_select_fusion, f32[640,640]{1,0:T(8,128)S(1)} %fusion.58, f32[640,640,1]{1,0,2:T(8,128)S(1)} %fusion.44), kind=kOutput, calls=%fused_computation.26 | convolution fusion | flops 629555200 | bytes 4587520 | tf_op jit(solution)/shard_map/dot_general | solution.py:127
  47.8 4.4 %collective-permute-start.7 = (f32[128,256]{1,0:T(8,128)S(1)}, f32[128,256]{1,0:T(8,128)S(1)}, u32[]{:S(2)}, u32[]{:S(2)}) collective-permute-start(f32[128,256]{1,0:T(8,128)S(1)} %get-tuple-element.13), channel_id=1, source_target_pairs={{0,4},{4,8},{8,12},{12,16},{16,20},{20,24},{24,28},{1,5},{5,9},{9,... | collective-permute-start | bytes 393224 | tf_op jit(solution)/shard_map/ppermute | solution.py:16
  52.2 1.3 %collective-permute-start.8 = (f32[128,256]{1,0:T(8,128)S(1)}, f32[128,256]{1,0:T(8,128)S(1)}, u32[]{:S(2)}, u32[]{:S(2)}) collective-permute-start(f32[128,256]{1,0:T(8,128)S(1)} %get-tuple-element.14), channel_id=1, source_target_pairs={{4,0},{8,4},{12,8},{16,12},{20,16},{24,20},{28,24},{5,1},{9,5},{13... | collective-permute-start | bytes 393224 | tf_op jit(solution)/shard_map/ppermute | solution.py:21
  53.5 1.2 %collective-permute-done.7 = f32[128,256]{1,0:T(8,128)S(1)} collective-permute-done((f32[128,256]{1,0:T(8,128)S(1)}, f32[128,256]{1,0:T(8,128)S(1)}, u32[]{:S(2)}, u32[]{:S(2)}) %collective-permute-start.7) | collective-permute-done | bytes 131104 | tf_op jit(solution)/shard_map/ppermute | solution.py:16
  54.7 6.1 %collective-permute-done.8 = f32[128,256]{1,0:T(8,128)S(1)} collective-permute-done((f32[128,256]{1,0:T(8,128)S(1)}, f32[128,256]{1,0:T(8,128)S(1)}, u32[]{:S(2)}, u32[]{:S(2)}) %collective-permute-start.8) | collective-permute-done | bytes 131104 | tf_op jit(solution)/shard_map/ppermute | solution.py:21
  60.8 0.8 %fusion.42 = f32[384,256]{1,0:T(8,128)} fusion(f32[384,256]{1,0:T(8,128)S(1)} %copy-done, f32[640,256]{1,0:T(8,128)S(1)} %multiply_select_fusion, f32[640,256]{1,0:T(8,128)S(1)} %fusion.14, f32[128,256]{1,0:T(8,128)S(1)} %collective-permute-done.8, f32[128,256]{1,0:T(8,128)S(1)} %collective-permute-done.7), kind=kLoop, calls=%fused_computation.70 | loop fusion | flops 491520 | bytes 1835008 | tf_op jit(solution)/shard_map/sub | solution.py:137
  (35 shorter events, 0.5 us)
Async XLA Ops:
  0.0 12.3 %copy-start.1 = (f32[2,512,512]{2,1,0:T(8,128)S(1)}, f32[2,512,512]{2,1,0:T(8,128)}, u32[]{:S(2)}) copy-start(f32[2,512,512]{2,1,0:T(8,128)} %param.8) | copy-start | bytes 6291460
  0.0 28.1 %collective-permute-start = (f32[4,16,128]{2,1,0:T(8,128)}, f32[4,16,128]{2,1,0:T(8,128)S(1)}, u32[]{:S(2)}, u32[]{:S(2)}) collective-permute-start(f32[4,16,128]{2,1,0:T(8,128)} %param.10), channel_id=1, source_target_pairs={{0,1},{1,2},{2,3},{3,0},{4,5},{5,6},{6,7},{7,4},{8,9},{9,10},{10,1... | collective-permute-start | bytes 98312 | tf_op jit(solution)/shard_map/ppermute | solution.py:30
  0.5 27.7 %collective-permute-start.1 = (f32[4,16,128]{2,1,0:T(8,128)}, f32[4,16,128]{2,1,0:T(8,128)S(1)}, u32[]{:S(2)}, u32[]{:S(2)}) collective-permute-start(f32[4,16,128]{2,1,0:T(8,128)} %param.10), channel_id=1, source_target_pairs={{0,2},{1,3},{2,0},{3,1},{4,6},{5,7},{6,4},{7,5},{8,10},{9,11},{10,... | collective-permute-start | bytes 98312 | tf_op jit(solution)/shard_map/ppermute | solution.py:30
  3.0 25.1 %collective-permute-start.2 = (f32[4,16,128]{2,1,0:T(8,128)}, f32[4,16,128]{2,1,0:T(8,128)S(1)}, u32[]{:S(2)}, u32[]{:S(2)}) collective-permute-start(f32[4,16,128]{2,1,0:T(8,128)} %param.10), channel_id=1, source_target_pairs={{0,3},{1,0},{2,1},{3,2},{4,7},{5,4},{6,5},{7,6},{8,11},{9,8},{10,9... | collective-permute-start | bytes 98312 | tf_op jit(solution)/shard_map/ppermute | solution.py:30
  5.4 24.4 %collective-permute-start.3 = (f32[128,256]{1,0:T(8,128)S(1)}, f32[128,256]{1,0:T(8,128)S(1)}, u32[]{:S(2)}, u32[]{:S(2)}) collective-permute-start(f32[128,256]{1,0:T(8,128)S(1)} %get-tuple-element.18), channel_id=1, source_target_pairs={{0,4},{4,8},{8,12},{12,16},{16,20},{20,24},{24,28},{1,5},{5,9},{9,... | collective-permute-start | bytes 393224 | tf_op jit(solution)/shard_map/ppermute | solution.py:16
  8.8 21.0 %collective-permute-start.4 = (f32[128,256]{1,0:T(8,128)S(1)}, f32[128,256]{1,0:T(8,128)S(1)}, u32[]{:S(2)}, u32[]{:S(2)}) collective-permute-start(f32[128,256]{1,0:T(8,128)S(1)} %get-tuple-element.17), channel_id=1, source_target_pairs={{4,0},{8,4},{12,8},{16,12},{20,16},{24,20},{28,24},{5,1},{9,5},{13... | collective-permute-start | bytes 393224 | tf_op jit(solution)/shard_map/ppermute | solution.py:21
  16.7 1.9 %copy-start.6 = (bf16[3072,640]{1,0:T(8,128)(2,1)}, bf16[3072,640]{1,0:T(8,128)(2,1)S(1)}, u32[]{:S(2)}) copy-start(bf16[3072,640]{1,0:T(8,128)(2,1)S(1)} %fusion.29) | copy-start | bytes 11796484
  17.0 3.6 %copy-start.5 = (s32[4]{0:T(128)S(1)}, s32[4]{0:T(128)}, u32[]{:S(2)}) copy-start(s32[4]{0:T(128)} %param.12) | copy-start | bytes 52
  18.8 1.9 %copy-start.2 = (bf16[640,3072]{1,0:T(8,128)(2,1)}, bf16[640,3072]{1,0:T(8,128)(2,1)S(1)}, u32[]{:S(2)}) copy-start(bf16[640,3072]{1,0:T(8,128)(2,1)S(1)} %fusion.40) | copy-start | bytes 11796484
  21.4 6.5 %copy-start.4 = (f32[4,16]{1,0:T(4,128)S(1)}, f32[4,16]{1,0:T(4,128)}, u32[]{:S(2)}) copy-start(f32[4,16]{1,0:T(4,128)} %param.11) | copy-start | bytes 772
  21.4 6.7 %copy-start.3 = (f32[4,16,128]{2,1,0:T(8,128)S(1)}, f32[4,16,128]{2,1,0:T(8,128)}, u32[]{:S(2)}) copy-start(f32[4,16,128]{2,1,0:T(8,128)} %param.10) | copy-start | bytes 98308
  28.8 1.0 %copy-start = (f32[384,256]{1,0:T(8,128)S(1)}, f32[384,256]{1,0:T(8,128)}, u32[]{:S(2)}) copy-start(f32[384,256]{1,0:T(8,128)} %param.7) | copy-start | bytes 1179652
  32.1 14.5 %collective-permute-start.5 = (f32[256,256]{1,0:T(8,128)S(1)}, f32[256,256]{1,0:T(8,128)S(1)}, u32[]{:S(2)}, u32[]{:S(2)}) collective-permute-start(f32[256,256]{1,0:T(8,128)S(1)} %get-tuple-element.15), channel_id=1, source_target_pairs={{0,4},{4,8},{8,12},{12,16},{16,20},{20,24},{24,28},{1,5},{5,9},{9,... | collective-permute-start | bytes 786440 | tf_op jit(solution)/shard_map/ppermute | solution.py:16
  36.7 9.9 %collective-permute-start.6 = (f32[256,256]{1,0:T(8,128)S(1)}, f32[256,256]{1,0:T(8,128)S(1)}, u32[]{:S(2)}, u32[]{:S(2)}) collective-permute-start(f32[256,256]{1,0:T(8,128)S(1)} %get-tuple-element.16), channel_id=1, source_target_pairs={{4,0},{8,4},{12,8},{16,12},{20,16},{24,20},{28,24},{5,1},{9,5},{13... | collective-permute-start | bytes 786440 | tf_op jit(solution)/shard_map/ppermute | solution.py:21
  47.8 6.9 %collective-permute-start.7 = (f32[128,256]{1,0:T(8,128)S(1)}, f32[128,256]{1,0:T(8,128)S(1)}, u32[]{:S(2)}, u32[]{:S(2)}) collective-permute-start(f32[128,256]{1,0:T(8,128)S(1)} %get-tuple-element.13), channel_id=1, source_target_pairs={{0,4},{4,8},{8,12},{12,16},{16,20},{20,24},{24,28},{1,5},{5,9},{9,... | collective-permute-start | bytes 393224 | tf_op jit(solution)/shard_map/ppermute | solution.py:16
  52.2 8.6 %collective-permute-start.8 = (f32[128,256]{1,0:T(8,128)S(1)}, f32[128,256]{1,0:T(8,128)S(1)}, u32[]{:S(2)}, u32[]{:S(2)}) collective-permute-start(f32[128,256]{1,0:T(8,128)S(1)} %get-tuple-element.14), channel_id=1, source_target_pairs={{4,0},{8,4},{12,8},{16,12},{20,16},{24,20},{28,24},{5,1},{9,5},{13... | collective-permute-start | bytes 393224 | tf_op jit(solution)/shard_map/ppermute | solution.py:21

commit v5 on v4

--- a/solution.py
+++ b/solution.py
@@ -70,21 +70,19 @@
     cells, nodes, _ = cell_matrix.shape
     rows = jnp.arange(ext, dtype=connectivity.dtype)
     onehot = (connectivity[:, :, None] == rows[None, None, :]).astype(jnp.bfloat16)
-    onehot_t = (rows[None, :, None] == connectivity[:, None, :]).astype(jnp.bfloat16)
-    lefts, rights = [], []
+    total = None
     for c in range(cells):
         moved = jnp.dot(
             split_parts(cell_matrix[c], 1),
             jnp.concatenate([onehot[c]] * 3, axis=0),
             preferred_element_type=jnp.float32,
         )
-        lefts += [onehot_t[c]] * 3
-        rights.append(split_parts(moved, 0))
-    return jnp.dot(
-        jnp.concatenate(lefts, axis=1),
-        jnp.concatenate(rights, axis=0),
-        preferred_element_type=jnp.float32,
-    )
+        part = lax.dot_general(
+            onehot[c].astype(jnp.float32), moved, (((0,), (0,)), ((), ())),
+            precision=lax.Precision.HIGH,
+        )
+        total = part if total is None else total + part
+    return total
 
 
 def on_device(

time: 62 us -> 59.9 us (0.966)
  matrix products: 14 us -> 11.5 us
  other arithmetic: 5.73 us -> 7.92 us
  local copies, waits for them, and re-layouts: 5.79 us -> 4.06 us
    dot_general x1 -> x2, matrix products: 6.52 us -> 2.65 us  [cell_operator(): lax.dot_general(onehot[c].astype(jnp.float32), moved, (((0,), (0,)), ((),...]
    another operation x1, other arithmetic: 0.54 us -> 3.27 us
    unnamed x21 -> x24, local copies, waits for them, and re-layouts: 3.87 us -> 1.54 us
    convert_element_type x2 -> x0, other arithmetic: 2.12 us -> none  [the longest x1 1.15 us: cell_operator(): (rows[None, :, None] == connectivity[:, None, :]).astype(jnp.bfloat16)]
    dot_general x2, matrix products: 2.82 us -> 4.12 us  [cell_operator(): jnp.dot(split_parts(cell_matrix[c], 1), jnp.concatenate([onehot[c]] * 3,...]
    eq x1, other arithmetic: 0.01 us -> 1.25 us  [shift_right(): x = jnp.where((amount >> b & 1)[:, None, None] == 1, moved, x)]
    another operation x1, other arithmetic: 0.01 us -> 0.77 us  [gather_band(): stacked = jnp.stack(pieces)]
    unnamed x3 -> x0, other arithmetic: 0.69 us -> none
  transfers between devices with their start and end apart: 9 -> 9, of which waited for: 3 -> 3; matrix products, arithmetic and copies ran while one was open for 29% -> 31% of each run, Pallas kernels for 0% -> 0%
where the time goes in v5:
time: 59.9 us; the launch traced here: 59.5 us
  starting transfers between devices  21.3 us (36%)
  waiting for transfers between devices  13.6 us (23%)
  matrix products  11.5 us (19%)
  other arithmetic  7.92 us (13%)
  local copies, waits for them, and re-layouts  4.06 us (7%)
  between operations  1.11 us (2%)
    ppermute x3, starting transfers between devices, from_left(): return lax.ppermute(x, axis, [(i, i + 1) for i in range(count - 1)])  13 us
    ppermute x3, waiting for transfers between devices, from_left(): return lax.ppermute(x, axis, [(i, i + 1) for i in range(count - 1)])  8.15 us
    ppermute x3, waiting for transfers between devices, from_right(): return lax.ppermute(x, axis, [(i + 1, i) for i in range(count - 1)])  5.48 us
    ppermute x3, starting transfers between devices, gather_band(): lax.ppermute(piece, 'band', [(i, (i + k) % count) for i in range(count)])  4.4 us
    dot_general x2, matrix products, cell_operator(): jnp.dot(split_parts(cell_matrix[c], 1), jnp.concatenate([onehot[c]] * 3,...  4.12 us
    ppermute x3, starting transfers between devices, from_right(): return lax.ppermute(x, axis, [(i + 1, i) for i in range(count - 1)])  3.86 us
    another operation x1, other arithmetic  3.27 us
    dot_general x2, matrix products, cell_operator(): lax.dot_general(onehot[c].astype(jnp.float32), moved, (((0,), (0,)), ((),...  2.65 us
  transfers between devices with their start and end apart: 9, of which 3 were waited for; matrix products, arithmetic and copies ran while one was open for 31% of the time, Pallas kernels for 0%

profile of v5, /device:TPU:0, one launch (start us, length us, event | category | flops | bytes accessed | tf_op | source)
XLA Modules:
  0.0 59.5 jit_solution(16398000533607378212)
XLA Ops:
  0.0 0.5 collective-permute-start
  0.5 2.5 %collective-permute-start.1 = (f32[4,16,128]{2,1,0:T(8,128)}, f32[4,16,128]{2,1,0:T(8,128)S(1)}, u32[]{:S(2)}, u32[]{:S(2)}) collective-permute-start(f32[4,16,128]{2,1,0:T(8,128)} %param.10), channel_id=1, source_target_pairs={{0,2},{1,3},{2,0},{3,1},{4,6},{5,7},{6,4},{7,5},{8,10},{9,11},{10,... | collective-permute-start | bytes 98312 | tf_op jit(solution)/shard_map/ppermute | solution.py:30
  3.0 1.4 %collective-permute-start.2 = (f32[4,16,128]{2,1,0:T(8,128)}, f32[4,16,128]{2,1,0:T(8,128)}, u32[]{:S(2)}, u32[]{:S(2)}) collective-permute-start(f32[4,16,128]{2,1,0:T(8,128)} %param.10), channel_id=1, source_target_pairs={{0,3},{1,0},{2,1},{3,2},{4,7},{5,4},{6,5},{7,6},{8,11},{9,8},{10,9... | collective-permute-start | bytes 98312 | tf_op jit(solution)/shard_map/ppermute | solution.py:30
  4.4 1.7 %fusion.43 = (f32[128,256]{1,0:T(8,128)}, f32[128,256]{1,0:T(8,128)}) fusion(f32[384,256]{1,0:T(8,128)} %param.7), kind=kLoop, calls=%fused_computation.102 | loop fusion | bytes 524288 | tf_op jit(solution)/shard_map/slice | solution.py:98
  6.1 4.1 %collective-permute-start.3 = (f32[128,256]{1,0:T(8,128)}, f32[128,256]{1,0:T(8,128)}, u32[]{:S(2)}, u32[]{:S(2)}) collective-permute-start(f32[128,256]{1,0:T(8,128)} %get-tuple-element.18), channel_id=1, source_target_pairs={{0,4},{4,8},{8,12},{12,16},{16,20},{20,24},{24,28},{1,5},{5,9},{9,... | collective-permute-start | bytes 393224 | tf_op jit(solution)/shard_map/ppermute | solution.py:16
  10.2 1.3 %collective-permute-start.4 = (f32[128,256]{1,0:T(8,128)}, f32[128,256]{1,0:T(8,128)S(1)}, u32[]{:S(2)}, u32[]{:S(2)}) collective-permute-start(f32[128,256]{1,0:T(8,128)} %get-tuple-element.17), channel_id=1, source_target_pairs={{4,0},{8,4},{12,8},{16,12},{20,16},{24,20},{28,24},{5,1},{9,5},{13... | collective-permute-start | bytes 393224 | tf_op jit(solution)/shard_map/ppermute | solution.py:21
  11.5 1.3 %and_compare_fusion.7 = (pred[4]{0:T(512)(128)(4,1)}, pred[4]{0:T(512)(128)(4,1)S(1)}, pred[4]{0:T(512)(128)(4,1)S(1)}, pred[4]{0:T(512)(128)(4,1)}, pred[4]{0:T...) fusion(s32[4]{0:T(128)} %param.12), kind=kLoop, calls=%fused_computation.96 | loop fusion | flops 100 | bytes 48 | tf_op jit(solution)/shard_map/eq | solution.py:45
  13.4 0.0 copy-start.3
  13.4 3.3 %reduce-precision_convert_fusion.1 = (bf16[512,512]{1,0:T(8,128)(2,1)S(1)}, bf16[512,512]{1,0:T(8,128)(2,1)S(1)}, bf16[512,512]{1,0:T(8,128)(2,1)}, bf16[512,512...) fusion(f32[2,512,512]{2,1,0:T(8,128)} %param.8), kind=kLoop, calls=%fused_computation.30 | loop fusion | flops 3670016 | bytes 5242880 | tf_op jit(solution)/shard_map/convert
  16.7 0.5 iota_compare_fusion
  17.2 0.0 copy-start.8
  17.2 0.1 slice_bitcast_fusion.4
  17.4 0.5 copy-done.8
  17.9 0.1 broadcast_multiply_fusion
  18.0 2.7 %fusion = f32[512,640]{1,0:T(8,128)S(1)} fusion(bf16[512,640]{1,0:T(8,128)(2,1)S(1)} %get-tuple-element.12, bf16[512,512]{1,0:T(8,128)(2,1)} %get-tuple-element.7, bf16[512,512]{1,0:T(8,128)(2,1)} %get-tuple-element.8, bf16[512,512]{1,0:T(8,128)(2,1)} %get-tuple-element.10), kind=kOutput, calls=%fused_computation.2 | convolution fusion | flops 1017249792 | bytes 3538944 | tf_op jit(solution)/shard_map/dot_general | solution.py:75
  20.7 1.3 %fusion.23 = f32[640,640]{1,0:T(8,128)S(1)} fusion(f32[512,640]{1,0:T(8,128)S(1)} %fusion, pred[2,512,640]{2,1,0:T(32,128)(4,1)S(1)} %get-tuple-element.19), kind=kOutput, calls=%fused_computation.37 | convolution fusion | flops 1258291200 | bytes 3276800 | tf_op jit(solution)/shard_map/dot_general | solution.py:80
  22.1 1.4 %fusion.6 = f32[512,640]{1,0:T(8,128)S(1)} fusion(bf16[512,640]{1,0:T(8,128)(2,1)S(1)} %get-tuple-element.11, bf16[512,512]{1,0:T(8,128)(2,1)S(1)} %get-tuple-element.6, bf16[512,512]{1,0:T(8,128)(2,1)S(1)} %copy-done.1, bf16[512,512]{1,0:T(8,128)(2,1)S(1)} %get-tuple-element.5), kind=kOutput, calls=%fused_computation.8 | convolution fusion | flops 1017249792 | bytes 3538944 | tf_op jit(solution)/shard_map/dot_general | solution.py:75
  23.4 0.0 copy-start.2
  23.5 1.3 %convolution_add_fusion = f32[640,640]{1,0:T(8,128)S(1)} fusion(f32[640,640]{1,0:T(8,128)S(1)} %fusion.23, f32[512,640]{1,0:T(8,128)S(1)} %fusion.6, pred[2,512,640]{2,1,0:T(32,128)(4,1)S(1)} %get-tuple-element.19), kind=kOutput, calls=%fused_computation.26 | convolution fusion | flops 1258700800 | bytes 4915200 | tf_op jit(solution)/shard_map/dot_general | solution.py:80
  24.9 0.1 mul.44
  25.0 0.0 collective-permute-done.1
  25.0 0.8 %pad_maximum_fusion = f32[4,4,16,128]{3,2,1,0:T(8,128)S(1)} fusion(f32[1,4,16,128]{3,2,1,0:T(8,128)} %bitcast.9, f32[1,4,16,128]{3,2,1,0:T(8,128)S(1)} %bitcast.68, f32[1,4,16,128]{3,2,1,0:T(8,128)S(1)} %bitcast.67, f32[1,4,16,128]{3,2,1,0:T(8,128)S(1)} %bitcast.66), kind=kLoop, calls=%fused_computation.62 | loop fusion | flops 98304 | bytes 262144 | tf_op jit(solution)/shard_map/stack | solution.py:32
  25.8 0.6 gather_fusion
  26.3 0.1 copy_bitcast_fusion
  26.5 0.1 pad_select_fusion
  26.6 0.1 pad_select_fusion.7
  26.7 0.0 copy-start
  26.7 0.1 pad_select_fusion.6
  26.9 0.1 pad_select_fusion.5
  27.0 0.1 pad_select_fusion.4
  27.1 0.1 pad_select_fusion.3
  27.2 0.1 pad_select_fusion.2
  27.4 0.1 pad_select_fusion.1
  27.5 0.9 %constant_dynamic-update-slice_fusion.2 = f32[640,256]{1,0:T(8,128)S(1)} fusion(f32[128,256]{1,0:T(8,128)} %collective-permute-done.3), kind=kLoop, calls=%fused_computation.68 | loop fusion | bytes 262144
  28.5 0.4 convolution_multiply_fusion
  28.9 0.7 %fusion.44 = f32[640,256]{1,0:T(8,128)S(1)} fusion(f32[64,640]{1,0:T(8,128)S(1)} %bitcast.59, f32[64,256]{1,0:T(8,128)S(1)} %convolution_multiply_fusion), kind=kOutput, calls=%fused_computation.103 | convolution fusion | flops 125829120 | bytes 884736 | tf_op jit(solution)/shard_map/dot_general | solution.py:106
  29.6 0.9 %convolution_add_fusion.1 = f32[640,256]{1,0:T(8,128)S(1)} fusion(f32[640,256]{1,0:T(8,128)S(1)} %fusion.44, f32[640,640]{1,0:T(8,128)S(1)} %convolution_add_fusion, f32[640,256]{1,0:T(8,128)S(1)} %constant_dynamic-update-slice_fusion), kind=kOutput, calls=%fused_computation.38 | convolution fusion | flops 629309440 | bytes 3604480 | tf_op jit(solution)/shard_map/dot_general | solution.py:106
  30.6 4.6 %collective-permute-start.5 = (f32[256,256]{1,0:T(8,128)S(1)}, f32[256,256]{1,0:T(8,128)S(1)}, u32[]{:S(2)}, u32[]{:S(2)}) collective-permute-start(f32[256,256]{1,0:T(8,128)S(1)} %get-tuple-element.15), channel_id=1, source_target_pairs={{0,4},{4,8},{8,12},{12,16},{16,20},{20,24},{24,28},{1,5},{5,9},{9,... | collective-permute-start | bytes 786440 | tf_op jit(solution)/shard_map/ppermute | solution.py:16
  35.2 1.3 %collective-permute-start.6 = (f32[256,256]{1,0:T(8,128)S(1)}, f32[256,256]{1,0:T(8,128)S(1)}, u32[]{:S(2)}, u32[]{:S(2)}) collective-permute-start(f32[256,256]{1,0:T(8,128)S(1)} %get-tuple-element.16), channel_id=1, source_target_pairs={{4,0},{8,4},{12,8},{16,12},{20,16},{24,20},{28,24},{5,1},{9,5},{13... | collective-permute-start | bytes 786440 | tf_op jit(solution)/shard_map/ppermute | solution.py:21
  36.5 1.6 %fusion.29 = f32[640,640,1]{1,0,2:T(8,128)S(1)} fusion(f32[4,16,640]{2,1,0:T(8,128)S(1)} %pad_select_fusion.1, f32[4,16]{1,0:T(4,128)S(1)} %broadcast_multiply_fusion), kind=kOutput, calls=%fused_computation.50 | convolution fusion | flops 314613760 | bytes 1802496 | tf_op jit(solution)/shard_map/dot_general | solution.py:103
  38.1 7.0 %collective-permute-done.5 = f32[256,256]{1,0:T(8,128)S(1)} collective-permute-done((f32[256,256]{1,0:T(8,128)S(1)}, f32[256,256]{1,0:T(8,128)S(1)}, u32[]{:S(2)}, u32[]{:S(2)}) %collective-permute-start.5) | collective-permute-done | bytes 262176 | tf_op jit(solution)/shard_map/ppermute | solution.py:16
  45.1 0.2 multiply_select_fusion
  45.2 1.0 %fusion.12 = f32[640,256]{1,0:T(8,128)S(1)} fusion(f32[640,256]{1,0:T(8,128)S(1)} %multiply_select_fusion, f32[640,640]{1,0:T(8,128)S(1)} %convolution_add_fusion, f32[640,640,1]{1,0,2:T(8,128)S(1)} %fusion.29), kind=kOutput, calls=%fused_computation.15 | convolution fusion | flops 629555200 | bytes 4587520 | tf_op jit(solution)/shard_map/dot_general | solution.py:125
  46.3 4.4 %collective-permute-start.7 = (f32[128,256]{1,0:T(8,128)S(1)}, f32[128,256]{1,0:T(8,128)S(1)}, u32[]{:S(2)}, u32[]{:S(2)}) collective-permute-start(f32[128,256]{1,0:T(8,128)S(1)} %get-tuple-element.13), channel_id=1, source_target_pairs={{0,4},{4,8},{8,12},{12,16},{16,20},{20,24},{24,28},{1,5},{5,9},{9,... | collective-permute-start | bytes 393224 | tf_op jit(solution)/shard_map/ppermute | solution.py:16
  50.7 1.3 %collective-permute-start.8 = (f32[128,256]{1,0:T(8,128)S(1)}, f32[128,256]{1,0:T(8,128)S(1)}, u32[]{:S(2)}, u32[]{:S(2)}) collective-permute-start(f32[128,256]{1,0:T(8,128)S(1)} %get-tuple-element.14), channel_id=1, source_target_pairs={{4,0},{8,4},{12,8},{16,12},{20,16},{24,20},{28,24},{5,1},{9,5},{13... | collective-permute-start | bytes 393224 | tf_op jit(solution)/shard_map/ppermute | solution.py:21
  52.0 1.2 %collective-permute-done.7 = f32[128,256]{1,0:T(8,128)S(1)} collective-permute-done((f32[128,256]{1,0:T(8,128)S(1)}, f32[128,256]{1,0:T(8,128)S(1)}, u32[]{:S(2)}, u32[]{:S(2)}) %collective-permute-start.7) | collective-permute-done | bytes 131104 | tf_op jit(solution)/shard_map/ppermute | solution.py:16
  53.2 5.5 %collective-permute-done.8 = f32[128,256]{1,0:T(8,128)S(1)} collective-permute-done((f32[128,256]{1,0:T(8,128)S(1)}, f32[128,256]{1,0:T(8,128)S(1)}, u32[]{:S(2)}, u32[]{:S(2)}) %collective-permute-start.8) | collective-permute-done | bytes 131104 | tf_op jit(solution)/shard_map/ppermute | solution.py:21
  58.6 0.8 %fusion.27 = f32[384,256]{1,0:T(8,128)} fusion(f32[384,256]{1,0:T(8,128)S(1)} %copy-done, f32[640,256]{1,0:T(8,128)S(1)} %multiply_select_fusion, f32[640,256]{1,0:T(8,128)S(1)} %fusion.12, f32[128,256]{1,0:T(8,128)S(1)} %collective-permute-done.8, f32[128,256]{1,0:T(8,128)S(1)} %collective-permute-done.7), kind=kLoop, calls=%fused_computation.47 | loop fusion | flops 491520 | bytes 1835008 | tf_op jit(solution)/shard_map/sub | solution.py:135
  (33 shorter events, 0.2 us)
Async XLA Ops:
  0.0 25.0 %collective-permute-start = (f32[4,16,128]{2,1,0:T(8,128)}, f32[4,16,128]{2,1,0:T(8,128)S(1)}, u32[]{:S(2)}, u32[]{:S(2)}) collective-permute-start(f32[4,16,128]{2,1,0:T(8,128)} %param.10), channel_id=1, source_target_pairs={{0,1},{1,2},{2,3},{3,0},{4,5},{5,6},{6,7},{7,4},{8,9},{9,10},{10,1... | collective-permute-start | bytes 98312 | tf_op jit(solution)/shard_map/ppermute | solution.py:30
  0.5 24.5 %collective-permute-start.1 = (f32[4,16,128]{2,1,0:T(8,128)}, f32[4,16,128]{2,1,0:T(8,128)S(1)}, u32[]{:S(2)}, u32[]{:S(2)}) collective-permute-start(f32[4,16,128]{2,1,0:T(8,128)} %param.10), channel_id=1, source_target_pairs={{0,2},{1,3},{2,0},{3,1},{4,6},{5,7},{6,4},{7,5},{8,10},{9,11},{10,... | collective-permute-start | bytes 98312 | tf_op jit(solution)/shard_map/ppermute | solution.py:30
  3.0 22.0 %collective-permute-start.2 = (f32[4,16,128]{2,1,0:T(8,128)}, f32[4,16,128]{2,1,0:T(8,128)}, u32[]{:S(2)}, u32[]{:S(2)}) collective-permute-start(f32[4,16,128]{2,1,0:T(8,128)} %param.10), channel_id=1, source_target_pairs={{0,3},{1,0},{2,1},{3,2},{4,7},{5,4},{6,5},{7,6},{8,11},{9,8},{10,9... | collective-permute-start | bytes 98312 | tf_op jit(solution)/shard_map/ppermute | solution.py:30
  6.1 21.4 %collective-permute-start.3 = (f32[128,256]{1,0:T(8,128)}, f32[128,256]{1,0:T(8,128)}, u32[]{:S(2)}, u32[]{:S(2)}) collective-permute-start(f32[128,256]{1,0:T(8,128)} %get-tuple-element.18), channel_id=1, source_target_pairs={{0,4},{4,8},{8,12},{12,16},{16,20},{20,24},{24,28},{1,5},{5,9},{9,... | collective-permute-start | bytes 393224 | tf_op jit(solution)/shard_map/ppermute | solution.py:16
  10.2 18.3 %collective-permute-start.4 = (f32[128,256]{1,0:T(8,128)}, f32[128,256]{1,0:T(8,128)S(1)}, u32[]{:S(2)}, u32[]{:S(2)}) collective-permute-start(f32[128,256]{1,0:T(8,128)} %get-tuple-element.17), channel_id=1, source_target_pairs={{4,0},{8,4},{12,8},{16,12},{20,16},{24,20},{28,24},{5,1},{9,5},{13... | collective-permute-start | bytes 393224 | tf_op jit(solution)/shard_map/ppermute | solution.py:21
  13.4 3.3 %copy-start.3 = (s32[2,512]{1,0:T(2,128)S(1)}, s32[2,512]{1,0:T(2,128)}, u32[]{:S(2)}) copy-start(s32[2,512]{1,0:T(2,128)} %param.9) | copy-start | bytes 12292
  17.2 0.7 %copy-start.8 = (f32[4,16]{1,0:T(4,128)S(1)}, f32[4,16]{1,0:T(4,128)}, u32[]{:S(2)}) copy-start(f32[4,16]{1,0:T(4,128)} %param.11) | copy-start | bytes 772
  20.7 1.3 %copy-start.1 = (bf16[512,512]{1,0:T(8,128)(2,1)S(1)}, bf16[512,512]{1,0:T(8,128)(2,1)}, u32[]{:S(2)}) copy-start(bf16[512,512]{1,0:T(8,128)(2,1)} %get-tuple-element.9) | copy-start | bytes 1572868
  23.4 1.6 %copy-start.2 = (f32[4,16,128]{2,1,0:T(8,128)S(1)}, f32[4,16,128]{2,1,0:T(8,128)}, u32[]{:S(2)}) copy-start(f32[4,16,128]{2,1,0:T(8,128)} %param.10) | copy-start | bytes 98308
  23.5 3.0 %copy-start.10 = (pred[4]{0:T(512)(128)(4,1)S(1)}, pred[4]{0:T(512)(128)(4,1)}, u32[]{:S(2)}) copy-start(pred[4]{0:T(512)(128)(4,1)} %get-tuple-element.28) | copy-start | bytes 16
  23.5 3.1 %copy-start.7 = (pred[4]{0:T(512)(128)(4,1)S(1)}, pred[4]{0:T(512)(128)(4,1)}, u32[]{:S(2)}) copy-start(pred[4]{0:T(512)(128)(4,1)} %get-tuple-element.27) | copy-start | bytes 16
  24.8 1.9 %copy-start.6 = (pred[4]{0:T(512)(128)(4,1)S(1)}, pred[4]{0:T(512)(128)(4,1)}, u32[]{:S(2)}) copy-start(pred[4]{0:T(512)(128)(4,1)} %get-tuple-element.26) | copy-start | bytes 16
  24.8 2.0 %copy-start.5 = (pred[4]{0:T(512)(128)(4,1)S(1)}, pred[4]{0:T(512)(128)(4,1)}, u32[]{:S(2)}) copy-start(pred[4]{0:T(512)(128)(4,1)} %get-tuple-element.25) | copy-start | bytes 16
  24.9 2.1 %copy-start.4 = (pred[4]{0:T(512)(128)(4,1)S(1)}, pred[4]{0:T(512)(128)(4,1)}, u32[]{:S(2)}) copy-start(pred[4]{0:T(512)(128)(4,1)} %get-tuple-element.24) | copy-start | bytes 16
  26.6 0.8 %copy-start.9 = (pred[4]{0:T(512)(128)(4,1)S(1)}, pred[4]{0:T(512)(128)(4,1)}, u32[]{:S(2)}) copy-start(pred[4]{0:T(512)(128)(4,1)} %get-tuple-element.21) | copy-start | bytes 16
  26.7 1.7 %copy-start = (f32[384,256]{1,0:T(8,128)S(1)}, f32[384,256]{1,0:T(8,128)}, u32[]{:S(2)}) copy-start(f32[384,256]{1,0:T(8,128)} %param.7) | copy-start | bytes 1179652
  30.6 14.4 %collective-permute-start.5 = (f32[256,256]{1,0:T(8,128)S(1)}, f32[256,256]{1,0:T(8,128)S(1)}, u32[]{:S(2)}, u32[]{:S(2)}) collective-permute-start(f32[256,256]{1,0:T(8,128)S(1)} %get-tuple-element.15), channel_id=1, source_target_pairs={{0,4},{4,8},{8,12},{12,16},{16,20},{20,24},{24,28},{1,5},{5,9},{9,... | collective-permute-start | bytes 786440 | tf_op jit(solution)/shard_map/ppermute | solution.py:16
  35.2 9.8 %collective-permute-start.6 = (f32[256,256]{1,0:T(8,128)S(1)}, f32[256,256]{1,0:T(8,128)S(1)}, u32[]{:S(2)}, u32[]{:S(2)}) collective-permute-start(f32[256,256]{1,0:T(8,128)S(1)} %get-tuple-element.16), channel_id=1, source_target_pairs={{4,0},{8,4},{12,8},{16,12},{20,16},{24,20},{28,24},{5,1},{9,5},{13... | collective-permute-start | bytes 786440 | tf_op jit(solution)/shard_map/ppermute | solution.py:21
  46.3 6.9 %collective-permute-start.7 = (f32[128,256]{1,0:T(8,128)S(1)}, f32[128,256]{1,0:T(8,128)S(1)}, u32[]{:S(2)}, u32[]{:S(2)}) collective-permute-start(f32[128,256]{1,0:T(8,128)S(1)} %get-tuple-element.13), channel_id=1, source_target_pairs={{0,4},{4,8},{8,12},{12,16},{16,20},{20,24},{24,28},{1,5},{5,9},{9,... | collective-permute-start | bytes 393224 | tf_op jit(solution)/shard_map/ppermute | solution.py:16
  50.7 8.0 %collective-permute-start.8 = (f32[128,256]{1,0:T(8,128)S(1)}, f32[128,256]{1,0:T(8,128)S(1)}, u32[]{:S(2)}, u32[]{:S(2)}) collective-permute-start(f32[128,256]{1,0:T(8,128)S(1)} %get-tuple-element.14), channel_id=1, source_target_pairs={{4,0},{8,4},{12,8},{16,12},{20,16},{24,20},{28,24},{5,1},{9,5},{13... | collective-permute-start | bytes 393224 | tf_op jit(solution)/shard_map/ppermute | solution.py:21

commit v6 on v5

--- a/solution.py
+++ b/solution.py
@@ -58,28 +58,15 @@
     return placed.reshape(slots * channels, ext), weights.reshape(slots * channels)
 
 
-def split_parts(x, axis):
-    hi = lax.reduce_precision(x, exponent_bits=8, mantissa_bits=7)
-    rest = x - hi
-    mid = lax.reduce_precision(rest, exponent_bits=8, mantissa_bits=7)
-    lo = rest - mid
-    return jnp.concatenate([hi, mid, lo], axis=axis).astype(jnp.bfloat16)
-
-
 def cell_operator(cell_matrix, connectivity, ext):
     cells, nodes, _ = cell_matrix.shape
     rows = jnp.arange(ext, dtype=connectivity.dtype)
-    onehot = (connectivity[:, :, None] == rows[None, None, :]).astype(jnp.bfloat16)
+    onehot = (connectivity[:, :, None] == rows[None, None, :]).astype(jnp.float32)
     total = None
     for c in range(cells):
-        moved = jnp.dot(
-            split_parts(cell_matrix[c], 1),
-            jnp.concatenate([onehot[c]] * 3, axis=0),
-            preferred_element_type=jnp.float32,
-        )
+        moved = jnp.dot(cell_matrix[c], onehot[c], precision=lax.Precision.HIGH)
         part = lax.dot_general(
-            onehot[c].astype(jnp.float32), moved, (((0,), (0,)), ((), ())),
-            precision=lax.Precision.HIGH,
+            onehot[c], moved, (((0,), (0,)), ((), ())), precision=lax.Precision.HIGH
         )
         total = part if total is None else total + part
     return total

time: 59.9 us -> 61.5 us (1.027)
  matrix products: 11.5 us -> 16.2 us
  other arithmetic: 7.92 us -> 6.06 us
  local copies, waits for them, and re-layouts: 4.06 us -> 2.71 us
    dot_general x4, matrix products: 6.77 us -> 11.6 us  [the longest x2 5.82 us: cell_operator(): moved = jnp.dot(cell_matrix[c], onehot[c], precision=lax.Precision.HIGH)]
    another operation x1 -> x0, other arithmetic: 3.27 us -> none
    select_n x8, other arithmetic: 0.86 us -> 2.12 us  [shift_right(): x = jnp.where((amount >> b & 1)[:, None, None] == 1, moved, x)]
    unnamed x24 -> x20, local copies, waits for them, and re-layouts: 1.54 us -> 0.31 us
    eq x1, other arithmetic: 0.54 us -> 1.27 us  [cell_operator(): connectivity[:, :, None] == rows[None, None, :]]
    ppermute x3, starting transfers between devices: 13 us -> 12.3 us  [from_left(): return lax.ppermute(x, axis, [(i, i + 1) for i in range(count - 1)])]
    eq x1, other arithmetic: 1.25 us -> 0.6 us  [shift_right(): x = jnp.where((amount >> b & 1)[:, None, None] == 1, moved, x)]
    ppermute x3, waiting for transfers between devices: 5.48 us -> 6.11 us  [from_right(): return lax.ppermute(x, axis, [(i + 1, i) for i in range(count - 1)])]
  transfers between devices with their start and end apart: 9 -> 9, of which waited for: 3 -> 3; matrix products, arithmetic and copies ran while one was open for 31% -> 34% of each run, Pallas kernels for 0% -> 0%
where the time goes in v6:
time: 61.5 us; the launch traced here: 61 us
  starting transfers between devices  20.8 us (34%)
  matrix products  16.2 us (26%)
  waiting for transfers between devices  14.1 us (23%)
  other arithmetic  6.06 us (10%)
  local copies, waits for them, and re-layouts  2.71 us (4%)
  between operations  1.04 us (2%)
    ppermute x3, starting transfers between devices, from_left(): return lax.ppermute(x, axis, [(i, i + 1) for i in range(count - 1)])  12.3 us
    ppermute x3, waiting for transfers between devices, from_left(): return lax.ppermute(x, axis, [(i, i + 1) for i in range(count - 1)])  8.01 us
    ppermute x3, waiting for transfers between devices, from_right(): return lax.ppermute(x, axis, [(i + 1, i) for i in range(count - 1)])  6.11 us
    dot_general x2, matrix products, cell_operator(): moved = jnp.dot(cell_matrix[c], onehot[c], precision=lax.Precision.HIGH)  5.82 us
    dot_general x2, matrix products, cell_operator(): lax.dot_general(onehot[c], moved, (((0,), (0,)), ((), ())), precision=lax...  5.74 us
    ppermute x3, starting transfers between devices, gather_band(): lax.ppermute(piece, 'band', [(i, (i + k) % count) for i in range(count)])  4.4 us
    ppermute x3, starting transfers between devices, from_right(): return lax.ppermute(x, axis, [(i + 1, i) for i in range(count - 1)])  4.06 us
    select_n x8, other arithmetic, shift_right(): x = jnp.where((amount >> b & 1)[:, None, None] == 1, moved, x)  2.12 us
  transfers between devices with their start and end apart: 9, of which 3 were waited for; matrix products, arithmetic and copies ran while one was open for 34% of the time, Pallas kernels for 0%

profile of v6, /device:TPU:0, one launch (start us, length us, event | category | flops | bytes accessed | tf_op | source)
XLA Modules:
  0.0 61.0 jit_solution(1323774009862851483)
XLA Ops:
  0.0 0.5 collective-permute-start
  0.5 2.5 %collective-permute-start.1 = (f32[4,16,128]{2,1,0:T(8,128)}, f32[4,16,128]{2,1,0:T(8,128)}, u32[]{:S(2)}, u32[]{:S(2)}) collective-permute-start(f32[4,16,128]{2,1,0:T(8,128)} %param.10), channel_id=1, source_target_pairs={{0,2},{1,3},{2,0},{3,1},{4,6},{5,7},{6,4},{7,5},{8,10},{9,11},{10,... | collective-permute-start | bytes 98312 | tf_op jit(solution)/shard_map/ppermute | solution.py:30
  3.0 1.4 %collective-permute-start.2 = (f32[4,16,128]{2,1,0:T(8,128)}, f32[4,16,128]{2,1,0:T(8,128)}, u32[]{:S(2)}, u32[]{:S(2)}) collective-permute-start(f32[4,16,128]{2,1,0:T(8,128)} %param.10), channel_id=1, source_target_pairs={{0,3},{1,0},{2,1},{3,2},{4,7},{5,4},{6,5},{7,6},{8,11},{9,8},{10,9... | collective-permute-start | bytes 98312 | tf_op jit(solution)/shard_map/ppermute | solution.py:30
  4.4 1.7 %fusion.28 = (f32[128,256]{1,0:T(8,128)}, f32[128,256]{1,0:T(8,128)}) fusion(f32[384,256]{1,0:T(8,128)} %param.7), kind=kLoop, calls=%fused_computation.73 | loop fusion | bytes 524288 | tf_op jit(solution)/shard_map/slice | solution.py:85
  6.1 3.4 %collective-permute-start.3 = (f32[128,256]{1,0:T(8,128)}, f32[128,256]{1,0:T(8,128)S(1)}, u32[]{:S(2)}, u32[]{:S(2)}) collective-permute-start(f32[128,256]{1,0:T(8,128)} %get-tuple-element.10), channel_id=1, source_target_pairs={{0,4},{4,8},{8,12},{12,16},{16,20},{20,24},{24,28},{1,5},{5,9},{9,... | collective-permute-start | bytes 393224 | tf_op jit(solution)/shard_map/ppermute | solution.py:16
  9.5 1.3 %collective-permute-start.4 = (f32[128,256]{1,0:T(8,128)}, f32[128,256]{1,0:T(8,128)S(1)}, u32[]{:S(2)}, u32[]{:S(2)}) collective-permute-start(f32[128,256]{1,0:T(8,128)} %get-tuple-element.9), channel_id=1, source_target_pairs={{4,0},{8,4},{12,8},{16,12},{20,16},{24,20},{28,24},{5,1},{9,5},{13... | collective-permute-start | bytes 393224 | tf_op jit(solution)/shard_map/ppermute | solution.py:21
  10.8 0.0 copy-start.2
  10.8 1.3 %iota_compare_fusion = pred[2,512,640]{2,1,0:T(32,128)(4,1)S(1)} fusion(s32[2,512]{1,0:T(2,128)} %param.9), kind=kLoop, calls=%fused_computation.1 | loop fusion | flops 655360 | bytes 659456 | tf_op jit(solution)/shard_map/eq | solution.py:64
  12.1 3.6 %fusion.5 = f32[640,512]{1,0:T(8,128)} fusion(f32[2,512,512]{2,1,0:T(8,128)} %param.8, pred[2,512,640]{2,1,0:T(32,128)(4,1)S(1)} %iota_compare_fusion), kind=kOutput, calls=%fused_computation.13 | convolution fusion | flops 1006960640 | bytes 2686976 | tf_op jit(solution)/shard_map/dot_general | solution.py:67
  15.7 2.2 %fusion.3 = f32[640,512]{1,0:T(8,128)} fusion(f32[2,512,512]{2,1,0:T(8,128)S(1)} %copy-done.2, pred[2,512,640]{2,1,0:T(32,128)(4,1)S(1)} %iota_compare_fusion), kind=kOutput, calls=%fused_computation.11 | convolution fusion | flops 1006960640 | bytes 2686976 | tf_op jit(solution)/shard_map/dot_general | solution.py:67
  17.9 0.6 and_compare_fusion.7
  19.2 0.0 copy-start.6
  19.2 2.8 %fusion.10 = f32[640,640]{1,0:T(8,128)S(1)} fusion(f32[640,512]{1,0:T(8,128)} %fusion.5, pred[2,512,640]{2,1,0:T(32,128)(4,1)S(1)} %iota_compare_fusion), kind=kOutput, calls=%fused_computation.17 | convolution fusion | flops 1258618880 | bytes 3276800 | tf_op jit(solution)/shard_map/dot_general | solution.py:68
  22.1 0.1 broadcast_multiply_fusion
  22.2 2.9 %convolution_add_fusion = f32[640,640]{1,0:T(8,128)S(1)} fusion(f32[640,640]{1,0:T(8,128)S(1)} %fusion.10, f32[640,512]{1,0:T(8,128)} %fusion.3, pred[2,512,640]{2,1,0:T(32,128)(4,1)} %copy-done), kind=kOutput, calls=%fused_computation.4 | convolution fusion | flops 1259028480 | bytes 4915200 | tf_op jit(solution)/shard_map/dot_general | solution.py:68
  25.1 0.1 mul.44
  25.2 0.0 collective-permute-done
  25.2 0.0 collective-permute-done.1
  25.2 0.0 collective-permute-done.2
  25.2 0.8 %pad_maximum_fusion = f32[4,4,16,128]{3,2,1,0:T(8,128)S(1)} fusion(f32[1,4,16,128]{3,2,1,0:T(8,128)} %bitcast.7, f32[1,4,16,128]{3,2,1,0:T(8,128)} %bitcast.6, f32[1,4,16,128]{3,2,1,0:T(8,128)} %bitcast.5, f32[1,4,16,128]{3,2,1,0:T(8,128)} %bitcast.60), kind=kLoop, calls=%fused_computation.36 | loop fusion | flops 98304 | bytes 262144 | tf_op jit(solution)/shard_map/stack | solution.py:32
  26.1 0.6 gather_fusion
  26.6 0.1 copy_bitcast_fusion
  26.7 0.7 %pad_select_fusion = f32[4,16,640]{2,1,0:T(8,128)S(1)} fusion(f32[4,16,512]{2,1,0:T(8,128)S(1)} %copy_bitcast_fusion, f32[4,16,639]{2,1,0:T(8,128)S(1)} %pad_slice_fusion, pred[4]{0:T(512)(128)(4,1)} %get-tuple-element.18), kind=kLoop, calls=%fused_computation.26 | loop fusion | flops 40960 | bytes 458500 | tf_op jit(solution)/shard_map/jit(_where)/select_n | solution.py:45
  27.5 0.7 %pad_select_fusion.7 = f32[4,16,640]{2,1,0:T(8,128)S(1)} fusion(f32[4,16,640]{2,1,0:T(8,128)S(1)} %pad_select_fusion, f32[4,16,638]{2,1,0:T(8,128)S(1)} %bitcast.54, pred[4]{0:T(512)(128)(4,1)} %get-tuple-element.17), kind=kLoop, calls=%fused_computation.34 | loop fusion | flops 40960 | bytes 491012 | tf_op jit(solution)/shard_map/jit(_where)/select_n | solution.py:45
  28.3 0.0 copy-start.1
  28.3 0.1 pad_select_fusion.6
  28.4 0.1 pad_select_fusion.5
  28.5 0.1 pad_select_fusion.4
  28.6 0.1 pad_select_fusion.3
  28.8 0.1 pad_select_fusion.2
  28.9 0.1 pad_select_fusion.1
  29.0 0.0 collective-permute-done.3
  29.0 0.2 copy-done.1
  29.3 0.0 collective-permute-done.4
  29.3 0.4 convolution_multiply_fusion
  29.8 0.7 %fusion.29 = f32[640,256]{1,0:T(8,128)S(1)} fusion(f32[64,640]{1,0:T(8,128)S(1)} %bitcast.53, f32[64,256]{1,0:T(8,128)S(1)} %convolution_multiply_fusion), kind=kOutput, calls=%fused_computation.74 | convolution fusion | flops 125829120 | bytes 884736 | tf_op jit(solution)/shard_map/dot_general | solution.py:93
  30.5 0.9 %convolution_add_fusion.1 = f32[640,256]{1,0:T(8,128)S(1)} fusion(f32[640,256]{1,0:T(8,128)S(1)} %fusion.29, f32[640,640]{1,0:T(8,128)S(1)} %convolution_add_fusion, f32[640,256]{1,0:T(8,128)S(1)} %constant_dynamic-update-slice_fusion), kind=kOutput, calls=%fused_computation.9 | convolution fusion | flops 629309440 | bytes 3604480 | tf_op jit(solution)/shard_map/dot_general | solution.py:93
  31.5 4.6 %collective-permute-start.5 = (f32[256,256]{1,0:T(8,128)S(1)}, f32[256,256]{1,0:T(8,128)S(1)}, u32[]{:S(2)}, u32[]{:S(2)}) collective-permute-start(f32[256,256]{1,0:T(8,128)S(1)} %get-tuple-element.7), channel_id=1, source_target_pairs={{0,4},{4,8},{8,12},{12,16},{16,20},{20,24},{24,28},{1,5},{5,9},{9,... | collective-permute-start | bytes 786440 | tf_op jit(solution)/shard_map/ppermute | solution.py:16
  36.1 1.5 %collective-permute-start.6 = (f32[256,256]{1,0:T(8,128)S(1)}, f32[256,256]{1,0:T(8,128)S(1)}, u32[]{:S(2)}, u32[]{:S(2)}) collective-permute-start(f32[256,256]{1,0:T(8,128)S(1)} %get-tuple-element.8), channel_id=1, source_target_pairs={{4,0},{8,4},{12,8},{16,12},{20,16},{24,20},{28,24},{5,1},{9,5},{13... | collective-permute-start | bytes 786440 | tf_op jit(solution)/shard_map/ppermute | solution.py:21
  37.5 1.6 %fusion.17 = f32[640,640,1]{1,0,2:T(8,128)S(1)} fusion(f32[4,16,640]{2,1,0:T(8,128)S(1)} %pad_select_fusion.1, f32[4,16]{1,0:T(4,128)S(1)} %broadcast_multiply_fusion), kind=kOutput, calls=%fused_computation.24 | convolution fusion | flops 314613760 | bytes 1802496 | tf_op jit(solution)/shard_map/dot_general | solution.py:90
  39.1 6.8 %collective-permute-done.5 = f32[256,256]{1,0:T(8,128)S(1)} collective-permute-done((f32[256,256]{1,0:T(8,128)S(1)}, f32[256,256]{1,0:T(8,128)S(1)}, u32[]{:S(2)}, u32[]{:S(2)}) %collective-permute-start.5) | collective-permute-done | bytes 262176 | tf_op jit(solution)/shard_map/ppermute | solution.py:16
  45.9 0.2 multiply_select_fusion
  46.1 1.0 %fusion = f32[640,256]{1,0:T(8,128)S(1)} fusion(f32[640,256]{1,0:T(8,128)S(1)} %multiply_select_fusion, f32[640,640]{1,0:T(8,128)S(1)} %convolution_add_fusion, f32[640,640,1]{1,0,2:T(8,128)S(1)} %fusion.17), kind=kOutput, calls=%fused_computation.3 | convolution fusion | flops 629555200 | bytes 4587520 | tf_op jit(solution)/shard_map/dot_general | solution.py:112
  47.2 4.4 %collective-permute-start.7 = (f32[128,256]{1,0:T(8,128)S(1)}, f32[128,256]{1,0:T(8,128)S(1)}, u32[]{:S(2)}, u32[]{:S(2)}) collective-permute-start(f32[128,256]{1,0:T(8,128)S(1)} %get-tuple-element.5), channel_id=1, source_target_pairs={{0,4},{4,8},{8,12},{12,16},{16,20},{20,24},{24,28},{1,5},{5,9},{9,... | collective-permute-start | bytes 393224 | tf_op jit(solution)/shard_map/ppermute | solution.py:16
  51.5 1.3 %collective-permute-start.8 = (f32[128,256]{1,0:T(8,128)S(1)}, f32[128,256]{1,0:T(8,128)S(1)}, u32[]{:S(2)}, u32[]{:S(2)}) collective-permute-start(f32[128,256]{1,0:T(8,128)S(1)} %get-tuple-element.6), channel_id=1, source_target_pairs={{4,0},{8,4},{12,8},{16,12},{20,16},{24,20},{28,24},{5,1},{9,5},{13... | collective-permute-start | bytes 393224 | tf_op jit(solution)/shard_map/ppermute | solution.py:21
  52.8 1.2 %collective-permute-done.7 = f32[128,256]{1,0:T(8,128)S(1)} collective-permute-done((f32[128,256]{1,0:T(8,128)S(1)}, f32[128,256]{1,0:T(8,128)S(1)}, u32[]{:S(2)}, u32[]{:S(2)}) %collective-permute-start.7) | collective-permute-done | bytes 131104 | tf_op jit(solution)/shard_map/ppermute | solution.py:16
  54.0 6.1 %collective-permute-done.8 = f32[128,256]{1,0:T(8,128)S(1)} collective-permute-done((f32[128,256]{1,0:T(8,128)S(1)}, f32[128,256]{1,0:T(8,128)S(1)}, u32[]{:S(2)}, u32[]{:S(2)}) %collective-permute-start.8) | collective-permute-done | bytes 131104 | tf_op jit(solution)/shard_map/ppermute | solution.py:21
  60.2 0.8 %fusion.15 = f32[384,256]{1,0:T(8,128)} fusion(f32[384,256]{1,0:T(8,128)S(1)} %copy-done.1, f32[640,256]{1,0:T(8,128)S(1)} %multiply_select_fusion, f32[640,256]{1,0:T(8,128)S(1)} %fusion, f32[128,256]{1,0:T(8,128)S(1)} %collective-permute-done.8, f32[128,256]{1,0:T(8,128)S(1)} %collective-permute-done.7), kind=kLoop, calls=%fused_computation.21 | loop fusion | flops 491520 | bytes 1835008 | tf_op jit(solution)/shard_map/sub | solution.py:122
  (27 shorter events, 0.2 us)
Async XLA Ops:
  0.0 25.2 %collective-permute-start = (f32[4,16,128]{2,1,0:T(8,128)}, f32[4,16,128]{2,1,0:T(8,128)}, u32[]{:S(2)}, u32[]{:S(2)}) collective-permute-start(f32[4,16,128]{2,1,0:T(8,128)} %param.10), channel_id=1, source_target_pairs={{0,1},{1,2},{2,3},{3,0},{4,5},{5,6},{6,7},{7,4},{8,9},{9,10},{10,1... | collective-permute-start | bytes 98312 | tf_op jit(solution)/shard_map/ppermute | solution.py:30
  0.5 24.8 %collective-permute-start.1 = (f32[4,16,128]{2,1,0:T(8,128)}, f32[4,16,128]{2,1,0:T(8,128)}, u32[]{:S(2)}, u32[]{:S(2)}) collective-permute-start(f32[4,16,128]{2,1,0:T(8,128)} %param.10), channel_id=1, source_target_pairs={{0,2},{1,3},{2,0},{3,1},{4,6},{5,7},{6,4},{7,5},{8,10},{9,11},{10,... | collective-permute-start | bytes 98312 | tf_op jit(solution)/shard_map/ppermute | solution.py:30
  3.0 22.3 %collective-permute-start.2 = (f32[4,16,128]{2,1,0:T(8,128)}, f32[4,16,128]{2,1,0:T(8,128)}, u32[]{:S(2)}, u32[]{:S(2)}) collective-permute-start(f32[4,16,128]{2,1,0:T(8,128)} %param.10), channel_id=1, source_target_pairs={{0,3},{1,0},{2,1},{3,2},{4,7},{5,4},{6,5},{7,6},{8,11},{9,8},{10,9... | collective-permute-start | bytes 98312 | tf_op jit(solution)/shard_map/ppermute | solution.py:30
  6.1 22.9 %collective-permute-start.3 = (f32[128,256]{1,0:T(8,128)}, f32[128,256]{1,0:T(8,128)S(1)}, u32[]{:S(2)}, u32[]{:S(2)}) collective-permute-start(f32[128,256]{1,0:T(8,128)} %get-tuple-element.10), channel_id=1, source_target_pairs={{0,4},{4,8},{8,12},{12,16},{16,20},{20,24},{24,28},{1,5},{5,9},{9,... | collective-permute-start | bytes 393224 | tf_op jit(solution)/shard_map/ppermute | solution.py:16
  9.5 19.8 %collective-permute-start.4 = (f32[128,256]{1,0:T(8,128)}, f32[128,256]{1,0:T(8,128)S(1)}, u32[]{:S(2)}, u32[]{:S(2)}) collective-permute-start(f32[128,256]{1,0:T(8,128)} %get-tuple-element.9), channel_id=1, source_target_pairs={{4,0},{8,4},{12,8},{16,12},{20,16},{24,20},{28,24},{5,1},{9,5},{13... | collective-permute-start | bytes 393224 | tf_op jit(solution)/shard_map/ppermute | solution.py:21
  10.8 4.9 %copy-start.2 = (f32[2,512,512]{2,1,0:T(8,128)S(1)}, f32[2,512,512]{2,1,0:T(8,128)}, u32[]{:S(2)}) copy-start(f32[2,512,512]{2,1,0:T(8,128)} %param.8) | copy-start | bytes 6291460
  12.1 7.1 %copy-start = (pred[2,512,640]{2,1,0:T(32,128)(4,1)}, pred[2,512,640]{2,1,0:T(32,128)(4,1)S(1)}, u32[]{:S(2)}) copy-start(pred[2,512,640]{2,1,0:T(32,128)(4,1)S(1)} %iota_compare_fusion) | copy-start | bytes 1966084
  15.7 2.2 %copy-start.8 = (s32[4]{0:T(128)S(1)}, s32[4]{0:T(128)}, u32[]{:S(2)}) copy-start(s32[4]{0:T(128)} %param.12) | copy-start | bytes 52
  19.2 2.9 %copy-start.6 = (f32[4,16]{1,0:T(4,128)S(1)}, f32[4,16]{1,0:T(4,128)}, u32[]{:S(2)}) copy-start(f32[4,16]{1,0:T(4,128)} %param.11) | copy-start | bytes 772
  25.1 3.2 %copy-start.5 = (pred[4]{0:T(512)(128)(4,1)S(1)}, pred[4]{0:T(512)(128)(4,1)}, u32[]{:S(2)}) copy-start(pred[4]{0:T(512)(128)(4,1)} %get-tuple-element.16) | copy-start | bytes 16
  25.1 3.3 %copy-start.4 = (pred[4]{0:T(512)(128)(4,1)S(1)}, pred[4]{0:T(512)(128)(4,1)}, u32[]{:S(2)}) copy-start(pred[4]{0:T(512)(128)(4,1)} %get-tuple-element.15) | copy-start | bytes 16
  25.1 3.4 %copy-start.3 = (pred[4]{0:T(512)(128)(4,1)S(1)}, pred[4]{0:T(512)(128)(4,1)}, u32[]{:S(2)}) copy-start(pred[4]{0:T(512)(128)(4,1)} %get-tuple-element.14) | copy-start | bytes 16
  27.5 1.4 %copy-start.7 = (pred[4]{0:T(512)(128)(4,1)S(1)}, pred[4]{0:T(512)(128)(4,1)}, u32[]{:S(2)}) copy-start(pred[4]{0:T(512)(128)(4,1)} %get-tuple-element.11) | copy-start | bytes 16
  28.3 1.0 %copy-start.1 = (f32[384,256]{1,0:T(8,128)S(1)}, f32[384,256]{1,0:T(8,128)}, u32[]{:S(2)}) copy-start(f32[384,256]{1,0:T(8,128)} %param.7) | copy-start | bytes 1179652
  31.5 14.4 %collective-permute-start.5 = (f32[256,256]{1,0:T(8,128)S(1)}, f32[256,256]{1,0:T(8,128)S(1)}, u32[]{:S(2)}, u32[]{:S(2)}) collective-permute-start(f32[256,256]{1,0:T(8,128)S(1)} %get-tuple-element.7), channel_id=1, source_target_pairs={{0,4},{4,8},{8,12},{12,16},{16,20},{20,24},{24,28},{1,5},{5,9},{9,... | collective-permute-start | bytes 786440 | tf_op jit(solution)/shard_map/ppermute | solution.py:16
  36.1 9.9 %collective-permute-start.6 = (f32[256,256]{1,0:T(8,128)S(1)}, f32[256,256]{1,0:T(8,128)S(1)}, u32[]{:S(2)}, u32[]{:S(2)}) collective-permute-start(f32[256,256]{1,0:T(8,128)S(1)} %get-tuple-element.8), channel_id=1, source_target_pairs={{4,0},{8,4},{12,8},{16,12},{20,16},{24,20},{28,24},{5,1},{9,5},{13... | collective-permute-start | bytes 786440 | tf_op jit(solution)/shard_map/ppermute | solution.py:21
  47.2 6.9 %collective-permute-start.7 = (f32[128,256]{1,0:T(8,128)S(1)}, f32[128,256]{1,0:T(8,128)S(1)}, u32[]{:S(2)}, u32[]{:S(2)}) collective-permute-start(f32[128,256]{1,0:T(8,128)S(1)} %get-tuple-element.5), channel_id=1, source_target_pairs={{0,4},{4,8},{8,12},{12,16},{16,20},{20,24},{24,28},{1,5},{5,9},{9,... | collective-permute-start | bytes 393224 | tf_op jit(solution)/shard_map/ppermute | solution.py:16
  51.5 8.6 %collective-permute-start.8 = (f32[128,256]{1,0:T(8,128)S(1)}, f32[128,256]{1,0:T(8,128)S(1)}, u32[]{:S(2)}, u32[]{:S(2)}) collective-permute-start(f32[128,256]{1,0:T(8,128)S(1)} %get-tuple-element.6), channel_id=1, source_target_pairs={{4,0},{8,4},{12,8},{16,12},{20,16},{24,20},{28,24},{5,1},{9,5},{13... | collective-permute-start | bytes 393224 | tf_op jit(solution)/shard_map/ppermute | solution.py:21

commit v7 on v6

--- a/solution.py
+++ b/solution.py
@@ -58,18 +58,20 @@
     return placed.reshape(slots * channels, ext), weights.reshape(slots * channels)
 
 
-def cell_operator(cell_matrix, connectivity, ext):
+def cell_maps(cell_matrix, connectivity, ext):
     cells, nodes, _ = cell_matrix.shape
     rows = jnp.arange(ext, dtype=connectivity.dtype)
     onehot = (connectivity[:, :, None] == rows[None, None, :]).astype(jnp.float32)
-    total = None
-    for c in range(cells):
-        moved = jnp.dot(cell_matrix[c], onehot[c], precision=lax.Precision.HIGH)
-        part = lax.dot_general(
-            onehot[c], moved, (((0,), (0,)), ((), ())), precision=lax.Precision.HIGH
-        )
-        total = part if total is None else total + part
-    return total
+    moved = jnp.stack(
+        [jnp.dot(cell_matrix[c], onehot[c], precision=lax.Precision.HIGH) for c in range(cells)]
+    )
+    return onehot.reshape(cells * nodes, ext), moved.reshape(cells * nodes, ext)
+
+
+def scatter_rows(onehot, values):
+    return lax.dot_general(
+        onehot, values, (((0,), (0,)), ((), ())), precision=lax.Precision.HIGH
+    )
 
 
 def on_device(
@@ -86,12 +88,15 @@
     extended = jnp.concatenate([low, wavefunctions, high], axis=0)
 
     placed, weights = atom_rows(gather_band(projector), coupling, atom_start, atom_count, ext)
-    cells = cell_operator(cell_matrix, connectivity, ext)
-    operator = cells + jnp.dot((placed * weights[:, None]).T, placed, precision=highest)
+    onehot, moved = cell_maps(cell_matrix, connectivity, ext)
 
     coefficients = jnp.dot(placed, extended, precision=highest) * weights[:, None]
-    first = jnp.dot(cells, extended, precision=lax.Precision.HIGH) + jnp.dot(
-        placed.T, coefficients, precision=highest
+    local = jnp.dot(moved, extended, precision=lax.Precision.HIGH)
+    first = scatter_rows(onehot, local) + jnp.dot(placed.T, coefficients, precision=highest)
+
+    moved, first = lax.optimization_barrier((moved, first))
+    operator = scatter_rows(onehot, moved) + jnp.dot(
+        (placed * weights[:, None]).T, placed, precision=highest
     )
     left_sums = from_left(first[ext - 2 * g :], "dom")
     right_sums = from_right(first[: 2 * g], "dom")
@@ -109,10 +114,11 @@
     step_ext = jnp.where(keep, step_ext, 0.0)
     step_one = step_ext[g : g + own]
 
-    second = jnp.dot(operator, step_ext, precision=lax.Precision.HIGH)
-    from_before = from_left(second[ext - g :], "dom")
-    from_after = from_right(second[:g], "dom")
-    owned = second[g : g + own]
+    edges = jnp.concatenate([operator[:g], operator[ext - g :]], axis=0)
+    second_edges = jnp.dot(edges, step_ext, precision=lax.Precision.HIGH)
+    from_before = from_left(second_edges[g:], "dom")
+    from_after = from_right(second_edges[:g], "dom")
+    owned = jnp.dot(operator[g : g + own], step_ext, precision=lax.Precision.HIGH)
     zeros_own = jnp.zeros((own - g, owned.shape[1]), jnp.float32)
     second_image = (
         owned

time: 61.5 us -> 55.8 us (0.907)
  waiting for transfers between devices: 14.1 us -> 11.3 us
  other arithmetic: 6.06 us -> 4.28 us
  local copies, waits for them, and re-layouts: 2.71 us -> 1.86 us
    ppermute x3, waiting for transfers between devices: 6.11 us -> 2.35 us  [from_right(): return lax.ppermute(x, axis, [(i + 1, i) for i in range(count - 1)])]
    another operation x0 -> x1, other arithmetic: none -> 1.89 us  [cell_maps(): jnp.stack([jnp.dot(cell_matrix[c], onehot[c], precision=lax.Precision.HIG...]
    ppermute x3, starting transfers between devices: 12.3 us -> 13.8 us  [from_left(): return lax.ppermute(x, axis, [(i, i + 1) for i in range(count - 1)])]
    select_n x8, other arithmetic: 2.12 us -> 0.86 us  [shift_right(): x = jnp.where((amount >> b & 1)[:, None, None] == 1, moved, x)]
    ppermute x3, starting transfers between devices: 4.4 us -> 3.17 us  [gather_band(): lax.ppermute(piece, 'band', [(i, (i + k) % count) for i in range(count)])]
    ppermute x3, waiting for transfers between devices: 8.01 us -> 8.96 us  [from_left(): return lax.ppermute(x, axis, [(i, i + 1) for i in range(count - 1)])]
    sub x1 -> x0, other arithmetic: 0.84 us -> none  [on_device(): 2.0 * (second_image - filter_center * step_one) / filter_half]
    another operation x1, other arithmetic: 0.82 us -> 0.01 us  [gather_band(): stacked = jnp.stack(pieces)]
  transfers between devices with their start and end apart: 9 -> 9, of which waited for: 3 -> 4; matrix products, arithmetic and copies ran while one was open for 34% -> 28% of each run, Pallas kernels for 0% -> 0%
where the time goes in v7:
time: 55.8 us; the launch traced here: 55.4 us
  starting transfers between devices  20.9 us (37%)
  matrix products  16.1 us (29%)
  waiting for transfers between devices  11.3 us (20%)
  other arithmetic  4.28 us (8%)
  local copies, waits for them, and re-layouts  1.86 us (3%)
  between operations  1.02 us (2%)
    ppermute x3, starting transfers between devices, from_left(): return lax.ppermute(x, axis, [(i, i + 1) for i in range(count - 1)])  13.8 us
    ppermute x3, waiting for transfers between devices, from_left(): return lax.ppermute(x, axis, [(i, i + 1) for i in range(count - 1)])  8.96 us
    dot_general x2, matrix products, cell_maps(): jnp.dot(cell_matrix[c], onehot[c], precision=lax.Precision.HIGH)  5.59 us
    dot_general x2, matrix products, scatter_rows(): lax.dot_general(onehot, values, (((0,), (0,)), ((), ())), precision=lax.P...  4.45 us
    ppermute x3, starting transfers between devices, from_right(): return lax.ppermute(x, axis, [(i + 1, i) for i in range(count - 1)])  3.88 us
    ppermute x3, starting transfers between devices, gather_band(): lax.ppermute(piece, 'band', [(i, (i + k) % count) for i in range(count)])  3.17 us
    ppermute x3, waiting for transfers between devices, from_right(): return lax.ppermute(x, axis, [(i + 1, i) for i in range(count - 1)])  2.35 us
    another operation x1, other arithmetic, cell_maps(): jnp.stack([jnp.dot(cell_matrix[c], onehot[c], precision=lax.Precision.HIG...  1.89 us
  transfers between devices with their start and end apart: 9, of which 4 were waited for; matrix products, arithmetic and copies ran while one was open for 28% of the time, Pallas kernels for 0%

profile of v7, /device:TPU:0, one launch (start us, length us, event | category | flops | bytes accessed | tf_op | source)
XLA Modules:
  0.0 55.4 jit_solution(11031636959806517779)
XLA Ops:
  0.0 2.4 %collective-permute-start.4 = (f32[4,16,128]{2,1,0:T(8,128)}, f32[4,16,128]{2,1,0:T(8,128)S(1)}, u32[]{:S(2)}, u32[]{:S(2)}) collective-permute-start(f32[4,16,128]{2,1,0:T(8,128)} %param.10), channel_id=1, source_target_pairs={{0,3},{1,0},{2,1},{3,2},{4,7},{5,4},{6,5},{7,6},{8,11},{9,8},{10,9... | collective-permute-start | bytes 98312 | tf_op jit(solution)/shard_map/ppermute | solution.py:30
  2.4 0.6 %collective-permute-start.3 = (f32[4,16,128]{2,1,0:T(8,128)}, f32[4,16,128]{2,1,0:T(8,128)S(1)}, u32[]{:S(2)}, u32[]{:S(2)}) collective-permute-start(f32[4,16,128]{2,1,0:T(8,128)} %param.10), channel_id=1, source_target_pairs={{0,2},{1,3},{2,0},{3,1},{4,6},{5,7},{6,4},{7,5},{8,10},{9,11},{10,... | collective-permute-start | bytes 98312 | tf_op jit(solution)/shard_map/ppermute | solution.py:30
  3.0 0.2 collective-permute-start.2
  3.2 1.0 %fusion.28 = (f32[128,256]{1,0:T(8,128)S(1)}, f32[128,256]{1,0:T(8,128)S(1)}) fusion(f32[384,256]{1,0:T(8,128)} %param.7), kind=kLoop, calls=%fused_computation.78 | loop fusion | bytes 524288 | tf_op jit(solution)/shard_map/slice | solution.py:87
  4.2 3.4 %collective-permute-start = (f32[128,256]{1,0:T(8,128)S(1)}, f32[128,256]{1,0:T(8,128)S(1)}, u32[]{:S(2)}, u32[]{:S(2)}) collective-permute-start(f32[128,256]{1,0:T(8,128)S(1)} %get-tuple-element.14), channel_id=1, source_target_pairs={{0,4},{4,8},{8,12},{12,16},{16,20},{20,24},{24,28},{1,5},{5,9},{9,... | collective-permute-start | bytes 393224 | tf_op jit(solution)/shard_map/ppermute | solution.py:16
  7.6 1.3 %collective-permute-start.1 = (f32[128,256]{1,0:T(8,128)S(1)}, f32[128,256]{1,0:T(8,128)S(1)}, u32[]{:S(2)}, u32[]{:S(2)}) collective-permute-start(f32[128,256]{1,0:T(8,128)S(1)} %get-tuple-element.13), channel_id=1, source_target_pairs={{4,0},{8,4},{12,8},{16,12},{20,16},{24,20},{28,24},{5,1},{9,5},{13... | collective-permute-start | bytes 393224 | tf_op jit(solution)/shard_map/ppermute | solution.py:21
  8.9 1.1 %iota_compare_fusion = pred[2,512,640]{2,1,0:T(32,128)(4,1)S(1)} fusion(s32[2,512]{1,0:T(2,128)} %param.9), kind=kLoop, calls=%fused_computation.2 | loop fusion | flops 655360 | bytes 659456 | tf_op jit(solution)/shard_map/eq | solution.py:64
  10.0 0.0 copy-start.5
  10.0 3.4 %convolution_bitcast_fusion = f32[1,512,640]{2,1,0:T(8,128)} fusion(pred[2,512,640]{2,1,0:T(32,128)(4,1)S(1)} %iota_compare_fusion, f32[2,512,512]{2,1,0:T(8,128)} %param.8), kind=kOutput, calls=%fused_computation.7 | convolution fusion | flops 1006632960 | bytes 2686976 | tf_op jit(solution)/shard_map/dot_general | solution.py:66
  13.5 2.1 %convolution_bitcast_fusion.1 = f32[1,512,640]{2,1,0:T(8,128)} fusion(pred[2,512,640]{2,1,0:T(32,128)(4,1)S(1)} %iota_compare_fusion, f32[2,512,512]{2,1,0:T(8,128)S(1)} %copy-done.1), kind=kOutput, calls=%fused_computation.8 | convolution fusion | flops 1006632960 | bytes 2686976 | tf_op jit(solution)/shard_map/dot_general | solution.py:66
  16.4 0.0 copy-start.4
  16.4 0.0 copy-start.3
  16.4 0.0 copy-start.2
  16.4 1.9 %pad_maximum_fusion = f32[2,512,640]{2,1,0:T(8,128)S(1)} fusion(f32[1,512,640]{2,1,0:T(8,128)} %convolution_bitcast_fusion, f32[1,512,640]{2,1,0:T(8,128)} %convolution_bitcast_fusion.1), kind=kLoop, calls=%fused_computation.1 | loop fusion | flops 655360 | bytes 5242880 | tf_op jit(solution)/shard_map/stack | solution.py:65
  18.3 0.1 broadcast_multiply_fusion
  18.4 0.1 mul.42
  18.5 0.0 collective-permute-done.4
  18.5 0.0 collective-permute-done.3
  18.5 0.0 collective-permute-done.2
  18.5 0.6 %gather_fusion = f32[4,4,16,128]{3,2,1,0:T(8,128)S(1)} fusion(f32[4,4,16,128]{3,2,1,0:T(8,128)S(1)} %pad_maximum_fusion.1, s32[1024]{0:T(1024)S(1)} %pad_clamp_fusion), kind=kCustom, calls=%fused_computation | custom fusion | bytes 262160 | tf_op jit(solution)/shard_map/jit(_take)/gather | solution.py:34
  19.1 0.1 copy_bitcast_fusion
  19.2 0.0 copy-start
  19.2 0.1 pad_select_fusion
  19.3 0.1 pad_select_fusion.7
  19.5 0.1 pad_select_fusion.6
  19.6 0.1 pad_select_fusion.5
  19.7 0.1 pad_select_fusion.4
  19.8 0.1 pad_select_fusion.3
  19.9 0.1 pad_select_fusion.2
  20.1 0.1 pad_select_fusion.1
  20.2 0.0 copy-done
  20.3 0.4 convolution_multiply_fusion
  20.7 0.7 %fusion.31 = f32[640,256]{1,0:T(8,128)S(1)} fusion(f32[64,640]{1,0:T(8,128)S(1)} %bitcast.60, f32[64,256]{1,0:T(8,128)S(1)} %convolution_multiply_fusion), kind=kOutput, calls=%fused_computation.81 | convolution fusion | flops 125829120 | bytes 884736 | tf_op jit(solution)/shard_map/dot_general | solution.py:95
  21.4 1.4 %fusion.30 = f32[1024,256]{1,0:T(8,128)S(1)} fusion(f32[1024,640]{1,0:T(8,128)S(1)} %bitcast.57, f32[640,256]{1,0:T(8,128)S(1)} %constant_dynamic-update-slice_fusion), kind=kOutput, calls=%fused_computation.80 | convolution fusion | flops 1006632960 | bytes 4325376 | tf_op jit(solution)/shard_map/dot_general | solution.py:94
  22.9 1.7 %fusion.4 = f32[640,256]{1,0:T(8,128)S(1)} fusion(f32[640,256]{1,0:T(8,128)S(1)} %fusion.31, f32[1024,256]{1,0:T(8,128)S(1)} %fusion.30, s32[1024]{0:T(1024)S(1)} %bitcast.72), kind=kOutput, calls=%fused_computation.13 | convolution fusion | flops 1007452160 | bytes 2363392 | tf_op jit(solution)/shard_map/dot_general | solution.py:72
  24.6 1.3 %collective-permute-start.6 = (f32[256,256]{1,0:T(8,128)S(1)}, f32[256,256]{1,0:T(8,128)S(1)}, u32[]{:S(2)}, u32[]{:S(2)}) collective-permute-start(f32[256,256]{1,0:T(8,128)S(1)} %get-tuple-element.12), channel_id=1, source_target_pairs={{4,0},{8,4},{12,8},{16,12},{20,16},{24,20},{28,24},{5,1},{9,5},{13... | collective-permute-start | bytes 786440 | tf_op jit(solution)/shard_map/ppermute | solution.py:21
  25.9 5.4 %collective-permute-start.5 = (f32[256,256]{1,0:T(8,128)S(1)}, f32[256,256]{1,0:T(8,128)S(1)}, u32[]{:S(2)}, u32[]{:S(2)}) collective-permute-start(f32[256,256]{1,0:T(8,128)S(1)} %get-tuple-element.11), channel_id=1, source_target_pairs={{0,4},{4,8},{8,12},{12,16},{16,20},{20,24},{24,28},{1,5},{5,9},{9,... | collective-permute-start | bytes 786440 | tf_op jit(solution)/shard_map/ppermute | solution.py:16
  31.3 2.7 %fusion = f32[640,640]{1,0:T(8,128)S(1)} fusion(f32[1024,640]{1,0:T(8,128)S(1)} %bitcast.58, s32[1024]{0:T(1024)S(1)} %bitcast.73), kind=kOutput, calls=%fused_computation.4 | convolution fusion | flops 2517237760 | bytes 4263936 | tf_op jit(solution)/shard_map/dot_general | solution.py:72
  34.0 1.6 %bitcast_add_fusion = f32[640,640]{1,0:T(8,128)S(1)} fusion(f32[640,640]{1,0:T(8,128)S(1)} %fusion, f32[4,16,640]{2,1,0:T(8,128)S(1)} %pad_select_fusion.1, f32[4,16]{1,0:T(4,128)S(1)} %broadcast_multiply_fusion), kind=kOutput, calls=%fused_computation.6 | convolution fusion | flops 315023360 | bytes 3440896 | tf_op jit(solution)/shard_map/dot_general | solution.py:98
  35.7 0.5 collective-permute-done.6
  36.2 6.0 %collective-permute-done.5 = f32[256,256]{1,0:T(8,128)S(1)} collective-permute-done((f32[256,256]{1,0:T(8,128)S(1)}, f32[256,256]{1,0:T(8,128)S(1)}, u32[]{:S(2)}, u32[]{:S(2)}) %collective-permute-start.5) | collective-permute-done | bytes 262176 | tf_op jit(solution)/shard_map/ppermute | solution.py:16
  42.2 0.2 multiply_select_fusion
  42.4 0.5 fusion.11
  42.9 1.3 %collective-permute-start.8 = (f32[128,256]{1,0:T(8,128)S(1)}, f32[128,256]{1,0:T(8,128)S(1)}, u32[]{:S(2)}, u32[]{:S(2)}) collective-permute-start(f32[128,256]{1,0:T(8,128)S(1)} %get-tuple-element.16), channel_id=1, source_target_pairs={{4,0},{8,4},{12,8},{16,12},{20,16},{24,20},{28,24},{5,1},{9,5},{13... | collective-permute-start | bytes 393224 | tf_op jit(solution)/shard_map/ppermute | solution.py:21
  44.2 5.0 %collective-permute-start.7 = (f32[128,256]{1,0:T(8,128)S(1)}, f32[128,256]{1,0:T(8,128)S(1)}, u32[]{:S(2)}, u32[]{:S(2)}) collective-permute-start(f32[128,256]{1,0:T(8,128)S(1)} %get-tuple-element.15), channel_id=1, source_target_pairs={{0,4},{4,8},{8,12},{12,16},{16,20},{20,24},{24,28},{1,5},{5,9},{9,... | collective-permute-start | bytes 393224 | tf_op jit(solution)/shard_map/ppermute | solution.py:16
  49.3 1.8 %collective-permute-done.8 = f32[128,256]{1,0:T(8,128)S(1)} collective-permute-done((f32[128,256]{1,0:T(8,128)S(1)}, f32[128,256]{1,0:T(8,128)S(1)}, u32[]{:S(2)}, u32[]{:S(2)}) %collective-permute-start.8) | collective-permute-done | bytes 131104 | tf_op jit(solution)/shard_map/ppermute | solution.py:21
  51.1 3.0 %collective-permute-done.7 = f32[128,256]{1,0:T(8,128)S(1)} collective-permute-done((f32[128,256]{1,0:T(8,128)S(1)}, f32[128,256]{1,0:T(8,128)S(1)}, u32[]{:S(2)}, u32[]{:S(2)}) %collective-permute-start.7) | collective-permute-done | bytes 131104 | tf_op jit(solution)/shard_map/ppermute | solution.py:16
  54.0 1.4 %fusion.16 = f32[384,256]{1,0:T(8,128)} fusion(f32[384,256]{1,0:T(8,128)S(1)} %copy-done, f32[640,256]{1,0:T(8,128)S(1)} %multiply_select_fusion, f32[128,256]{1,0:T(8,128)S(1)} %collective-permute-done.8, f32[128,256]{1,0:T(8,128)S(1)} %collective-permute-done.7, f32[640,640]{1,0:T(8,128)S(1)} %bitcast_add_fusion), kind=kOutput, calls=%fused_computation.28 | convolution fusion | flops 377978880 | bytes 3080192 | tf_op jit(solution)/shard_map/dot_general | solution.py:121
  (24 shorter events, 0.3 us)
Async XLA Ops:
  0.0 13.5 %copy-start.1 = (f32[2,512,512]{2,1,0:T(8,128)S(1)}, f32[2,512,512]{2,1,0:T(8,128)}, u32[]{:S(2)}) copy-start(f32[2,512,512]{2,1,0:T(8,128)} %param.8) | copy-start | bytes 6291460
  0.0 18.5 %collective-permute-start.4 = (f32[4,16,128]{2,1,0:T(8,128)}, f32[4,16,128]{2,1,0:T(8,128)S(1)}, u32[]{:S(2)}, u32[]{:S(2)}) collective-permute-start(f32[4,16,128]{2,1,0:T(8,128)} %param.10), channel_id=1, source_target_pairs={{0,3},{1,0},{2,1},{3,2},{4,7},{5,4},{6,5},{7,6},{8,11},{9,8},{10,9... | collective-permute-start | bytes 98312 | tf_op jit(solution)/shard_map/ppermute | solution.py:30
  2.4 16.1 %collective-permute-start.3 = (f32[4,16,128]{2,1,0:T(8,128)}, f32[4,16,128]{2,1,0:T(8,128)S(1)}, u32[]{:S(2)}, u32[]{:S(2)}) collective-permute-start(f32[4,16,128]{2,1,0:T(8,128)} %param.10), channel_id=1, source_target_pairs={{0,2},{1,3},{2,0},{3,1},{4,6},{5,7},{6,4},{7,5},{8,10},{9,11},{10,... | collective-permute-start | bytes 98312 | tf_op jit(solution)/shard_map/ppermute | solution.py:30
  3.0 15.5 %collective-permute-start.2 = (f32[4,16,128]{2,1,0:T(8,128)}, f32[4,16,128]{2,1,0:T(8,128)S(1)}, u32[]{:S(2)}, u32[]{:S(2)}) collective-permute-start(f32[4,16,128]{2,1,0:T(8,128)} %param.10), channel_id=1, source_target_pairs={{0,1},{1,2},{2,3},{3,0},{4,5},{5,6},{6,7},{7,4},{8,9},{9,10},{10,1... | collective-permute-start | bytes 98312 | tf_op jit(solution)/shard_map/ppermute | solution.py:30
  4.2 16.0 %collective-permute-start = (f32[128,256]{1,0:T(8,128)S(1)}, f32[128,256]{1,0:T(8,128)S(1)}, u32[]{:S(2)}, u32[]{:S(2)}) collective-permute-start(f32[128,256]{1,0:T(8,128)S(1)} %get-tuple-element.14), channel_id=1, source_target_pairs={{0,4},{4,8},{8,12},{12,16},{16,20},{20,24},{24,28},{1,5},{5,9},{9,... | collective-permute-start | bytes 393224 | tf_op jit(solution)/shard_map/ppermute | solution.py:16
  7.6 12.6 %collective-permute-start.1 = (f32[128,256]{1,0:T(8,128)S(1)}, f32[128,256]{1,0:T(8,128)S(1)}, u32[]{:S(2)}, u32[]{:S(2)}) collective-permute-start(f32[128,256]{1,0:T(8,128)S(1)} %get-tuple-element.13), channel_id=1, source_target_pairs={{4,0},{8,4},{12,8},{16,12},{20,16},{24,20},{28,24},{5,1},{9,5},{13... | collective-permute-start | bytes 393224 | tf_op jit(solution)/shard_map/ppermute | solution.py:21
  10.0 5.6 %copy-start.5 = (s32[4]{0:T(128)S(1)}, s32[4]{0:T(128)}, u32[]{:S(2)}) copy-start(s32[4]{0:T(128)} %param.12) | copy-start | bytes 52
  16.4 1.9 %copy-start.4 = (f32[4,16]{1,0:T(4,128)S(1)}, f32[4,16]{1,0:T(4,128)}, u32[]{:S(2)}) copy-start(f32[4,16]{1,0:T(4,128)} %param.11) | copy-start | bytes 772
  16.4 2.1 %copy-start.3 = (s32[2,512]{1,0:T(2,128)S(1)}, s32[2,512]{1,0:T(2,128)}, u32[]{:S(2)}) copy-start(s32[2,512]{1,0:T(2,128)} %param.9) | copy-start | bytes 12292
  16.4 2.1 %copy-start.2 = (f32[4,16,128]{2,1,0:T(8,128)S(1)}, f32[4,16,128]{2,1,0:T(8,128)}, u32[]{:S(2)}) copy-start(f32[4,16,128]{2,1,0:T(8,128)} %param.10) | copy-start | bytes 98308
  19.2 1.0 %copy-start = (f32[384,256]{1,0:T(8,128)S(1)}, f32[384,256]{1,0:T(8,128)}, u32[]{:S(2)}) copy-start(f32[384,256]{1,0:T(8,128)} %param.7) | copy-start | bytes 1179652
  24.6 11.6 %collective-permute-start.6 = (f32[256,256]{1,0:T(8,128)S(1)}, f32[256,256]{1,0:T(8,128)S(1)}, u32[]{:S(2)}, u32[]{:S(2)}) collective-permute-start(f32[256,256]{1,0:T(8,128)S(1)} %get-tuple-element.12), channel_id=1, source_target_pairs={{4,0},{8,4},{12,8},{16,12},{20,16},{24,20},{28,24},{5,1},{9,5},{13... | collective-permute-start | bytes 786440 | tf_op jit(solution)/shard_map/ppermute | solution.py:21
  25.9 16.3 %collective-permute-start.5 = (f32[256,256]{1,0:T(8,128)S(1)}, f32[256,256]{1,0:T(8,128)S(1)}, u32[]{:S(2)}, u32[]{:S(2)}) collective-permute-start(f32[256,256]{1,0:T(8,128)S(1)} %get-tuple-element.11), channel_id=1, source_target_pairs={{0,4},{4,8},{8,12},{12,16},{16,20},{20,24},{24,28},{1,5},{5,9},{9,... | collective-permute-start | bytes 786440 | tf_op jit(solution)/shard_map/ppermute | solution.py:16
  42.9 8.1 %collective-permute-start.8 = (f32[128,256]{1,0:T(8,128)S(1)}, f32[128,256]{1,0:T(8,128)S(1)}, u32[]{:S(2)}, u32[]{:S(2)}) collective-permute-start(f32[128,256]{1,0:T(8,128)S(1)} %get-tuple-element.16), channel_id=1, source_target_pairs={{4,0},{8,4},{12,8},{16,12},{20,16},{24,20},{28,24},{5,1},{9,5},{13... | collective-permute-start | bytes 393224 | tf_op jit(solution)/shard_map/ppermute | solution.py:21
  44.2 9.8 %collective-permute-start.7 = (f32[128,256]{1,0:T(8,128)S(1)}, f32[128,256]{1,0:T(8,128)S(1)}, u32[]{:S(2)}, u32[]{:S(2)}) collective-permute-start(f32[128,256]{1,0:T(8,128)S(1)} %get-tuple-element.15), channel_id=1, source_target_pairs={{0,4},{4,8},{8,12},{12,16},{16,20},{20,24},{24,28},{1,5},{5,9},{9,... | collective-permute-start | bytes 393224 | tf_op jit(solution)/shard_map/ppermute | solution.py:16

commit v8 on v7

--- a/solution.py
+++ b/solution.py
@@ -62,9 +62,7 @@
     cells, nodes, _ = cell_matrix.shape
     rows = jnp.arange(ext, dtype=connectivity.dtype)
     onehot = (connectivity[:, :, None] == rows[None, None, :]).astype(jnp.float32)
-    moved = jnp.stack(
-        [jnp.dot(cell_matrix[c], onehot[c], precision=lax.Precision.HIGH) for c in range(cells)]
-    )
+    moved = jnp.einsum("cij,cjq->ciq", cell_matrix, onehot, precision=lax.Precision.HIGH)
     return onehot.reshape(cells * nodes, ext), moved.reshape(cells * nodes, ext)
 
 
@@ -118,7 +116,9 @@
     second_edges = jnp.dot(edges, step_ext, precision=lax.Precision.HIGH)
     from_before = from_left(second_edges[g:], "dom")
     from_after = from_right(second_edges[:g], "dom")
-    owned = jnp.dot(operator[g : g + own], step_ext, precision=lax.Precision.HIGH)
+    owned = lax.optimization_barrier(
+        jnp.dot(operator[g : g + own], step_ext, precision=lax.Precision.HIGH)
+    )
     zeros_own = jnp.zeros((own - g, owned.shape[1]), jnp.float32)
     second_image = (
         owned

time: 55.8 us -> 51.5 us (0.923)
  matrix products: 16.1 us -> 14 us
  other arithmetic: 4.28 us -> 2.76 us
  waiting for transfers between devices: 11.3 us -> 10.6 us
    dot_general x3 -> x2, matrix products: 6.99 us -> 4.83 us  [the longest x1 4.19 us: cell_maps(): jnp.einsum('cij,cjq->ciq', cell_matrix, onehot, precision=lax.Precision.H...]
    another operation x1 -> x0, other arithmetic: 1.89 us -> none  [cell_maps(): jnp.stack([jnp.dot(cell_matrix[c], onehot[c], precision=lax.Precision.HIG...]
    eq x1 -> x0, other arithmetic: 1.12 us -> none  [cell_maps(): connectivity[:, :, None] == rows[None, None, :]]
    sub x0 -> x1, other arithmetic: none -> 0.84 us  [on_device(): 2.0 * (second_image - filter_center * step_one) / filter_half]
    ppermute x3, waiting for transfers between devices: 2.35 us -> 1.68 us  [from_right(): return lax.ppermute(x, axis, [(i + 1, i) for i in range(count - 1)])]
    eq x1, other arithmetic: 0.01 us -> 0.67 us  [shift_right(): x = jnp.where((amount >> b & 1)[:, None, None] == 1, moved, x)]
  transfers between devices with their start and end apart: 9 -> 9, of which waited for: 4 -> 4; matrix products, arithmetic and copies ran while one was open for 28% -> 25% of each run, Pallas kernels for 0% -> 0%
where the time goes in v8:
time: 51.5 us; the launch traced here: 51.1 us
  starting transfers between devices  20.9 us (41%)
  matrix products  14 us (27%)
  waiting for transfers between devices  10.6 us (21%)
  other arithmetic  2.76 us (5%)
  local copies, waits for them, and re-layouts  1.83 us (4%)
  between operations  1.02 us (2%)
    ppermute x3, starting transfers between devices, from_left(): return lax.ppermute(x, axis, [(i, i + 1) for i in range(count - 1)])  13.8 us
    ppermute x3, waiting for transfers between devices, from_left(): return lax.ppermute(x, axis, [(i, i + 1) for i in range(count - 1)])  8.93 us
    dot_general x2, matrix products, scatter_rows(): lax.dot_general(onehot, values, (((0,), (0,)), ((), ())), precision=lax.P...  4.48 us
    dot_general x1, matrix products, cell_maps(): jnp.einsum('cij,cjq->ciq', cell_matrix, onehot, precision=lax.Precision.H...  4.19 us
    ppermute x3, starting transfers between devices, from_right(): return lax.ppermute(x, axis, [(i + 1, i) for i in range(count - 1)])  3.88 us
    ppermute x3, starting transfers between devices, gather_band(): lax.ppermute(piece, 'band', [(i, (i + k) % count) for i in range(count)])  3.24 us
    ppermute x3, waiting for transfers between devices, from_right(): return lax.ppermute(x, axis, [(i + 1, i) for i in range(count - 1)])  1.68 us
    dot_general x1, matrix products, on_device(): jnp.dot((placed * weights[:, None]).T, placed, precision=highest)  1.61 us
  transfers between devices with their start and end apart: 9, of which 4 were waited for; matrix products, arithmetic and copies ran while one was open for 25% of the time, Pallas kernels for 0%

profile of v8, /device:TPU:0, one launch (start us, length us, event | category | flops | bytes accessed | tf_op | source)
XLA Modules:
  0.0 51.1 jit_solution(17188746018840104026)
XLA Ops:
  0.0 0.0 copy-start
  0.0 2.4 %collective-permute-start.4 = (f32[4,16,128]{2,1,0:T(8,128)}, f32[4,16,128]{2,1,0:T(8,128)S(1)}, u32[]{:S(2)}, u32[]{:S(2)}) collective-permute-start(f32[4,16,128]{2,1,0:T(8,128)} %param.10), channel_id=1, source_target_pairs={{0,3},{1,0},{2,1},{3,2},{4,7},{5,4},{6,5},{7,6},{8,11},{9,8},{10,9... | collective-permute-start | bytes 98312 | tf_op jit(solution)/shard_map/ppermute | solution.py:30
  2.5 0.6 %collective-permute-start.3 = (f32[4,16,128]{2,1,0:T(8,128)}, f32[4,16,128]{2,1,0:T(8,128)S(1)}, u32[]{:S(2)}, u32[]{:S(2)}) collective-permute-start(f32[4,16,128]{2,1,0:T(8,128)} %param.10), channel_id=1, source_target_pairs={{0,2},{1,3},{2,0},{3,1},{4,6},{5,7},{6,4},{7,5},{8,10},{9,11},{10,... | collective-permute-start | bytes 98312 | tf_op jit(solution)/shard_map/ppermute | solution.py:30
  3.1 0.2 collective-permute-start.2
  3.3 1.0 %fusion.26 = (f32[128,256]{1,0:T(8,128)S(1)}, f32[128,256]{1,0:T(8,128)S(1)}) fusion(f32[384,256]{1,0:T(8,128)} %param.7), kind=kLoop, calls=%fused_computation.71 | loop fusion | bytes 524288 | tf_op jit(solution)/shard_map/slice | solution.py:85
  4.2 3.4 %collective-permute-start = (f32[128,256]{1,0:T(8,128)S(1)}, f32[128,256]{1,0:T(8,128)S(1)}, u32[]{:S(2)}, u32[]{:S(2)}) collective-permute-start(f32[128,256]{1,0:T(8,128)S(1)} %get-tuple-element.14), channel_id=1, source_target_pairs={{0,4},{4,8},{8,12},{12,16},{16,20},{20,24},{24,28},{1,5},{5,9},{9,... | collective-permute-start | bytes 393224 | tf_op jit(solution)/shard_map/ppermute | solution.py:16
  7.7 1.3 %collective-permute-start.1 = (f32[128,256]{1,0:T(8,128)S(1)}, f32[128,256]{1,0:T(8,128)S(1)}, u32[]{:S(2)}, u32[]{:S(2)}) collective-permute-start(f32[128,256]{1,0:T(8,128)S(1)} %get-tuple-element.13), channel_id=1, source_target_pairs={{4,0},{8,4},{12,8},{16,12},{20,16},{24,20},{28,24},{5,1},{9,5},{13... | collective-permute-start | bytes 393224 | tf_op jit(solution)/shard_map/ppermute | solution.py:21
  9.0 0.7 %and_compare_fusion.7 = (pred[4]{0:T(512)(128)(4,1)S(1)}, pred[4]{0:T(512)(128)(4,1)S(1)}, pred[4]{0:T(512)(128)(4,1)S(1)}, pred[4]{0:T(512)(128)(4,1)S(1)}, pre...) fusion(s32[4]{0:T(128)} %param.12), kind=kLoop, calls=%fused_computation.66 | loop fusion | flops 100 | bytes 48 | tf_op jit(solution)/shard_map/eq | solution.py:45
  10.4 0.0 copy-done
  10.4 4.2 %fusion.2 = f32[2,640,512]{1,2,0:T(8,128)} fusion(f32[2,512,512]{2,1,0:T(8,128)S(1)} %copy-done, s32[2,512]{1,0:T(2,128)} %param.9), kind=kOutput, calls=%fused_computation.5 | convolution fusion | flops 2013921280 | bytes 4722688 | tf_op jit(solution)/shard_map/cij,cjq->ciq/dot_general | solution.py:65
  14.6 0.0 copy-done.5
  14.6 0.1 broadcast_multiply_fusion
  14.7 0.1 mul.42
  14.7 0.0 collective-permute-done.4
  14.7 0.0 collective-permute-done.3
  14.8 0.0 collective-permute-done.2
  14.8 0.0 copy-start.2
  14.8 0.6 %gather_fusion = f32[4,4,16,128]{3,2,1,0:T(8,128)S(1)} fusion(f32[4,4,16,128]{3,2,1,0:T(8,128)S(1)} %pad_maximum_fusion, s32[1024]{0:T(1024)S(1)} %pad_clamp_fusion), kind=kCustom, calls=%fused_computation | custom fusion | bytes 262160 | tf_op jit(solution)/shard_map/jit(_take)/gather | solution.py:34
  15.4 0.1 copy_bitcast_fusion
  15.5 0.1 pad_select_fusion
  15.6 0.1 pad_select_fusion.7
  15.7 0.1 pad_select_fusion.6
  15.8 0.1 pad_select_fusion.5
  16.0 0.1 pad_select_fusion.4
  16.1 0.1 pad_select_fusion.3
  16.2 0.1 pad_select_fusion.2
  16.3 0.1 pad_select_fusion.1
  16.4 0.0 collective-permute-done
  16.5 0.0 collective-permute-done.1
  16.5 0.5 convolution_multiply_fusion
  17.0 0.7 %fusion.29 = f32[640,256]{1,0:T(8,128)S(1)} fusion(f32[64,640]{1,0:T(8,128)S(1)} %bitcast.43, f32[64,256]{1,0:T(8,128)S(1)} %convolution_multiply_fusion), kind=kOutput, calls=%fused_computation.74 | convolution fusion | flops 125829120 | bytes 884736 | tf_op jit(solution)/shard_map/dot_general | solution.py:93
  17.7 0.0 copy-done.1
  17.7 1.4 %fusion.28 = f32[1024,256]{1,0:T(8,128)S(1)} fusion(f32[1024,640]{1,0:T(8,128)S(1)} %bitcast.40, f32[640,256]{1,0:T(8,128)S(1)} %constant_dynamic-update-slice_fusion), kind=kOutput, calls=%fused_computation.73 | convolution fusion | flops 1006632960 | bytes 4325376 | tf_op jit(solution)/shard_map/dot_general | solution.py:92
  19.1 1.7 %fusion.6 = f32[640,256]{1,0:T(8,128)S(1)} fusion(f32[640,256]{1,0:T(8,128)S(1)} %fusion.29, f32[1024,256]{1,0:T(8,128)S(1)} %fusion.28, s32[1024]{0:T(1024)S(1)} %bitcast.55), kind=kOutput, calls=%fused_computation.10 | convolution fusion | flops 1007452160 | bytes 2363392 | tf_op jit(solution)/shard_map/dot_general | solution.py:70
  20.9 1.3 %collective-permute-start.6 = (f32[256,256]{1,0:T(8,128)S(1)}, f32[256,256]{1,0:T(8,128)S(1)}, u32[]{:S(2)}, u32[]{:S(2)}) collective-permute-start(f32[256,256]{1,0:T(8,128)S(1)} %get-tuple-element.12), channel_id=1, source_target_pairs={{4,0},{8,4},{12,8},{16,12},{20,16},{24,20},{28,24},{5,1},{9,5},{13... | collective-permute-start | bytes 786440 | tf_op jit(solution)/shard_map/ppermute | solution.py:21
  22.2 5.4 %collective-permute-start.5 = (f32[256,256]{1,0:T(8,128)S(1)}, f32[256,256]{1,0:T(8,128)S(1)}, u32[]{:S(2)}, u32[]{:S(2)}) collective-permute-start(f32[256,256]{1,0:T(8,128)S(1)} %get-tuple-element.11), channel_id=1, source_target_pairs={{0,4},{4,8},{8,12},{12,16},{16,20},{20,24},{24,28},{1,5},{5,9},{9,... | collective-permute-start | bytes 786440 | tf_op jit(solution)/shard_map/ppermute | solution.py:16
  27.6 2.7 %fusion = f32[640,640]{1,0:T(8,128)S(1)} fusion(f32[1024,640]{1,0:T(8,128)S(1)} %bitcast.41, s32[1024]{0:T(1024)S(1)} %bitcast.56), kind=kOutput, calls=%fused_computation.3 | convolution fusion | flops 2517237760 | bytes 4263936 | tf_op jit(solution)/shard_map/dot_general | solution.py:70
  30.4 1.6 %bitcast_add_fusion = f32[640,640]{1,0:T(8,128)S(1)} fusion(f32[640,640]{1,0:T(8,128)S(1)} %fusion, f32[4,16,640]{2,1,0:T(8,128)S(1)} %pad_select_fusion.1, f32[4,16]{1,0:T(4,128)S(1)} %broadcast_multiply_fusion), kind=kOutput, calls=%fused_computation.6 | convolution fusion | flops 315023360 | bytes 3440896 | tf_op jit(solution)/shard_map/dot_general | solution.py:96
  32.0 0.5 %collective-permute-done.6 = f32[256,256]{1,0:T(8,128)S(1)} collective-permute-done((f32[256,256]{1,0:T(8,128)S(1)}, f32[256,256]{1,0:T(8,128)S(1)}, u32[]{:S(2)}, u32[]{:S(2)}) %collective-permute-start.6) | collective-permute-done | bytes 262176 | tf_op jit(solution)/shard_map/ppermute | solution.py:21
  32.5 6.0 %collective-permute-done.5 = f32[256,256]{1,0:T(8,128)S(1)} collective-permute-done((f32[256,256]{1,0:T(8,128)S(1)}, f32[256,256]{1,0:T(8,128)S(1)}, u32[]{:S(2)}, u32[]{:S(2)}) %collective-permute-start.5) | collective-permute-done | bytes 262176 | tf_op jit(solution)/shard_map/ppermute | solution.py:16
  38.5 0.2 multiply_select_fusion
  38.7 0.5 fusion.9
  39.2 1.3 %collective-permute-start.8 = (f32[128,256]{1,0:T(8,128)S(1)}, f32[128,256]{1,0:T(8,128)S(1)}, u32[]{:S(2)}, u32[]{:S(2)}) collective-permute-start(f32[128,256]{1,0:T(8,128)S(1)} %get-tuple-element.16), channel_id=1, source_target_pairs={{4,0},{8,4},{12,8},{16,12},{20,16},{24,20},{28,24},{5,1},{9,5},{13... | collective-permute-start | bytes 393224 | tf_op jit(solution)/shard_map/ppermute | solution.py:21
  40.5 5.0 %collective-permute-start.7 = (f32[128,256]{1,0:T(8,128)S(1)}, f32[128,256]{1,0:T(8,128)S(1)}, u32[]{:S(2)}, u32[]{:S(2)}) collective-permute-start(f32[128,256]{1,0:T(8,128)S(1)} %get-tuple-element.15), channel_id=1, source_target_pairs={{0,4},{4,8},{8,12},{12,16},{16,20},{20,24},{24,28},{1,5},{5,9},{9,... | collective-permute-start | bytes 393224 | tf_op jit(solution)/shard_map/ppermute | solution.py:16
  45.5 0.6 %fusion.7 = f32[384,256]{1,0:T(8,128)S(1)} fusion(f32[640,256]{1,0:T(8,128)S(1)} %multiply_select_fusion, f32[640,640]{1,0:T(8,128)S(1)} %bitcast_add_fusion), kind=kOutput, calls=%fused_computation.12 | convolution fusion | flops 377487360 | bytes 2031616 | tf_op jit(solution)/shard_map/dot_general | solution.py:120
  46.2 1.2 %collective-permute-done.8 = f32[128,256]{1,0:T(8,128)S(1)} collective-permute-done((f32[128,256]{1,0:T(8,128)S(1)}, f32[128,256]{1,0:T(8,128)S(1)}, u32[]{:S(2)}, u32[]{:S(2)}) %collective-permute-start.8) | collective-permute-done | bytes 131104 | tf_op jit(solution)/shard_map/ppermute | solution.py:21
  47.3 3.0 %collective-permute-done.7 = f32[128,256]{1,0:T(8,128)S(1)} collective-permute-done((f32[128,256]{1,0:T(8,128)S(1)}, f32[128,256]{1,0:T(8,128)S(1)}, u32[]{:S(2)}, u32[]{:S(2)}) %collective-permute-start.7) | collective-permute-done | bytes 131104 | tf_op jit(solution)/shard_map/ppermute | solution.py:16
  50.3 0.8 %fusion.14 = f32[384,256]{1,0:T(8,128)} fusion(f32[384,256]{1,0:T(8,128)S(1)} %copy-done.2, f32[640,256]{1,0:T(8,128)S(1)} %multiply_select_fusion, f32[128,256]{1,0:T(8,128)S(1)} %collective-permute-done.8, f32[384,256]{1,0:T(8,128)S(1)} %fusion.7, f32[128,256]{1,0:T(8,128)S(1)} %collective-permute-done.7), kind=kLoop, calls=%fused_computation.21 | loop fusion | flops 491520 | bytes 1835008 | tf_op jit(solution)/shard_map/sub | solution.py:128
  (22 shorter events, 0.2 us)
Async XLA Ops:
  0.0 10.4 %copy-start = (f32[2,512,512]{2,1,0:T(8,128)S(1)}, f32[2,512,512]{2,1,0:T(8,128)}, u32[]{:S(2)}) copy-start(f32[2,512,512]{2,1,0:T(8,128)} %param.8) | copy-start | bytes 6291460
  0.0 14.8 %copy-start.3 = (f32[4,16,128]{2,1,0:T(8,128)S(1)}, f32[4,16,128]{2,1,0:T(8,128)}, u32[]{:S(2)}) copy-start(f32[4,16,128]{2,1,0:T(8,128)} %param.10) | copy-start | bytes 98308
  0.0 14.7 %copy-start.4 = (s32[2,512]{1,0:T(2,128)S(1)}, s32[2,512]{1,0:T(2,128)}, u32[]{:S(2)}) copy-start(s32[2,512]{1,0:T(2,128)} %param.9) | copy-start | bytes 12292
  0.0 14.6 %copy-start.5 = (f32[4,16]{1,0:T(4,128)S(1)}, f32[4,16]{1,0:T(4,128)}, u32[]{:S(2)}) copy-start(f32[4,16]{1,0:T(4,128)} %param.11) | copy-start | bytes 772
  0.0 14.7 %collective-permute-start.4 = (f32[4,16,128]{2,1,0:T(8,128)}, f32[4,16,128]{2,1,0:T(8,128)S(1)}, u32[]{:S(2)}, u32[]{:S(2)}) collective-permute-start(f32[4,16,128]{2,1,0:T(8,128)} %param.10), channel_id=1, source_target_pairs={{0,3},{1,0},{2,1},{3,2},{4,7},{5,4},{6,5},{7,6},{8,11},{9,8},{10,9... | collective-permute-start | bytes 98312 | tf_op jit(solution)/shard_map/ppermute | solution.py:30
  2.5 12.3 %collective-permute-start.3 = (f32[4,16,128]{2,1,0:T(8,128)}, f32[4,16,128]{2,1,0:T(8,128)S(1)}, u32[]{:S(2)}, u32[]{:S(2)}) collective-permute-start(f32[4,16,128]{2,1,0:T(8,128)} %param.10), channel_id=1, source_target_pairs={{0,2},{1,3},{2,0},{3,1},{4,6},{5,7},{6,4},{7,5},{8,10},{9,11},{10,... | collective-permute-start | bytes 98312 | tf_op jit(solution)/shard_map/ppermute | solution.py:30
  3.1 11.7 %collective-permute-start.2 = (f32[4,16,128]{2,1,0:T(8,128)}, f32[4,16,128]{2,1,0:T(8,128)S(1)}, u32[]{:S(2)}, u32[]{:S(2)}) collective-permute-start(f32[4,16,128]{2,1,0:T(8,128)} %param.10), channel_id=1, source_target_pairs={{0,1},{1,2},{2,3},{3,0},{4,5},{5,6},{6,7},{7,4},{8,9},{9,10},{10,1... | collective-permute-start | bytes 98312 | tf_op jit(solution)/shard_map/ppermute | solution.py:30
  4.2 12.2 %collective-permute-start = (f32[128,256]{1,0:T(8,128)S(1)}, f32[128,256]{1,0:T(8,128)S(1)}, u32[]{:S(2)}, u32[]{:S(2)}) collective-permute-start(f32[128,256]{1,0:T(8,128)S(1)} %get-tuple-element.14), channel_id=1, source_target_pairs={{0,4},{4,8},{8,12},{12,16},{16,20},{20,24},{24,28},{1,5},{5,9},{9,... | collective-permute-start | bytes 393224 | tf_op jit(solution)/shard_map/ppermute | solution.py:16
  7.7 8.8 %collective-permute-start.1 = (f32[128,256]{1,0:T(8,128)S(1)}, f32[128,256]{1,0:T(8,128)S(1)}, u32[]{:S(2)}, u32[]{:S(2)}) collective-permute-start(f32[128,256]{1,0:T(8,128)S(1)} %get-tuple-element.13), channel_id=1, source_target_pairs={{4,0},{8,4},{12,8},{16,12},{20,16},{24,20},{28,24},{5,1},{9,5},{13... | collective-permute-start | bytes 393224 | tf_op jit(solution)/shard_map/ppermute | solution.py:21
  14.8 1.6 %copy-start.2 = (f32[384,256]{1,0:T(8,128)S(1)}, f32[384,256]{1,0:T(8,128)}, u32[]{:S(2)}) copy-start(f32[384,256]{1,0:T(8,128)} %param.7) | copy-start | bytes 1179652
  15.9 1.8 %copy-start.1 = (f32[2,640,512]{1,2,0:T(8,128)S(1)}, f32[2,640,512]{1,2,0:T(8,128)}, u32[]{:S(2)}) copy-start(f32[2,640,512]{1,2,0:T(8,128)} %fusion.2) | copy-start | bytes 7864324
  20.9 11.6 %collective-permute-start.6 = (f32[256,256]{1,0:T(8,128)S(1)}, f32[256,256]{1,0:T(8,128)S(1)}, u32[]{:S(2)}, u32[]{:S(2)}) collective-permute-start(f32[256,256]{1,0:T(8,128)S(1)} %get-tuple-element.12), channel_id=1, source_target_pairs={{4,0},{8,4},{12,8},{16,12},{20,16},{24,20},{28,24},{5,1},{9,5},{13... | collective-permute-start | bytes 786440 | tf_op jit(solution)/shard_map/ppermute | solution.py:21
  22.2 16.3 %collective-permute-start.5 = (f32[256,256]{1,0:T(8,128)S(1)}, f32[256,256]{1,0:T(8,128)S(1)}, u32[]{:S(2)}, u32[]{:S(2)}) collective-permute-start(f32[256,256]{1,0:T(8,128)S(1)} %get-tuple-element.11), channel_id=1, source_target_pairs={{0,4},{4,8},{8,12},{12,16},{16,20},{20,24},{24,28},{1,5},{5,9},{9,... | collective-permute-start | bytes 786440 | tf_op jit(solution)/shard_map/ppermute | solution.py:16
  39.2 8.1 %collective-permute-start.8 = (f32[128,256]{1,0:T(8,128)S(1)}, f32[128,256]{1,0:T(8,128)S(1)}, u32[]{:S(2)}, u32[]{:S(2)}) collective-permute-start(f32[128,256]{1,0:T(8,128)S(1)} %get-tuple-element.16), channel_id=1, source_target_pairs={{4,0},{8,4},{12,8},{16,12},{20,16},{24,20},{28,24},{5,1},{9,5},{13... | collective-permute-start | bytes 393224 | tf_op jit(solution)/shard_map/ppermute | solution.py:21
  40.5 9.8 %collective-permute-start.7 = (f32[128,256]{1,0:T(8,128)S(1)}, f32[128,256]{1,0:T(8,128)S(1)}, u32[]{:S(2)}, u32[]{:S(2)}) collective-permute-start(f32[128,256]{1,0:T(8,128)S(1)} %get-tuple-element.15), channel_id=1, source_target_pairs={{0,4},{4,8},{8,12},{12,16},{16,20},{20,24},{24,28},{1,5},{5,9},{9,... | collective-permute-start | bytes 393224 | tf_op jit(solution)/shard_map/ppermute | solution.py:16

commit v9 on v8

--- a/solution.py
+++ b/solution.py
@@ -58,12 +58,11 @@
     return placed.reshape(slots * channels, ext), weights.reshape(slots * channels)
 
 
-def cell_maps(cell_matrix, connectivity, ext):
-    cells, nodes, _ = cell_matrix.shape
+def cell_rows(connectivity, ext):
+    cells, nodes = connectivity.shape
     rows = jnp.arange(ext, dtype=connectivity.dtype)
     onehot = (connectivity[:, :, None] == rows[None, None, :]).astype(jnp.float32)
-    moved = jnp.einsum("cij,cjq->ciq", cell_matrix, onehot, precision=lax.Precision.HIGH)
-    return onehot.reshape(cells * nodes, ext), moved.reshape(cells * nodes, ext)
+    return onehot.reshape(cells * nodes, ext)
 
 
 def scatter_rows(onehot, values):
@@ -86,14 +85,22 @@
     extended = jnp.concatenate([low, wavefunctions, high], axis=0)
 
     placed, weights = atom_rows(gather_band(projector), coupling, atom_start, atom_count, ext)
-    onehot, moved = cell_maps(cell_matrix, connectivity, ext)
+    onehot = cell_rows(connectivity, ext)
+    cells, nodes, _ = cell_matrix.shape
+    high = lax.Precision.HIGH
 
     coefficients = jnp.dot(placed, extended, precision=highest) * weights[:, None]
-    local = jnp.dot(moved, extended, precision=lax.Precision.HIGH)
-    first = scatter_rows(onehot, local) + jnp.dot(placed.T, coefficients, precision=highest)
+    gathered = jnp.dot(onehot, extended, precision=high).reshape(cells, nodes, -1)
+    local = jnp.einsum("cij,cjb->cib", cell_matrix, gathered, precision=high)
+    first = scatter_rows(onehot, local.reshape(cells * nodes, -1)) + jnp.dot(
+        placed.T, coefficients, precision=highest
+    )
 
-    moved, first = lax.optimization_barrier((moved, first))
-    operator = scatter_rows(onehot, moved) + jnp.dot(
+    matrices, first = lax.optimization_barrier((cell_matrix, first))
+    moved = jnp.einsum(
+        "cij,cjq->ciq", matrices, onehot.reshape(cells, nodes, ext), precision=high
+    )
+    operator = scatter_rows(onehot, moved.reshape(cells * nodes, ext)) + jnp.dot(
         (placed * weights[:, None]).T, placed, precision=highest
     )
     left_sums = from_left(first[ext - 2 * g :], "dom")

time: 51.5 us -> 49.7 us (0.965)
  matrix products: 14 us -> 11.6 us
  waiting for transfers between devices: 10.6 us -> 8.72 us
  other arithmetic: 2.76 us -> 4.22 us
  starting transfers between devices: 20.9 us -> 22 us
    ppermute x3, waiting for transfers between devices: 8.93 us -> 4.34 us  [from_left(): return lax.ppermute(x, axis, [(i, i + 1) for i in range(count - 1)])]
    ppermute x3, waiting for transfers between devices: 1.68 us -> 4.37 us  [from_right(): return lax.ppermute(x, axis, [(i + 1, i) for i in range(count - 1)])]
    ppermute x3, starting transfers between devices: 3.24 us -> 4.68 us  [gather_band(): lax.ppermute(piece, 'band', [(i, (i + k) % count) for i in range(count)])]
    dot_general x2, matrix products: 4.48 us -> 3.17 us  [scatter_rows(): lax.dot_general(onehot, values, (((0,), (0,)), ((), ())), precision=lax.P...]
    dot_general x2 -> x3, matrix products: 5.6 us -> 4.52 us  [the longest x1 1.95 us: on_device(): jnp.einsum('cij,cjq->ciq', matrices, onehot.reshape(cells, nodes, ext), p...]
    another operation x1, other arithmetic: 0.01 us -> 0.77 us  [gather_band(): stacked = jnp.stack(pieces)]
    mul x1, other arithmetic: 0.07 us -> 0.75 us  [atom_rows(): weights = coupling * live.astype(jnp.float32)]
    ppermute x3, starting transfers between devices: 13.8 us -> 13.3 us  [from_left(): return lax.ppermute(x, axis, [(i, i + 1) for i in range(count - 1)])]
  transfers between devices with their start and end apart: 9 -> 9, of which waited for: 4 -> 3; matrix products, arithmetic and copies ran while one was open for 25% -> 23% of each run, Pallas kernels for 0% -> 0%
where the time goes in v9:
time: 49.7 us; the launch traced here: 49.4 us
  starting transfers between devices  22 us (44%)
  matrix products  11.6 us (23%)
  waiting for transfers between devices  8.72 us (18%)
  other arithmetic  4.22 us (8%)
  local copies, waits for them, and re-layouts  1.81 us (4%)
  between operations  1.01 us (2%)
    ppermute x3, starting transfers between devices, from_left(): return lax.ppermute(x, axis, [(i, i + 1) for i in range(count - 1)])  13.3 us
    ppermute x3, starting transfers between devices, gather_band(): lax.ppermute(piece, 'band', [(i, (i + k) % count) for i in range(count)])  4.68 us
    ppermute x3, waiting for transfers between devices, from_right(): return lax.ppermute(x, axis, [(i + 1, i) for i in range(count - 1)])  4.37 us
    ppermute x3, waiting for transfers between devices, from_left(): return lax.ppermute(x, axis, [(i, i + 1) for i in range(count - 1)])  4.34 us
    ppermute x3, starting transfers between devices, from_right(): return lax.ppermute(x, axis, [(i + 1, i) for i in range(count - 1)])  4.06 us
    dot_general x2, matrix products, scatter_rows(): lax.dot_general(onehot, values, (((0,), (0,)), ((), ())), precision=lax.P...  3.17 us
    dot_general x1, matrix products, on_device(): jnp.einsum('cij,cjq->ciq', matrices, onehot.reshape(cells, nodes, ext), p...  1.95 us
    dot_general x1, matrix products, on_device(): jnp.dot((placed * weights[:, None]).T, placed, precision=highest)  1.58 us
  transfers between devices with their start and end apart: 9, of which 3 were waited for; matrix products, arithmetic and copies ran while one was open for 23% of the time, Pallas kernels for 0%

profile of v9, /device:TPU:0, one launch (start us, length us, event | category | flops | bytes accessed | tf_op | source)
XLA Modules:
  0.0 49.4 jit_solution(13574379557284054507)
XLA Ops:
  0.0 0.5 collective-permute-start.2
  0.5 2.0 %collective-permute-start.4 = (f32[4,16,128]{2,1,0:T(8,128)}, f32[4,16,128]{2,1,0:T(8,128)S(1)}, u32[]{:S(2)}, u32[]{:S(2)}) collective-permute-start(f32[4,16,128]{2,1,0:T(8,128)} %param.10), channel_id=1, source_target_pairs={{0,3},{1,0},{2,1},{3,2},{4,7},{5,4},{6,5},{7,6},{8,11},{9,8},{10,9... | collective-permute-start | bytes 98312 | tf_op jit(solution)/shard_map/ppermute | solution.py:30
  2.4 2.2 %collective-permute-start.3 = (f32[4,16,128]{2,1,0:T(8,128)}, f32[4,16,128]{2,1,0:T(8,128)S(1)}, u32[]{:S(2)}, u32[]{:S(2)}) collective-permute-start(f32[4,16,128]{2,1,0:T(8,128)} %param.10), channel_id=1, source_target_pairs={{0,2},{1,3},{2,0},{3,1},{4,6},{5,7},{6,4},{7,5},{8,10},{9,11},{10,... | collective-permute-start | bytes 98312 | tf_op jit(solution)/shard_map/ppermute | solution.py:30
  4.7 1.0 %fusion.30 = (f32[128,256]{1,0:T(8,128)S(1)}, f32[128,256]{1,0:T(8,128)S(1)}) fusion(f32[384,256]{1,0:T(8,128)} %param.7), kind=kLoop, calls=%fused_computation.76 | loop fusion | bytes 524288 | tf_op jit(solution)/shard_map/slice | solution.py:84
  5.7 1.3 %collective-permute-start.1 = (f32[128,256]{1,0:T(8,128)S(1)}, f32[128,256]{1,0:T(8,128)S(1)}, u32[]{:S(2)}, u32[]{:S(2)}) collective-permute-start(f32[128,256]{1,0:T(8,128)S(1)} %get-tuple-element.13), channel_id=1, source_target_pairs={{4,0},{8,4},{12,8},{16,12},{20,16},{24,20},{28,24},{5,1},{9,5},{13... | collective-permute-start | bytes 393224 | tf_op jit(solution)/shard_map/ppermute | solution.py:21
  7.0 4.6 %collective-permute-start = (f32[128,256]{1,0:T(8,128)S(1)}, f32[128,256]{1,0:T(8,128)S(1)}, u32[]{:S(2)}, u32[]{:S(2)}) collective-permute-start(f32[128,256]{1,0:T(8,128)S(1)} %get-tuple-element.14), channel_id=1, source_target_pairs={{0,4},{4,8},{8,12},{12,16},{16,20},{20,24},{24,28},{1,5},{5,9},{9,... | collective-permute-start | bytes 393224 | tf_op jit(solution)/shard_map/ppermute | solution.py:16
  12.2 0.7 %and_compare_fusion.7 = (pred[4]{0:T(512)(128)(4,1)S(1)}, pred[4]{0:T(512)(128)(4,1)S(1)}, pred[4]{0:T(512)(128)(4,1)S(1)}, pred[4]{0:T(512)(128)(4,1)S(1)}, pre...) fusion(s32[4]{0:T(128)} %param.12), kind=kLoop, calls=%fused_computation.71 | loop fusion | flops 100 | bytes 48 | tf_op jit(solution)/shard_map/eq | solution.py:45
  12.9 0.8 %broadcast_multiply_fusion = f32[4,16]{1,0:T(4,128)S(1)} fusion(f32[4,16]{1,0:T(4,128)} %param.11, f32[4]{0:T(128)S(1)} %compare_convert_fusion), kind=kLoop, calls=%fused_computation.60 | loop fusion | flops 64 | bytes 528 | tf_op jit(solution)/shard_map/mul | solution.py:57
  13.7 0.1 mul.42
  13.8 0.0 collective-permute-done.2
  13.8 0.0 collective-permute-done.4
  13.8 0.0 collective-permute-done.3
  13.8 0.8 %pad_maximum_fusion = f32[4,4,16,128]{3,2,1,0:T(8,128)S(1)} fusion(f32[1,4,16,128]{3,2,1,0:T(8,128)S(1)} %bitcast.54, f32[1,4,16,128]{3,2,1,0:T(8,128)S(1)} %bitcast.55, f32[1,4,16,128]{3,2,1,0:T(8,128)S(1)} %bitcast.53, f32[1,4,16,128]{3,2,1,0:T(8,128)} %bitcast.52), kind=kLoop, calls=%fused_computation.38 | loop fusion | flops 98304 | bytes 262144 | tf_op jit(solution)/shard_map/stack | solution.py:32
  14.6 0.6 %gather_fusion = f32[4,4,16,128]{3,2,1,0:T(8,128)S(1)} fusion(f32[4,4,16,128]{3,2,1,0:T(8,128)S(1)} %pad_maximum_fusion, s32[1024]{0:T(1024)S(1)} %pad_clamp_fusion), kind=kCustom, calls=%fused_computation | custom fusion | bytes 262160 | tf_op jit(solution)/shard_map/jit(_take)/gather | solution.py:34
  15.1 0.1 copy_bitcast_fusion
  15.2 0.1 pad_select_fusion
  15.4 0.1 pad_select_fusion.7
  15.5 0.1 pad_select_fusion.6
  15.6 0.1 pad_select_fusion.5
  15.7 0.1 pad_select_fusion.4
  15.8 0.0 copy-start.1
  15.8 0.1 pad_select_fusion.3
  16.0 0.1 pad_select_fusion.2
  16.1 0.0 copy-start.2
  16.1 0.1 pad_select_fusion.1
  16.2 1.6 %fusion.18 = f32[640,640,1]{1,0,2:T(8,128)S(1)} fusion(f32[4,16,640]{2,1,0:T(8,128)S(1)} %pad_select_fusion.1, f32[4,16]{1,0:T(4,128)S(1)} %broadcast_multiply_fusion), kind=kOutput, calls=%fused_computation.26 | convolution fusion | flops 314613760 | bytes 1802496 | tf_op jit(solution)/shard_map/dot_general | solution.py:103
  17.8 0.0 collective-permute-done
  17.9 0.0 collective-permute-done.1
  17.9 1.6 %fusion.3 = f32[2,512,256]{2,1,0:T(8,128)S(1)} fusion(s32[2,512]{1,0:T(2,128)S(1)} %copy-done.2, f32[640,256]{1,0:T(8,128)S(1)} %constant_dynamic-update-slice_fusion), kind=kOutput, calls=%fused_computation.5 | convolution fusion | flops 1007288320 | bytes 1708032 | tf_op jit(solution)/shard_map/dot_general | solution.py:93
  19.5 0.0 copy-done
  19.5 1.0 %convolution_bitcast_fusion = f32[2,512,256]{2,1,0:T(8,128)S(1)} fusion(f32[2,512,256]{2,1,0:T(8,128)S(1)} %fusion.3, f32[2,512,512]{2,1,0:T(8,128)S(1)} %copy-done), kind=kOutput, calls=%fused_computation.7 | convolution fusion | flops 805306368 | bytes 4194304 | tf_op jit(solution)/shard_map/cij,cjb->cib/dot_general | solution.py:94
  20.5 0.8 %fusion.8 = f32[640,256]{1,0:T(8,128)S(1)} fusion(f32[2,512,256]{2,1,0:T(8,128)S(1)} %convolution_bitcast_fusion, s32[2,512]{1,0:T(2,128)S(1)} %copy-done.2), kind=kOutput, calls=%fused_computation.12 | convolution fusion | flops 1007288320 | bytes 1708032 | tf_op jit(solution)/shard_map/dot_general | solution.py:69
  21.4 0.5 convolution_multiply_fusion
  21.8 0.7 %convolution_add_fusion = f32[640,256]{1,0:T(8,128)S(1)} fusion(f32[640,256]{1,0:T(8,128)S(1)} %fusion.8, f32[64,640]{1,0:T(8,128)S(1)} %bitcast.45, f32[64,256]{1,0:T(8,128)S(1)} %convolution_multiply_fusion), kind=kOutput, calls=%fused_computation.13 | convolution fusion | flops 125992960 | bytes 1540096 | tf_op jit(solution)/shard_map/dot_general | solution.py:95
  22.6 4.3 %collective-permute-start.5 = (f32[256,256]{1,0:T(8,128)S(1)}, f32[256,256]{1,0:T(8,128)S(1)}, u32[]{:S(2)}, u32[]{:S(2)}) collective-permute-start(f32[256,256]{1,0:T(8,128)S(1)} %get-tuple-element.11), channel_id=1, source_target_pairs={{0,4},{4,8},{8,12},{12,16},{16,20},{20,24},{24,28},{1,5},{5,9},{9,... | collective-permute-start | bytes 786440 | tf_op jit(solution)/shard_map/ppermute | solution.py:16
  26.9 1.5 %collective-permute-start.6 = (f32[256,256]{1,0:T(8,128)S(1)}, f32[256,256]{1,0:T(8,128)S(1)}, u32[]{:S(2)}, u32[]{:S(2)}) collective-permute-start(f32[256,256]{1,0:T(8,128)S(1)} %get-tuple-element.12), channel_id=1, source_target_pairs={{4,0},{8,4},{12,8},{16,12},{20,16},{24,20},{28,24},{5,1},{9,5},{13... | collective-permute-start | bytes 786440 | tf_op jit(solution)/shard_map/ppermute | solution.py:21
  28.4 1.9 %fusion.1 = f32[2,512,640]{2,1,0:T(8,128)S(1)} fusion(f32[2,512,512]{2,1,0:T(8,128)S(1)} %copy-done, s32[2,512]{1,0:T(2,128)S(1)} %copy-done.2), kind=kOutput, calls=%fused_computation.3 | convolution fusion | flops 2013921280 | bytes 4722688 | tf_op jit(solution)/shard_map/cij,cjq->ciq/dot_general | solution.py:100
  30.4 2.3 %bitcast_add_fusion = f32[640,640]{1,0:T(8,128)S(1)} fusion(f32[640,640,1]{1,0,2:T(8,128)S(1)} %fusion.18, f32[2,512,640]{2,1,0:T(8,128)S(1)} %fusion.1, s32[2,512]{1,0:T(2,128)S(1)} %copy-done.2), kind=kOutput, calls=%fused_computation.6 | convolution fusion | flops 2517647360 | bytes 5902336 | tf_op jit(solution)/shard_map/dot_general | solution.py:69
  32.7 3.8 %collective-permute-done.5 = f32[256,256]{1,0:T(8,128)S(1)} collective-permute-done((f32[256,256]{1,0:T(8,128)S(1)}, f32[256,256]{1,0:T(8,128)S(1)}, u32[]{:S(2)}, u32[]{:S(2)}) %collective-permute-start.5) | collective-permute-done | bytes 262176 | tf_op jit(solution)/shard_map/ppermute | solution.py:16
  36.5 0.0 collective-permute-done.6
  36.5 0.2 multiply_select_fusion
  36.7 0.5 %fusion.11 = f32[256,256]{1,0:T(8,128)S(1)} fusion(f32[640,256]{1,0:T(8,128)S(1)} %multiply_select_fusion, f32[128,640]{1,0:T(8,128)S(1)} %get-tuple-element.10, f32[128,640]{1,0:T(8,128)S(1)} %get-tuple-element.9), kind=kOutput, calls=%fused_computation.17 | convolution fusion | flops 251822080 | bytes 1572864 | tf_op jit(solution)/shard_map/dot_general | solution.py:123
  37.3 4.4 %collective-permute-start.7 = (f32[128,256]{1,0:T(8,128)S(1)}, f32[128,256]{1,0:T(8,128)S(1)}, u32[]{:S(2)}, u32[]{:S(2)}) collective-permute-start(f32[128,256]{1,0:T(8,128)S(1)} %get-tuple-element.15), channel_id=1, source_target_pairs={{0,4},{4,8},{8,12},{12,16},{16,20},{20,24},{24,28},{1,5},{5,9},{9,... | collective-permute-start | bytes 393224 | tf_op jit(solution)/shard_map/ppermute | solution.py:16
  41.7 1.3 %collective-permute-start.8 = (f32[128,256]{1,0:T(8,128)S(1)}, f32[128,256]{1,0:T(8,128)S(1)}, u32[]{:S(2)}, u32[]{:S(2)}) collective-permute-start(f32[128,256]{1,0:T(8,128)S(1)} %get-tuple-element.16), channel_id=1, source_target_pairs={{4,0},{8,4},{12,8},{16,12},{20,16},{24,20},{28,24},{5,1},{9,5},{13... | collective-permute-start | bytes 393224 | tf_op jit(solution)/shard_map/ppermute | solution.py:21
  43.0 0.7 %fusion.9 = f32[384,256]{1,0:T(8,128)S(1)} fusion(f32[640,256]{1,0:T(8,128)S(1)} %multiply_select_fusion, f32[640,640]{1,0:T(8,128)S(1)} %bitcast_add_fusion), kind=kOutput, calls=%fused_computation.15 | convolution fusion | flops 377487360 | bytes 2031616 | tf_op jit(solution)/shard_map/dot_general | solution.py:127
  43.6 0.5 %collective-permute-done.7 = f32[128,256]{1,0:T(8,128)S(1)} collective-permute-done((f32[128,256]{1,0:T(8,128)S(1)}, f32[128,256]{1,0:T(8,128)S(1)}, u32[]{:S(2)}, u32[]{:S(2)}) %collective-permute-start.7) | collective-permute-done | bytes 131104 | tf_op jit(solution)/shard_map/ppermute | solution.py:16
  44.2 4.4 %collective-permute-done.8 = f32[128,256]{1,0:T(8,128)S(1)} collective-permute-done((f32[128,256]{1,0:T(8,128)S(1)}, f32[128,256]{1,0:T(8,128)S(1)}, u32[]{:S(2)}, u32[]{:S(2)}) %collective-permute-start.8) | collective-permute-done | bytes 131104 | tf_op jit(solution)/shard_map/ppermute | solution.py:21
  48.5 0.9 %fusion.17 = f32[384,256]{1,0:T(8,128)} fusion(f32[384,256]{1,0:T(8,128)S(1)} %copy-done.1, f32[640,256]{1,0:T(8,128)S(1)} %multiply_select_fusion, f32[128,256]{1,0:T(8,128)S(1)} %collective-permute-done.8, f32[384,256]{1,0:T(8,128)S(1)} %fusion.9, f32[128,256]{1,0:T(8,128)S(1)} %collective-permute-done.7), kind=kLoop, calls=%fused_computation.25 | loop fusion | flops 491520 | bytes 1835008 | tf_op jit(solution)/shard_map/sub | solution.py:135
  (16 shorter events, 0.2 us)
Async XLA Ops:
  0.0 19.5 %copy-start = (f32[2,512,512]{2,1,0:T(8,128)S(1)}, f32[2,512,512]{2,1,0:T(8,128)}, u32[]{:S(2)}) copy-start(f32[2,512,512]{2,1,0:T(8,128)} %param.8) | copy-start | bytes 6291460
  0.0 13.8 %collective-permute-start.2 = (f32[4,16,128]{2,1,0:T(8,128)}, f32[4,16,128]{2,1,0:T(8,128)S(1)}, u32[]{:S(2)}, u32[]{:S(2)}) collective-permute-start(f32[4,16,128]{2,1,0:T(8,128)} %param.10), channel_id=1, source_target_pairs={{0,1},{1,2},{2,3},{3,0},{4,5},{5,6},{6,7},{7,4},{8,9},{9,10},{10,1... | collective-permute-start | bytes 98312 | tf_op jit(solution)/shard_map/ppermute | solution.py:30
  0.5 13.3 %collective-permute-start.4 = (f32[4,16,128]{2,1,0:T(8,128)}, f32[4,16,128]{2,1,0:T(8,128)S(1)}, u32[]{:S(2)}, u32[]{:S(2)}) collective-permute-start(f32[4,16,128]{2,1,0:T(8,128)} %param.10), channel_id=1, source_target_pairs={{0,3},{1,0},{2,1},{3,2},{4,7},{5,4},{6,5},{7,6},{8,11},{9,8},{10,9... | collective-permute-start | bytes 98312 | tf_op jit(solution)/shard_map/ppermute | solution.py:30
  2.4 11.4 %collective-permute-start.3 = (f32[4,16,128]{2,1,0:T(8,128)}, f32[4,16,128]{2,1,0:T(8,128)S(1)}, u32[]{:S(2)}, u32[]{:S(2)}) collective-permute-start(f32[4,16,128]{2,1,0:T(8,128)} %param.10), channel_id=1, source_target_pairs={{0,2},{1,3},{2,0},{3,1},{4,6},{5,7},{6,4},{7,5},{8,10},{9,11},{10,... | collective-permute-start | bytes 98312 | tf_op jit(solution)/shard_map/ppermute | solution.py:30
  5.7 12.2 %collective-permute-start.1 = (f32[128,256]{1,0:T(8,128)S(1)}, f32[128,256]{1,0:T(8,128)S(1)}, u32[]{:S(2)}, u32[]{:S(2)}) collective-permute-start(f32[128,256]{1,0:T(8,128)S(1)} %get-tuple-element.13), channel_id=1, source_target_pairs={{4,0},{8,4},{12,8},{16,12},{20,16},{24,20},{28,24},{5,1},{9,5},{13... | collective-permute-start | bytes 393224 | tf_op jit(solution)/shard_map/ppermute | solution.py:21
  7.0 10.8 %collective-permute-start = (f32[128,256]{1,0:T(8,128)S(1)}, f32[128,256]{1,0:T(8,128)S(1)}, u32[]{:S(2)}, u32[]{:S(2)}) collective-permute-start(f32[128,256]{1,0:T(8,128)S(1)} %get-tuple-element.14), channel_id=1, source_target_pairs={{0,4},{4,8},{8,12},{12,16},{16,20},{20,24},{24,28},{1,5},{5,9},{9,... | collective-permute-start | bytes 393224 | tf_op jit(solution)/shard_map/ppermute | solution.py:16
  15.8 2.0 %copy-start.1 = (f32[384,256]{1,0:T(8,128)S(1)}, f32[384,256]{1,0:T(8,128)}, u32[]{:S(2)}) copy-start(f32[384,256]{1,0:T(8,128)} %param.7) | copy-start | bytes 1179652
  16.1 1.8 %copy-start.2 = (s32[2,512]{1,0:T(2,128)S(1)}, s32[2,512]{1,0:T(2,128)}, u32[]{:S(2)}) copy-start(s32[2,512]{1,0:T(2,128)} %param.9) | copy-start | bytes 12292
  22.6 14.0 %collective-permute-start.5 = (f32[256,256]{1,0:T(8,128)S(1)}, f32[256,256]{1,0:T(8,128)S(1)}, u32[]{:S(2)}, u32[]{:S(2)}) collective-permute-start(f32[256,256]{1,0:T(8,128)S(1)} %get-tuple-element.11), channel_id=1, source_target_pairs={{0,4},{4,8},{8,12},{12,16},{16,20},{20,24},{24,28},{1,5},{5,9},{9,... | collective-permute-start | bytes 786440 | tf_op jit(solution)/shard_map/ppermute | solution.py:16
  26.9 9.6 %collective-permute-start.6 = (f32[256,256]{1,0:T(8,128)S(1)}, f32[256,256]{1,0:T(8,128)S(1)}, u32[]{:S(2)}, u32[]{:S(2)}) collective-permute-start(f32[256,256]{1,0:T(8,128)S(1)} %get-tuple-element.12), channel_id=1, source_target_pairs={{4,0},{8,4},{12,8},{16,12},{20,16},{24,20},{28,24},{5,1},{9,5},{13... | collective-permute-start | bytes 786440 | tf_op jit(solution)/shard_map/ppermute | solution.py:21
  37.3 6.9 %collective-permute-start.7 = (f32[128,256]{1,0:T(8,128)S(1)}, f32[128,256]{1,0:T(8,128)S(1)}, u32[]{:S(2)}, u32[]{:S(2)}) collective-permute-start(f32[128,256]{1,0:T(8,128)S(1)} %get-tuple-element.15), channel_id=1, source_target_pairs={{0,4},{4,8},{8,12},{12,16},{16,20},{20,24},{24,28},{1,5},{5,9},{9,... | collective-permute-start | bytes 393224 | tf_op jit(solution)/shard_map/ppermute | solution.py:16
  41.7 6.9 %collective-permute-start.8 = (f32[128,256]{1,0:T(8,128)S(1)}, f32[128,256]{1,0:T(8,128)S(1)}, u32[]{:S(2)}, u32[]{:S(2)}) collective-permute-start(f32[128,256]{1,0:T(8,128)S(1)} %get-tuple-element.16), channel_id=1, source_target_pairs={{4,0},{8,4},{12,8},{16,12},{20,16},{24,20},{28,24},{5,1},{9,5},{13... | collective-permute-start | bytes 393224 | tf_op jit(solution)/shard_map/ppermute | solution.py:21

commit v10 on v9

--- a/solution.py
+++ b/solution.py
@@ -23,17 +23,10 @@
 
 def gather_band(piece):
     count = lax.axis_size("band")
-    me = lax.axis_index("band")
-    pieces = [piece]
+    total = piece
     for k in range(1, count):
-        pieces.append(
-            lax.ppermute(piece, "band", [(i, (i + k) % count) for i in range(count)])
-        )
-    stacked = jnp.stack(pieces)
-    order = (me - jnp.arange(count)) % count
-    ordered = jnp.take(stacked, order, axis=0)
-    slots, channels, width = piece.shape
-    return ordered.transpose(1, 2, 0, 3).reshape(slots, channels, count * width)
+        total = total + lax.ppermute(piece, "band", [(i, (i + k) % count) for i in range(count)])
+    return total
 
 
 def shift_right(x, amount, bits):
@@ -46,13 +39,15 @@
     return x
 
 
-def atom_rows(projector_full, coupling, atom_start, atom_count, ext):
-    slots, channels, support = projector_full.shape
+def atom_rows(projector, coupling, atom_start, atom_count, ext):
+    slots, channels, width = projector.shape
+    support = width * lax.axis_size("band")
     first = jnp.clip(atom_start.astype(jnp.int32), 0, ext - support)
+    offset = first + lax.axis_index("band").astype(jnp.int32) * width
     padded = jnp.concatenate(
-        [projector_full, jnp.zeros((slots, channels, ext - support), projector_full.dtype)], axis=-1
+        [projector, jnp.zeros((slots, channels, ext - width), projector.dtype)], axis=-1
     )
-    placed = shift_right(padded, first, (ext - support).bit_length())
+    placed = gather_band(shift_right(padded, offset, (ext - width).bit_length()))
     live = jnp.arange(slots, dtype=jnp.int32)[:, None] < atom_count.astype(jnp.int32)[None, :]
     weights = coupling * live.astype(jnp.float32)
     return placed.reshape(slots * channels, ext), weights.reshape(slots * channels)
@@ -84,7 +79,7 @@
     high = from_right(wavefunctions[:g], "dom")
     extended = jnp.concatenate([low, wavefunctions, high], axis=0)
 
-    placed, weights = atom_rows(gather_band(projector), coupling, atom_start, atom_count, ext)
+    placed, weights = atom_rows(projector, coupling, atom_start, atom_count, ext)
     onehot = cell_rows(connectivity, ext)
     cells, nodes, _ = cell_matrix.shape
     high = lax.Precision.HIGH

time: 49.7 us -> 53.8 us (1.082)
  waiting for transfers between devices: 8.72 us -> 14.9 us
  starting transfers between devices: 22 us -> 20.5 us
    ppermute x3, waiting for transfers between devices: 4.34 us -> 9.01 us  [from_left(): return lax.ppermute(x, axis, [(i, i + 1) for i in range(count - 1)])]
    ppermute x3, waiting for transfers between devices: 4.37 us -> 5.89 us  [from_right(): return lax.ppermute(x, axis, [(i + 1, i) for i in range(count - 1)])]
    ppermute x3, starting transfers between devices: 4.68 us -> 3.23 us  [gather_band(): lax.ppermute(piece, 'band', [(i, (i + k) % count) for i in range(count)])]
    select_n x8 -> x10, other arithmetic: 0.86 us -> 1.78 us  [shift_right(): x = jnp.where((amount >> b & 1)[:, None, None] == 1, moved, x)]
    slice x2 -> x4, local copies, waits for them, and re-layouts: 0.02 us -> 0.79 us  [shift_right(): x[..., :-step]]
    another operation x1 -> x0, other arithmetic: 0.77 us -> none  [gather_band(): stacked = jnp.stack(pieces)]
    mul x1, other arithmetic: 0.75 us -> 0.07 us  [atom_rows(): weights = coupling * live.astype(jnp.float32)]
    gather x1 -> x0, local copies, waits for them, and re-layouts: 0.56 us -> none  [gather_band(): ordered = jnp.take(stacked, order, axis=0)]
  transfers between devices with their start and end apart: 9 -> 9, of which waited for: 3 -> 4; matrix products, arithmetic and copies ran while one was open for 23% -> 20% of each run, Pallas kernels for 0% -> 0%
where the time goes in v10:
time: 53.8 us; the launch traced here: 53.5 us
  starting transfers between devices  20.5 us (38%)
  waiting for transfers between devices  14.9 us (28%)
  matrix products  11.5 us (21%)
  other arithmetic  3.74 us (7%)
  local copies, waits for them, and re-layouts  1.73 us (3%)
  between operations  1.01 us (2%)
    ppermute x3, starting transfers between devices, from_left(): return lax.ppermute(x, axis, [(i, i + 1) for i in range(count - 1)])  13.2 us
    ppermute x3, waiting for transfers between devices, from_left(): return lax.ppermute(x, axis, [(i, i + 1) for i in range(count - 1)])  9.01 us
    ppermute x3, waiting for transfers between devices, from_right(): return lax.ppermute(x, axis, [(i + 1, i) for i in range(count - 1)])  5.89 us
    ppermute x3, starting transfers between devices, from_right(): return lax.ppermute(x, axis, [(i + 1, i) for i in range(count - 1)])  4.04 us
    ppermute x3, starting transfers between devices, gather_band(): lax.ppermute(piece, 'band', [(i, (i + k) % count) for i in range(count)])  3.23 us
    dot_general x2, matrix products, scatter_rows(): lax.dot_general(onehot, values, (((0,), (0,)), ((), ())), precision=lax.P...  3.11 us
    dot_general x1, matrix products, on_device(): jnp.einsum('cij,cjq->ciq', matrices, onehot.reshape(cells, nodes, ext), p...  1.95 us
    select_n x10, other arithmetic, shift_right(): x = jnp.where((amount >> b & 1)[:, None, None] == 1, moved, x)  1.78 us
  transfers between devices with their start and end apart: 9, of which 4 were waited for; matrix products, arithmetic and copies ran while one was open for 20% of the time, Pallas kernels for 0%

profile of v10, /device:TPU:0, one launch (start us, length us, event | category | flops | bytes accessed | tf_op | source)
XLA Modules:
  0.0 53.5 jit_solution(10711171423703847705)
XLA Ops:
  0.0 0.8 %and_compare_fusion.9 = (pred[4]{0:T(512)(128)(4,1)S(1)}, s32[4]{0:T(128)S(1)}) fusion(s32[]{:T(128)S(6)} %mul.43, s32[4]{0:T(128)} %param.12), kind=kLoop, calls=%fused_computation.58 | loop fusion | flops 20 | bytes 40 | tf_op jit(solution)/shard_map/eq | solution.py:38
  0.8 0.8 %pad_slice_fusion = f32[4,16,639]{2,1,0:T(8,128)S(1)} fusion(f32[4,16,128]{2,1,0:T(8,128)} %param.10), kind=kLoop, calls=%fused_computation.27 | loop fusion | bytes 196352 | tf_op jit(solution)/shard_map/slice | solution.py:36
  1.6 0.9 %pad_select_fusion = f32[4,16,640]{2,1,0:T(8,128)S(1)} fusion(f32[4,16,128]{2,1,0:T(8,128)} %param.10, f32[4,16,639]{2,1,0:T(8,128)S(1)} %pad_slice_fusion, pred[4]{0:T(512)(128)(4,1)S(1)} %get-tuple-element.27), kind=kLoop, calls=%fused_computation.26 | loop fusion | flops 40960 | bytes 360196 | tf_op jit(solution)/shard_map/jit(_where)/select_n | solution.py:38
  2.5 0.1 pad_select_fusion.9
  2.6 0.0 copy-start.1
  2.6 0.1 pad_select_fusion.8
  2.7 0.0 copy-start.3
  2.7 0.1 pad_select_fusion.7
  2.9 0.1 pad_select_fusion.6
  3.0 0.1 pad_select_fusion.5
  3.1 0.0 copy-start.2
  3.1 0.1 pad_select_fusion.4
  3.2 0.1 pad_select_fusion.3
  3.3 0.1 pad_select_fusion.2
  3.4 0.1 pad_select_fusion.1
  3.5 2.4 %collective-permute-start.4 = (f32[4,16,640]{2,1,0:T(8,128)S(1)}, f32[4,16,640]{2,1,0:T(8,128)S(1)}, u32[]{:S(2)}, u32[]{:S(2)}) collective-permute-start(f32[4,16,640]{2,1,0:T(8,128)S(1)} %pad_select_fusion.1), channel_id=1, source_target_pairs={{0,3},{1,0},{2,1},{3,2},{4,7},{5,4},{6,5},{7,6},{8,11},{9,8},{10,9... | collective-permute-start | bytes 491528 | tf_op jit(solution)/shard_map/ppermute | solution.py:28
  6.0 0.6 %collective-permute-start.3 = (f32[4,16,640]{2,1,0:T(8,128)S(1)}, f32[4,16,640]{2,1,0:T(8,128)S(1)}, u32[]{:S(2)}, u32[]{:S(2)}) collective-permute-start(f32[4,16,640]{2,1,0:T(8,128)S(1)} %pad_select_fusion.1), channel_id=1, source_target_pairs={{0,2},{1,3},{2,0},{3,1},{4,6},{5,7},{6,4},{7,5},{8,10},{9,11},{10,... | collective-permute-start | bytes 491528 | tf_op jit(solution)/shard_map/ppermute | solution.py:28
  6.6 0.2 collective-permute-start.2
  6.8 0.7 %fusion.26 = (f32[128,256]{1,0:T(8,128)S(1)}, f32[128,256]{1,0:T(8,128)}) fusion(f32[384,256]{1,0:T(8,128)S(1)} %copy-done.1), kind=kLoop, calls=%fused_computation.63 | loop fusion | bytes 524288 | tf_op jit(solution)/shard_map/slice | solution.py:79
  7.4 1.3 %collective-permute-start.1 = (f32[128,256]{1,0:T(8,128)S(1)}, f32[128,256]{1,0:T(8,128)S(1)}, u32[]{:S(2)}, u32[]{:S(2)}) collective-permute-start(f32[128,256]{1,0:T(8,128)S(1)} %get-tuple-element.15), channel_id=1, source_target_pairs={{4,0},{8,4},{12,8},{16,12},{20,16},{24,20},{28,24},{5,1},{9,5},{13... | collective-permute-start | bytes 393224 | tf_op jit(solution)/shard_map/ppermute | solution.py:21
  8.7 4.6 %collective-permute-start = (f32[128,256]{1,0:T(8,128)}, f32[128,256]{1,0:T(8,128)S(1)}, u32[]{:S(2)}, u32[]{:S(2)}) collective-permute-start(f32[128,256]{1,0:T(8,128)} %get-tuple-element.16), channel_id=1, source_target_pairs={{0,4},{4,8},{8,12},{12,16},{16,20},{20,24},{24,28},{1,5},{5,9},{9,... | collective-permute-start | bytes 393224 | tf_op jit(solution)/shard_map/ppermute | solution.py:16
  14.0 0.1 broadcast_multiply_fusion
  14.0 0.1 mul.46
  14.1 4.4 %collective-permute-done = f32[128,256]{1,0:T(8,128)S(1)} collective-permute-done((f32[128,256]{1,0:T(8,128)}, f32[128,256]{1,0:T(8,128)S(1)}, u32[]{:S(2)}, u32[]{:S(2)}) %collective-permute-start) | collective-permute-done | bytes 131104 | tf_op jit(solution)/shard_map/ppermute | solution.py:16
  18.6 0.0 collective-permute-done.1
  18.6 1.6 %fusion.3 = f32[2,512,256]{2,1,0:T(8,128)S(1)} fusion(s32[2,512]{1,0:T(2,128)S(1)} %copy-done.2, f32[640,256]{1,0:T(8,128)S(1)} %constant_dynamic-update-slice_fusion), kind=kOutput, calls=%fused_computation.4 | convolution fusion | flops 1007288320 | bytes 1708032 | tf_op jit(solution)/shard_map/dot_general | solution.py:88
  20.2 1.0 %convolution_bitcast_fusion = f32[2,512,256]{2,1,0:T(8,128)S(1)} fusion(f32[2,512,256]{2,1,0:T(8,128)S(1)} %fusion.3, f32[2,512,512]{2,1,0:T(8,128)S(1)} %copy-done), kind=kOutput, calls=%fused_computation.6 | convolution fusion | flops 805306368 | bytes 4194304 | tf_op jit(solution)/shard_map/cij,cjb->cib/dot_general | solution.py:89
  21.2 0.8 %fusion.8 = f32[640,256]{1,0:T(8,128)S(1)} fusion(f32[2,512,256]{2,1,0:T(8,128)S(1)} %convolution_bitcast_fusion, s32[2,512]{1,0:T(2,128)S(1)} %copy-done.2), kind=kOutput, calls=%fused_computation.11 | convolution fusion | flops 1007288320 | bytes 1708032 | tf_op jit(solution)/shard_map/dot_general | solution.py:64
  22.1 0.0 collective-permute-done.4
  22.1 0.0 collective-permute-done.3
  22.1 0.0 collective-permute-done.2
  22.2 0.5 convolution_multiply_fusion
  22.6 0.7 %convolution_add_fusion = f32[640,256]{1,0:T(8,128)S(1)} fusion(f32[640,256]{1,0:T(8,128)S(1)} %fusion.8, f32[64,640]{1,0:T(8,128)S(1)} %bitcast.33, f32[64,256]{1,0:T(8,128)S(1)} %convolution_multiply_fusion), kind=kOutput, calls=%fused_computation.12 | convolution fusion | flops 125992960 | bytes 1540096 | tf_op jit(solution)/shard_map/dot_general | solution.py:90
  23.4 4.3 %collective-permute-start.5 = (f32[256,256]{1,0:T(8,128)S(1)}, f32[256,256]{1,0:T(8,128)S(1)}, u32[]{:S(2)}, u32[]{:S(2)}) collective-permute-start(f32[256,256]{1,0:T(8,128)S(1)} %get-tuple-element.13), channel_id=1, source_target_pairs={{0,4},{4,8},{8,12},{12,16},{16,20},{20,24},{24,28},{1,5},{5,9},{9,... | collective-permute-start | bytes 786440 | tf_op jit(solution)/shard_map/ppermute | solution.py:16
  27.7 1.5 %collective-permute-start.6 = (f32[256,256]{1,0:T(8,128)S(1)}, f32[256,256]{1,0:T(8,128)S(1)}, u32[]{:S(2)}, u32[]{:S(2)}) collective-permute-start(f32[256,256]{1,0:T(8,128)S(1)} %get-tuple-element.14), channel_id=1, source_target_pairs={{4,0},{8,4},{12,8},{16,12},{20,16},{24,20},{28,24},{5,1},{9,5},{13... | collective-permute-start | bytes 786440 | tf_op jit(solution)/shard_map/ppermute | solution.py:21
  29.2 1.9 %fusion.1 = f32[2,512,640]{2,1,0:T(8,128)S(1)} fusion(f32[2,512,512]{2,1,0:T(8,128)S(1)} %copy-done, s32[2,512]{1,0:T(2,128)S(1)} %copy-done.2), kind=kOutput, calls=%fused_computation.2 | convolution fusion | flops 2013921280 | bytes 4722688 | tf_op jit(solution)/shard_map/cij,cjq->ciq/dot_general | solution.py:95
  31.1 2.3 %fusion = f32[640,640,1]{1,0,2:T(8,128)S(1)} fusion(f32[2,512,640]{2,1,0:T(8,128)S(1)} %fusion.1, s32[2,512]{1,0:T(2,128)S(1)} %copy-done.2), kind=kOutput, calls=%fused_computation.1 | convolution fusion | flops 2517237760 | bytes 4263936 | tf_op jit(solution)/shard_map/dot_general | solution.py:64
  33.4 1.6 %bitcast_add_fusion = f32[640,640]{1,0:T(8,128)S(1)} fusion(f32[640,640,1]{1,0,2:T(8,128)S(1)} %fusion, f32[4,16,640]{2,1,0:T(8,128)S(1)} %add_add_fusion, f32[4,16]{1,0:T(4,128)S(1)} %broadcast_multiply_fusion), kind=kOutput, calls=%fused_computation.5 | convolution fusion | flops 315023360 | bytes 3440896 | tf_op jit(solution)/shard_map/dot_general | solution.py:98
  35.1 4.0 %collective-permute-done.5 = f32[256,256]{1,0:T(8,128)S(1)} collective-permute-done((f32[256,256]{1,0:T(8,128)S(1)}, f32[256,256]{1,0:T(8,128)S(1)}, u32[]{:S(2)}, u32[]{:S(2)}) %collective-permute-start.5) | collective-permute-done | bytes 262176 | tf_op jit(solution)/shard_map/ppermute | solution.py:16
  39.1 0.0 collective-permute-done.6
  39.1 0.2 multiply_select_fusion
  39.3 0.5 fusion.11
  39.8 4.4 %collective-permute-start.7 = (f32[128,256]{1,0:T(8,128)S(1)}, f32[128,256]{1,0:T(8,128)S(1)}, u32[]{:S(2)}, u32[]{:S(2)}) collective-permute-start(f32[128,256]{1,0:T(8,128)S(1)} %get-tuple-element.17), channel_id=1, source_target_pairs={{0,4},{4,8},{8,12},{12,16},{16,20},{20,24},{24,28},{1,5},{5,9},{9,... | collective-permute-start | bytes 393224 | tf_op jit(solution)/shard_map/ppermute | solution.py:16
  44.2 1.3 %collective-permute-start.8 = (f32[128,256]{1,0:T(8,128)S(1)}, f32[128,256]{1,0:T(8,128)S(1)}, u32[]{:S(2)}, u32[]{:S(2)}) collective-permute-start(f32[128,256]{1,0:T(8,128)S(1)} %get-tuple-element.18), channel_id=1, source_target_pairs={{4,0},{8,4},{12,8},{16,12},{20,16},{24,20},{28,24},{5,1},{9,5},{13... | collective-permute-start | bytes 393224 | tf_op jit(solution)/shard_map/ppermute | solution.py:21
  45.5 0.6 %fusion.9 = f32[384,256]{1,0:T(8,128)S(1)} fusion(f32[640,256]{1,0:T(8,128)S(1)} %multiply_select_fusion, f32[640,640]{1,0:T(8,128)S(1)} %bitcast_add_fusion), kind=kOutput, calls=%fused_computation.14 | convolution fusion | flops 377487360 | bytes 2031616 | tf_op jit(solution)/shard_map/dot_general | solution.py:122
  46.2 0.6 %collective-permute-done.7 = f32[128,256]{1,0:T(8,128)S(1)} collective-permute-done((f32[128,256]{1,0:T(8,128)S(1)}, f32[128,256]{1,0:T(8,128)S(1)}, u32[]{:S(2)}, u32[]{:S(2)}) %collective-permute-start.7) | collective-permute-done | bytes 131104 | tf_op jit(solution)/shard_map/ppermute | solution.py:16
  46.7 5.9 %collective-permute-done.8 = f32[128,256]{1,0:T(8,128)S(1)} collective-permute-done((f32[128,256]{1,0:T(8,128)S(1)}, f32[128,256]{1,0:T(8,128)S(1)}, u32[]{:S(2)}, u32[]{:S(2)}) %collective-permute-start.8) | collective-permute-done | bytes 131104 | tf_op jit(solution)/shard_map/ppermute | solution.py:21
  52.6 0.8 %fusion.17 = f32[384,256]{1,0:T(8,128)} fusion(f32[384,256]{1,0:T(8,128)S(1)} %copy-done.1, f32[640,256]{1,0:T(8,128)S(1)} %multiply_select_fusion, f32[128,256]{1,0:T(8,128)S(1)} %collective-permute-done.8, f32[384,256]{1,0:T(8,128)S(1)} %fusion.9, f32[128,256]{1,0:T(8,128)S(1)} %collective-permute-done.7), kind=kLoop, calls=%fused_computation.24 | loop fusion | flops 491520 | bytes 1835008 | tf_op jit(solution)/shard_map/sub | solution.py:130
  (18 shorter events, 0.2 us)
Async XLA Ops:
  0.0 20.2 %copy-start = (f32[2,512,512]{2,1,0:T(8,128)S(1)}, f32[2,512,512]{2,1,0:T(8,128)}, u32[]{:S(2)}) copy-start(f32[2,512,512]{2,1,0:T(8,128)} %param.8) | copy-start | bytes 6291460
  2.6 4.2 %copy-start.1 = (f32[384,256]{1,0:T(8,128)S(1)}, f32[384,256]{1,0:T(8,128)}, u32[]{:S(2)}) copy-start(f32[384,256]{1,0:T(8,128)} %param.7) | copy-start | bytes 1179652
  2.7 11.2 %copy-start.3 = (f32[4,16]{1,0:T(4,128)S(1)}, f32[4,16]{1,0:T(4,128)}, u32[]{:S(2)}) copy-start(f32[4,16]{1,0:T(4,128)} %param.11) | copy-start | bytes 772
  3.1 15.5 %copy-start.2 = (s32[2,512]{1,0:T(2,128)S(1)}, s32[2,512]{1,0:T(2,128)}, u32[]{:S(2)}) copy-start(s32[2,512]{1,0:T(2,128)} %param.9) | copy-start | bytes 12292
  3.5 18.6 %collective-permute-start.4 = (f32[4,16,640]{2,1,0:T(8,128)S(1)}, f32[4,16,640]{2,1,0:T(8,128)S(1)}, u32[]{:S(2)}, u32[]{:S(2)}) collective-permute-start(f32[4,16,640]{2,1,0:T(8,128)S(1)} %pad_select_fusion.1), channel_id=1, source_target_pairs={{0,3},{1,0},{2,1},{3,2},{4,7},{5,4},{6,5},{7,6},{8,11},{9,8},{10,9... | collective-permute-start | bytes 491528 | tf_op jit(solution)/shard_map/ppermute | solution.py:28
  6.0 16.1 %collective-permute-start.3 = (f32[4,16,640]{2,1,0:T(8,128)S(1)}, f32[4,16,640]{2,1,0:T(8,128)S(1)}, u32[]{:S(2)}, u32[]{:S(2)}) collective-permute-start(f32[4,16,640]{2,1,0:T(8,128)S(1)} %pad_select_fusion.1), channel_id=1, source_target_pairs={{0,2},{1,3},{2,0},{3,1},{4,6},{5,7},{6,4},{7,5},{8,10},{9,11},{10,... | collective-permute-start | bytes 491528 | tf_op jit(solution)/shard_map/ppermute | solution.py:28
  6.6 15.5 %collective-permute-start.2 = (f32[4,16,640]{2,1,0:T(8,128)S(1)}, f32[4,16,640]{2,1,0:T(8,128)S(1)}, u32[]{:S(2)}, u32[]{:S(2)}) collective-permute-start(f32[4,16,640]{2,1,0:T(8,128)S(1)} %pad_select_fusion.1), channel_id=1, source_target_pairs={{0,1},{1,2},{2,3},{3,0},{4,5},{5,6},{6,7},{7,4},{8,9},{9,10},{10,1... | collective-permute-start | bytes 491528 | tf_op jit(solution)/shard_map/ppermute | solution.py:28
  7.4 11.2 %collective-permute-start.1 = (f32[128,256]{1,0:T(8,128)S(1)}, f32[128,256]{1,0:T(8,128)S(1)}, u32[]{:S(2)}, u32[]{:S(2)}) collective-permute-start(f32[128,256]{1,0:T(8,128)S(1)} %get-tuple-element.15), channel_id=1, source_target_pairs={{4,0},{8,4},{12,8},{16,12},{20,16},{24,20},{28,24},{5,1},{9,5},{13... | collective-permute-start | bytes 393224 | tf_op jit(solution)/shard_map/ppermute | solution.py:21
  8.7 9.8 %collective-permute-start = (f32[128,256]{1,0:T(8,128)}, f32[128,256]{1,0:T(8,128)S(1)}, u32[]{:S(2)}, u32[]{:S(2)}) collective-permute-start(f32[128,256]{1,0:T(8,128)} %get-tuple-element.16), channel_id=1, source_target_pairs={{0,4},{4,8},{8,12},{12,16},{16,20},{20,24},{24,28},{1,5},{5,9},{9,... | collective-permute-start | bytes 393224 | tf_op jit(solution)/shard_map/ppermute | solution.py:16
  23.4 15.7 %collective-permute-start.5 = (f32[256,256]{1,0:T(8,128)S(1)}, f32[256,256]{1,0:T(8,128)S(1)}, u32[]{:S(2)}, u32[]{:S(2)}) collective-permute-start(f32[256,256]{1,0:T(8,128)S(1)} %get-tuple-element.13), channel_id=1, source_target_pairs={{0,4},{4,8},{8,12},{12,16},{16,20},{20,24},{24,28},{1,5},{5,9},{9,... | collective-permute-start | bytes 786440 | tf_op jit(solution)/shard_map/ppermute | solution.py:16
  27.7 11.4 %collective-permute-start.6 = (f32[256,256]{1,0:T(8,128)S(1)}, f32[256,256]{1,0:T(8,128)S(1)}, u32[]{:S(2)}, u32[]{:S(2)}) collective-permute-start(f32[256,256]{1,0:T(8,128)S(1)} %get-tuple-element.14), channel_id=1, source_target_pairs={{4,0},{8,4},{12,8},{16,12},{20,16},{24,20},{28,24},{5,1},{9,5},{13... | collective-permute-start | bytes 786440 | tf_op jit(solution)/shard_map/ppermute | solution.py:21
  39.8 6.9 %collective-permute-start.7 = (f32[128,256]{1,0:T(8,128)S(1)}, f32[128,256]{1,0:T(8,128)S(1)}, u32[]{:S(2)}, u32[]{:S(2)}) collective-permute-start(f32[128,256]{1,0:T(8,128)S(1)} %get-tuple-element.17), channel_id=1, source_target_pairs={{0,4},{4,8},{8,12},{12,16},{16,20},{20,24},{24,28},{1,5},{5,9},{9,... | collective-permute-start | bytes 393224 | tf_op jit(solution)/shard_map/ppermute | solution.py:16
  44.2 8.4 %collective-permute-start.8 = (f32[128,256]{1,0:T(8,128)S(1)}, f32[128,256]{1,0:T(8,128)S(1)}, u32[]{:S(2)}, u32[]{:S(2)}) collective-permute-start(f32[128,256]{1,0:T(8,128)S(1)} %get-tuple-element.18), channel_id=1, source_target_pairs={{4,0},{8,4},{12,8},{16,12},{20,16},{24,20},{28,24},{5,1},{9,5},{13... | collective-permute-start | bytes 393224 | tf_op jit(solution)/shard_map/ppermute | solution.py:21

commit v11 on v9

--- a/solution.py
+++ b/solution.py
@@ -22,18 +22,7 @@
 
 
 def gather_band(piece):
-    count = lax.axis_size("band")
-    me = lax.axis_index("band")
-    pieces = [piece]
-    for k in range(1, count):
-        pieces.append(
-            lax.ppermute(piece, "band", [(i, (i + k) % count) for i in range(count)])
-        )
-    stacked = jnp.stack(pieces)
-    order = (me - jnp.arange(count)) % count
-    ordered = jnp.take(stacked, order, axis=0)
-    slots, channels, width = piece.shape
-    return ordered.transpose(1, 2, 0, 3).reshape(slots, channels, count * width)
+    return lax.all_gather(piece, "band", axis=2, tiled=True)
 
 
 def shift_right(x, amount, bits):
@@ -89,11 +78,11 @@
     cells, nodes, _ = cell_matrix.shape
     high = lax.Precision.HIGH
 
-    coefficients = jnp.dot(placed, extended, precision=highest) * weights[:, None]
+    coefficients = jnp.dot(placed, extended, precision=high) * weights[:, None]
     gathered = jnp.dot(onehot, extended, precision=high).reshape(cells, nodes, -1)
     local = jnp.einsum("cij,cjb->cib", cell_matrix, gathered, precision=high)
     first = scatter_rows(onehot, local.reshape(cells * nodes, -1)) + jnp.dot(
-        placed.T, coefficients, precision=highest
+        placed.T, coefficients, precision=high
     )
 
     matrices, first = lax.optimization_barrier((cell_matrix, first))

time: 49.7 us -> 52.9 us (1.064)
  blocking collectives: 0 us -> 5.74 us
  starting transfers between devices: 22 us -> 18.7 us
  waiting for transfers between devices: 8.72 us -> 10.7 us
  other arithmetic: 4.22 us -> 2.63 us
  matrix products: 11.6 us -> 12.4 us
    all_gather x0 -> x1, blocking collectives: none -> 5.74 us  [gather_band(): return lax.all_gather(piece, 'band', axis=2, tiled=True)]
    ppermute x3 -> x0, starting transfers between devices: 4.68 us -> none  [gather_band(): lax.ppermute(piece, 'band', [(i, (i + k) % count) for i in range(count)])]
    ppermute x3, waiting for transfers between devices: 4.34 us -> 6.37 us  [from_left(): return lax.ppermute(x, axis, [(i, i + 1) for i in range(count - 1)])]
    ppermute x3, starting transfers between devices: 13.3 us -> 14.6 us  [from_left(): return lax.ppermute(x, axis, [(i, i + 1) for i in range(count - 1)])]
    dot_general x1, matrix products: 1.58 us -> 2.75 us  [on_device(): jnp.dot((placed * weights[:, None]).T, placed, precision=highest)]
    another operation x1 -> x0, other arithmetic: 0.77 us -> none  [gather_band(): stacked = jnp.stack(pieces)]
    mul x1, other arithmetic: 0.75 us -> 0.07 us  [atom_rows(): weights = coupling * live.astype(jnp.float32)]
    gather x1 -> x0, local copies, waits for them, and re-layouts: 0.56 us -> none  [gather_band(): ordered = jnp.take(stacked, order, axis=0)]
  transfers between devices with their start and end apart: 9 -> 6, of which waited for: 3 -> 3; matrix products, arithmetic and copies ran while one was open for 23% -> 18% of each run, Pallas kernels for 0% -> 0%
where the time goes in v11:
time: 52.9 us; the launch traced here: 52.6 us
  starting transfers between devices  18.7 us (35%)
  matrix products  12.4 us (23%)
  waiting for transfers between devices  10.7 us (20%)
  blocking collectives  5.74 us (11%)
  other arithmetic  2.63 us (5%)
  local copies, waits for them, and re-layouts  1.42 us (3%)
  between operations  0.98 us (2%)
    ppermute x3, starting transfers between devices, from_left(): return lax.ppermute(x, axis, [(i, i + 1) for i in range(count - 1)])  14.6 us
    ppermute x3, waiting for transfers between devices, from_left(): return lax.ppermute(x, axis, [(i, i + 1) for i in range(count - 1)])  6.37 us
    all_gather x1, blocking collectives, gather_band(): return lax.all_gather(piece, 'band', axis=2, tiled=True)  5.74 us
    ppermute x3, waiting for transfers between devices, from_right(): return lax.ppermute(x, axis, [(i + 1, i) for i in range(count - 1)])  4.37 us
    ppermute x3, starting transfers between devices, from_right(): return lax.ppermute(x, axis, [(i + 1, i) for i in range(count - 1)])  4.01 us
    dot_general x2, matrix products, scatter_rows(): lax.dot_general(onehot, values, (((0,), (0,)), ((), ())), precision=lax.P...  3.2 us
    dot_general x1, matrix products, on_device(): jnp.dot((placed * weights[:, None]).T, placed, precision=highest)  2.75 us
    dot_general x1, matrix products, on_device(): jnp.einsum('cij,cjq->ciq', matrices, onehot.reshape(cells, nodes, ext), p...  1.95 us
  transfers between devices with their start and end apart: 6, of which 3 were waited for; matrix products, arithmetic and copies ran while one was open for 18% of the time, Pallas kernels for 0%

profile of v11, /device:TPU:0, one launch (start us, length us, event | category | flops | bytes accessed | tf_op | source)
XLA Modules:
  0.0 52.6 jit_solution(8587172336822369947)
XLA Ops:
  0.0 0.0 copy-start
  0.0 1.1 %fusion.27 = (f32[128,256]{1,0:T(8,128)S(1)}, f32[128,256]{1,0:T(8,128)S(1)}) fusion(f32[384,256]{1,0:T(8,128)} %param.7), kind=kLoop, calls=%fused_computation.59 | loop fusion | bytes 524288 | tf_op jit(solution)/shard_map/slice | solution.py:73
  1.1 0.0 copy-start.3
  1.2 1.3 %collective-permute-start.1 = (f32[128,256]{1,0:T(8,128)S(1)}, f32[128,256]{1,0:T(8,128)S(1)}, u32[]{:S(2)}, u32[]{:S(2)}) collective-permute-start(f32[128,256]{1,0:T(8,128)S(1)} %get-tuple-element.13), channel_id=1, source_target_pairs={{4,0},{8,4},{12,8},{16,12},{20,16},{24,20},{28,24},{5,1},{9,5},{13... | collective-permute-start | bytes 393224 | tf_op jit(solution)/shard_map/ppermute | solution.py:21
  2.5 5.5 %collective-permute-start = (f32[128,256]{1,0:T(8,128)S(1)}, f32[128,256]{1,0:T(8,128)S(1)}, u32[]{:S(2)}, u32[]{:S(2)}) collective-permute-start(f32[128,256]{1,0:T(8,128)S(1)} %get-tuple-element.14), channel_id=1, source_target_pairs={{0,4},{4,8},{8,12},{12,16},{16,20},{20,24},{24,28},{1,5},{5,9},{9,... | collective-permute-start | bytes 393224 | tf_op jit(solution)/shard_map/ppermute | solution.py:16
  8.6 0.7 %and_compare_fusion.7 = (pred[4]{0:T(512)(128)(4,1)S(1)}, pred[4]{0:T(512)(128)(4,1)S(1)}, pred[4]{0:T(512)(128)(4,1)S(1)}, pred[4]{0:T(512)(128)(4,1)S(1)}, pre...) fusion(s32[4]{0:T(128)} %param.12), kind=kLoop, calls=%fused_computation.54 | loop fusion | flops 100 | bytes 48 | tf_op jit(solution)/shard_map/eq | solution.py:34
  9.3 5.7 %all_gather.3 = f32[4,16,512]{2,1,0:T(8,128)S(1)} all-gather(f32[4,16,128]{2,1,0:T(8,128)} %param.10), channel_id=1, replica_groups=mesh['dom'=8,'band'=4] {'band'}, dimensions={2}, use_global_device_ids=true | all-gather | bytes 163840 | tf_op jit(solution)/shard_map/all_gather | solution.py:25
  15.1 0.1 pad_select_fusion
  15.2 0.1 pad_select_fusion.7
  15.3 0.1 pad_select_fusion.6
  15.4 0.1 pad_select_fusion.5
  15.5 0.1 pad_select_fusion.4
  15.6 0.0 copy-start.1
  15.7 0.1 pad_select_fusion.3
  15.8 0.1 pad_select_fusion.2
  15.9 0.0 copy-done.3
  15.9 0.0 copy-start.2
  15.9 0.1 broadcast_multiply_fusion
  16.0 0.1 pad_select_fusion.1
  16.1 2.8 %fusion.18 = f32[640,640,1]{1,0,2:T(8,128)} fusion(f32[4,16,640]{2,1,0:T(8,128)S(1)} %pad_select_fusion.1, f32[4,16]{1,0:T(4,128)S(1)} %broadcast_multiply_fusion), kind=kOutput, calls=%fused_computation.25 | convolution fusion | flops 314613760 | bytes 1802496 | tf_op jit(solution)/shard_map/dot_general | solution.py:92
  18.8 0.1 mul.42
  18.9 0.0 collective-permute-done
  19.0 0.0 copy-done.1
  19.0 0.0 collective-permute-done.1
  19.0 0.0 copy-done.2
  19.0 1.6 %fusion.3 = f32[2,512,256]{2,1,0:T(8,128)S(1)} fusion(s32[2,512]{1,0:T(2,128)S(1)} %copy-done.2, f32[640,256]{1,0:T(8,128)S(1)} %constant_dynamic-update-slice_fusion), kind=kOutput, calls=%fused_computation.4 | convolution fusion | flops 1007288320 | bytes 1708032 | tf_op jit(solution)/shard_map/dot_general | solution.py:82
  20.6 0.0 copy-done
  20.6 1.0 %convolution_bitcast_fusion = f32[2,512,256]{2,1,0:T(8,128)S(1)} fusion(f32[2,512,256]{2,1,0:T(8,128)S(1)} %fusion.3, f32[2,512,512]{2,1,0:T(8,128)S(1)} %copy-done), kind=kOutput, calls=%fused_computation.6 | convolution fusion | flops 805306368 | bytes 4194304 | tf_op jit(solution)/shard_map/cij,cjb->cib/dot_general | solution.py:83
  21.6 0.8 %fusion.8 = f32[640,256]{1,0:T(8,128)S(1)} fusion(f32[2,512,256]{2,1,0:T(8,128)S(1)} %convolution_bitcast_fusion, s32[2,512]{1,0:T(2,128)S(1)} %copy-done.2), kind=kOutput, calls=%fused_computation.11 | convolution fusion | flops 1007288320 | bytes 1708032 | tf_op jit(solution)/shard_map/dot_general | solution.py:58
  22.5 0.3 convolution_multiply_fusion
  22.8 0.5 convolution_add_fusion
  23.3 4.7 %collective-permute-start.2 = (f32[256,256]{1,0:T(8,128)S(1)}, f32[256,256]{1,0:T(8,128)S(1)}, u32[]{:S(2)}, u32[]{:S(2)}) collective-permute-start(f32[256,256]{1,0:T(8,128)S(1)} %get-tuple-element.11), channel_id=1, source_target_pairs={{0,4},{4,8},{8,12},{12,16},{16,20},{20,24},{24,28},{1,5},{5,9},{9,... | collective-permute-start | bytes 786440 | tf_op jit(solution)/shard_map/ppermute | solution.py:16
  28.1 0.0 copy-start.4
  28.1 1.4 %collective-permute-start.3 = (f32[256,256]{1,0:T(8,128)S(1)}, f32[256,256]{1,0:T(8,128)S(1)}, u32[]{:S(2)}, u32[]{:S(2)}) collective-permute-start(f32[256,256]{1,0:T(8,128)S(1)} %get-tuple-element.12), channel_id=1, source_target_pairs={{4,0},{8,4},{12,8},{16,12},{20,16},{24,20},{28,24},{5,1},{9,5},{13... | collective-permute-start | bytes 786440 | tf_op jit(solution)/shard_map/ppermute | solution.py:21
  29.5 1.9 %fusion.1 = f32[2,512,640]{2,1,0:T(8,128)S(1)} fusion(f32[2,512,512]{2,1,0:T(8,128)S(1)} %copy-done, s32[2,512]{1,0:T(2,128)S(1)} %copy-done.2), kind=kOutput, calls=%fused_computation.2 | convolution fusion | flops 2013921280 | bytes 4722688 | tf_op jit(solution)/shard_map/cij,cjq->ciq/dot_general | solution.py:89
  31.5 0.0 copy-done.4
  31.5 2.4 %bitcast_add_fusion = f32[640,640]{1,0:T(8,128)S(1)} fusion(f32[640,640,1]{1,0,2:T(8,128)S(1)} %copy-done.4, f32[2,512,640]{2,1,0:T(8,128)S(1)} %fusion.1, s32[2,512]{1,0:T(2,128)S(1)} %copy-done.2), kind=kOutput, calls=%fused_computation.5 | convolution fusion | flops 2517647360 | bytes 5902336 | tf_op jit(solution)/shard_map/dot_general | solution.py:58
  33.9 5.8 %collective-permute-done.2 = f32[256,256]{1,0:T(8,128)S(1)} collective-permute-done((f32[256,256]{1,0:T(8,128)S(1)}, f32[256,256]{1,0:T(8,128)S(1)}, u32[]{:S(2)}, u32[]{:S(2)}) %collective-permute-start.2) | collective-permute-done | bytes 262176 | tf_op jit(solution)/shard_map/ppermute | solution.py:16
  39.7 0.0 collective-permute-done.3
  39.7 0.2 multiply_select_fusion
  39.9 0.5 fusion.11
  40.5 4.4 %collective-permute-start.4 = (f32[128,256]{1,0:T(8,128)S(1)}, f32[128,256]{1,0:T(8,128)S(1)}, u32[]{:S(2)}, u32[]{:S(2)}) collective-permute-start(f32[128,256]{1,0:T(8,128)S(1)} %get-tuple-element.15), channel_id=1, source_target_pairs={{0,4},{4,8},{8,12},{12,16},{16,20},{20,24},{24,28},{1,5},{5,9},{9,... | collective-permute-start | bytes 393224 | tf_op jit(solution)/shard_map/ppermute | solution.py:16
  44.9 1.3 %collective-permute-start.5 = (f32[128,256]{1,0:T(8,128)S(1)}, f32[128,256]{1,0:T(8,128)S(1)}, u32[]{:S(2)}, u32[]{:S(2)}) collective-permute-start(f32[128,256]{1,0:T(8,128)S(1)} %get-tuple-element.16), channel_id=1, source_target_pairs={{4,0},{8,4},{12,8},{16,12},{20,16},{24,20},{28,24},{5,1},{9,5},{13... | collective-permute-start | bytes 393224 | tf_op jit(solution)/shard_map/ppermute | solution.py:21
  46.2 0.7 %fusion.9 = f32[384,256]{1,0:T(8,128)S(1)} fusion(f32[640,256]{1,0:T(8,128)S(1)} %multiply_select_fusion, f32[640,640]{1,0:T(8,128)S(1)} %bitcast_add_fusion), kind=kOutput, calls=%fused_computation.14 | convolution fusion | flops 377487360 | bytes 2031616 | tf_op jit(solution)/shard_map/dot_general | solution.py:116
  46.8 0.5 %collective-permute-done.4 = f32[128,256]{1,0:T(8,128)S(1)} collective-permute-done((f32[128,256]{1,0:T(8,128)S(1)}, f32[128,256]{1,0:T(8,128)S(1)}, u32[]{:S(2)}, u32[]{:S(2)}) %collective-permute-start.4) | collective-permute-done | bytes 131104 | tf_op jit(solution)/shard_map/ppermute | solution.py:16
  47.4 4.4 %collective-permute-done.5 = f32[128,256]{1,0:T(8,128)S(1)} collective-permute-done((f32[128,256]{1,0:T(8,128)S(1)}, f32[128,256]{1,0:T(8,128)S(1)}, u32[]{:S(2)}, u32[]{:S(2)}) %collective-permute-start.5) | collective-permute-done | bytes 131104 | tf_op jit(solution)/shard_map/ppermute | solution.py:21
  51.7 0.8 %fusion.17 = f32[384,256]{1,0:T(8,128)} fusion(f32[384,256]{1,0:T(8,128)S(1)} %copy-done.1, f32[640,256]{1,0:T(8,128)S(1)} %multiply_select_fusion, f32[128,256]{1,0:T(8,128)S(1)} %collective-permute-done.5, f32[384,256]{1,0:T(8,128)S(1)} %fusion.9, f32[128,256]{1,0:T(8,128)S(1)} %collective-permute-done.4), kind=kLoop, calls=%fused_computation.24 | loop fusion | flops 491520 | bytes 1835008 | tf_op jit(solution)/shard_map/sub | solution.py:124
  (10 shorter events, 0.2 us)
Async XLA Ops:
  0.0 20.6 %copy-start = (f32[2,512,512]{2,1,0:T(8,128)S(1)}, f32[2,512,512]{2,1,0:T(8,128)}, u32[]{:S(2)}) copy-start(f32[2,512,512]{2,1,0:T(8,128)} %param.8) | copy-start | bytes 6291460
  1.1 14.8 %copy-start.3 = (f32[4,16]{1,0:T(4,128)S(1)}, f32[4,16]{1,0:T(4,128)}, u32[]{:S(2)}) copy-start(f32[4,16]{1,0:T(4,128)} %param.11) | copy-start | bytes 772
  1.2 17.8 %collective-permute-start.1 = (f32[128,256]{1,0:T(8,128)S(1)}, f32[128,256]{1,0:T(8,128)S(1)}, u32[]{:S(2)}, u32[]{:S(2)}) collective-permute-start(f32[128,256]{1,0:T(8,128)S(1)} %get-tuple-element.13), channel_id=1, source_target_pairs={{4,0},{8,4},{12,8},{16,12},{20,16},{24,20},{28,24},{5,1},{9,5},{13... | collective-permute-start | bytes 393224 | tf_op jit(solution)/shard_map/ppermute | solution.py:21
  2.5 16.5 %collective-permute-start = (f32[128,256]{1,0:T(8,128)S(1)}, f32[128,256]{1,0:T(8,128)S(1)}, u32[]{:S(2)}, u32[]{:S(2)}) collective-permute-start(f32[128,256]{1,0:T(8,128)S(1)} %get-tuple-element.14), channel_id=1, source_target_pairs={{0,4},{4,8},{8,12},{12,16},{16,20},{20,24},{24,28},{1,5},{5,9},{9,... | collective-permute-start | bytes 393224 | tf_op jit(solution)/shard_map/ppermute | solution.py:16
  15.6 3.3 %copy-start.1 = (f32[384,256]{1,0:T(8,128)S(1)}, f32[384,256]{1,0:T(8,128)}, u32[]{:S(2)}) copy-start(f32[384,256]{1,0:T(8,128)} %param.7) | copy-start | bytes 1179652
  15.9 3.1 %copy-start.2 = (s32[2,512]{1,0:T(2,128)S(1)}, s32[2,512]{1,0:T(2,128)}, u32[]{:S(2)}) copy-start(s32[2,512]{1,0:T(2,128)} %param.9) | copy-start | bytes 12292
  23.3 16.4 %collective-permute-start.2 = (f32[256,256]{1,0:T(8,128)S(1)}, f32[256,256]{1,0:T(8,128)S(1)}, u32[]{:S(2)}, u32[]{:S(2)}) collective-permute-start(f32[256,256]{1,0:T(8,128)S(1)} %get-tuple-element.11), channel_id=1, source_target_pairs={{0,4},{4,8},{8,12},{12,16},{16,20},{20,24},{24,28},{1,5},{5,9},{9,... | collective-permute-start | bytes 786440 | tf_op jit(solution)/shard_map/ppermute | solution.py:16
  28.1 3.4 %copy-start.4 = (f32[640,640,1]{1,0,2:T(8,128)S(1)}, f32[640,640,1]{1,0,2:T(8,128)}, u32[]{:S(2)}) copy-start(f32[640,640,1]{1,0,2:T(8,128)} %fusion.18) | copy-start | bytes 4915204
  28.1 11.7 %collective-permute-start.3 = (f32[256,256]{1,0:T(8,128)S(1)}, f32[256,256]{1,0:T(8,128)S(1)}, u32[]{:S(2)}, u32[]{:S(2)}) collective-permute-start(f32[256,256]{1,0:T(8,128)S(1)} %get-tuple-element.12), channel_id=1, source_target_pairs={{4,0},{8,4},{12,8},{16,12},{20,16},{24,20},{28,24},{5,1},{9,5},{13... | collective-permute-start | bytes 786440 | tf_op jit(solution)/shard_map/ppermute | solution.py:21
  40.5 6.9 %collective-permute-start.4 = (f32[128,256]{1,0:T(8,128)S(1)}, f32[128,256]{1,0:T(8,128)S(1)}, u32[]{:S(2)}, u32[]{:S(2)}) collective-permute-start(f32[128,256]{1,0:T(8,128)S(1)} %get-tuple-element.15), channel_id=1, source_target_pairs={{0,4},{4,8},{8,12},{12,16},{16,20},{20,24},{24,28},{1,5},{5,9},{9,... | collective-permute-start | bytes 393224 | tf_op jit(solution)/shard_map/ppermute | solution.py:16
  44.9 6.9 %collective-permute-start.5 = (f32[128,256]{1,0:T(8,128)S(1)}, f32[128,256]{1,0:T(8,128)S(1)}, u32[]{:S(2)}, u32[]{:S(2)}) collective-permute-start(f32[128,256]{1,0:T(8,128)S(1)} %get-tuple-element.16), channel_id=1, source_target_pairs={{4,0},{8,4},{12,8},{16,12},{20,16},{24,20},{28,24},{5,1},{9,5},{13... | collective-permute-start | bytes 393224 | tf_op jit(solution)/shard_map/ppermute | solution.py:21

commit v12 on v9

--- a/solution.py
+++ b/solution.py
@@ -96,12 +96,14 @@
         placed.T, coefficients, precision=highest
     )
 
-    matrices, first = lax.optimization_barrier((cell_matrix, first))
+    matrices, placed_late, weights_late, first = lax.optimization_barrier(
+        (cell_matrix, placed, weights, first)
+    )
     moved = jnp.einsum(
         "cij,cjq->ciq", matrices, onehot.reshape(cells, nodes, ext), precision=high
     )
     operator = scatter_rows(onehot, moved.reshape(cells * nodes, ext)) + jnp.dot(
-        (placed * weights[:, None]).T, placed, precision=highest
+        (placed_late * weights_late[:, None]).T, placed_late, precision=highest
     )
     left_sums = from_left(first[ext - 2 * g :], "dom")
     right_sums = from_right(first[: 2 * g], "dom")

time: 49.7 us -> 48.1 us (0.968)
  waiting for transfers between devices: 8.72 us -> 7 us
    ppermute x3, waiting for transfers between devices: 4.34 us -> 2.62 us  [from_left(): return lax.ppermute(x, axis, [(i, i + 1) for i in range(count - 1)])]
  transfers between devices with their start and end apart: 9 -> 9, of which waited for: 3 -> 3; matrix products, arithmetic and copies ran while one was open for 23% -> 24% of each run, Pallas kernels for 0% -> 0%
where the time goes in v12:
time: 48.1 us; the launch traced here: 47.7 us
  starting transfers between devices  22 us (46%)
  matrix products  11.6 us (24%)
  waiting for transfers between devices  7 us (15%)
  other arithmetic  4.22 us (9%)
  local copies, waits for them, and re-layouts  1.85 us (4%)
  between operations  0.99 us (2%)
    ppermute x3, starting transfers between devices, from_left(): return lax.ppermute(x, axis, [(i, i + 1) for i in range(count - 1)])  13.3 us
    ppermute x3, starting transfers between devices, gather_band(): lax.ppermute(piece, 'band', [(i, (i + k) % count) for i in range(count)])  4.68 us
    ppermute x3, waiting for transfers between devices, from_right(): return lax.ppermute(x, axis, [(i + 1, i) for i in range(count - 1)])  4.37 us
    ppermute x3, starting transfers between devices, from_right(): return lax.ppermute(x, axis, [(i + 1, i) for i in range(count - 1)])  4.06 us
    dot_general x2, matrix products, scatter_rows(): lax.dot_general(onehot, values, (((0,), (0,)), ((), ())), precision=lax.P...  3.17 us
    ppermute x3, waiting for transfers between devices, from_left(): return lax.ppermute(x, axis, [(i, i + 1) for i in range(count - 1)])  2.62 us
    dot_general x1, matrix products, on_device(): jnp.einsum('cij,cjq->ciq', matrices, onehot.reshape(cells, nodes, ext), p...  1.95 us
    dot_general x1, matrix products, on_device(): jnp.dot((placed_late * weights_late[:, None]).T, placed_late, precision=h...  1.57 us
  transfers between devices with their start and end apart: 9, of which 3 were waited for; matrix products, arithmetic and copies ran while one was open for 24% of the time, Pallas kernels for 0%

profile of v12, /device:TPU:0, one launch (start us, length us, event | category | flops | bytes accessed | tf_op | source)
XLA Modules:
  0.0 47.7 jit_solution(10136703114662928992)
XLA Ops:
  0.0 0.5 collective-permute-start
  0.5 2.0 %collective-permute-start.2 = (f32[4,16,128]{2,1,0:T(8,128)}, f32[4,16,128]{2,1,0:T(8,128)S(1)}, u32[]{:S(2)}, u32[]{:S(2)}) collective-permute-start(f32[4,16,128]{2,1,0:T(8,128)} %param.10), channel_id=1, source_target_pairs={{0,3},{1,0},{2,1},{3,2},{4,7},{5,4},{6,5},{7,6},{8,11},{9,8},{10,9... | collective-permute-start | bytes 98312 | tf_op jit(solution)/shard_map/ppermute | solution.py:30
  2.4 2.2 %collective-permute-start.1 = (f32[4,16,128]{2,1,0:T(8,128)}, f32[4,16,128]{2,1,0:T(8,128)S(1)}, u32[]{:S(2)}, u32[]{:S(2)}) collective-permute-start(f32[4,16,128]{2,1,0:T(8,128)} %param.10), channel_id=1, source_target_pairs={{0,2},{1,3},{2,0},{3,1},{4,6},{5,7},{6,4},{7,5},{8,10},{9,11},{10,... | collective-permute-start | bytes 98312 | tf_op jit(solution)/shard_map/ppermute | solution.py:30
  4.7 1.0 %fusion.30 = (f32[128,256]{1,0:T(8,128)S(1)}, f32[128,256]{1,0:T(8,128)S(1)}) fusion(f32[384,256]{1,0:T(8,128)} %param.7), kind=kLoop, calls=%fused_computation.76 | loop fusion | bytes 524288 | tf_op jit(solution)/shard_map/slice | solution.py:84
  5.7 1.3 %collective-permute-start.4 = (f32[128,256]{1,0:T(8,128)S(1)}, f32[128,256]{1,0:T(8,128)S(1)}, u32[]{:S(2)}, u32[]{:S(2)}) collective-permute-start(f32[128,256]{1,0:T(8,128)S(1)} %get-tuple-element.17), channel_id=1, source_target_pairs={{4,0},{8,4},{12,8},{16,12},{20,16},{24,20},{28,24},{5,1},{9,5},{13... | collective-permute-start | bytes 393224 | tf_op jit(solution)/shard_map/ppermute | solution.py:21
  7.0 4.6 %collective-permute-start.3 = (f32[128,256]{1,0:T(8,128)S(1)}, f32[128,256]{1,0:T(8,128)S(1)}, u32[]{:S(2)}, u32[]{:S(2)}) collective-permute-start(f32[128,256]{1,0:T(8,128)S(1)} %get-tuple-element.18), channel_id=1, source_target_pairs={{0,4},{4,8},{8,12},{12,16},{16,20},{20,24},{24,28},{1,5},{5,9},{9,... | collective-permute-start | bytes 393224 | tf_op jit(solution)/shard_map/ppermute | solution.py:16
  12.2 0.7 %and_compare_fusion.7 = (pred[4]{0:T(512)(128)(4,1)S(1)}, pred[4]{0:T(512)(128)(4,1)S(1)}, pred[4]{0:T(512)(128)(4,1)S(1)}, pred[4]{0:T(512)(128)(4,1)S(1)}, pre...) fusion(s32[4]{0:T(128)} %param.12), kind=kLoop, calls=%fused_computation.71 | loop fusion | flops 100 | bytes 48 | tf_op jit(solution)/shard_map/eq | solution.py:45
  12.9 0.8 %broadcast_multiply_fusion = f32[4,16]{1,0:T(4,128)S(1)} fusion(f32[4,16]{1,0:T(4,128)} %param.11, f32[4]{0:T(128)S(1)} %compare_convert_fusion), kind=kLoop, calls=%fused_computation.60 | loop fusion | flops 64 | bytes 528 | tf_op jit(solution)/shard_map/mul | solution.py:57
  13.7 0.1 reshape.123
  13.8 0.0 collective-permute-done
  13.8 0.0 collective-permute-done.2
  13.8 0.0 collective-permute-done.1
  13.8 0.8 %pad_maximum_fusion = f32[4,4,16,128]{3,2,1,0:T(8,128)S(1)} fusion(f32[1,4,16,128]{3,2,1,0:T(8,128)S(1)} %bitcast.53, f32[1,4,16,128]{3,2,1,0:T(8,128)S(1)} %bitcast.54, f32[1,4,16,128]{3,2,1,0:T(8,128)S(1)} %bitcast.52, f32[1,4,16,128]{3,2,1,0:T(8,128)} %bitcast.51), kind=kLoop, calls=%fused_computation.38 | loop fusion | flops 98304 | bytes 262144 | tf_op jit(solution)/shard_map/stack | solution.py:32
  14.6 0.6 %gather_fusion = f32[4,4,16,128]{3,2,1,0:T(8,128)S(1)} fusion(f32[4,4,16,128]{3,2,1,0:T(8,128)S(1)} %pad_maximum_fusion, s32[1024]{0:T(1024)S(1)} %pad_clamp_fusion), kind=kCustom, calls=%fused_computation | custom fusion | bytes 262160 | tf_op jit(solution)/shard_map/jit(_take)/gather | solution.py:34
  15.1 0.1 copy_bitcast_fusion
  15.2 0.0 copy-start.1
  15.3 0.1 pad_select_fusion
  15.4 0.1 pad_select_fusion.7
  15.5 0.1 pad_select_fusion.6
  15.6 0.0 copy-start.2
  15.6 0.1 pad_select_fusion.5
  15.7 0.1 pad_select_fusion.4
  15.9 0.1 pad_select_fusion.3
  16.0 0.1 pad_select_fusion.2
  16.1 0.1 pad_select_fusion.1
  16.2 0.0 copy-done.1
  16.3 0.0 collective-permute-done.4
  16.3 0.0 copy-done.2
  16.3 1.6 %fusion.3 = f32[2,512,256]{2,1,0:T(8,128)S(1)} fusion(s32[2,512]{1,0:T(2,128)S(1)} %copy-done.2, f32[640,256]{1,0:T(8,128)S(1)} %constant_dynamic-update-slice_fusion), kind=kOutput, calls=%fused_computation.5 | convolution fusion | flops 1007288320 | bytes 1708032 | tf_op jit(solution)/shard_map/dot_general | solution.py:93
  17.9 1.0 %convolution_bitcast_fusion = f32[2,512,256]{2,1,0:T(8,128)S(1)} fusion(f32[2,512,256]{2,1,0:T(8,128)S(1)} %fusion.3, f32[2,512,512]{2,1,0:T(8,128)S(1)} %copy-done), kind=kOutput, calls=%fused_computation.7 | convolution fusion | flops 805306368 | bytes 4194304 | tf_op jit(solution)/shard_map/cij,cjb->cib/dot_general | solution.py:94
  18.9 0.9 %fusion.8 = f32[640,256]{1,0:T(8,128)S(1)} fusion(f32[2,512,256]{2,1,0:T(8,128)S(1)} %convolution_bitcast_fusion, s32[2,512]{1,0:T(2,128)S(1)} %copy-done.2), kind=kOutput, calls=%fused_computation.12 | convolution fusion | flops 1007288320 | bytes 1708032 | tf_op jit(solution)/shard_map/dot_general | solution.py:69
  19.8 0.4 convolution_multiply_fusion
  20.2 0.7 %convolution_add_fusion = f32[640,256]{1,0:T(8,128)S(1)} fusion(f32[640,256]{1,0:T(8,128)S(1)} %fusion.8, f32[64,640]{1,0:T(8,128)S(1)} %bitcast.43, f32[64,256]{1,0:T(8,128)S(1)} %convolution_multiply_fusion), kind=kOutput, calls=%fused_computation.13 | convolution fusion | flops 125992960 | bytes 1540096 | tf_op jit(solution)/shard_map/dot_general | solution.py:95
  21.0 4.3 %collective-permute-start.5 = (f32[256,256]{1,0:T(8,128)S(1)}, f32[256,256]{1,0:T(8,128)S(1)}, u32[]{:S(2)}, u32[]{:S(2)}) collective-permute-start(f32[256,256]{1,0:T(8,128)S(1)} %get-tuple-element.15), channel_id=1, source_target_pairs={{0,4},{4,8},{8,12},{12,16},{16,20},{20,24},{24,28},{1,5},{5,9},{9,... | collective-permute-start | bytes 786440 | tf_op jit(solution)/shard_map/ppermute | solution.py:16
  25.4 1.5 %collective-permute-start.6 = (f32[256,256]{1,0:T(8,128)S(1)}, f32[256,256]{1,0:T(8,128)S(1)}, u32[]{:S(2)}, u32[]{:S(2)}) collective-permute-start(f32[256,256]{1,0:T(8,128)S(1)} %get-tuple-element.16), channel_id=1, source_target_pairs={{4,0},{8,4},{12,8},{16,12},{20,16},{24,20},{28,24},{5,1},{9,5},{13... | collective-permute-start | bytes 786440 | tf_op jit(solution)/shard_map/ppermute | solution.py:21
  26.8 1.9 %fusion.1 = f32[2,512,640]{2,1,0:T(8,128)S(1)} fusion(f32[2,512,512]{2,1,0:T(8,128)S(1)} %copy-done, s32[2,512]{1,0:T(2,128)S(1)} %copy-done.2), kind=kOutput, calls=%fused_computation.3 | convolution fusion | flops 2013921280 | bytes 4722688 | tf_op jit(solution)/shard_map/cij,cjq->ciq/dot_general | solution.py:102
  28.8 1.6 %fusion.18 = f32[640,640]{1,0:T(8,128)S(1)} fusion(f32[64,640]{1,0:T(8,128)S(1)} %bitcast.44, f32[64]{0:T(128)S(1)} %reshape.123), kind=kOutput, calls=%fused_computation.26 | convolution fusion | flops 314613760 | bytes 1802496 | tf_op jit(solution)/shard_map/dot_general | solution.py:105
  30.4 2.3 %bitcast_add_fusion = f32[640,640]{1,0:T(8,128)S(1)} fusion(f32[640,640]{1,0:T(8,128)S(1)} %fusion.18, f32[2,512,640]{2,1,0:T(8,128)S(1)} %fusion.1, s32[2,512]{1,0:T(2,128)S(1)} %copy-done.2), kind=kOutput, calls=%fused_computation.6 | convolution fusion | flops 2517647360 | bytes 5902336 | tf_op jit(solution)/shard_map/dot_general | solution.py:69
  32.8 2.1 %collective-permute-done.5 = f32[256,256]{1,0:T(8,128)S(1)} collective-permute-done((f32[256,256]{1,0:T(8,128)S(1)}, f32[256,256]{1,0:T(8,128)S(1)}, u32[]{:S(2)}, u32[]{:S(2)}) %collective-permute-start.5) | collective-permute-done | bytes 262176 | tf_op jit(solution)/shard_map/ppermute | solution.py:16
  34.8 0.0 collective-permute-done.6
  34.8 0.2 multiply_select_fusion
  35.0 0.5 %fusion.11 = f32[256,256]{1,0:T(8,128)S(1)} fusion(f32[640,256]{1,0:T(8,128)S(1)} %multiply_select_fusion, f32[128,640]{1,0:T(8,128)S(1)} %get-tuple-element.14, f32[128,640]{1,0:T(8,128)S(1)} %get-tuple-element.13), kind=kOutput, calls=%fused_computation.17 | convolution fusion | flops 251822080 | bytes 1572864 | tf_op jit(solution)/shard_map/dot_general | solution.py:125
  35.6 4.4 %collective-permute-start.7 = (f32[128,256]{1,0:T(8,128)S(1)}, f32[128,256]{1,0:T(8,128)S(1)}, u32[]{:S(2)}, u32[]{:S(2)}) collective-permute-start(f32[128,256]{1,0:T(8,128)S(1)} %get-tuple-element.19), channel_id=1, source_target_pairs={{0,4},{4,8},{8,12},{12,16},{16,20},{20,24},{24,28},{1,5},{5,9},{9,... | collective-permute-start | bytes 393224 | tf_op jit(solution)/shard_map/ppermute | solution.py:16
  40.0 1.3 %collective-permute-start.8 = (f32[128,256]{1,0:T(8,128)S(1)}, f32[128,256]{1,0:T(8,128)S(1)}, u32[]{:S(2)}, u32[]{:S(2)}) collective-permute-start(f32[128,256]{1,0:T(8,128)S(1)} %get-tuple-element.20), channel_id=1, source_target_pairs={{4,0},{8,4},{12,8},{16,12},{20,16},{24,20},{28,24},{5,1},{9,5},{13... | collective-permute-start | bytes 393224 | tf_op jit(solution)/shard_map/ppermute | solution.py:21
  41.3 0.7 %fusion.9 = f32[384,256]{1,0:T(8,128)S(1)} fusion(f32[640,256]{1,0:T(8,128)S(1)} %multiply_select_fusion, f32[640,640]{1,0:T(8,128)S(1)} %bitcast_add_fusion), kind=kOutput, calls=%fused_computation.15 | convolution fusion | flops 377487360 | bytes 2031616 | tf_op jit(solution)/shard_map/dot_general | solution.py:129
  41.9 0.5 %collective-permute-done.7 = f32[128,256]{1,0:T(8,128)S(1)} collective-permute-done((f32[128,256]{1,0:T(8,128)S(1)}, f32[128,256]{1,0:T(8,128)S(1)}, u32[]{:S(2)}, u32[]{:S(2)}) %collective-permute-start.7) | collective-permute-done | bytes 131104 | tf_op jit(solution)/shard_map/ppermute | solution.py:16
  42.5 4.4 %collective-permute-done.8 = f32[128,256]{1,0:T(8,128)S(1)} collective-permute-done((f32[128,256]{1,0:T(8,128)S(1)}, f32[128,256]{1,0:T(8,128)S(1)}, u32[]{:S(2)}, u32[]{:S(2)}) %collective-permute-start.8) | collective-permute-done | bytes 131104 | tf_op jit(solution)/shard_map/ppermute | solution.py:21
  46.8 0.9 %fusion.17 = f32[384,256]{1,0:T(8,128)} fusion(f32[384,256]{1,0:T(8,128)S(1)} %copy-done.1, f32[640,256]{1,0:T(8,128)S(1)} %multiply_select_fusion, f32[128,256]{1,0:T(8,128)S(1)} %collective-permute-done.8, f32[384,256]{1,0:T(8,128)S(1)} %fusion.9, f32[128,256]{1,0:T(8,128)S(1)} %collective-permute-done.7), kind=kLoop, calls=%fused_computation.25 | loop fusion | flops 491520 | bytes 1835008 | tf_op jit(solution)/shard_map/sub | solution.py:137
  (16 shorter events, 0.2 us)
Async XLA Ops:
  0.0 17.9 %copy-start = (f32[2,512,512]{2,1,0:T(8,128)S(1)}, f32[2,512,512]{2,1,0:T(8,128)}, u32[]{:S(2)}) copy-start(f32[2,512,512]{2,1,0:T(8,128)} %param.8) | copy-start | bytes 6291460
  0.0 13.8 %collective-permute-start = (f32[4,16,128]{2,1,0:T(8,128)}, f32[4,16,128]{2,1,0:T(8,128)S(1)}, u32[]{:S(2)}, u32[]{:S(2)}) collective-permute-start(f32[4,16,128]{2,1,0:T(8,128)} %param.10), channel_id=1, source_target_pairs={{0,1},{1,2},{2,3},{3,0},{4,5},{5,6},{6,7},{7,4},{8,9},{9,10},{10,1... | collective-permute-start | bytes 98312 | tf_op jit(solution)/shard_map/ppermute | solution.py:30
  0.5 13.3 %collective-permute-start.2 = (f32[4,16,128]{2,1,0:T(8,128)}, f32[4,16,128]{2,1,0:T(8,128)S(1)}, u32[]{:S(2)}, u32[]{:S(2)}) collective-permute-start(f32[4,16,128]{2,1,0:T(8,128)} %param.10), channel_id=1, source_target_pairs={{0,3},{1,0},{2,1},{3,2},{4,7},{5,4},{6,5},{7,6},{8,11},{9,8},{10,9... | collective-permute-start | bytes 98312 | tf_op jit(solution)/shard_map/ppermute | solution.py:30
  2.4 11.4 %collective-permute-start.1 = (f32[4,16,128]{2,1,0:T(8,128)}, f32[4,16,128]{2,1,0:T(8,128)S(1)}, u32[]{:S(2)}, u32[]{:S(2)}) collective-permute-start(f32[4,16,128]{2,1,0:T(8,128)} %param.10), channel_id=1, source_target_pairs={{0,2},{1,3},{2,0},{3,1},{4,6},{5,7},{6,4},{7,5},{8,10},{9,11},{10,... | collective-permute-start | bytes 98312 | tf_op jit(solution)/shard_map/ppermute | solution.py:30
  5.7 10.6 %collective-permute-start.4 = (f32[128,256]{1,0:T(8,128)S(1)}, f32[128,256]{1,0:T(8,128)S(1)}, u32[]{:S(2)}, u32[]{:S(2)}) collective-permute-start(f32[128,256]{1,0:T(8,128)S(1)} %get-tuple-element.17), channel_id=1, source_target_pairs={{4,0},{8,4},{12,8},{16,12},{20,16},{24,20},{28,24},{5,1},{9,5},{13... | collective-permute-start | bytes 393224 | tf_op jit(solution)/shard_map/ppermute | solution.py:21
  7.0 9.2 %collective-permute-start.3 = (f32[128,256]{1,0:T(8,128)S(1)}, f32[128,256]{1,0:T(8,128)S(1)}, u32[]{:S(2)}, u32[]{:S(2)}) collective-permute-start(f32[128,256]{1,0:T(8,128)S(1)} %get-tuple-element.18), channel_id=1, source_target_pairs={{0,4},{4,8},{8,12},{12,16},{16,20},{20,24},{24,28},{1,5},{5,9},{9,... | collective-permute-start | bytes 393224 | tf_op jit(solution)/shard_map/ppermute | solution.py:16
  15.2 1.0 %copy-start.1 = (f32[384,256]{1,0:T(8,128)S(1)}, f32[384,256]{1,0:T(8,128)}, u32[]{:S(2)}) copy-start(f32[384,256]{1,0:T(8,128)} %param.7) | copy-start | bytes 1179652
  15.6 0.7 %copy-start.2 = (s32[2,512]{1,0:T(2,128)S(1)}, s32[2,512]{1,0:T(2,128)}, u32[]{:S(2)}) copy-start(s32[2,512]{1,0:T(2,128)} %param.9) | copy-start | bytes 12292
  21.0 13.8 %collective-permute-start.5 = (f32[256,256]{1,0:T(8,128)S(1)}, f32[256,256]{1,0:T(8,128)S(1)}, u32[]{:S(2)}, u32[]{:S(2)}) collective-permute-start(f32[256,256]{1,0:T(8,128)S(1)} %get-tuple-element.15), channel_id=1, source_target_pairs={{0,4},{4,8},{8,12},{12,16},{16,20},{20,24},{24,28},{1,5},{5,9},{9,... | collective-permute-start | bytes 786440 | tf_op jit(solution)/shard_map/ppermute | solution.py:16
  25.4 9.5 %collective-permute-start.6 = (f32[256,256]{1,0:T(8,128)S(1)}, f32[256,256]{1,0:T(8,128)S(1)}, u32[]{:S(2)}, u32[]{:S(2)}) collective-permute-start(f32[256,256]{1,0:T(8,128)S(1)} %get-tuple-element.16), channel_id=1, source_target_pairs={{4,0},{8,4},{12,8},{16,12},{20,16},{24,20},{28,24},{5,1},{9,5},{13... | collective-permute-start | bytes 786440 | tf_op jit(solution)/shard_map/ppermute | solution.py:21
  35.6 6.9 %collective-permute-start.7 = (f32[128,256]{1,0:T(8,128)S(1)}, f32[128,256]{1,0:T(8,128)S(1)}, u32[]{:S(2)}, u32[]{:S(2)}) collective-permute-start(f32[128,256]{1,0:T(8,128)S(1)} %get-tuple-element.19), channel_id=1, source_target_pairs={{0,4},{4,8},{8,12},{12,16},{16,20},{20,24},{24,28},{1,5},{5,9},{9,... | collective-permute-start | bytes 393224 | tf_op jit(solution)/shard_map/ppermute | solution.py:16
  40.0 6.9 %collective-permute-start.8 = (f32[128,256]{1,0:T(8,128)S(1)}, f32[128,256]{1,0:T(8,128)S(1)}, u32[]{:S(2)}, u32[]{:S(2)}) collective-permute-start(f32[128,256]{1,0:T(8,128)S(1)} %get-tuple-element.20), channel_id=1, source_target_pairs={{4,0},{8,4},{12,8},{16,12},{20,16},{24,20},{28,24},{5,1},{9,5},{13... | collective-permute-start | bytes 393224 | tf_op jit(solution)/shard_map/ppermute | solution.py:21

commit v13 on v12

--- a/solution.py
+++ b/solution.py
@@ -29,9 +29,14 @@
         pieces.append(
             lax.ppermute(piece, "band", [(i, (i + k) % count) for i in range(count)])
         )
-    stacked = jnp.stack(pieces)
-    order = (me - jnp.arange(count)) % count
-    ordered = jnp.take(stacked, order, axis=0)
+    ordered = []
+    for src in range(count):
+        shift = (me - src) % count
+        block = jnp.zeros_like(piece)
+        for k in range(count):
+            block = block + jnp.where(shift == k, pieces[k], 0.0)
+        ordered.append(block)
+    ordered = jnp.stack(ordered)
     slots, channels, width = piece.shape
     return ordered.transpose(1, 2, 0, 3).reshape(slots, channels, count * width)
 

time: 48.1 us -> 48.6 us (1.010)
  waiting for transfers between devices: 7 us -> 8.12 us
  local copies, waits for them, and re-layouts: 1.85 us -> 1.3 us
    ppermute x3, waiting for transfers between devices: 2.62 us -> 3.55 us  [from_left(): return lax.ppermute(x, axis, [(i, i + 1) for i in range(count - 1)])]
    gather x1 -> x0, local copies, waits for them, and re-layouts: 0.56 us -> none  [gather_band(): ordered = jnp.take(stacked, order, axis=0)]
  transfers between devices with their start and end apart: 9 -> 9, of which waited for: 3 -> 3; matrix products, arithmetic and copies ran while one was open for 24% -> 22% of each run, Pallas kernels for 0% -> 0%
where the time goes in v13:
time: 48.6 us; the launch traced here: 48.2 us
  starting transfers between devices  22 us (45%)
  matrix products  11.6 us (24%)
  waiting for transfers between devices  8.12 us (17%)
  other arithmetic  4.16 us (9%)
  local copies, waits for them, and re-layouts  1.3 us (3%)
  between operations  0.98 us (2%)
    ppermute x3, starting transfers between devices, from_left(): return lax.ppermute(x, axis, [(i, i + 1) for i in range(count - 1)])  13.3 us
    ppermute x3, starting transfers between devices, gather_band(): lax.ppermute(piece, 'band', [(i, (i + k) % count) for i in range(count)])  4.68 us
    ppermute x3, waiting for transfers between devices, from_right(): return lax.ppermute(x, axis, [(i + 1, i) for i in range(count - 1)])  4.56 us
    ppermute x3, starting transfers between devices, from_right(): return lax.ppermute(x, axis, [(i + 1, i) for i in range(count - 1)])  4.06 us
    ppermute x3, waiting for transfers between devices, from_left(): return lax.ppermute(x, axis, [(i, i + 1) for i in range(count - 1)])  3.55 us
    dot_general x2, matrix products, scatter_rows(): lax.dot_general(onehot, values, (((0,), (0,)), ((), ())), precision=lax.P...  3.17 us
    dot_general x1, matrix products, on_device(): jnp.einsum('cij,cjq->ciq', matrices, onehot.reshape(cells, nodes, ext), p...  1.95 us
    dot_general x1, matrix products, on_device(): jnp.dot((placed_late * weights_late[:, None]).T, placed_late, precision=h...  1.57 us
  transfers between devices with their start and end apart: 9, of which 3 were waited for; matrix products, arithmetic and copies ran while one was open for 22% of the time, Pallas kernels for 0%

profile of v13, /device:TPU:0, one launch (start us, length us, event | category | flops | bytes accessed | tf_op | source)
XLA Modules:
  0.0 48.2 jit_solution(10678450990570873701)
XLA Ops:
  0.0 0.0 copy-start
  0.0 2.9 %collective-permute-start.1 = (f32[4,16,128]{2,1,0:T(8,128)}, f32[4,16,128]{2,1,0:T(8,128)S(1)}, u32[]{:S(2)}, u32[]{:S(2)}) collective-permute-start(f32[4,16,128]{2,1,0:T(8,128)} %param.10), channel_id=1, source_target_pairs={{0,2},{1,3},{2,0},{3,1},{4,6},{5,7},{6,4},{7,5},{8,10},{9,11},{10,... | collective-permute-start | bytes 98312 | tf_op jit(solution)/shard_map/ppermute | solution.py:30
  2.9 0.0 collective-permute-start
  2.9 1.7 %collective-permute-start.2 = (f32[4,16,128]{2,1,0:T(8,128)}, f32[4,16,128]{2,1,0:T(8,128)S(1)}, u32[]{:S(2)}, u32[]{:S(2)}) collective-permute-start(f32[4,16,128]{2,1,0:T(8,128)} %param.10), channel_id=1, source_target_pairs={{0,3},{1,0},{2,1},{3,2},{4,7},{5,4},{6,5},{7,6},{8,11},{9,8},{10,9... | collective-permute-start | bytes 98312 | tf_op jit(solution)/shard_map/ppermute | solution.py:30
  4.7 1.0 %fusion.27 = (f32[128,256]{1,0:T(8,128)S(1)}, f32[128,256]{1,0:T(8,128)S(1)}) fusion(f32[384,256]{1,0:T(8,128)} %param.7), kind=kLoop, calls=%fused_computation.65 | loop fusion | bytes 524288 | tf_op jit(solution)/shard_map/slice | solution.py:89
  5.7 1.3 %collective-permute-start.4 = (f32[128,256]{1,0:T(8,128)S(1)}, f32[128,256]{1,0:T(8,128)S(1)}, u32[]{:S(2)}, u32[]{:S(2)}) collective-permute-start(f32[128,256]{1,0:T(8,128)S(1)} %get-tuple-element.17), channel_id=1, source_target_pairs={{4,0},{8,4},{12,8},{16,12},{20,16},{24,20},{28,24},{5,1},{9,5},{13... | collective-permute-start | bytes 393224 | tf_op jit(solution)/shard_map/ppermute | solution.py:21
  7.0 4.6 %collective-permute-start.3 = (f32[128,256]{1,0:T(8,128)S(1)}, f32[128,256]{1,0:T(8,128)S(1)}, u32[]{:S(2)}, u32[]{:S(2)}) collective-permute-start(f32[128,256]{1,0:T(8,128)S(1)} %get-tuple-element.18), channel_id=1, source_target_pairs={{0,4},{4,8},{8,12},{12,16},{16,20},{20,24},{24,28},{1,5},{5,9},{9,... | collective-permute-start | bytes 393224 | tf_op jit(solution)/shard_map/ppermute | solution.py:16
  12.2 0.7 %and_compare_fusion.7 = (pred[4]{0:T(512)(128)(4,1)S(1)}, pred[4]{0:T(512)(128)(4,1)S(1)}, pred[4]{0:T(512)(128)(4,1)S(1)}, pred[4]{0:T(512)(128)(4,1)S(1)}, pre...) fusion(s32[4]{0:T(128)} %param.12), kind=kLoop, calls=%fused_computation.60 | loop fusion | flops 100 | bytes 48 | tf_op jit(solution)/shard_map/eq | solution.py:50
  12.9 0.8 %broadcast_multiply_fusion = f32[4,16]{1,0:T(4,128)S(1)} fusion(f32[4,16]{1,0:T(4,128)} %param.11, f32[4]{0:T(128)S(1)} %compare_convert_fusion), kind=kLoop, calls=%fused_computation.52 | loop fusion | flops 64 | bytes 528 | tf_op jit(solution)/shard_map/mul | solution.py:62
  13.6 0.1 reshape.69
  13.7 0.0 collective-permute-done.1
  13.7 0.0 collective-permute-done
  13.7 0.0 collective-permute-done.2
  13.8 0.8 %add_bitcast_fusion.3 = (f32[1,4,16,128]{3,2,1,0:T(8,128)S(1)}, f32[1,4,16,128]{3,2,1,0:T(8,128)S(1)}, f32[1,4,16,128]{3,2,1,0:T(8,128)S(1)}) fusion(f32[4,16,128]{2,1,0:T(8,128)S(1)} %collective-permute-done.2, f32[4,16,128]{2,1,0:T(8,128)S(1)} %collective-permute-done.1, f32[4,16,128]{2,1,0:T(8,128)S(1)} %collective-permute-done, f32[4,16,128]{2,1,0:T(8,128)} %param.10, ...), kind=kLoop, calls=%fused_computation.42 | loop fusion | flops 172032 | bytes 229388 | tf_op jit(solution)/shard_map/stack | solution.py:39
  14.6 0.0 copy-start.1
  14.6 0.1 pad_select_fusion
  14.7 0.1 pad_select_fusion.7
  14.9 0.1 pad_select_fusion.6
  15.0 0.0 copy-start.2
  15.0 0.1 pad_select_fusion.5
  15.1 0.1 pad_select_fusion.4
  15.2 0.1 pad_select_fusion.3
  15.3 0.1 pad_select_fusion.2
  15.5 0.1 pad_select_fusion.1
  15.6 0.0 collective-permute-done.3
  15.6 0.0 copy-done.1
  15.6 0.0 collective-permute-done.4
  15.7 0.0 copy-done.2
  15.7 1.6 %fusion.3 = f32[2,512,256]{2,1,0:T(8,128)S(1)} fusion(s32[2,512]{1,0:T(2,128)S(1)} %copy-done.2, f32[640,256]{1,0:T(8,128)S(1)} %constant_dynamic-update-slice_fusion), kind=kOutput, calls=%fused_computation.4 | convolution fusion | flops 1007288320 | bytes 1708032 | tf_op jit(solution)/shard_map/dot_general | solution.py:98
  17.3 1.0 %convolution_bitcast_fusion = f32[2,512,256]{2,1,0:T(8,128)S(1)} fusion(f32[2,512,256]{2,1,0:T(8,128)S(1)} %fusion.3, f32[2,512,512]{2,1,0:T(8,128)S(1)} %copy-done), kind=kOutput, calls=%fused_computation.6 | convolution fusion | flops 805306368 | bytes 4194304 | tf_op jit(solution)/shard_map/cij,cjb->cib/dot_general | solution.py:99
  18.3 0.9 %fusion.8 = f32[640,256]{1,0:T(8,128)S(1)} fusion(f32[2,512,256]{2,1,0:T(8,128)S(1)} %convolution_bitcast_fusion, s32[2,512]{1,0:T(2,128)S(1)} %copy-done.2), kind=kOutput, calls=%fused_computation.11 | convolution fusion | flops 1007288320 | bytes 1708032 | tf_op jit(solution)/shard_map/dot_general | solution.py:74
  19.2 0.4 convolution_multiply_fusion
  19.6 0.7 %convolution_add_fusion = f32[640,256]{1,0:T(8,128)S(1)} fusion(f32[640,256]{1,0:T(8,128)S(1)} %fusion.8, f32[64,640]{1,0:T(8,128)S(1)} %bitcast.45, f32[64,256]{1,0:T(8,128)S(1)} %convolution_multiply_fusion), kind=kOutput, calls=%fused_computation.12 | convolution fusion | flops 125992960 | bytes 1540096 | tf_op jit(solution)/shard_map/dot_general | solution.py:100
  20.4 4.3 %collective-permute-start.5 = (f32[256,256]{1,0:T(8,128)S(1)}, f32[256,256]{1,0:T(8,128)S(1)}, u32[]{:S(2)}, u32[]{:S(2)}) collective-permute-start(f32[256,256]{1,0:T(8,128)S(1)} %get-tuple-element.15), channel_id=1, source_target_pairs={{0,4},{4,8},{8,12},{12,16},{16,20},{20,24},{24,28},{1,5},{5,9},{9,... | collective-permute-start | bytes 786440 | tf_op jit(solution)/shard_map/ppermute | solution.py:16
  24.7 1.5 %collective-permute-start.6 = (f32[256,256]{1,0:T(8,128)S(1)}, f32[256,256]{1,0:T(8,128)S(1)}, u32[]{:S(2)}, u32[]{:S(2)}) collective-permute-start(f32[256,256]{1,0:T(8,128)S(1)} %get-tuple-element.16), channel_id=1, source_target_pairs={{4,0},{8,4},{12,8},{16,12},{20,16},{24,20},{28,24},{5,1},{9,5},{13... | collective-permute-start | bytes 786440 | tf_op jit(solution)/shard_map/ppermute | solution.py:21
  26.2 1.9 %fusion.1 = f32[2,512,640]{2,1,0:T(8,128)S(1)} fusion(f32[2,512,512]{2,1,0:T(8,128)S(1)} %copy-done, s32[2,512]{1,0:T(2,128)S(1)} %copy-done.2), kind=kOutput, calls=%fused_computation.2 | convolution fusion | flops 2013921280 | bytes 4722688 | tf_op jit(solution)/shard_map/cij,cjq->ciq/dot_general | solution.py:107
  28.2 1.6 %fusion.18 = f32[640,640]{1,0:T(8,128)S(1)} fusion(f32[64,640]{1,0:T(8,128)S(1)} %bitcast.46, f32[64]{0:T(128)S(1)} %reshape.69), kind=kOutput, calls=%fused_computation.25 | convolution fusion | flops 314613760 | bytes 1802496 | tf_op jit(solution)/shard_map/dot_general | solution.py:110
  29.7 2.3 %bitcast_add_fusion = f32[640,640]{1,0:T(8,128)S(1)} fusion(f32[640,640]{1,0:T(8,128)S(1)} %fusion.18, f32[2,512,640]{2,1,0:T(8,128)S(1)} %fusion.1, s32[2,512]{1,0:T(2,128)S(1)} %copy-done.2), kind=kOutput, calls=%fused_computation.5 | convolution fusion | flops 2517647360 | bytes 5902336 | tf_op jit(solution)/shard_map/dot_general | solution.py:74
  32.1 3.0 %collective-permute-done.5 = f32[256,256]{1,0:T(8,128)S(1)} collective-permute-done((f32[256,256]{1,0:T(8,128)S(1)}, f32[256,256]{1,0:T(8,128)S(1)}, u32[]{:S(2)}, u32[]{:S(2)}) %collective-permute-start.5) | collective-permute-done | bytes 262176 | tf_op jit(solution)/shard_map/ppermute | solution.py:16
  35.1 0.0 collective-permute-done.6
  35.1 0.2 multiply_select_fusion
  35.3 0.5 %fusion.11 = f32[256,256]{1,0:T(8,128)S(1)} fusion(f32[640,256]{1,0:T(8,128)S(1)} %multiply_select_fusion, f32[128,640]{1,0:T(8,128)S(1)} %get-tuple-element.14, f32[128,640]{1,0:T(8,128)S(1)} %get-tuple-element.13), kind=kOutput, calls=%fused_computation.16 | convolution fusion | flops 251822080 | bytes 1572864 | tf_op jit(solution)/shard_map/dot_general | solution.py:130
  35.9 4.4 %collective-permute-start.7 = (f32[128,256]{1,0:T(8,128)S(1)}, f32[128,256]{1,0:T(8,128)S(1)}, u32[]{:S(2)}, u32[]{:S(2)}) collective-permute-start(f32[128,256]{1,0:T(8,128)S(1)} %get-tuple-element.19), channel_id=1, source_target_pairs={{0,4},{4,8},{8,12},{12,16},{16,20},{20,24},{24,28},{1,5},{5,9},{9,... | collective-permute-start | bytes 393224 | tf_op jit(solution)/shard_map/ppermute | solution.py:16
  40.3 1.3 %collective-permute-start.8 = (f32[128,256]{1,0:T(8,128)S(1)}, f32[128,256]{1,0:T(8,128)S(1)}, u32[]{:S(2)}, u32[]{:S(2)}) collective-permute-start(f32[128,256]{1,0:T(8,128)S(1)} %get-tuple-element.20), channel_id=1, source_target_pairs={{4,0},{8,4},{12,8},{16,12},{20,16},{24,20},{28,24},{5,1},{9,5},{13... | collective-permute-start | bytes 393224 | tf_op jit(solution)/shard_map/ppermute | solution.py:21
  41.6 0.7 %fusion.9 = f32[384,256]{1,0:T(8,128)S(1)} fusion(f32[640,256]{1,0:T(8,128)S(1)} %multiply_select_fusion, f32[640,640]{1,0:T(8,128)S(1)} %bitcast_add_fusion), kind=kOutput, calls=%fused_computation.14 | convolution fusion | flops 377487360 | bytes 2031616 | tf_op jit(solution)/shard_map/dot_general | solution.py:134
  42.2 0.5 %collective-permute-done.7 = f32[128,256]{1,0:T(8,128)S(1)} collective-permute-done((f32[128,256]{1,0:T(8,128)S(1)}, f32[128,256]{1,0:T(8,128)S(1)}, u32[]{:S(2)}, u32[]{:S(2)}) %collective-permute-start.7) | collective-permute-done | bytes 131104 | tf_op jit(solution)/shard_map/ppermute | solution.py:16
  42.8 4.6 %collective-permute-done.8 = f32[128,256]{1,0:T(8,128)S(1)} collective-permute-done((f32[128,256]{1,0:T(8,128)S(1)}, f32[128,256]{1,0:T(8,128)S(1)}, u32[]{:S(2)}, u32[]{:S(2)}) %collective-permute-start.8) | collective-permute-done | bytes 131104 | tf_op jit(solution)/shard_map/ppermute | solution.py:21
  47.3 0.9 %fusion.17 = f32[384,256]{1,0:T(8,128)} fusion(f32[384,256]{1,0:T(8,128)S(1)} %copy-done.1, f32[640,256]{1,0:T(8,128)S(1)} %multiply_select_fusion, f32[128,256]{1,0:T(8,128)S(1)} %collective-permute-done.8, f32[384,256]{1,0:T(8,128)S(1)} %fusion.9, f32[128,256]{1,0:T(8,128)S(1)} %collective-permute-done.7), kind=kLoop, calls=%fused_computation.24 | loop fusion | flops 491520 | bytes 1835008 | tf_op jit(solution)/shard_map/sub | solution.py:142
  (13 shorter events, 0.2 us)
Async XLA Ops:
  0.0 17.3 %copy-start = (f32[2,512,512]{2,1,0:T(8,128)S(1)}, f32[2,512,512]{2,1,0:T(8,128)}, u32[]{:S(2)}) copy-start(f32[2,512,512]{2,1,0:T(8,128)} %param.8) | copy-start | bytes 6291460
  0.0 13.7 %collective-permute-start.1 = (f32[4,16,128]{2,1,0:T(8,128)}, f32[4,16,128]{2,1,0:T(8,128)S(1)}, u32[]{:S(2)}, u32[]{:S(2)}) collective-permute-start(f32[4,16,128]{2,1,0:T(8,128)} %param.10), channel_id=1, source_target_pairs={{0,2},{1,3},{2,0},{3,1},{4,6},{5,7},{6,4},{7,5},{8,10},{9,11},{10,... | collective-permute-start | bytes 98312 | tf_op jit(solution)/shard_map/ppermute | solution.py:30
  2.9 10.8 %collective-permute-start = (f32[4,16,128]{2,1,0:T(8,128)}, f32[4,16,128]{2,1,0:T(8,128)S(1)}, u32[]{:S(2)}, u32[]{:S(2)}) collective-permute-start(f32[4,16,128]{2,1,0:T(8,128)} %param.10), channel_id=1, source_target_pairs={{0,1},{1,2},{2,3},{3,0},{4,5},{5,6},{6,7},{7,4},{8,9},{9,10},{10,1... | collective-permute-start | bytes 98312 | tf_op jit(solution)/shard_map/ppermute | solution.py:30
  2.9 10.8 %collective-permute-start.2 = (f32[4,16,128]{2,1,0:T(8,128)}, f32[4,16,128]{2,1,0:T(8,128)S(1)}, u32[]{:S(2)}, u32[]{:S(2)}) collective-permute-start(f32[4,16,128]{2,1,0:T(8,128)} %param.10), channel_id=1, source_target_pairs={{0,3},{1,0},{2,1},{3,2},{4,7},{5,4},{6,5},{7,6},{8,11},{9,8},{10,9... | collective-permute-start | bytes 98312 | tf_op jit(solution)/shard_map/ppermute | solution.py:30
  5.7 10.0 %collective-permute-start.4 = (f32[128,256]{1,0:T(8,128)S(1)}, f32[128,256]{1,0:T(8,128)S(1)}, u32[]{:S(2)}, u32[]{:S(2)}) collective-permute-start(f32[128,256]{1,0:T(8,128)S(1)} %get-tuple-element.17), channel_id=1, source_target_pairs={{4,0},{8,4},{12,8},{16,12},{20,16},{24,20},{28,24},{5,1},{9,5},{13... | collective-permute-start | bytes 393224 | tf_op jit(solution)/shard_map/ppermute | solution.py:21
  7.0 8.6 %collective-permute-start.3 = (f32[128,256]{1,0:T(8,128)S(1)}, f32[128,256]{1,0:T(8,128)S(1)}, u32[]{:S(2)}, u32[]{:S(2)}) collective-permute-start(f32[128,256]{1,0:T(8,128)S(1)} %get-tuple-element.18), channel_id=1, source_target_pairs={{0,4},{4,8},{8,12},{12,16},{16,20},{20,24},{24,28},{1,5},{5,9},{9,... | collective-permute-start | bytes 393224 | tf_op jit(solution)/shard_map/ppermute | solution.py:16
  14.6 1.0 %copy-start.1 = (f32[384,256]{1,0:T(8,128)S(1)}, f32[384,256]{1,0:T(8,128)}, u32[]{:S(2)}) copy-start(f32[384,256]{1,0:T(8,128)} %param.7) | copy-start | bytes 1179652
  15.0 0.7 %copy-start.2 = (s32[2,512]{1,0:T(2,128)S(1)}, s32[2,512]{1,0:T(2,128)}, u32[]{:S(2)}) copy-start(s32[2,512]{1,0:T(2,128)} %param.9) | copy-start | bytes 12292
  20.4 14.7 %collective-permute-start.5 = (f32[256,256]{1,0:T(8,128)S(1)}, f32[256,256]{1,0:T(8,128)S(1)}, u32[]{:S(2)}, u32[]{:S(2)}) collective-permute-start(f32[256,256]{1,0:T(8,128)S(1)} %get-tuple-element.15), channel_id=1, source_target_pairs={{0,4},{4,8},{8,12},{12,16},{16,20},{20,24},{24,28},{1,5},{5,9},{9,... | collective-permute-start | bytes 786440 | tf_op jit(solution)/shard_map/ppermute | solution.py:16
  24.7 10.4 %collective-permute-start.6 = (f32[256,256]{1,0:T(8,128)S(1)}, f32[256,256]{1,0:T(8,128)S(1)}, u32[]{:S(2)}, u32[]{:S(2)}) collective-permute-start(f32[256,256]{1,0:T(8,128)S(1)} %get-tuple-element.16), channel_id=1, source_target_pairs={{4,0},{8,4},{12,8},{16,12},{20,16},{24,20},{28,24},{5,1},{9,5},{13... | collective-permute-start | bytes 786440 | tf_op jit(solution)/shard_map/ppermute | solution.py:21
  35.9 6.9 %collective-permute-start.7 = (f32[128,256]{1,0:T(8,128)S(1)}, f32[128,256]{1,0:T(8,128)S(1)}, u32[]{:S(2)}, u32[]{:S(2)}) collective-permute-start(f32[128,256]{1,0:T(8,128)S(1)} %get-tuple-element.19), channel_id=1, source_target_pairs={{0,4},{4,8},{8,12},{12,16},{16,20},{20,24},{24,28},{1,5},{5,9},{9,... | collective-permute-start | bytes 393224 | tf_op jit(solution)/shard_map/ppermute | solution.py:16
  40.3 7.1 %collective-permute-start.8 = (f32[128,256]{1,0:T(8,128)S(1)}, f32[128,256]{1,0:T(8,128)S(1)}, u32[]{:S(2)}, u32[]{:S(2)}) collective-permute-start(f32[128,256]{1,0:T(8,128)S(1)} %get-tuple-element.20), channel_id=1, source_target_pairs={{4,0},{8,4},{12,8},{16,12},{20,16},{24,20},{28,24},{5,1},{9,5},{13... | collective-permute-start | bytes 393224 | tf_op jit(solution)/shard_map/ppermute | solution.py:21

commit v14 on v13

--- a/solution.py
+++ b/solution.py
@@ -58,9 +58,13 @@
         [projector_full, jnp.zeros((slots, channels, ext - support), projector_full.dtype)], axis=-1
     )
     placed = shift_right(padded, first, (ext - support).bit_length())
+    return placed.reshape(slots * channels, ext), atom_weights(coupling, atom_count)
+
+
+def atom_weights(coupling, atom_count):
+    slots, channels = coupling.shape
     live = jnp.arange(slots, dtype=jnp.int32)[:, None] < atom_count.astype(jnp.int32)[None, :]
-    weights = coupling * live.astype(jnp.float32)
-    return placed.reshape(slots * channels, ext), weights.reshape(slots * channels)
+    return (coupling * live.astype(jnp.float32)).reshape(slots * channels)
 
 
 def cell_rows(connectivity, ext):
@@ -101,9 +105,10 @@
         placed.T, coefficients, precision=highest
     )
 
-    matrices, placed_late, weights_late, first = lax.optimization_barrier(
-        (cell_matrix, placed, weights, first)
+    matrices, placed_late, coupling_late, count_late, first = lax.optimization_barrier(
+        (cell_matrix, placed, coupling, atom_count, first)
     )
+    weights_late = atom_weights(coupling_late, count_late)
     moved = jnp.einsum(
         "cij,cjq->ciq", matrices, onehot.reshape(cells, nodes, ext), precision=high
     )

time: 48.6 us -> 50.4 us (1.037)
  local copies, waits for them, and re-layouts: 1.3 us -> 2.91 us
    unnamed x8 -> x14, local copies, waits for them, and re-layouts: 0.09 us -> 0.97 us
    slice x1, local copies, waits for them, and re-layouts: 0.99 us -> 1.64 us  [on_device(): high = from_right(wavefunctions[:g], 'dom')]
  transfers between devices with their start and end apart: 9 -> 9, of which waited for: 3 -> 3; matrix products, arithmetic and copies ran while one was open for 22% -> 25% of each run, Pallas kernels for 0% -> 0%
where the time goes in v14:
time: 50.4 us; the launch traced here: 50 us
  starting transfers between devices  22 us (44%)
  matrix products  11.6 us (23%)
  waiting for transfers between devices  8.21 us (16%)
  other arithmetic  4.23 us (8%)
  local copies, waits for them, and re-layouts  2.91 us (6%)
  between operations  1.02 us (2%)
    ppermute x3, starting transfers between devices, from_left(): return lax.ppermute(x, axis, [(i, i + 1) for i in range(count - 1)])  13.3 us
    ppermute x3, starting transfers between devices, gather_band(): lax.ppermute(piece, 'band', [(i, (i + k) % count) for i in range(count)])  4.68 us
    ppermute x3, waiting for transfers between devices, from_right(): return lax.ppermute(x, axis, [(i + 1, i) for i in range(count - 1)])  4.65 us
    ppermute x3, starting transfers between devices, from_right(): return lax.ppermute(x, axis, [(i + 1, i) for i in range(count - 1)])  4.04 us
    ppermute x3, waiting for transfers between devices, from_left(): return lax.ppermute(x, axis, [(i, i + 1) for i in range(count - 1)])  3.55 us
    dot_general x2, matrix products, scatter_rows(): lax.dot_general(onehot, values, (((0,), (0,)), ((), ())), precision=lax.P...  3.16 us
    dot_general x1, matrix products, on_device(): jnp.einsum('cij,cjq->ciq', matrices, onehot.reshape(cells, nodes, ext), p...  1.95 us
    slice x1, local copies, waits for them, and re-layouts, on_device(): high = from_right(wavefunctions[:g], 'dom')  1.64 us
  transfers between devices with their start and end apart: 9, of which 3 were waited for; matrix products, arithmetic and copies ran while one was open for 25% of the time, Pallas kernels for 0%

profile of v14, /device:TPU:0, one launch (start us, length us, event | category | flops | bytes accessed | tf_op | source)
XLA Modules:
  0.0 50.0 jit_solution(3620014866363387781)
XLA Ops:
  0.0 2.9 %collective-permute-start.1 = (f32[4,16,128]{2,1,0:T(8,128)}, f32[4,16,128]{2,1,0:T(8,128)S(1)}, u32[]{:S(2)}, u32[]{:S(2)}) collective-permute-start(f32[4,16,128]{2,1,0:T(8,128)} %param.10), channel_id=1, source_target_pairs={{0,2},{1,3},{2,0},{3,1},{4,6},{5,7},{6,4},{7,5},{8,10},{9,11},{10,... | collective-permute-start | bytes 98312 | tf_op jit(solution)/shard_map/ppermute | solution.py:30
  2.9 0.0 collective-permute-start
  2.9 1.7 %collective-permute-start.2 = (f32[4,16,128]{2,1,0:T(8,128)}, f32[4,16,128]{2,1,0:T(8,128)S(1)}, u32[]{:S(2)}, u32[]{:S(2)}) collective-permute-start(f32[4,16,128]{2,1,0:T(8,128)} %param.10), channel_id=1, source_target_pairs={{0,3},{1,0},{2,1},{3,2},{4,7},{5,4},{6,5},{7,6},{8,11},{9,8},{10,9... | collective-permute-start | bytes 98312 | tf_op jit(solution)/shard_map/ppermute | solution.py:30
  4.7 1.6 %fusion.27 = (f32[128,256]{1,0:T(8,128)}, f32[128,256]{1,0:T(8,128)S(1)}) fusion(f32[384,256]{1,0:T(8,128)} %param.7), kind=kLoop, calls=%fused_computation.67 | loop fusion | bytes 524288 | tf_op jit(solution)/shard_map/slice | solution.py:93
  6.3 1.3 %collective-permute-start.4 = (f32[128,256]{1,0:T(8,128)}, f32[128,256]{1,0:T(8,128)S(1)}, u32[]{:S(2)}, u32[]{:S(2)}) collective-permute-start(f32[128,256]{1,0:T(8,128)} %get-tuple-element.19), channel_id=1, source_target_pairs={{4,0},{8,4},{12,8},{16,12},{20,16},{24,20},{28,24},{5,1},{9,5},{13... | collective-permute-start | bytes 393224 | tf_op jit(solution)/shard_map/ppermute | solution.py:21
  7.6 5.2 %collective-permute-start.3 = (f32[128,256]{1,0:T(8,128)S(1)}, f32[128,256]{1,0:T(8,128)}, u32[]{:S(2)}, u32[]{:S(2)}) collective-permute-start(f32[128,256]{1,0:T(8,128)S(1)} %get-tuple-element.20), channel_id=1, source_target_pairs={{0,4},{4,8},{8,12},{12,16},{16,20},{20,24},{24,28},{1,5},{5,9},{9,... | collective-permute-start | bytes 393224 | tf_op jit(solution)/shard_map/ppermute | solution.py:16
  13.5 0.7 %and_compare_fusion.7 = (pred[4]{0:T(512)(128)(4,1)S(1)}, pred[4]{0:T(512)(128)(4,1)S(1)}, pred[4]{0:T(512)(128)(4,1)S(1)}, pred[4]{0:T(512)(128)(4,1)S(1)}, pre...) fusion(s32[4]{0:T(128)} %param.12), kind=kLoop, calls=%fused_computation.62 | loop fusion | flops 100 | bytes 48 | tf_op jit(solution)/shard_map/eq | solution.py:50
  14.2 0.8 %broadcast_multiply_fusion.1 = f32[4,16]{1,0:T(4,128)S(1)} fusion(f32[4,16]{1,0:T(4,128)} %param.11, f32[4]{0:T(128)S(1)} %compare_convert_fusion.1), kind=kLoop, calls=%fused_computation.54 | loop fusion | flops 64 | bytes 528 | tf_op jit(solution)/shard_map/mul | solution.py:67
  14.9 0.1 mul.51
  15.0 0.0 collective-permute-done.1
  15.0 0.0 collective-permute-done
  15.0 0.0 collective-permute-done.2
  15.1 0.8 %add_bitcast_fusion.3 = (f32[1,4,16,128]{3,2,1,0:T(8,128)S(1)}, f32[1,4,16,128]{3,2,1,0:T(8,128)S(1)}, f32[1,4,16,128]{3,2,1,0:T(8,128)S(1)}) fusion(f32[4,16,128]{2,1,0:T(8,128)S(1)} %collective-permute-done.2, f32[4,16,128]{2,1,0:T(8,128)S(1)} %collective-permute-done.1, f32[4,16,128]{2,1,0:T(8,128)S(1)} %collective-permute-done, f32[4,16,128]{2,1,0:T(8,128)} %param.10, ...), kind=kLoop, calls=%fused_computation.42 | loop fusion | flops 172032 | bytes 229388 | tf_op jit(solution)/shard_map/stack | solution.py:39
  15.9 0.0 copy-start.3
  15.9 0.1 pad_select_fusion
  16.0 0.1 pad_select_fusion.7
  16.1 0.1 pad_select_fusion.6
  16.3 0.0 copy-start.5
  16.3 0.1 pad_select_fusion.5
  16.4 0.1 pad_select_fusion.4
  16.5 0.1 pad_select_fusion.3
  16.6 0.1 pad_select_fusion.2
  16.8 0.1 pad_select_fusion.1
  16.9 0.9 %constant_dynamic-update-slice_fusion.2 = f32[640,256]{1,0:T(8,128)S(1)} fusion(f32[128,256]{1,0:T(8,128)} %collective-permute-done.3), kind=kLoop, calls=%fused_computation.45 | loop fusion | bytes 262144
  17.8 0.0 collective-permute-done.4
  17.9 1.6 %fusion.3 = f32[2,512,256]{2,1,0:T(8,128)S(1)} fusion(s32[2,512]{1,0:T(2,128)S(1)} %copy-done.5, f32[640,256]{1,0:T(8,128)S(1)} %constant_dynamic-update-slice_fusion), kind=kOutput, calls=%fused_computation.4 | convolution fusion | flops 1007288320 | bytes 1708032 | tf_op jit(solution)/shard_map/dot_general | solution.py:102
  19.4 1.0 %convolution_bitcast_fusion = f32[2,512,256]{2,1,0:T(8,128)S(1)} fusion(f32[2,512,256]{2,1,0:T(8,128)S(1)} %fusion.3, f32[2,512,512]{2,1,0:T(8,128)S(1)} %copy-done), kind=kOutput, calls=%fused_computation.6 | convolution fusion | flops 805306368 | bytes 4194304 | tf_op jit(solution)/shard_map/cij,cjb->cib/dot_general | solution.py:103
  20.5 0.0 copy-start.4
  20.5 0.8 %fusion.8 = f32[640,256]{1,0:T(8,128)S(1)} fusion(f32[2,512,256]{2,1,0:T(8,128)S(1)} %convolution_bitcast_fusion, s32[2,512]{1,0:T(2,128)S(1)} %copy-done.5), kind=kOutput, calls=%fused_computation.11 | convolution fusion | flops 1007288320 | bytes 1708032 | tf_op jit(solution)/shard_map/dot_general | solution.py:78
  21.3 0.4 convolution_multiply_fusion
  21.8 0.7 %convolution_add_fusion = f32[640,256]{1,0:T(8,128)S(1)} fusion(f32[640,256]{1,0:T(8,128)S(1)} %fusion.8, f32[64,640]{1,0:T(8,128)S(1)} %bitcast.47, f32[64,256]{1,0:T(8,128)S(1)} %convolution_multiply_fusion), kind=kOutput, calls=%fused_computation.12 | convolution fusion | flops 125992960 | bytes 1540096 | tf_op jit(solution)/shard_map/dot_general | solution.py:104
  22.5 0.1 broadcast_multiply_fusion
  22.6 0.1 mul.56
  22.7 3.7 %collective-permute-start.5 = (f32[256,256]{1,0:T(8,128)S(1)}, f32[256,256]{1,0:T(8,128)S(1)}, u32[]{:S(2)}, u32[]{:S(2)}) collective-permute-start(f32[256,256]{1,0:T(8,128)S(1)} %get-tuple-element.17), channel_id=1, source_target_pairs={{0,4},{4,8},{8,12},{12,16},{16,20},{20,24},{24,28},{1,5},{5,9},{9,... | collective-permute-start | bytes 786440 | tf_op jit(solution)/shard_map/ppermute | solution.py:16
  26.5 1.5 %collective-permute-start.6 = (f32[256,256]{1,0:T(8,128)S(1)}, f32[256,256]{1,0:T(8,128)S(1)}, u32[]{:S(2)}, u32[]{:S(2)}) collective-permute-start(f32[256,256]{1,0:T(8,128)S(1)} %get-tuple-element.18), channel_id=1, source_target_pairs={{4,0},{8,4},{12,8},{16,12},{20,16},{24,20},{28,24},{5,1},{9,5},{13... | collective-permute-start | bytes 786440 | tf_op jit(solution)/shard_map/ppermute | solution.py:21
  27.9 1.9 %fusion.1 = f32[2,512,640]{2,1,0:T(8,128)S(1)} fusion(f32[2,512,512]{2,1,0:T(8,128)S(1)} %copy-done, s32[2,512]{1,0:T(2,128)S(1)} %copy-done.5), kind=kOutput, calls=%fused_computation.2 | convolution fusion | flops 2013921280 | bytes 4722688 | tf_op jit(solution)/shard_map/cij,cjq->ciq/dot_general | solution.py:112
  29.9 1.6 %fusion.18 = f32[640,640]{1,0:T(8,128)S(1)} fusion(f32[64,640]{1,0:T(8,128)S(1)} %bitcast.48, f32[64]{0:T(128)S(1)} %mul.56), kind=kOutput, calls=%fused_computation.25 | convolution fusion | flops 314613760 | bytes 1802496 | tf_op jit(solution)/shard_map/dot_general | solution.py:115
  31.5 2.3 %bitcast_add_fusion = f32[640,640]{1,0:T(8,128)S(1)} fusion(f32[640,640]{1,0:T(8,128)S(1)} %fusion.18, f32[2,512,640]{2,1,0:T(8,128)S(1)} %fusion.1, s32[2,512]{1,0:T(2,128)S(1)} %copy-done.5), kind=kOutput, calls=%fused_computation.5 | convolution fusion | flops 2517647360 | bytes 5902336 | tf_op jit(solution)/shard_map/dot_general | solution.py:78
  33.8 3.0 %collective-permute-done.5 = f32[256,256]{1,0:T(8,128)S(1)} collective-permute-done((f32[256,256]{1,0:T(8,128)S(1)}, f32[256,256]{1,0:T(8,128)S(1)}, u32[]{:S(2)}, u32[]{:S(2)}) %collective-permute-start.5) | collective-permute-done | bytes 262176 | tf_op jit(solution)/shard_map/ppermute | solution.py:16
  36.9 0.0 collective-permute-done.6
  36.9 0.2 multiply_select_fusion
  37.1 0.5 fusion.11
  37.6 4.4 %collective-permute-start.7 = (f32[128,256]{1,0:T(8,128)S(1)}, f32[128,256]{1,0:T(8,128)S(1)}, u32[]{:S(2)}, u32[]{:S(2)}) collective-permute-start(f32[128,256]{1,0:T(8,128)S(1)} %get-tuple-element.21), channel_id=1, source_target_pairs={{0,4},{4,8},{8,12},{12,16},{16,20},{20,24},{24,28},{1,5},{5,9},{9,... | collective-permute-start | bytes 393224 | tf_op jit(solution)/shard_map/ppermute | solution.py:16
  42.0 1.3 %collective-permute-start.8 = (f32[128,256]{1,0:T(8,128)S(1)}, f32[128,256]{1,0:T(8,128)S(1)}, u32[]{:S(2)}, u32[]{:S(2)}) collective-permute-start(f32[128,256]{1,0:T(8,128)S(1)} %get-tuple-element.22), channel_id=1, source_target_pairs={{4,0},{8,4},{12,8},{16,12},{20,16},{24,20},{28,24},{5,1},{9,5},{13... | collective-permute-start | bytes 393224 | tf_op jit(solution)/shard_map/ppermute | solution.py:21
  43.3 0.7 %fusion.9 = f32[384,256]{1,0:T(8,128)S(1)} fusion(f32[640,256]{1,0:T(8,128)S(1)} %multiply_select_fusion, f32[640,640]{1,0:T(8,128)S(1)} %bitcast_add_fusion), kind=kOutput, calls=%fused_computation.14 | convolution fusion | flops 377487360 | bytes 2031616 | tf_op jit(solution)/shard_map/dot_general | solution.py:139
  44.0 0.5 %collective-permute-done.7 = f32[128,256]{1,0:T(8,128)S(1)} collective-permute-done((f32[128,256]{1,0:T(8,128)S(1)}, f32[128,256]{1,0:T(8,128)S(1)}, u32[]{:S(2)}, u32[]{:S(2)}) %collective-permute-start.7) | collective-permute-done | bytes 131104 | tf_op jit(solution)/shard_map/ppermute | solution.py:16
  44.5 4.6 %collective-permute-done.8 = f32[128,256]{1,0:T(8,128)S(1)} collective-permute-done((f32[128,256]{1,0:T(8,128)S(1)}, f32[128,256]{1,0:T(8,128)S(1)}, u32[]{:S(2)}, u32[]{:S(2)}) %collective-permute-start.8) | collective-permute-done | bytes 131104 | tf_op jit(solution)/shard_map/ppermute | solution.py:21
  49.1 0.8 %fusion.17 = f32[384,256]{1,0:T(8,128)} fusion(f32[384,256]{1,0:T(8,128)S(1)} %copy-done.3, f32[640,256]{1,0:T(8,128)S(1)} %multiply_select_fusion, f32[128,256]{1,0:T(8,128)S(1)} %collective-permute-done.8, f32[384,256]{1,0:T(8,128)S(1)} %fusion.9, f32[128,256]{1,0:T(8,128)S(1)} %collective-permute-done.7), kind=kLoop, calls=%fused_computation.24 | loop fusion | flops 491520 | bytes 1835008 | tf_op jit(solution)/shard_map/sub | solution.py:147
  (22 shorter events, 0.2 us)
Async XLA Ops:
  0.0 19.4 %copy-start = (f32[2,512,512]{2,1,0:T(8,128)S(1)}, f32[2,512,512]{2,1,0:T(8,128)}, u32[]{:S(2)}) copy-start(f32[2,512,512]{2,1,0:T(8,128)} %param.8) | copy-start | bytes 6291460
  0.0 15.0 %collective-permute-start.1 = (f32[4,16,128]{2,1,0:T(8,128)}, f32[4,16,128]{2,1,0:T(8,128)S(1)}, u32[]{:S(2)}, u32[]{:S(2)}) collective-permute-start(f32[4,16,128]{2,1,0:T(8,128)} %param.10), channel_id=1, source_target_pairs={{0,2},{1,3},{2,0},{3,1},{4,6},{5,7},{6,4},{7,5},{8,10},{9,11},{10,... | collective-permute-start | bytes 98312 | tf_op jit(solution)/shard_map/ppermute | solution.py:30
  2.9 12.1 %collective-permute-start = (f32[4,16,128]{2,1,0:T(8,128)}, f32[4,16,128]{2,1,0:T(8,128)S(1)}, u32[]{:S(2)}, u32[]{:S(2)}) collective-permute-start(f32[4,16,128]{2,1,0:T(8,128)} %param.10), channel_id=1, source_target_pairs={{0,1},{1,2},{2,3},{3,0},{4,5},{5,6},{6,7},{7,4},{8,9},{9,10},{10,1... | collective-permute-start | bytes 98312 | tf_op jit(solution)/shard_map/ppermute | solution.py:30
  2.9 12.1 %collective-permute-start.2 = (f32[4,16,128]{2,1,0:T(8,128)}, f32[4,16,128]{2,1,0:T(8,128)S(1)}, u32[]{:S(2)}, u32[]{:S(2)}) collective-permute-start(f32[4,16,128]{2,1,0:T(8,128)} %param.10), channel_id=1, source_target_pairs={{0,3},{1,0},{2,1},{3,2},{4,7},{5,4},{6,5},{7,6},{8,11},{9,8},{10,9... | collective-permute-start | bytes 98312 | tf_op jit(solution)/shard_map/ppermute | solution.py:30
  6.3 11.5 %collective-permute-start.4 = (f32[128,256]{1,0:T(8,128)}, f32[128,256]{1,0:T(8,128)S(1)}, u32[]{:S(2)}, u32[]{:S(2)}) collective-permute-start(f32[128,256]{1,0:T(8,128)} %get-tuple-element.19), channel_id=1, source_target_pairs={{4,0},{8,4},{12,8},{16,12},{20,16},{24,20},{28,24},{5,1},{9,5},{13... | collective-permute-start | bytes 393224 | tf_op jit(solution)/shard_map/ppermute | solution.py:21
  7.6 9.2 %collective-permute-start.3 = (f32[128,256]{1,0:T(8,128)S(1)}, f32[128,256]{1,0:T(8,128)}, u32[]{:S(2)}, u32[]{:S(2)}) collective-permute-start(f32[128,256]{1,0:T(8,128)S(1)} %get-tuple-element.20), channel_id=1, source_target_pairs={{0,4},{4,8},{8,12},{12,16},{16,20},{20,24},{24,28},{1,5},{5,9},{9,... | collective-permute-start | bytes 393224 | tf_op jit(solution)/shard_map/ppermute | solution.py:16
  15.9 1.9 %copy-start.3 = (f32[384,256]{1,0:T(8,128)S(1)}, f32[384,256]{1,0:T(8,128)}, u32[]{:S(2)}) copy-start(f32[384,256]{1,0:T(8,128)} %param.7) | copy-start | bytes 1179652
  16.3 1.6 %copy-start.5 = (s32[2,512]{1,0:T(2,128)S(1)}, s32[2,512]{1,0:T(2,128)}, u32[]{:S(2)}) copy-start(s32[2,512]{1,0:T(2,128)} %param.9) | copy-start | bytes 12292
  17.9 3.5 %copy-start.1 = (f32[640,256]{1,0:T(8,128)}, f32[640,256]{1,0:T(8,128)S(1)}, u32[]{:S(2)}) copy-start(f32[640,256]{1,0:T(8,128)S(1)} %constant_dynamic-update-slice_fusion) | copy-start | bytes 1966084
  20.5 2.1 %copy-start.4 = (f32[4,16]{1,0:T(4,128)S(1)}, f32[4,16]{1,0:T(4,128)}, u32[]{:S(2)}) copy-start(f32[4,16]{1,0:T(4,128)} %param.11) | copy-start | bytes 772
  22.7 14.1 %collective-permute-start.5 = (f32[256,256]{1,0:T(8,128)S(1)}, f32[256,256]{1,0:T(8,128)S(1)}, u32[]{:S(2)}, u32[]{:S(2)}) collective-permute-start(f32[256,256]{1,0:T(8,128)S(1)} %get-tuple-element.17), channel_id=1, source_target_pairs={{0,4},{4,8},{8,12},{12,16},{16,20},{20,24},{24,28},{1,5},{5,9},{9,... | collective-permute-start | bytes 786440 | tf_op jit(solution)/shard_map/ppermute | solution.py:16
  26.5 10.4 %collective-permute-start.6 = (f32[256,256]{1,0:T(8,128)S(1)}, f32[256,256]{1,0:T(8,128)S(1)}, u32[]{:S(2)}, u32[]{:S(2)}) collective-permute-start(f32[256,256]{1,0:T(8,128)S(1)} %get-tuple-element.18), channel_id=1, source_target_pairs={{4,0},{8,4},{12,8},{16,12},{20,16},{24,20},{28,24},{5,1},{9,5},{13... | collective-permute-start | bytes 786440 | tf_op jit(solution)/shard_map/ppermute | solution.py:21
  31.5 5.4 %copy-start.2 = (f32[640,256]{1,0:T(8,128)S(1)}, f32[640,256]{1,0:T(8,128)}, u32[]{:S(2)}) copy-start(f32[640,256]{1,0:T(8,128)} %copy-done.1) | copy-start | bytes 1966084
  37.6 6.9 %collective-permute-start.7 = (f32[128,256]{1,0:T(8,128)S(1)}, f32[128,256]{1,0:T(8,128)S(1)}, u32[]{:S(2)}, u32[]{:S(2)}) collective-permute-start(f32[128,256]{1,0:T(8,128)S(1)} %get-tuple-element.21), channel_id=1, source_target_pairs={{0,4},{4,8},{8,12},{12,16},{16,20},{20,24},{24,28},{1,5},{5,9},{9,... | collective-permute-start | bytes 393224 | tf_op jit(solution)/shard_map/ppermute | solution.py:16
  42.0 7.1 %collective-permute-start.8 = (f32[128,256]{1,0:T(8,128)S(1)}, f32[128,256]{1,0:T(8,128)S(1)}, u32[]{:S(2)}, u32[]{:S(2)}) collective-permute-start(f32[128,256]{1,0:T(8,128)S(1)} %get-tuple-element.22), channel_id=1, source_target_pairs={{4,0},{8,4},{12,8},{16,12},{20,16},{24,20},{28,24},{5,1},{9,5},{13... | collective-permute-start | bytes 393224 | tf_op jit(solution)/shard_map/ppermute | solution.py:21

commit v15 on v12

--- a/solution.py
+++ b/solution.py
@@ -23,15 +23,8 @@
 
 def gather_band(piece):
     count = lax.axis_size("band")
-    me = lax.axis_index("band")
-    pieces = [piece]
-    for k in range(1, count):
-        pieces.append(
-            lax.ppermute(piece, "band", [(i, (i + k) % count) for i in range(count)])
-        )
-    stacked = jnp.stack(pieces)
-    order = (me - jnp.arange(count)) % count
-    ordered = jnp.take(stacked, order, axis=0)
+    copies = jnp.broadcast_to(piece[None], (count,) + piece.shape)
+    ordered = lax.all_to_all(copies, "band", 0, 0, tiled=True)
     slots, channels, width = piece.shape
     return ordered.transpose(1, 2, 0, 3).reshape(slots, channels, count * width)
 

time: 48.1 us -> 51.8 us (1.077)
  waiting for transfers between devices: 7 us -> 11.4 us
  local copies, waits for them, and re-layouts: 1.85 us -> 2.84 us
  other arithmetic: 4.22 us -> 3.33 us
    ppermute x3 -> x0, starting transfers between devices: 4.68 us -> none  [gather_band(): lax.ppermute(piece, 'band', [(i, (i + k) % count) for i in range(count)])]
    all_to_all x0 -> x1, starting transfers between devices: none -> 4.21 us  [gather_band(): ordered = lax.all_to_all(copies, 'band', 0, 0, tiled=True)]
    ppermute x3, waiting for transfers between devices: 2.62 us -> 6.67 us  [from_left(): return lax.ppermute(x, axis, [(i, i + 1) for i in range(count - 1)])]
    broadcast_in_dim x0 -> x1, local copies, waits for them, and re-layouts: none -> 1.57 us  [gather_band(): copies = jnp.broadcast_to(piece[None], (count,) + piece.shape)]
    another operation x1 -> x0, other arithmetic: 0.77 us -> none  [gather_band(): stacked = jnp.stack(pieces)]
    gather x1 -> x0, local copies, waits for them, and re-layouts: 0.56 us -> none  [gather_band(): ordered = jnp.take(stacked, order, axis=0)]
  transfers between devices with their start and end apart: 9 -> 7, of which waited for: 3 -> 4; matrix products, arithmetic and copies ran while one was open for 24% -> 19% of each run, Pallas kernels for 0% -> 0%
where the time goes in v15:
time: 51.8 us; the launch traced here: 51.3 us
  starting transfers between devices  21.5 us (42%)
  waiting for transfers between devices  11.4 us (22%)
  matrix products  11.3 us (22%)
  other arithmetic  3.33 us (6%)
  local copies, waits for them, and re-layouts  2.84 us (5%)
  between operations  0.98 us (2%)
    ppermute x3, starting transfers between devices, from_left(): return lax.ppermute(x, axis, [(i, i + 1) for i in range(count - 1)])  13.4 us
    ppermute x3, waiting for transfers between devices, from_left(): return lax.ppermute(x, axis, [(i, i + 1) for i in range(count - 1)])  6.67 us
    ppermute x3, waiting for transfers between devices, from_right(): return lax.ppermute(x, axis, [(i + 1, i) for i in range(count - 1)])  4.75 us
    all_to_all x1, starting transfers between devices, gather_band(): ordered = lax.all_to_all(copies, 'band', 0, 0, tiled=True)  4.21 us
    ppermute x3, starting transfers between devices, from_right(): return lax.ppermute(x, axis, [(i + 1, i) for i in range(count - 1)])  3.88 us
    dot_general x2, matrix products, scatter_rows(): lax.dot_general(onehot, values, (((0,), (0,)), ((), ())), precision=lax.P...  3.2 us
    dot_general x1, matrix products, on_device(): jnp.einsum('cij,cjq->ciq', matrices, onehot.reshape(cells, nodes, ext), p...  1.94 us
    dot_general x1, matrix products, on_device(): jnp.dot((placed_late * weights_late[:, None]).T, placed_late, precision=h...  1.57 us
  transfers between devices with their start and end apart: 7, of which 4 were waited for; matrix products, arithmetic and copies ran while one was open for 19% of the time, Pallas kernels for 0%

profile of v15, /device:TPU:0, one launch (start us, length us, event | category | flops | bytes accessed | tf_op | source)
XLA Modules:
  0.0 51.3 jit_solution(17176950770125847279)
XLA Ops:
  0.0 0.0 copy-start
  0.0 1.6 %broadcast_in_dim.91 = f32[4,4,16,128]{3,2,1,0:T(8,128)} broadcast(f32[4,16,128]{2,1,0:T(8,128)} %param.10), dimensions={1,2,3} | broadcast | bytes 163840 | tf_op jit(solution)/shard_map/broadcast_in_dim | solution.py:26
  1.6 4.2 %all-to-all-start = ((f32[4,4,16,128]{3,2,1,0:T(8,128)}), f32[4,4,16,128]{3,2,1,0:T(8,128)S(1)}, u32[]{:S(2)}, u32[]{:S(2)}) async-start(f32[4,4,16,128]{3,2,1,0:T(8,128)} %broadcast_in_dim.91), calls=%async_computation | async-start | bytes 262144 | tf_op jit(solution)/shard_map/all_to_all | solution.py:27
  5.8 1.0 %fusion.27 = (f32[128,256]{1,0:T(8,128)S(1)}, f32[128,256]{1,0:T(8,128)S(1)}) fusion(f32[384,256]{1,0:T(8,128)} %param.7), kind=kLoop, calls=%fused_computation.60 | loop fusion | bytes 524288 | tf_op jit(solution)/shard_map/slice | solution.py:77
  6.8 1.3 %collective-permute-start.1 = (f32[128,256]{1,0:T(8,128)S(1)}, f32[128,256]{1,0:T(8,128)S(1)}, u32[]{:S(2)}, u32[]{:S(2)}) collective-permute-start(f32[128,256]{1,0:T(8,128)S(1)} %get-tuple-element.17), channel_id=1, source_target_pairs={{4,0},{8,4},{12,8},{16,12},{20,16},{24,20},{28,24},{5,1},{9,5},{13... | collective-permute-start | bytes 393224 | tf_op jit(solution)/shard_map/ppermute | solution.py:21
  8.1 4.6 %collective-permute-start = (f32[128,256]{1,0:T(8,128)S(1)}, f32[128,256]{1,0:T(8,128)S(1)}, u32[]{:S(2)}, u32[]{:S(2)}) collective-permute-start(f32[128,256]{1,0:T(8,128)S(1)} %get-tuple-element.18), channel_id=1, source_target_pairs={{0,4},{4,8},{8,12},{12,16},{16,20},{20,24},{24,28},{1,5},{5,9},{9,... | collective-permute-start | bytes 393224 | tf_op jit(solution)/shard_map/ppermute | solution.py:16
  13.4 0.8 %broadcast_multiply_fusion = f32[4,16]{1,0:T(4,128)S(1)} fusion(f32[4,16]{1,0:T(4,128)} %param.11, f32[4]{0:T(128)S(1)} %compare_convert_fusion), kind=kLoop, calls=%fused_computation.47 | loop fusion | flops 64 | bytes 528 | tf_op jit(solution)/shard_map/mul | solution.py:50
  14.1 0.1 reshape.70
  14.2 0.7 %and_compare_fusion.7 = (pred[4]{0:T(512)(128)(4,1)S(1)}, pred[4]{0:T(512)(128)(4,1)S(1)}, pred[4]{0:T(512)(128)(4,1)S(1)}, pred[4]{0:T(512)(128)(4,1)S(1)}, pre...) fusion(s32[4]{0:T(128)} %param.12), kind=kLoop, calls=%fused_computation.55 | loop fusion | flops 100 | bytes 48 | tf_op jit(solution)/shard_map/eq | solution.py:38
  14.9 0.0 all-to-all-done
  15.0 0.0 copy-start.1
  15.0 0.1 pad_select_fusion
  15.1 0.1 pad_select_fusion.7
  15.2 0.1 pad_select_fusion.6
  15.3 0.0 copy-start.2
  15.3 0.1 pad_select_fusion.5
  15.4 0.1 pad_select_fusion.4
  15.6 0.1 pad_select_fusion.3
  15.7 0.1 pad_select_fusion.2
  15.8 0.1 pad_select_fusion.1
  15.9 2.0 %collective-permute-done = f32[128,256]{1,0:T(8,128)S(1)} collective-permute-done((f32[128,256]{1,0:T(8,128)S(1)}, f32[128,256]{1,0:T(8,128)S(1)}, u32[]{:S(2)}, u32[]{:S(2)}) %collective-permute-start) | collective-permute-done | bytes 131104 | tf_op jit(solution)/shard_map/ppermute | solution.py:16
  17.9 0.0 copy-done.1
  17.9 0.0 collective-permute-done.1
  18.0 0.0 copy-done.2
  18.0 1.1 %fusion.3 = f32[2,512,256]{1,2,0:T(8,128)S(1)} fusion(s32[2,512]{1,0:T(2,128)S(1)} %copy-done.2, f32[640,256]{1,0:T(8,128)S(1)} %constant_dynamic-update-slice_fusion), kind=kOutput, calls=%fused_computation.4 | convolution fusion | flops 1007288320 | bytes 1708032 | tf_op jit(solution)/shard_map/dot_general | solution.py:86
  19.1 0.0 copy-done
  19.1 1.1 %convolution_bitcast_fusion = f32[2,512,256]{1,2,0:T(8,128)S(1)} fusion(f32[2,512,256]{1,2,0:T(8,128)S(1)} %fusion.3, f32[2,512,512]{2,1,0:T(8,128)S(1)} %copy-done), kind=kOutput, calls=%fused_computation.6 | convolution fusion | flops 805306368 | bytes 4194304 | tf_op jit(solution)/shard_map/cij,cjb->cib/dot_general | solution.py:87
  20.2 0.9 %fusion.8 = f32[640,256]{1,0:T(8,128)S(1)} fusion(f32[2,512,256]{1,2,0:T(8,128)S(1)} %convolution_bitcast_fusion, s32[2,512]{1,0:T(2,128)S(1)} %copy-done.2), kind=kOutput, calls=%fused_computation.11 | convolution fusion | flops 1007288320 | bytes 1708032 | tf_op jit(solution)/shard_map/dot_general | solution.py:62
  21.1 0.4 convolution_multiply_fusion
  21.6 0.7 %convolution_add_fusion = f32[640,256]{1,0:T(8,128)S(1)} fusion(f32[640,256]{1,0:T(8,128)S(1)} %fusion.8, f32[64,640]{1,0:T(8,128)S(1)} %bitcast.37, f32[64,256]{1,0:T(8,128)S(1)} %convolution_multiply_fusion), kind=kOutput, calls=%fused_computation.12 | convolution fusion | flops 125992960 | bytes 1540096 | tf_op jit(solution)/shard_map/dot_general | solution.py:88
  22.4 4.4 %collective-permute-start.2 = (f32[256,256]{1,0:T(8,128)S(1)}, f32[256,256]{1,0:T(8,128)S(1)}, u32[]{:S(2)}, u32[]{:S(2)}) collective-permute-start(f32[256,256]{1,0:T(8,128)S(1)} %get-tuple-element.15), channel_id=1, source_target_pairs={{0,4},{4,8},{8,12},{12,16},{16,20},{20,24},{24,28},{1,5},{5,9},{9,... | collective-permute-start | bytes 786440 | tf_op jit(solution)/shard_map/ppermute | solution.py:16
  26.7 1.3 %collective-permute-start.3 = (f32[256,256]{1,0:T(8,128)S(1)}, f32[256,256]{1,0:T(8,128)S(1)}, u32[]{:S(2)}, u32[]{:S(2)}) collective-permute-start(f32[256,256]{1,0:T(8,128)S(1)} %get-tuple-element.16), channel_id=1, source_target_pairs={{4,0},{8,4},{12,8},{16,12},{20,16},{24,20},{28,24},{5,1},{9,5},{13... | collective-permute-start | bytes 786440 | tf_op jit(solution)/shard_map/ppermute | solution.py:21
  28.0 1.9 %fusion.1 = f32[2,512,640]{2,1,0:T(8,128)S(1)} fusion(f32[2,512,512]{2,1,0:T(8,128)S(1)} %copy-done, s32[2,512]{1,0:T(2,128)S(1)} %copy-done.2), kind=kOutput, calls=%fused_computation.2 | convolution fusion | flops 2013921280 | bytes 4722688 | tf_op jit(solution)/shard_map/cij,cjq->ciq/dot_general | solution.py:95
  30.0 1.6 %fusion.18 = f32[640,640]{1,0:T(8,128)S(1)} fusion(f32[64,640]{1,0:T(8,128)S(1)} %bitcast.38, f32[64]{0:T(128)S(1)} %reshape.70), kind=kOutput, calls=%fused_computation.25 | convolution fusion | flops 314613760 | bytes 1802496 | tf_op jit(solution)/shard_map/dot_general | solution.py:98
  31.6 2.3 %bitcast_add_fusion = f32[640,640]{1,0:T(8,128)S(1)} fusion(f32[640,640]{1,0:T(8,128)S(1)} %fusion.18, f32[2,512,640]{2,1,0:T(8,128)S(1)} %fusion.1, s32[2,512]{1,0:T(2,128)S(1)} %copy-done.2), kind=kOutput, calls=%fused_computation.5 | convolution fusion | flops 2517647360 | bytes 5902336 | tf_op jit(solution)/shard_map/dot_general | solution.py:62
  34.0 4.2 %collective-permute-done.2 = f32[256,256]{1,0:T(8,128)S(1)} collective-permute-done((f32[256,256]{1,0:T(8,128)S(1)}, f32[256,256]{1,0:T(8,128)S(1)}, u32[]{:S(2)}, u32[]{:S(2)}) %collective-permute-start.2) | collective-permute-done | bytes 262176 | tf_op jit(solution)/shard_map/ppermute | solution.py:16
  38.1 0.0 collective-permute-done.3
  38.1 0.2 multiply_select_fusion
  38.3 0.5 fusion.11
  38.8 4.4 %collective-permute-start.4 = (f32[128,256]{1,0:T(8,128)S(1)}, f32[128,256]{1,0:T(8,128)S(1)}, u32[]{:S(2)}, u32[]{:S(2)}) collective-permute-start(f32[128,256]{1,0:T(8,128)S(1)} %get-tuple-element.19), channel_id=1, source_target_pairs={{0,4},{4,8},{8,12},{12,16},{16,20},{20,24},{24,28},{1,5},{5,9},{9,... | collective-permute-start | bytes 393224 | tf_op jit(solution)/shard_map/ppermute | solution.py:16
  43.2 1.3 %collective-permute-start.5 = (f32[128,256]{1,0:T(8,128)S(1)}, f32[128,256]{1,0:T(8,128)S(1)}, u32[]{:S(2)}, u32[]{:S(2)}) collective-permute-start(f32[128,256]{1,0:T(8,128)S(1)} %get-tuple-element.20), channel_id=1, source_target_pairs={{4,0},{8,4},{12,8},{16,12},{20,16},{24,20},{28,24},{5,1},{9,5},{13... | collective-permute-start | bytes 393224 | tf_op jit(solution)/shard_map/ppermute | solution.py:21
  44.5 0.7 %fusion.9 = f32[384,256]{1,0:T(8,128)S(1)} fusion(f32[640,256]{1,0:T(8,128)S(1)} %multiply_select_fusion, f32[640,640]{1,0:T(8,128)S(1)} %bitcast_add_fusion), kind=kOutput, calls=%fused_computation.14 | convolution fusion | flops 377487360 | bytes 2031616 | tf_op jit(solution)/shard_map/dot_general | solution.py:122
  45.2 0.5 %collective-permute-done.4 = f32[128,256]{1,0:T(8,128)S(1)} collective-permute-done((f32[128,256]{1,0:T(8,128)S(1)}, f32[128,256]{1,0:T(8,128)S(1)}, u32[]{:S(2)}, u32[]{:S(2)}) %collective-permute-start.4) | collective-permute-done | bytes 131104 | tf_op jit(solution)/shard_map/ppermute | solution.py:16
  45.7 4.7 %collective-permute-done.5 = f32[128,256]{1,0:T(8,128)S(1)} collective-permute-done((f32[128,256]{1,0:T(8,128)S(1)}, f32[128,256]{1,0:T(8,128)S(1)}, u32[]{:S(2)}, u32[]{:S(2)}) %collective-permute-start.5) | collective-permute-done | bytes 131104 | tf_op jit(solution)/shard_map/ppermute | solution.py:21
  50.5 0.9 %fusion.17 = f32[384,256]{1,0:T(8,128)} fusion(f32[384,256]{1,0:T(8,128)S(1)} %copy-done.1, f32[640,256]{1,0:T(8,128)S(1)} %multiply_select_fusion, f32[128,256]{1,0:T(8,128)S(1)} %collective-permute-done.5, f32[384,256]{1,0:T(8,128)S(1)} %fusion.9, f32[128,256]{1,0:T(8,128)S(1)} %collective-permute-done.4), kind=kLoop, calls=%fused_computation.24 | loop fusion | flops 491520 | bytes 1835008 | tf_op jit(solution)/shard_map/sub | solution.py:130
  (11 shorter events, 0.2 us)
Async XLA Ops:
  0.0 19.1 %copy-start = (f32[2,512,512]{2,1,0:T(8,128)S(1)}, f32[2,512,512]{2,1,0:T(8,128)}, u32[]{:S(2)}) copy-start(f32[2,512,512]{2,1,0:T(8,128)} %param.8) | copy-start | bytes 6291460
  1.6 13.3 %all-to-all-start = ((f32[4,4,16,128]{3,2,1,0:T(8,128)}), f32[4,4,16,128]{3,2,1,0:T(8,128)S(1)}, u32[]{:S(2)}, u32[]{:S(2)}) async-start(f32[4,4,16,128]{3,2,1,0:T(8,128)} %broadcast_in_dim.91), calls=%async_computation | async-start | bytes 262144 | tf_op jit(solution)/shard_map/all_to_all | solution.py:27
  6.8 11.2 %collective-permute-start.1 = (f32[128,256]{1,0:T(8,128)S(1)}, f32[128,256]{1,0:T(8,128)S(1)}, u32[]{:S(2)}, u32[]{:S(2)}) collective-permute-start(f32[128,256]{1,0:T(8,128)S(1)} %get-tuple-element.17), channel_id=1, source_target_pairs={{4,0},{8,4},{12,8},{16,12},{20,16},{24,20},{28,24},{5,1},{9,5},{13... | collective-permute-start | bytes 393224 | tf_op jit(solution)/shard_map/ppermute | solution.py:21
  8.1 9.8 %collective-permute-start = (f32[128,256]{1,0:T(8,128)S(1)}, f32[128,256]{1,0:T(8,128)S(1)}, u32[]{:S(2)}, u32[]{:S(2)}) collective-permute-start(f32[128,256]{1,0:T(8,128)S(1)} %get-tuple-element.18), channel_id=1, source_target_pairs={{0,4},{4,8},{8,12},{12,16},{16,20},{20,24},{24,28},{1,5},{5,9},{9,... | collective-permute-start | bytes 393224 | tf_op jit(solution)/shard_map/ppermute | solution.py:16
  15.0 2.9 %copy-start.1 = (f32[384,256]{1,0:T(8,128)S(1)}, f32[384,256]{1,0:T(8,128)}, u32[]{:S(2)}) copy-start(f32[384,256]{1,0:T(8,128)} %param.7) | copy-start | bytes 1179652
  15.3 2.6 %copy-start.2 = (s32[2,512]{1,0:T(2,128)S(1)}, s32[2,512]{1,0:T(2,128)}, u32[]{:S(2)}) copy-start(s32[2,512]{1,0:T(2,128)} %param.9) | copy-start | bytes 12292
  22.4 15.8 %collective-permute-start.2 = (f32[256,256]{1,0:T(8,128)S(1)}, f32[256,256]{1,0:T(8,128)S(1)}, u32[]{:S(2)}, u32[]{:S(2)}) collective-permute-start(f32[256,256]{1,0:T(8,128)S(1)} %get-tuple-element.15), channel_id=1, source_target_pairs={{0,4},{4,8},{8,12},{12,16},{16,20},{20,24},{24,28},{1,5},{5,9},{9,... | collective-permute-start | bytes 786440 | tf_op jit(solution)/shard_map/ppermute | solution.py:16
  26.7 11.4 %collective-permute-start.3 = (f32[256,256]{1,0:T(8,128)S(1)}, f32[256,256]{1,0:T(8,128)S(1)}, u32[]{:S(2)}, u32[]{:S(2)}) collective-permute-start(f32[256,256]{1,0:T(8,128)S(1)} %get-tuple-element.16), channel_id=1, source_target_pairs={{4,0},{8,4},{12,8},{16,12},{20,16},{24,20},{28,24},{5,1},{9,5},{13... | collective-permute-start | bytes 786440 | tf_op jit(solution)/shard_map/ppermute | solution.py:21
  38.8 6.9 %collective-permute-start.4 = (f32[128,256]{1,0:T(8,128)S(1)}, f32[128,256]{1,0:T(8,128)S(1)}, u32[]{:S(2)}, u32[]{:S(2)}) collective-permute-start(f32[128,256]{1,0:T(8,128)S(1)} %get-tuple-element.19), channel_id=1, source_target_pairs={{0,4},{4,8},{8,12},{12,16},{16,20},{20,24},{24,28},{1,5},{5,9},{9,... | collective-permute-start | bytes 393224 | tf_op jit(solution)/shard_map/ppermute | solution.py:16
  43.2 7.2 %collective-permute-start.5 = (f32[128,256]{1,0:T(8,128)S(1)}, f32[128,256]{1,0:T(8,128)S(1)}, u32[]{:S(2)}, u32[]{:S(2)}) collective-permute-start(f32[128,256]{1,0:T(8,128)S(1)} %get-tuple-element.20), channel_id=1, source_target_pairs={{4,0},{8,4},{12,8},{16,12},{20,16},{24,20},{28,24},{5,1},{9,5},{13... | collective-permute-start | bytes 393224 | tf_op jit(solution)/shard_map/ppermute | solution.py:21

commit v16 on v12

--- a/solution.py
+++ b/solution.py
@@ -89,11 +89,11 @@
     cells, nodes, _ = cell_matrix.shape
     high = lax.Precision.HIGH
 
-    coefficients = jnp.dot(placed, extended, precision=highest) * weights[:, None]
+    coefficients = jnp.dot(placed, extended, precision=high) * weights[:, None]
     gathered = jnp.dot(onehot, extended, precision=high).reshape(cells, nodes, -1)
     local = jnp.einsum("cij,cjb->cib", cell_matrix, gathered, precision=high)
     first = scatter_rows(onehot, local.reshape(cells * nodes, -1)) + jnp.dot(
-        placed.T, coefficients, precision=highest
+        placed.T, coefficients, precision=high
     )
 
     matrices, placed_late, weights_late, first = lax.optimization_barrier(
@@ -127,6 +127,7 @@
     from_after = from_right(second_edges[:g], "dom")
     owned = lax.optimization_barrier(
         jnp.dot(operator[g : g + own], step_ext, precision=lax.Precision.HIGH)
+        - filter_center * step_one
     )
     zeros_own = jnp.zeros((own - g, owned.shape[1]), jnp.float32)
     second_image = (
@@ -134,7 +135,7 @@
         + jnp.concatenate([from_before, zeros_own], axis=0)
         + jnp.concatenate([zeros_own, from_after], axis=0)
     )
-    filtered = 2.0 * (second_image - filter_center * step_one) / filter_half - wavefunctions
+    filtered = 2.0 * second_image / filter_half - wavefunctions
     return filtered
 
 

time: 48.1 us -> 47.6 us (0.990)
  no operation moved by 1% of the time
where the time goes in v16:
time: 47.6 us; the launch traced here: 47.3 us
  starting transfers between devices  21.8 us (46%)
  matrix products  11.2 us (24%)
  waiting for transfers between devices  7.18 us (15%)
  other arithmetic  4.2 us (9%)
  local copies, waits for them, and re-layouts  1.85 us (4%)
  between operations  0.99 us (2%)
    ppermute x3, starting transfers between devices, from_left(): return lax.ppermute(x, axis, [(i, i + 1) for i in range(count - 1)])  13.3 us
    ppermute x3, starting transfers between devices, gather_band(): lax.ppermute(piece, 'band', [(i, (i + k) % count) for i in range(count)])  4.68 us
    ppermute x3, waiting for transfers between devices, from_right(): return lax.ppermute(x, axis, [(i + 1, i) for i in range(count - 1)])  4.37 us
    ppermute x3, starting transfers between devices, from_right(): return lax.ppermute(x, axis, [(i + 1, i) for i in range(count - 1)])  3.88 us
    dot_general x2, matrix products, scatter_rows(): lax.dot_general(onehot, values, (((0,), (0,)), ((), ())), precision=lax.P...  3.16 us
    ppermute x3, waiting for transfers between devices, from_left(): return lax.ppermute(x, axis, [(i, i + 1) for i in range(count - 1)])  2.8 us
    dot_general x1, matrix products, on_device(): jnp.einsum('cij,cjq->ciq', matrices, onehot.reshape(cells, nodes, ext), p...  1.95 us
    dot_general x1, matrix products, on_device(): jnp.dot((placed_late * weights_late[:, None]).T, placed_late, precision=h...  1.58 us
  transfers between devices with their start and end apart: 9, of which 3 were waited for; matrix products, arithmetic and copies ran while one was open for 24% of the time, Pallas kernels for 0%

profile of v16, /device:TPU:0, one launch (start us, length us, event | category | flops | bytes accessed | tf_op | source)
XLA Modules:
  0.0 47.3 jit_solution(5328683556985121764)
XLA Ops:
  0.0 0.5 collective-permute-start
  0.5 2.0 %collective-permute-start.2 = (f32[4,16,128]{2,1,0:T(8,128)}, f32[4,16,128]{2,1,0:T(8,128)S(1)}, u32[]{:S(2)}, u32[]{:S(2)}) collective-permute-start(f32[4,16,128]{2,1,0:T(8,128)} %param.10), channel_id=1, source_target_pairs={{0,3},{1,0},{2,1},{3,2},{4,7},{5,4},{6,5},{7,6},{8,11},{9,8},{10,9... | collective-permute-start | bytes 98312 | tf_op jit(solution)/shard_map/ppermute | solution.py:30
  2.4 2.2 %collective-permute-start.1 = (f32[4,16,128]{2,1,0:T(8,128)}, f32[4,16,128]{2,1,0:T(8,128)S(1)}, u32[]{:S(2)}, u32[]{:S(2)}) collective-permute-start(f32[4,16,128]{2,1,0:T(8,128)} %param.10), channel_id=1, source_target_pairs={{0,2},{1,3},{2,0},{3,1},{4,6},{5,7},{6,4},{7,5},{8,10},{9,11},{10,... | collective-permute-start | bytes 98312 | tf_op jit(solution)/shard_map/ppermute | solution.py:30
  4.7 1.0 %fusion.27 = (f32[128,256]{1,0:T(8,128)S(1)}, f32[128,256]{1,0:T(8,128)S(1)}) fusion(f32[384,256]{1,0:T(8,128)} %param.7), kind=kLoop, calls=%fused_computation.75 | loop fusion | bytes 524288 | tf_op jit(solution)/shard_map/slice | solution.py:84
  5.7 1.3 %collective-permute-start.4 = (f32[128,256]{1,0:T(8,128)S(1)}, f32[128,256]{1,0:T(8,128)S(1)}, u32[]{:S(2)}, u32[]{:S(2)}) collective-permute-start(f32[128,256]{1,0:T(8,128)S(1)} %get-tuple-element.17), channel_id=1, source_target_pairs={{4,0},{8,4},{12,8},{16,12},{20,16},{24,20},{28,24},{5,1},{9,5},{13... | collective-permute-start | bytes 393224 | tf_op jit(solution)/shard_map/ppermute | solution.py:21
  7.0 4.6 %collective-permute-start.3 = (f32[128,256]{1,0:T(8,128)S(1)}, f32[128,256]{1,0:T(8,128)S(1)}, u32[]{:S(2)}, u32[]{:S(2)}) collective-permute-start(f32[128,256]{1,0:T(8,128)S(1)} %get-tuple-element.18), channel_id=1, source_target_pairs={{0,4},{4,8},{8,12},{12,16},{16,20},{20,24},{24,28},{1,5},{5,9},{9,... | collective-permute-start | bytes 393224 | tf_op jit(solution)/shard_map/ppermute | solution.py:16
  12.2 0.7 %and_compare_fusion.7 = (pred[4]{0:T(512)(128)(4,1)S(1)}, pred[4]{0:T(512)(128)(4,1)S(1)}, pred[4]{0:T(512)(128)(4,1)S(1)}, pred[4]{0:T(512)(128)(4,1)S(1)}, pre...) fusion(s32[4]{0:T(128)} %param.12), kind=kLoop, calls=%fused_computation.70 | loop fusion | flops 100 | bytes 48 | tf_op jit(solution)/shard_map/eq | solution.py:45
  12.9 0.8 %broadcast_multiply_fusion = f32[4,16]{1,0:T(4,128)S(1)} fusion(f32[4,16]{1,0:T(4,128)} %param.11, f32[4]{0:T(128)S(1)} %compare_convert_fusion), kind=kLoop, calls=%fused_computation.59 | loop fusion | flops 64 | bytes 528 | tf_op jit(solution)/shard_map/mul | solution.py:57
  13.7 0.1 reshape.123
  13.8 0.0 collective-permute-done
  13.8 0.0 collective-permute-done.2
  13.8 0.0 collective-permute-done.1
  13.8 0.8 %pad_maximum_fusion = f32[4,4,16,128]{3,2,1,0:T(8,128)S(1)} fusion(f32[1,4,16,128]{3,2,1,0:T(8,128)S(1)} %bitcast.53, f32[1,4,16,128]{3,2,1,0:T(8,128)S(1)} %bitcast.54, f32[1,4,16,128]{3,2,1,0:T(8,128)S(1)} %bitcast.52, f32[1,4,16,128]{3,2,1,0:T(8,128)} %bitcast.51), kind=kLoop, calls=%fused_computation.37 | loop fusion | flops 98304 | bytes 262144 | tf_op jit(solution)/shard_map/stack | solution.py:32
  14.6 0.6 %gather_fusion = f32[4,4,16,128]{3,2,1,0:T(8,128)S(1)} fusion(f32[4,4,16,128]{3,2,1,0:T(8,128)S(1)} %pad_maximum_fusion, s32[1024]{0:T(1024)S(1)} %pad_clamp_fusion), kind=kCustom, calls=%fused_computation | custom fusion | bytes 262160 | tf_op jit(solution)/shard_map/jit(_take)/gather | solution.py:34
  15.1 0.1 copy_bitcast_fusion
  15.2 0.0 copy-start.1
  15.3 0.1 pad_select_fusion
  15.4 0.1 pad_select_fusion.7
  15.5 0.1 pad_select_fusion.6
  15.6 0.0 copy-start.2
  15.6 0.1 pad_select_fusion.5
  15.7 0.1 pad_select_fusion.4
  15.9 0.1 pad_select_fusion.3
  16.0 0.1 pad_select_fusion.2
  16.1 0.1 pad_select_fusion.1
  16.2 0.0 copy-done.1
  16.3 0.0 collective-permute-done.4
  16.3 0.0 copy-done.2
  16.3 1.6 %fusion.3 = f32[2,512,256]{2,1,0:T(8,128)S(1)} fusion(s32[2,512]{1,0:T(2,128)S(1)} %copy-done.2, f32[640,256]{1,0:T(8,128)S(1)} %constant_dynamic-update-slice_fusion), kind=kOutput, calls=%fused_computation.5 | convolution fusion | flops 1007288320 | bytes 1708032 | tf_op jit(solution)/shard_map/dot_general | solution.py:93
  17.9 1.0 %convolution_bitcast_fusion = f32[2,512,256]{2,1,0:T(8,128)S(1)} fusion(f32[2,512,256]{2,1,0:T(8,128)S(1)} %fusion.3, f32[2,512,512]{2,1,0:T(8,128)S(1)} %copy-done), kind=kOutput, calls=%fused_computation.7 | convolution fusion | flops 805306368 | bytes 4194304 | tf_op jit(solution)/shard_map/cij,cjb->cib/dot_general | solution.py:94
  18.9 0.9 %fusion.8 = f32[640,256]{1,0:T(8,128)S(1)} fusion(f32[2,512,256]{2,1,0:T(8,128)S(1)} %convolution_bitcast_fusion, s32[2,512]{1,0:T(2,128)S(1)} %copy-done.2), kind=kOutput, calls=%fused_computation.12 | convolution fusion | flops 1007288320 | bytes 1708032 | tf_op jit(solution)/shard_map/dot_general | solution.py:69
  19.8 0.3 convolution_multiply_fusion
  20.1 0.5 %convolution_add_fusion = f32[640,256]{1,0:T(8,128)S(1)} fusion(f32[640,256]{1,0:T(8,128)S(1)} %fusion.8, f32[64,640]{1,0:T(8,128)S(1)} %bitcast.43, f32[64,256]{1,0:T(8,128)S(1)} %convolution_multiply_fusion), kind=kOutput, calls=%fused_computation.13 | convolution fusion | flops 63078400 | bytes 1540096 | tf_op jit(solution)/shard_map/dot_general | solution.py:95
  20.6 4.3 %collective-permute-start.5 = (f32[256,256]{1,0:T(8,128)S(1)}, f32[256,256]{1,0:T(8,128)S(1)}, u32[]{:S(2)}, u32[]{:S(2)}) collective-permute-start(f32[256,256]{1,0:T(8,128)S(1)} %get-tuple-element.15), channel_id=1, source_target_pairs={{0,4},{4,8},{8,12},{12,16},{16,20},{20,24},{24,28},{1,5},{5,9},{9,... | collective-permute-start | bytes 786440 | tf_op jit(solution)/shard_map/ppermute | solution.py:16
  25.0 1.3 %collective-permute-start.6 = (f32[256,256]{1,0:T(8,128)S(1)}, f32[256,256]{1,0:T(8,128)S(1)}, u32[]{:S(2)}, u32[]{:S(2)}) collective-permute-start(f32[256,256]{1,0:T(8,128)S(1)} %get-tuple-element.16), channel_id=1, source_target_pairs={{4,0},{8,4},{12,8},{16,12},{20,16},{24,20},{28,24},{5,1},{9,5},{13... | collective-permute-start | bytes 786440 | tf_op jit(solution)/shard_map/ppermute | solution.py:21
  26.3 1.9 %fusion.1 = f32[2,512,640]{2,1,0:T(8,128)S(1)} fusion(f32[2,512,512]{2,1,0:T(8,128)S(1)} %copy-done, s32[2,512]{1,0:T(2,128)S(1)} %copy-done.2), kind=kOutput, calls=%fused_computation.3 | convolution fusion | flops 2013921280 | bytes 4722688 | tf_op jit(solution)/shard_map/cij,cjq->ciq/dot_general | solution.py:102
  28.2 1.6 %fusion.15 = f32[640,640]{1,0:T(8,128)S(1)} fusion(f32[64,640]{1,0:T(8,128)S(1)} %bitcast.44, f32[64]{0:T(128)S(1)} %reshape.123), kind=kOutput, calls=%fused_computation.25 | convolution fusion | flops 314613760 | bytes 1802496 | tf_op jit(solution)/shard_map/dot_general | solution.py:105
  29.8 2.3 %bitcast_add_fusion = f32[640,640]{1,0:T(8,128)S(1)} fusion(f32[640,640]{1,0:T(8,128)S(1)} %fusion.15, f32[2,512,640]{2,1,0:T(8,128)S(1)} %fusion.1, s32[2,512]{1,0:T(2,128)S(1)} %copy-done.2), kind=kOutput, calls=%fused_computation.6 | convolution fusion | flops 2517647360 | bytes 5902336 | tf_op jit(solution)/shard_map/dot_general | solution.py:69
  32.2 2.3 %collective-permute-done.5 = f32[256,256]{1,0:T(8,128)S(1)} collective-permute-done((f32[256,256]{1,0:T(8,128)S(1)}, f32[256,256]{1,0:T(8,128)S(1)}, u32[]{:S(2)}, u32[]{:S(2)}) %collective-permute-start.5) | collective-permute-done | bytes 262176 | tf_op jit(solution)/shard_map/ppermute | solution.py:16
  34.4 0.0 collective-permute-done.6
  34.4 0.2 multiply_select_fusion
  34.6 0.5 %fusion.10 = f32[256,256]{1,0:T(8,128)S(1)} fusion(f32[640,256]{1,0:T(8,128)S(1)} %multiply_select_fusion, f32[128,640]{1,0:T(8,128)S(1)} %get-tuple-element.14, f32[128,640]{1,0:T(8,128)S(1)} %get-tuple-element.13), kind=kOutput, calls=%fused_computation.17 | convolution fusion | flops 251822080 | bytes 1572864 | tf_op jit(solution)/shard_map/dot_general | solution.py:125
  35.2 4.4 %collective-permute-start.7 = (f32[128,256]{1,0:T(8,128)S(1)}, f32[128,256]{1,0:T(8,128)S(1)}, u32[]{:S(2)}, u32[]{:S(2)}) collective-permute-start(f32[128,256]{1,0:T(8,128)S(1)} %get-tuple-element.19), channel_id=1, source_target_pairs={{0,4},{4,8},{8,12},{12,16},{16,20},{20,24},{24,28},{1,5},{5,9},{9,... | collective-permute-start | bytes 393224 | tf_op jit(solution)/shard_map/ppermute | solution.py:16
  39.6 1.3 %collective-permute-start.8 = (f32[128,256]{1,0:T(8,128)S(1)}, f32[128,256]{1,0:T(8,128)S(1)}, u32[]{:S(2)}, u32[]{:S(2)}) collective-permute-start(f32[128,256]{1,0:T(8,128)S(1)} %get-tuple-element.20), channel_id=1, source_target_pairs={{4,0},{8,4},{12,8},{16,12},{20,16},{24,20},{28,24},{5,1},{9,5},{13... | collective-permute-start | bytes 393224 | tf_op jit(solution)/shard_map/ppermute | solution.py:21
  40.9 0.7 %convolution_subtract_fusion = f32[384,256]{1,0:T(8,128)S(1)} fusion(f32[640,256]{1,0:T(8,128)S(1)} %multiply_select_fusion, f32[640,640]{1,0:T(8,128)S(1)} %bitcast_add_fusion), kind=kOutput, calls=%fused_computation.14 | convolution fusion | flops 377683968 | bytes 2424832 | tf_op jit(solution)/shard_map/dot_general | solution.py:129
  41.5 0.5 %collective-permute-done.7 = f32[128,256]{1,0:T(8,128)S(1)} collective-permute-done((f32[128,256]{1,0:T(8,128)S(1)}, f32[128,256]{1,0:T(8,128)S(1)}, u32[]{:S(2)}, u32[]{:S(2)}) %collective-permute-start.7) | collective-permute-done | bytes 131104 | tf_op jit(solution)/shard_map/ppermute | solution.py:16
  42.1 4.4 %collective-permute-done.8 = f32[128,256]{1,0:T(8,128)S(1)} collective-permute-done((f32[128,256]{1,0:T(8,128)S(1)}, f32[128,256]{1,0:T(8,128)S(1)}, u32[]{:S(2)}, u32[]{:S(2)}) %collective-permute-start.8) | collective-permute-done | bytes 131104 | tf_op jit(solution)/shard_map/ppermute | solution.py:21
  46.4 0.8 %add_subtract_fusion = f32[384,256]{1,0:T(8,128)} fusion(f32[384,256]{1,0:T(8,128)S(1)} %copy-done.1, f32[128,256]{1,0:T(8,128)S(1)} %collective-permute-done.8, f32[384,256]{1,0:T(8,128)S(1)} %convolution_subtract_fusion, f32[128,256]{1,0:T(8,128)S(1)} %collective-permute-done.7), kind=kLoop, calls=%fused_computation.24 | loop fusion | flops 294912 | bytes 1441792 | tf_op jit(solution)/shard_map/sub | solution.py:138
  (16 shorter events, 0.2 us)
Async XLA Ops:
  0.0 17.9 %copy-start = (f32[2,512,512]{2,1,0:T(8,128)S(1)}, f32[2,512,512]{2,1,0:T(8,128)}, u32[]{:S(2)}) copy-start(f32[2,512,512]{2,1,0:T(8,128)} %param.8) | copy-start | bytes 6291460
  0.0 13.8 %collective-permute-start = (f32[4,16,128]{2,1,0:T(8,128)}, f32[4,16,128]{2,1,0:T(8,128)S(1)}, u32[]{:S(2)}, u32[]{:S(2)}) collective-permute-start(f32[4,16,128]{2,1,0:T(8,128)} %param.10), channel_id=1, source_target_pairs={{0,1},{1,2},{2,3},{3,0},{4,5},{5,6},{6,7},{7,4},{8,9},{9,10},{10,1... | collective-permute-start | bytes 98312 | tf_op jit(solution)/shard_map/ppermute | solution.py:30
  0.5 13.3 %collective-permute-start.2 = (f32[4,16,128]{2,1,0:T(8,128)}, f32[4,16,128]{2,1,0:T(8,128)S(1)}, u32[]{:S(2)}, u32[]{:S(2)}) collective-permute-start(f32[4,16,128]{2,1,0:T(8,128)} %param.10), channel_id=1, source_target_pairs={{0,3},{1,0},{2,1},{3,2},{4,7},{5,4},{6,5},{7,6},{8,11},{9,8},{10,9... | collective-permute-start | bytes 98312 | tf_op jit(solution)/shard_map/ppermute | solution.py:30
  2.4 11.4 %collective-permute-start.1 = (f32[4,16,128]{2,1,0:T(8,128)}, f32[4,16,128]{2,1,0:T(8,128)S(1)}, u32[]{:S(2)}, u32[]{:S(2)}) collective-permute-start(f32[4,16,128]{2,1,0:T(8,128)} %param.10), channel_id=1, source_target_pairs={{0,2},{1,3},{2,0},{3,1},{4,6},{5,7},{6,4},{7,5},{8,10},{9,11},{10,... | collective-permute-start | bytes 98312 | tf_op jit(solution)/shard_map/ppermute | solution.py:30
  5.7 10.6 %collective-permute-start.4 = (f32[128,256]{1,0:T(8,128)S(1)}, f32[128,256]{1,0:T(8,128)S(1)}, u32[]{:S(2)}, u32[]{:S(2)}) collective-permute-start(f32[128,256]{1,0:T(8,128)S(1)} %get-tuple-element.17), channel_id=1, source_target_pairs={{4,0},{8,4},{12,8},{16,12},{20,16},{24,20},{28,24},{5,1},{9,5},{13... | collective-permute-start | bytes 393224 | tf_op jit(solution)/shard_map/ppermute | solution.py:21
  7.0 9.2 %collective-permute-start.3 = (f32[128,256]{1,0:T(8,128)S(1)}, f32[128,256]{1,0:T(8,128)S(1)}, u32[]{:S(2)}, u32[]{:S(2)}) collective-permute-start(f32[128,256]{1,0:T(8,128)S(1)} %get-tuple-element.18), channel_id=1, source_target_pairs={{0,4},{4,8},{8,12},{12,16},{16,20},{20,24},{24,28},{1,5},{5,9},{9,... | collective-permute-start | bytes 393224 | tf_op jit(solution)/shard_map/ppermute | solution.py:16
  15.2 1.0 %copy-start.1 = (f32[384,256]{1,0:T(8,128)S(1)}, f32[384,256]{1,0:T(8,128)}, u32[]{:S(2)}) copy-start(f32[384,256]{1,0:T(8,128)} %param.7) | copy-start | bytes 1179652
  15.6 0.7 %copy-start.2 = (s32[2,512]{1,0:T(2,128)S(1)}, s32[2,512]{1,0:T(2,128)}, u32[]{:S(2)}) copy-start(s32[2,512]{1,0:T(2,128)} %param.9) | copy-start | bytes 12292
  20.6 13.8 %collective-permute-start.5 = (f32[256,256]{1,0:T(8,128)S(1)}, f32[256,256]{1,0:T(8,128)S(1)}, u32[]{:S(2)}, u32[]{:S(2)}) collective-permute-start(f32[256,256]{1,0:T(8,128)S(1)} %get-tuple-element.15), channel_id=1, source_target_pairs={{0,4},{4,8},{8,12},{12,16},{16,20},{20,24},{24,28},{1,5},{5,9},{9,... | collective-permute-start | bytes 786440 | tf_op jit(solution)/shard_map/ppermute | solution.py:16
  25.0 9.5 %collective-permute-start.6 = (f32[256,256]{1,0:T(8,128)S(1)}, f32[256,256]{1,0:T(8,128)S(1)}, u32[]{:S(2)}, u32[]{:S(2)}) collective-permute-start(f32[256,256]{1,0:T(8,128)S(1)} %get-tuple-element.16), channel_id=1, source_target_pairs={{4,0},{8,4},{12,8},{16,12},{20,16},{24,20},{28,24},{5,1},{9,5},{13... | collective-permute-start | bytes 786440 | tf_op jit(solution)/shard_map/ppermute | solution.py:21
  35.2 6.9 %collective-permute-start.7 = (f32[128,256]{1,0:T(8,128)S(1)}, f32[128,256]{1,0:T(8,128)S(1)}, u32[]{:S(2)}, u32[]{:S(2)}) collective-permute-start(f32[128,256]{1,0:T(8,128)S(1)} %get-tuple-element.19), channel_id=1, source_target_pairs={{0,4},{4,8},{8,12},{12,16},{16,20},{20,24},{24,28},{1,5},{5,9},{9,... | collective-permute-start | bytes 393224 | tf_op jit(solution)/shard_map/ppermute | solution.py:16
  39.6 6.9 %collective-permute-start.8 = (f32[128,256]{1,0:T(8,128)S(1)}, f32[128,256]{1,0:T(8,128)S(1)}, u32[]{:S(2)}, u32[]{:S(2)}) collective-permute-start(f32[128,256]{1,0:T(8,128)S(1)} %get-tuple-element.20), channel_id=1, source_target_pairs={{4,0},{8,4},{12,8},{16,12},{20,16},{24,20},{28,24},{5,1},{9,5},{13... | collective-permute-start | bytes 393224 | tf_op jit(solution)/shard_map/ppermute | solution.py:21

commit v17 on v16

--- a/solution.py
+++ b/solution.py
@@ -92,21 +92,30 @@
     coefficients = jnp.dot(placed, extended, precision=high) * weights[:, None]
     gathered = jnp.dot(onehot, extended, precision=high).reshape(cells, nodes, -1)
     local = jnp.einsum("cij,cjb->cib", cell_matrix, gathered, precision=high)
-    first = scatter_rows(onehot, local.reshape(cells * nodes, -1)) + jnp.dot(
-        placed.T, coefficients, precision=high
+    local = local.reshape(cells * nodes, -1)
+    scaled = placed.T
+    first_outer = jnp.concatenate(
+        [
+            scatter_rows(onehot[:, part], local) + jnp.dot(scaled[part], coefficients, precision=high)
+            for part in (slice(0, 2 * g), slice(ext - 2 * g, ext))
+        ],
+        axis=0,
     )
-
-    matrices, placed_late, weights_late, first = lax.optimization_barrier(
-        (cell_matrix, placed, weights, first)
+    matrices, placed_late, weights_late, local, coefficients, first_outer = (
+        lax.optimization_barrier((cell_matrix, placed, weights, local, coefficients, first_outer))
     )
+    middle = scatter_rows(onehot[:, 2 * g : ext - 2 * g], local) + jnp.dot(
+        placed_late.T[2 * g : ext - 2 * g], coefficients, precision=high
+    )
+    first = jnp.concatenate([first_outer[: 2 * g], middle, first_outer[2 * g :]], axis=0)
     moved = jnp.einsum(
         "cij,cjq->ciq", matrices, onehot.reshape(cells, nodes, ext), precision=high
     )
     operator = scatter_rows(onehot, moved.reshape(cells * nodes, ext)) + jnp.dot(
         (placed_late * weights_late[:, None]).T, placed_late, precision=highest
     )
-    left_sums = from_left(first[ext - 2 * g :], "dom")
-    right_sums = from_right(first[: 2 * g], "dom")
+    left_sums = from_left(first_outer[2 * g :], "dom")
+    right_sums = from_right(first_outer[: 2 * g], "dom")
     zeros_side = jnp.zeros((ext - 2 * g, first.shape[1]), jnp.float32)
     first_image = (
         first

time: 47.6 us -> 56.7 us (1.19)
  matrix products: 11.2 us -> 16.1 us
  local copies, waits for them, and re-layouts: 1.85 us -> 4.92 us
  waiting for transfers between devices: 7.18 us -> 5.77 us
  other arithmetic: 4.2 us -> 5.52 us
  starting transfers between devices: 21.8 us -> 22.7 us
    dot_general x2 -> x4, matrix products: 3.16 us -> 7.03 us  [scatter_rows(): lax.dot_general(onehot, values, (((0,), (0,)), ((), ())), precision=lax.P...]
    dot_general x0 -> x1, local copies, waits for them, and re-layouts: none -> 1.55 us  [on_device(): local = jnp.einsum('cij,cjb->cib', cell_matrix, gathered, precision=high)]
    unnamed x8 -> x15, local copies, waits for them, and re-layouts: 0.09 us -> 1.61 us
    eq x0 -> x1, other arithmetic: none -> 1.31 us  [cell_rows(): connectivity[:, :, None] == rows[None, None, :]]
    ppermute x3, waiting for transfers between devices: 2.8 us -> 1.64 us  [from_left(): return lax.ppermute(x, axis, [(i, i + 1) for i in range(count - 1)])]
    dot_general x1, matrix products: 1.02 us -> 2.06 us  [on_device(): local = jnp.einsum('cij,cjb->cib', cell_matrix, gathered, precision=high)]
    ppermute x3, starting transfers between devices: 13.3 us -> 14.1 us  [from_left(): return lax.ppermute(x, axis, [(i, i + 1) for i in range(count - 1)])]
  transfers between devices with their start and end apart: 9 -> 9, of which waited for: 3 -> 3; matrix products, arithmetic and copies ran while one was open for 24% -> 27% of each run, Pallas kernels for 0% -> 0%
where the time goes in v17:
time: 56.7 us; the launch traced here: 56.1 us
  starting transfers between devices  22.7 us (40%)
  matrix products  16.1 us (28%)
  waiting for transfers between devices  5.77 us (10%)
  other arithmetic  5.52 us (10%)
  local copies, waits for them, and re-layouts  4.92 us (9%)
  between operations  1.07 us (2%)
    ppermute x3, starting transfers between devices, from_left(): return lax.ppermute(x, axis, [(i, i + 1) for i in range(count - 1)])  14.1 us
    dot_general x4, matrix products, scatter_rows(): lax.dot_general(onehot, values, (((0,), (0,)), ((), ())), precision=lax.P...  7.03 us
    ppermute x3, starting transfers between devices, gather_band(): lax.ppermute(piece, 'band', [(i, (i + k) % count) for i in range(count)])  4.68 us
    ppermute x3, waiting for transfers between devices, from_right(): return lax.ppermute(x, axis, [(i + 1, i) for i in range(count - 1)])  4.13 us
    ppermute x3, starting transfers between devices, from_right(): return lax.ppermute(x, axis, [(i + 1, i) for i in range(count - 1)])  3.88 us
    dot_general x1, matrix products, on_device(): local = jnp.einsum('cij,cjb->cib', cell_matrix, gathered, precision=high)  2.06 us
    dot_general x1, matrix products, on_device(): jnp.einsum('cij,cjq->ciq', matrices, onehot.reshape(cells, nodes, ext), p...  1.95 us
    ppermute x3, waiting for transfers between devices, from_left(): return lax.ppermute(x, axis, [(i, i + 1) for i in range(count - 1)])  1.64 us
  transfers between devices with their start and end apart: 9, of which 3 were waited for; matrix products, arithmetic and copies ran while one was open for 27% of the time, Pallas kernels for 0%

profile of v17, /device:TPU:0, one launch (start us, length us, event | category | flops | bytes accessed | tf_op | source)
XLA Modules:
  0.0 56.1 jit_solution(5135094637395070398)
XLA Ops:
  0.0 0.5 collective-permute-start
  0.5 2.0 %collective-permute-start.2 = (f32[4,16,128]{2,1,0:T(8,128)}, f32[4,16,128]{2,1,0:T(8,128)S(1)}, u32[]{:S(2)}, u32[]{:S(2)}) collective-permute-start(f32[4,16,128]{2,1,0:T(8,128)} %param.10), channel_id=1, source_target_pairs={{0,3},{1,0},{2,1},{3,2},{4,7},{5,4},{6,5},{7,6},{8,11},{9,8},{10,9... | collective-permute-start | bytes 98312 | tf_op jit(solution)/shard_map/ppermute | solution.py:30
  2.4 2.2 %collective-permute-start.1 = (f32[4,16,128]{2,1,0:T(8,128)}, f32[4,16,128]{2,1,0:T(8,128)S(1)}, u32[]{:S(2)}, u32[]{:S(2)}) collective-permute-start(f32[4,16,128]{2,1,0:T(8,128)} %param.10), channel_id=1, source_target_pairs={{0,2},{1,3},{2,0},{3,1},{4,6},{5,7},{6,4},{7,5},{8,10},{9,11},{10,... | collective-permute-start | bytes 98312 | tf_op jit(solution)/shard_map/ppermute | solution.py:30
  4.7 1.0 %fusion.37 = (f32[128,256]{1,0:T(8,128)S(1)}, f32[128,256]{1,0:T(8,128)S(1)}) fusion(f32[384,256]{1,0:T(8,128)} %param.7), kind=kLoop, calls=%fused_computation.89 | loop fusion | bytes 524288 | tf_op jit(solution)/shard_map/slice | solution.py:84
  5.7 1.3 %collective-permute-start.4 = (f32[128,256]{1,0:T(8,128)S(1)}, f32[128,256]{1,0:T(8,128)S(1)}, u32[]{:S(2)}, u32[]{:S(2)}) collective-permute-start(f32[128,256]{1,0:T(8,128)S(1)} %get-tuple-element.21), channel_id=1, source_target_pairs={{4,0},{8,4},{12,8},{16,12},{20,16},{24,20},{28,24},{5,1},{9,5},{13... | collective-permute-start | bytes 393224 | tf_op jit(solution)/shard_map/ppermute | solution.py:21
  7.0 4.6 %collective-permute-start.3 = (f32[128,256]{1,0:T(8,128)S(1)}, f32[128,256]{1,0:T(8,128)S(1)}, u32[]{:S(2)}, u32[]{:S(2)}) collective-permute-start(f32[128,256]{1,0:T(8,128)S(1)} %get-tuple-element.22), channel_id=1, source_target_pairs={{0,4},{4,8},{8,12},{12,16},{16,20},{20,24},{24,28},{1,5},{5,9},{9,... | collective-permute-start | bytes 393224 | tf_op jit(solution)/shard_map/ppermute | solution.py:16
  12.2 0.7 %copy.11 = s32[1,4,2,128]{3,1,2,0:T(4,128)S(1)} copy(s32[1,4,2,128]{3,2,1,0:T(2,128)} %bitcast.68) | data formatting | bytes 8192
  12.9 0.7 %and_compare_fusion.7 = (pred[4]{0:T(512)(128)(4,1)S(1)}, pred[4]{0:T(512)(128)(4,1)S(1)}, pred[4]{0:T(512)(128)(4,1)S(1)}, pred[4]{0:T(512)(128)(4,1)S(1)}, pre...) fusion(s32[4]{0:T(128)} %param.12), kind=kLoop, calls=%fused_computation.84 | loop fusion | flops 100 | bytes 48 | tf_op jit(solution)/shard_map/eq | solution.py:45
  13.6 1.3 %iota_compare_fusion = pred[1024,640]{1,0:T(32,128)(4,1)} fusion(s32[1024]{0:T(1024)S(1)} %bitcast.67), kind=kLoop, calls=%fused_computation.1 | loop fusion | flops 655360 | bytes 659456 | tf_op jit(solution)/shard_map/eq | solution.py:64
  14.9 0.8 %broadcast_multiply_fusion = f32[4,16]{1,0:T(4,128)S(1)} fusion(f32[4,16]{1,0:T(4,128)} %param.11, f32[4]{0:T(128)S(1)} %compare_convert_fusion), kind=kLoop, calls=%fused_computation.73 | loop fusion | flops 64 | bytes 528 | tf_op jit(solution)/shard_map/mul | solution.py:57
  15.7 0.1 reshape.125
  15.8 0.8 %pad_maximum_fusion.1 = f32[4,4,16,128]{3,2,1,0:T(8,128)S(1)} fusion(f32[1,4,16,128]{3,2,1,0:T(8,128)S(1)} %bitcast.65, f32[1,4,16,128]{3,2,1,0:T(8,128)S(1)} %bitcast.66, f32[1,4,16,128]{3,2,1,0:T(8,128)S(1)} %bitcast.64, f32[1,4,16,128]{3,2,1,0:T(8,128)} %bitcast.63), kind=kLoop, calls=%fused_computation.47 | loop fusion | flops 98304 | bytes 262144 | tf_op jit(solution)/shard_map/stack | solution.py:32
  16.6 0.6 gather_fusion
  17.1 0.1 copy_bitcast_fusion
  17.2 0.1 pad_select_fusion
  17.4 0.1 pad_select_fusion.7
  17.5 0.1 pad_select_fusion.6
  17.6 0.1 pad_select_fusion.5
  17.7 0.1 pad_select_fusion.4
  17.8 0.1 pad_select_fusion.3
  18.0 0.1 pad_select_fusion.2
  18.1 0.1 pad_select_fusion.1
  18.2 0.0 copy-done.3
  18.3 0.8 %copy-done.1 = f32[640,256]{1,0:T(8,128)} copy-done((f32[640,256]{1,0:T(8,128)}, f32[640,256]{1,0:T(8,128)S(1)}, u32[]{:S(2)}) %copy-start.1) | copy-done | bytes 655384
  19.1 1.1 %fusion.2 = f32[2,512,256]{1,2,0:T(8,128)S(1)} fusion(s32[2,512]{1,0:T(2,128)S(1)} %copy-done.5, f32[640,256]{1,0:T(8,128)S(1)} %constant_dynamic-update-slice_fusion), kind=kOutput, calls=%fused_computation.5 | convolution fusion | flops 1007288320 | bytes 1708032 | tf_op jit(solution)/shard_map/dot_general | solution.py:93
  20.3 2.1 %convolution_bitcast_fusion = f32[2,512,256]{1,2,0:T(8,128)} fusion(f32[2,512,256]{1,2,0:T(8,128)S(1)} %fusion.2, f32[2,512,512]{2,1,0:T(8,128)S(1)} %copy-done), kind=kOutput, calls=%fused_computation.7 | convolution fusion | flops 805306368 | bytes 4194304 | tf_op jit(solution)/shard_map/cij,cjb->cib/dot_general | solution.py:94
  22.3 1.6 %copy.9 = f32[2,512,256]{2,1,0:T(8,128)S(1)} copy(f32[2,512,256]{1,2,0:T(8,128)} %convolution_bitcast_fusion) | data formatting | bytes 2097152 | tf_op jit(solution)/shard_map/cij,cjb->cib/dot_general | solution.py:94
  23.9 1.8 %fusion.6 = f32[256,256]{1,0:T(8,128)S(1)} fusion(f32[1024,256]{1,0:T(8,128)S(1)} %bitcast.49, pred[1024,640]{1,0:T(32,128)(4,1)} %iota_compare_fusion), kind=kOutput, calls=%fused_computation.16 | convolution fusion | flops 402653184 | bytes 1572864 | tf_op jit(solution)/shard_map/dot_general | solution.py:69
  25.7 1.7 %fusion.8 = f32[256,256]{1,0:T(8,128)S(1)} fusion(f32[1024,256]{1,0:T(8,128)S(1)} %bitcast.50, pred[1024,640]{1,0:T(32,128)(4,1)} %iota_compare_fusion), kind=kOutput, calls=%fused_computation.18 | convolution fusion | flops 402653184 | bytes 1572864 | tf_op jit(solution)/shard_map/dot_general | solution.py:69
  27.4 0.3 convolution_multiply_fusion
  27.7 0.3 convolution_add_fusion
  28.0 0.3 convolution_add_fusion.1
  28.4 1.3 %collective-permute-start.6 = (f32[256,256]{1,0:T(8,128)S(1)}, f32[256,256]{1,0:T(8,128)S(1)}, u32[]{:S(2)}, u32[]{:S(2)}) collective-permute-start(f32[256,256]{1,0:T(8,128)S(1)} %get-tuple-element.19), channel_id=1, source_target_pairs={{4,0},{8,4},{12,8},{16,12},{20,16},{24,20},{28,24},{5,1},{9,5},{13... | collective-permute-start | bytes 786440 | tf_op jit(solution)/shard_map/ppermute | solution.py:21
  29.7 5.1 %collective-permute-start.5 = (f32[256,256]{1,0:T(8,128)S(1)}, f32[256,256]{1,0:T(8,128)S(1)}, u32[]{:S(2)}, u32[]{:S(2)}) collective-permute-start(f32[256,256]{1,0:T(8,128)S(1)} %get-tuple-element.20), channel_id=1, source_target_pairs={{0,4},{4,8},{8,12},{12,16},{16,20},{20,24},{24,28},{1,5},{5,9},{9,... | collective-permute-start | bytes 786440 | tf_op jit(solution)/shard_map/ppermute | solution.py:16
  34.9 1.9 %fusion.1 = f32[2,512,640]{2,1,0:T(8,128)S(1)} fusion(f32[2,512,512]{2,1,0:T(8,128)S(1)} %copy-done, s32[2,512]{1,0:T(2,128)S(1)} %copy-done.5), kind=kOutput, calls=%fused_computation.4 | convolution fusion | flops 2013921280 | bytes 4722688 | tf_op jit(solution)/shard_map/cij,cjq->ciq/dot_general | solution.py:111
  36.8 1.6 %fusion.21 = f32[640,640]{1,0:T(8,128)S(1)} fusion(f32[64,640]{1,0:T(8,128)S(1)} %bitcast.55, f32[64]{0:T(128)S(1)} %reshape.125), kind=kOutput, calls=%fused_computation.35 | convolution fusion | flops 314613760 | bytes 1802496 | tf_op jit(solution)/shard_map/dot_general | solution.py:114
  38.4 2.3 %bitcast_add_fusion = f32[640,640]{1,0:T(8,128)S(1)} fusion(f32[640,640]{1,0:T(8,128)S(1)} %fusion.21, f32[2,512,640]{2,1,0:T(8,128)S(1)} %fusion.1, s32[2,512]{1,0:T(2,128)S(1)} %copy-done.5), kind=kOutput, calls=%fused_computation.6 | convolution fusion | flops 2517647360 | bytes 5902336 | tf_op jit(solution)/shard_map/dot_general | solution.py:69
  40.8 0.3 fusion.26
  41.1 1.3 %convolution_add_fusion.2 = f32[128,256]{1,0:T(8,128)S(1)} fusion(f32[128,256]{1,0:T(8,128)S(1)} %fusion.26, f32[1024,256]{1,0:T(8,128)S(1)} %bitcast.51, pred[1024,640]{1,0:T(32,128)(4,1)} %iota_compare_fusion), kind=kOutput, calls=%fused_computation.14 | convolution fusion | flops 201359360 | bytes 1441792 | tf_op jit(solution)/shard_map/dot_general | solution.py:69
  42.4 0.7 %collective-permute-done.5 = f32[256,256]{1,0:T(8,128)S(1)} collective-permute-done((f32[256,256]{1,0:T(8,128)S(1)}, f32[256,256]{1,0:T(8,128)S(1)}, u32[]{:S(2)}, u32[]{:S(2)}) %collective-permute-start.5) | collective-permute-done | bytes 262176 | tf_op jit(solution)/shard_map/ppermute | solution.py:16
  43.1 0.2 fusion.14
  43.3 0.5 fusion.15
  43.8 4.4 %collective-permute-start.7 = (f32[128,256]{1,0:T(8,128)S(1)}, f32[128,256]{1,0:T(8,128)S(1)}, u32[]{:S(2)}, u32[]{:S(2)}) collective-permute-start(f32[128,256]{1,0:T(8,128)S(1)} %get-tuple-element.23), channel_id=1, source_target_pairs={{0,4},{4,8},{8,12},{12,16},{16,20},{20,24},{24,28},{1,5},{5,9},{9,... | collective-permute-start | bytes 393224 | tf_op jit(solution)/shard_map/ppermute | solution.py:16
  48.2 1.3 %collective-permute-start.8 = (f32[128,256]{1,0:T(8,128)S(1)}, f32[128,256]{1,0:T(8,128)S(1)}, u32[]{:S(2)}, u32[]{:S(2)}) collective-permute-start(f32[128,256]{1,0:T(8,128)S(1)} %get-tuple-element.24), channel_id=1, source_target_pairs={{4,0},{8,4},{12,8},{16,12},{20,16},{24,20},{28,24},{5,1},{9,5},{13... | collective-permute-start | bytes 393224 | tf_op jit(solution)/shard_map/ppermute | solution.py:21
  49.5 0.7 %convolution_subtract_fusion = f32[384,256]{1,0:T(8,128)S(1)} fusion(f32[640,256]{1,0:T(8,128)S(1)} %fusion.14, f32[640,640]{1,0:T(8,128)S(1)} %bitcast_add_fusion), kind=kOutput, calls=%fused_computation.11 | convolution fusion | flops 377683968 | bytes 2424832 | tf_op jit(solution)/shard_map/dot_general | solution.py:138
  50.2 0.9 %collective-permute-done.7 = f32[128,256]{1,0:T(8,128)S(1)} collective-permute-done((f32[128,256]{1,0:T(8,128)S(1)}, f32[128,256]{1,0:T(8,128)S(1)}, u32[]{:S(2)}, u32[]{:S(2)}) %collective-permute-start.7) | collective-permute-done | bytes 131104 | tf_op jit(solution)/shard_map/ppermute | solution.py:16
  51.1 4.1 %collective-permute-done.8 = f32[128,256]{1,0:T(8,128)S(1)} collective-permute-done((f32[128,256]{1,0:T(8,128)S(1)}, f32[128,256]{1,0:T(8,128)S(1)}, u32[]{:S(2)}, u32[]{:S(2)}) %collective-permute-start.8) | collective-permute-done | bytes 131104 | tf_op jit(solution)/shard_map/ppermute | solution.py:21
  55.2 0.8 %add_subtract_fusion = f32[384,256]{1,0:T(8,128)} fusion(f32[384,256]{1,0:T(8,128)S(1)} %copy-done.4, f32[128,256]{1,0:T(8,128)S(1)} %collective-permute-done.8, f32[384,256]{1,0:T(8,128)S(1)} %convolution_subtract_fusion, f32[128,256]{1,0:T(8,128)S(1)} %collective-permute-done.7), kind=kLoop, calls=%fused_computation.34 | loop fusion | flops 294912 | bytes 1441792 | tf_op jit(solution)/shard_map/sub | solution.py:147
  (30 shorter events, 0.3 us)
Async XLA Ops:
  0.0 20.3 %copy-start = (f32[2,512,512]{2,1,0:T(8,128)S(1)}, f32[2,512,512]{2,1,0:T(8,128)}, u32[]{:S(2)}) copy-start(f32[2,512,512]{2,1,0:T(8,128)} %param.8) | copy-start | bytes 6291460
  0.0 15.8 %collective-permute-start = (f32[4,16,128]{2,1,0:T(8,128)}, f32[4,16,128]{2,1,0:T(8,128)S(1)}, u32[]{:S(2)}, u32[]{:S(2)}) collective-permute-start(f32[4,16,128]{2,1,0:T(8,128)} %param.10), channel_id=1, source_target_pairs={{0,1},{1,2},{2,3},{3,0},{4,5},{5,6},{6,7},{7,4},{8,9},{9,10},{10,1... | collective-permute-start | bytes 98312 | tf_op jit(solution)/shard_map/ppermute | solution.py:30
  0.5 15.3 %collective-permute-start.2 = (f32[4,16,128]{2,1,0:T(8,128)}, f32[4,16,128]{2,1,0:T(8,128)S(1)}, u32[]{:S(2)}, u32[]{:S(2)}) collective-permute-start(f32[4,16,128]{2,1,0:T(8,128)} %param.10), channel_id=1, source_target_pairs={{0,3},{1,0},{2,1},{3,2},{4,7},{5,4},{6,5},{7,6},{8,11},{9,8},{10,9... | collective-permute-start | bytes 98312 | tf_op jit(solution)/shard_map/ppermute | solution.py:30
  2.4 13.3 %collective-permute-start.1 = (f32[4,16,128]{2,1,0:T(8,128)}, f32[4,16,128]{2,1,0:T(8,128)S(1)}, u32[]{:S(2)}, u32[]{:S(2)}) collective-permute-start(f32[4,16,128]{2,1,0:T(8,128)} %param.10), channel_id=1, source_target_pairs={{0,2},{1,3},{2,0},{3,1},{4,6},{5,7},{6,4},{7,5},{8,10},{9,11},{10,... | collective-permute-start | bytes 98312 | tf_op jit(solution)/shard_map/ppermute | solution.py:30
  5.7 12.6 %collective-permute-start.4 = (f32[128,256]{1,0:T(8,128)S(1)}, f32[128,256]{1,0:T(8,128)S(1)}, u32[]{:S(2)}, u32[]{:S(2)}) collective-permute-start(f32[128,256]{1,0:T(8,128)S(1)} %get-tuple-element.21), channel_id=1, source_target_pairs={{4,0},{8,4},{12,8},{16,12},{20,16},{24,20},{28,24},{5,1},{9,5},{13... | collective-permute-start | bytes 393224 | tf_op jit(solution)/shard_map/ppermute | solution.py:21
  7.0 11.2 %collective-permute-start.3 = (f32[128,256]{1,0:T(8,128)S(1)}, f32[128,256]{1,0:T(8,128)S(1)}, u32[]{:S(2)}, u32[]{:S(2)}) collective-permute-start(f32[128,256]{1,0:T(8,128)S(1)} %get-tuple-element.22), channel_id=1, source_target_pairs={{0,4},{4,8},{8,12},{12,16},{16,20},{20,24},{24,28},{1,5},{5,9},{9,... | collective-permute-start | bytes 393224 | tf_op jit(solution)/shard_map/ppermute | solution.py:16
  17.2 1.0 %copy-start.3 = (f32[384,256]{1,0:T(8,128)S(1)}, f32[384,256]{1,0:T(8,128)}, u32[]{:S(2)}) copy-start(f32[384,256]{1,0:T(8,128)} %param.7) | copy-start | bytes 1179652
  17.6 1.5 %copy-start.5 = (s32[2,512]{1,0:T(2,128)S(1)}, s32[2,512]{1,0:T(2,128)}, u32[]{:S(2)}) copy-start(s32[2,512]{1,0:T(2,128)} %param.9) | copy-start | bytes 12292
  18.3 0.8 %copy-start.1 = (f32[640,256]{1,0:T(8,128)}, f32[640,256]{1,0:T(8,128)S(1)}, u32[]{:S(2)}) copy-start(f32[640,256]{1,0:T(8,128)S(1)} %constant_dynamic-update-slice_fusion) | copy-start | bytes 1966084
  23.9 3.5 %copy-start.2 = (f32[640,256]{1,0:T(8,128)S(1)}, f32[640,256]{1,0:T(8,128)}, u32[]{:S(2)}) copy-start(f32[640,256]{1,0:T(8,128)} %copy-done.1) | copy-start | bytes 1966084
  28.4 13.9 %collective-permute-start.6 = (f32[256,256]{1,0:T(8,128)S(1)}, f32[256,256]{1,0:T(8,128)S(1)}, u32[]{:S(2)}, u32[]{:S(2)}) collective-permute-start(f32[256,256]{1,0:T(8,128)S(1)} %get-tuple-element.19), channel_id=1, source_target_pairs={{4,0},{8,4},{12,8},{16,12},{20,16},{24,20},{28,24},{5,1},{9,5},{13... | collective-permute-start | bytes 786440 | tf_op jit(solution)/shard_map/ppermute | solution.py:21
  29.7 13.4 %collective-permute-start.5 = (f32[256,256]{1,0:T(8,128)S(1)}, f32[256,256]{1,0:T(8,128)S(1)}, u32[]{:S(2)}, u32[]{:S(2)}) collective-permute-start(f32[256,256]{1,0:T(8,128)S(1)} %get-tuple-element.20), channel_id=1, source_target_pairs={{0,4},{4,8},{8,12},{12,16},{16,20},{20,24},{24,28},{1,5},{5,9},{9,... | collective-permute-start | bytes 786440 | tf_op jit(solution)/shard_map/ppermute | solution.py:16
  43.3 12.0 %copy-start.4 = (f32[384,256]{1,0:T(8,128)S(1)}, f32[384,256]{1,0:T(8,128)}, u32[]{:S(2)}) copy-start(f32[384,256]{1,0:T(8,128)} %param.7) | copy-start | bytes 1179652
  43.8 7.3 %collective-permute-start.7 = (f32[128,256]{1,0:T(8,128)S(1)}, f32[128,256]{1,0:T(8,128)S(1)}, u32[]{:S(2)}, u32[]{:S(2)}) collective-permute-start(f32[128,256]{1,0:T(8,128)S(1)} %get-tuple-element.23), channel_id=1, source_target_pairs={{0,4},{4,8},{8,12},{12,16},{16,20},{20,24},{24,28},{1,5},{5,9},{9,... | collective-permute-start | bytes 393224 | tf_op jit(solution)/shard_map/ppermute | solution.py:16
  48.2 7.0 %collective-permute-start.8 = (f32[128,256]{1,0:T(8,128)S(1)}, f32[128,256]{1,0:T(8,128)S(1)}, u32[]{:S(2)}, u32[]{:S(2)}) collective-permute-start(f32[128,256]{1,0:T(8,128)S(1)} %get-tuple-element.24), channel_id=1, source_target_pairs={{4,0},{8,4},{12,8},{16,12},{20,16},{24,20},{28,24},{5,1},{9,5},{13... | collective-permute-start | bytes 393224 | tf_op jit(solution)/shard_map/ppermute | solution.py:21

commit v18 on v16

--- a/solution.py
+++ b/solution.py
@@ -89,11 +89,13 @@
     cells, nodes, _ = cell_matrix.shape
     high = lax.Precision.HIGH
 
-    coefficients = jnp.dot(placed, extended, precision=high) * weights[:, None]
-    gathered = jnp.dot(onehot, extended, precision=high).reshape(cells, nodes, -1)
+    maps = jnp.concatenate([onehot, placed], axis=0)
+    picked = jnp.dot(maps, extended, precision=high)
+    gathered = picked[: cells * nodes].reshape(cells, nodes, -1)
+    coefficients = picked[cells * nodes :] * weights[:, None]
     local = jnp.einsum("cij,cjb->cib", cell_matrix, gathered, precision=high)
-    first = scatter_rows(onehot, local.reshape(cells * nodes, -1)) + jnp.dot(
-        placed.T, coefficients, precision=high
+    first = scatter_rows(
+        maps, jnp.concatenate([local.reshape(cells * nodes, -1), coefficients], axis=0)
     )
 
     matrices, placed_late, weights_late, first = lax.optimization_barrier(

time: 47.6 us -> 56.5 us (1.19)
  matrix products: 11.2 us -> 15.6 us
  waiting for transfers between devices: 7.18 us -> 10 us
  local copies, waits for them, and re-layouts: 1.85 us -> 4.15 us
  starting transfers between devices: 21.8 us -> 20.7 us
    ppermute x3, waiting for transfers between devices: 2.8 us -> 7.73 us  [from_left(): return lax.ppermute(x, axis, [(i, i + 1) for i in range(count - 1)])]
    dot_general x2, matrix products: 3.16 us -> 6.56 us  [scatter_rows(): lax.dot_general(onehot, values, (((0,), (0,)), ((), ())), precision=lax.P...]
    ppermute x3, waiting for transfers between devices: 4.37 us -> 2.29 us  [from_right(): return lax.ppermute(x, axis, [(i + 1, i) for i in range(count - 1)])]
    dot_general x1, matrix products: 1.02 us -> 2.91 us  [on_device(): local = jnp.einsum('cij,cjb->cib', cell_matrix, gathered, precision=high)]
    convert_element_type x0 -> x1, other arithmetic: none -> 1.74 us  [cell_rows(): (connectivity[:, :, None] == rows[None, None, :]).astype(jnp.float32)]
    dot_general x0 -> x1, local copies, waits for them, and re-layouts: none -> 1.55 us  [on_device(): local = jnp.einsum('cij,cjb->cib', cell_matrix, gathered, precision=high)]
    ppermute x3, starting transfers between devices: 4.68 us -> 3.24 us  [gather_band(): lax.ppermute(piece, 'band', [(i, (i + k) % count) for i in range(count)])]
    dot_general x3 -> x1, matrix products: 2.34 us -> 1.5 us  [on_device(): picked = jnp.dot(maps, extended, precision=high)]
  transfers between devices with their start and end apart: 9 -> 9, of which waited for: 3 -> 4; matrix products, arithmetic and copies ran while one was open for 24% -> 22% of each run, Pallas kernels for 0% -> 0%
where the time goes in v18:
time: 56.5 us; the launch traced here: 56.1 us
  starting transfers between devices  20.7 us (37%)
  matrix products  15.6 us (28%)
  waiting for transfers between devices  10 us (18%)
  other arithmetic  4.55 us (8%)
  local copies, waits for them, and re-layouts  4.15 us (7%)
  between operations  1.05 us (2%)
    ppermute x3, starting transfers between devices, from_left(): return lax.ppermute(x, axis, [(i, i + 1) for i in range(count - 1)])  13.6 us
    ppermute x3, waiting for transfers between devices, from_left(): return lax.ppermute(x, axis, [(i, i + 1) for i in range(count - 1)])  7.73 us
    dot_general x2, matrix products, scatter_rows(): lax.dot_general(onehot, values, (((0,), (0,)), ((), ())), precision=lax.P...  6.56 us
    ppermute x3, starting transfers between devices, from_right(): return lax.ppermute(x, axis, [(i + 1, i) for i in range(count - 1)])  3.88 us
    ppermute x3, starting transfers between devices, gather_band(): lax.ppermute(piece, 'band', [(i, (i + k) % count) for i in range(count)])  3.24 us
    dot_general x1, matrix products, on_device(): local = jnp.einsum('cij,cjb->cib', cell_matrix, gathered, precision=high)  2.91 us
    ppermute x3, waiting for transfers between devices, from_right(): return lax.ppermute(x, axis, [(i + 1, i) for i in range(count - 1)])  2.29 us
    dot_general x1, matrix products, on_device(): jnp.einsum('cij,cjq->ciq', matrices, onehot.reshape(cells, nodes, ext), p...  1.95 us
  transfers between devices with their start and end apart: 9, of which 4 were waited for; matrix products, arithmetic and copies ran while one was open for 22% of the time, Pallas kernels for 0%

profile of v18, /device:TPU:0, one launch (start us, length us, event | category | flops | bytes accessed | tf_op | source)
XLA Modules:
  0.0 56.1 jit_solution(1513269203793605780)
XLA Ops:
  0.0 2.4 %collective-permute-start.2 = (f32[4,16,128]{2,1,0:T(8,128)}, f32[4,16,128]{2,1,0:T(8,128)S(1)}, u32[]{:S(2)}, u32[]{:S(2)}) collective-permute-start(f32[4,16,128]{2,1,0:T(8,128)} %param.10), channel_id=1, source_target_pairs={{0,3},{1,0},{2,1},{3,2},{4,7},{5,4},{6,5},{7,6},{8,11},{9,8},{10,9... | collective-permute-start | bytes 98312 | tf_op jit(solution)/shard_map/ppermute | solution.py:30
  2.4 0.6 %collective-permute-start.1 = (f32[4,16,128]{2,1,0:T(8,128)}, f32[4,16,128]{2,1,0:T(8,128)S(1)}, u32[]{:S(2)}, u32[]{:S(2)}) collective-permute-start(f32[4,16,128]{2,1,0:T(8,128)} %param.10), channel_id=1, source_target_pairs={{0,2},{1,3},{2,0},{3,1},{4,6},{5,7},{6,4},{7,5},{8,10},{9,11},{10,... | collective-permute-start | bytes 98312 | tf_op jit(solution)/shard_map/ppermute | solution.py:30
  3.1 0.2 collective-permute-start
  3.2 1.0 %fusion.29 = (f32[128,256]{1,0:T(8,128)S(1)}, f32[128,256]{1,0:T(8,128)S(1)}) fusion(f32[384,256]{1,0:T(8,128)} %param.7), kind=kLoop, calls=%fused_computation.78 | loop fusion | bytes 524288 | tf_op jit(solution)/shard_map/slice | solution.py:84
  4.2 3.4 %collective-permute-start.3 = (f32[128,256]{1,0:T(8,128)S(1)}, f32[128,256]{1,0:T(8,128)S(1)}, u32[]{:S(2)}, u32[]{:S(2)}) collective-permute-start(f32[128,256]{1,0:T(8,128)S(1)} %get-tuple-element.18), channel_id=1, source_target_pairs={{0,4},{4,8},{8,12},{12,16},{16,20},{20,24},{24,28},{1,5},{5,9},{9,... | collective-permute-start | bytes 393224 | tf_op jit(solution)/shard_map/ppermute | solution.py:16
  7.7 1.3 %collective-permute-start.4 = (f32[128,256]{1,0:T(8,128)S(1)}, f32[128,256]{1,0:T(8,128)S(1)}, u32[]{:S(2)}, u32[]{:S(2)}) collective-permute-start(f32[128,256]{1,0:T(8,128)S(1)} %get-tuple-element.17), channel_id=1, source_target_pairs={{4,0},{8,4},{12,8},{16,12},{20,16},{24,20},{28,24},{5,1},{9,5},{13... | collective-permute-start | bytes 393224 | tf_op jit(solution)/shard_map/ppermute | solution.py:21
  9.0 0.7 %and_compare_fusion.7 = (pred[4]{0:T(512)(128)(4,1)S(1)}, pred[4]{0:T(512)(128)(4,1)S(1)}, pred[4]{0:T(512)(128)(4,1)S(1)}, pred[4]{0:T(512)(128)(4,1)S(1)}, pre...) fusion(s32[4]{0:T(128)} %param.12), kind=kLoop, calls=%fused_computation.71 | loop fusion | flops 100 | bytes 48 | tf_op jit(solution)/shard_map/eq | solution.py:45
  10.3 0.7 %copy.14 = s32[1,4,2,128]{3,1,2,0:T(4,128)S(1)} copy(s32[1,4,2,128]{3,2,1,0:T(2,128)} %bitcast.53) | data formatting | bytes 8192
  11.0 1.7 %fusion.2 = f32[1024,640]{1,0:T(8,128)} fusion(s32[1024]{0:T(1024)S(1)} %bitcast.52), kind=kLoop, calls=%fused_computation.6 | loop fusion | flops 1310720 | bytes 2625536 | tf_op jit(solution)/shard_map/convert_element_type | solution.py:64
  12.8 0.1 broadcast_multiply_fusion
  12.9 0.1 reshape.118
  13.0 0.0 collective-permute-done.2
  13.0 0.0 collective-permute-done.1
  13.0 0.0 collective-permute-done
  13.0 0.0 copy-start.4
  13.0 0.6 gather_fusion
  13.6 0.1 copy_bitcast_fusion
  13.7 0.1 pad_select_fusion
  13.8 0.1 pad_select_fusion.7
  13.9 0.1 pad_select_fusion.6
  14.0 0.1 pad_select_fusion.5
  14.2 0.1 pad_select_fusion.4
  14.3 0.1 pad_select_fusion.3
  14.4 0.1 pad_select_fusion.2
  14.5 0.1 pad_select_fusion.1
  14.7 1.2 %collective-permute-done.4 = f32[128,256]{1,0:T(8,128)S(1)} collective-permute-done((f32[128,256]{1,0:T(8,128)S(1)}, f32[128,256]{1,0:T(8,128)S(1)}, u32[]{:S(2)}, u32[]{:S(2)}) %collective-permute-start.4) | collective-permute-done | bytes 131104 | tf_op jit(solution)/shard_map/ppermute | solution.py:21
  15.9 1.5 %fusion.4 = f32[1088,256]{1,0:T(8,128)S(1)} fusion(f32[640,256]{1,0:T(8,128)S(1)} %constant_dynamic-update-slice_fusion, f32[64,640]{1,0:T(8,128)S(1)} %bitcast.39, f32[1024,640]{1,0:T(8,128)S(1)} %copy-done.1), kind=kOutput, calls=%fused_computation.8 | convolution fusion | flops 1070243840 | bytes 4554752 | tf_op jit(solution)/shard_map/dot_general | solution.py:93
  17.4 0.1 slice.89
  17.5 0.1 slice_multiply_fusion.1
  17.6 2.9 %convolution_bitcast_fusion = f32[2,512,256]{1,2,0:T(8,128)} fusion(f32[2,512,256]{2,1,0:T(8,128)S(1)} %bitcast.38, f32[2,512,512]{2,1,0:T(8,128)S(1)} %copy-done), kind=kOutput, calls=%fused_computation.10 | convolution fusion | flops 805306368 | bytes 4194304 | tf_op jit(solution)/shard_map/cij,cjb->cib/dot_general | solution.py:96
  20.5 1.6 %copy.11 = f32[2,512,256]{2,1,0:T(8,128)S(1)} copy(f32[2,512,256]{1,2,0:T(8,128)} %convolution_bitcast_fusion) | data formatting | bytes 2097152 | tf_op jit(solution)/shard_map/cij,cjb->cib/dot_general | solution.py:96
  22.0 0.0 copy-start.7
  22.0 4.2 %fusion.3 = f32[640,256]{1,0:T(8,128)S(1)} fusion(f32[64,640]{1,0:T(8,128)S(1)} %bitcast.40, f32[1024,640]{1,0:T(8,128)} %fusion.2, f32[64,256]{1,0:T(8,128)S(1)} %slice_multiply_fusion.1, f32[1024,256]{1,0:T(8,128)S(1)} %bitcast.37), kind=kOutput, calls=%fused_computation.7 | convolution fusion | flops 1070522368 | bytes 4554752 | tf_op jit(solution)/shard_map/dot_general | solution.py:69
  26.3 1.3 %collective-permute-start.6 = (f32[256,256]{1,0:T(8,128)S(1)}, f32[256,256]{1,0:T(8,128)S(1)}, u32[]{:S(2)}, u32[]{:S(2)}) collective-permute-start(f32[256,256]{1,0:T(8,128)S(1)} %get-tuple-element.16), channel_id=1, source_target_pairs={{4,0},{8,4},{12,8},{16,12},{20,16},{24,20},{28,24},{5,1},{9,5},{13... | collective-permute-start | bytes 786440 | tf_op jit(solution)/shard_map/ppermute | solution.py:21
  27.6 5.1 %collective-permute-start.5 = (f32[256,256]{1,0:T(8,128)S(1)}, f32[256,256]{1,0:T(8,128)S(1)}, u32[]{:S(2)}, u32[]{:S(2)}) collective-permute-start(f32[256,256]{1,0:T(8,128)S(1)} %get-tuple-element.15), channel_id=1, source_target_pairs={{0,4},{4,8},{8,12},{12,16},{16,20},{20,24},{24,28},{1,5},{5,9},{9,... | collective-permute-start | bytes 786440 | tf_op jit(solution)/shard_map/ppermute | solution.py:16
  32.8 1.9 %fusion.1 = f32[2,512,640]{2,1,0:T(8,128)S(1)} fusion(f32[2,512,512]{2,1,0:T(8,128)S(1)} %copy-done, s32[2,512]{1,0:T(2,128)S(1)} %copy-done.7), kind=kOutput, calls=%fused_computation.5 | convolution fusion | flops 2013921280 | bytes 4722688 | tf_op jit(solution)/shard_map/cij,cjq->ciq/dot_general | solution.py:104
  34.8 1.6 %fusion.15 = f32[640,640]{1,0:T(8,128)S(1)} fusion(f32[64,640]{1,0:T(8,128)S(1)} %bitcast.41, f32[64]{0:T(128)S(1)} %reshape.118), kind=kOutput, calls=%fused_computation.25 | convolution fusion | flops 314613760 | bytes 1802496 | tf_op jit(solution)/shard_map/dot_general | solution.py:107
  36.3 2.3 %bitcast_add_fusion = f32[640,640]{1,0:T(8,128)S(1)} fusion(f32[640,640]{1,0:T(8,128)S(1)} %fusion.15, f32[2,512,640]{2,1,0:T(8,128)S(1)} %fusion.1, s32[2,512]{1,0:T(2,128)S(1)} %copy-done.7), kind=kOutput, calls=%fused_computation.9 | convolution fusion | flops 2517647360 | bytes 5902336 | tf_op jit(solution)/shard_map/dot_general | solution.py:69
  38.7 4.8 %collective-permute-done.5 = f32[256,256]{1,0:T(8,128)S(1)} collective-permute-done((f32[256,256]{1,0:T(8,128)S(1)}, f32[256,256]{1,0:T(8,128)S(1)}, u32[]{:S(2)}, u32[]{:S(2)}) %collective-permute-start.5) | collective-permute-done | bytes 262176 | tf_op jit(solution)/shard_map/ppermute | solution.py:16
  43.5 0.2 multiply_select_fusion
  43.7 0.0 copy-start.5
  43.7 0.5 fusion.11
  44.2 1.3 %collective-permute-start.8 = (f32[128,256]{1,0:T(8,128)S(1)}, f32[128,256]{1,0:T(8,128)S(1)}, u32[]{:S(2)}, u32[]{:S(2)}) collective-permute-start(f32[128,256]{1,0:T(8,128)S(1)} %get-tuple-element.20), channel_id=1, source_target_pairs={{4,0},{8,4},{12,8},{16,12},{20,16},{24,20},{28,24},{5,1},{9,5},{13... | collective-permute-start | bytes 393224 | tf_op jit(solution)/shard_map/ppermute | solution.py:21
  45.5 5.0 %collective-permute-start.7 = (f32[128,256]{1,0:T(8,128)S(1)}, f32[128,256]{1,0:T(8,128)S(1)}, u32[]{:S(2)}, u32[]{:S(2)}) collective-permute-start(f32[128,256]{1,0:T(8,128)S(1)} %get-tuple-element.19), channel_id=1, source_target_pairs={{0,4},{4,8},{8,12},{12,16},{16,20},{20,24},{24,28},{1,5},{5,9},{9,... | collective-permute-start | bytes 393224 | tf_op jit(solution)/shard_map/ppermute | solution.py:16
  50.5 0.7 %convolution_subtract_fusion = f32[384,256]{1,0:T(8,128)S(1)} fusion(f32[640,256]{1,0:T(8,128)S(1)} %multiply_select_fusion, f32[640,640]{1,0:T(8,128)S(1)} %bitcast_add_fusion), kind=kOutput, calls=%fused_computation.13 | convolution fusion | flops 377683968 | bytes 2424832 | tf_op jit(solution)/shard_map/dot_general | solution.py:131
  51.2 1.1 %collective-permute-done.8 = f32[128,256]{1,0:T(8,128)S(1)} collective-permute-done((f32[128,256]{1,0:T(8,128)S(1)}, f32[128,256]{1,0:T(8,128)S(1)}, u32[]{:S(2)}, u32[]{:S(2)}) %collective-permute-start.8) | collective-permute-done | bytes 131104 | tf_op jit(solution)/shard_map/ppermute | solution.py:21
  52.3 3.0 %collective-permute-done.7 = f32[128,256]{1,0:T(8,128)S(1)} collective-permute-done((f32[128,256]{1,0:T(8,128)S(1)}, f32[128,256]{1,0:T(8,128)S(1)}, u32[]{:S(2)}, u32[]{:S(2)}) %collective-permute-start.7) | collective-permute-done | bytes 131104 | tf_op jit(solution)/shard_map/ppermute | solution.py:16
  55.3 0.8 %add_subtract_fusion = f32[384,256]{1,0:T(8,128)} fusion(f32[384,256]{1,0:T(8,128)S(1)} %copy-done.5, f32[128,256]{1,0:T(8,128)S(1)} %collective-permute-done.8, f32[384,256]{1,0:T(8,128)S(1)} %convolution_subtract_fusion, f32[128,256]{1,0:T(8,128)S(1)} %collective-permute-done.7), kind=kLoop, calls=%fused_computation.24 | loop fusion | flops 294912 | bytes 1441792 | tf_op jit(solution)/shard_map/sub | solution.py:140
  (31 shorter events, 0.3 us)
Async XLA Ops:
  0.0 17.6 %copy-start = (f32[2,512,512]{2,1,0:T(8,128)S(1)}, f32[2,512,512]{2,1,0:T(8,128)}, u32[]{:S(2)}) copy-start(f32[2,512,512]{2,1,0:T(8,128)} %param.8) | copy-start | bytes 6291460
  0.0 13.0 %copy-start.6 = (f32[4,16,128]{2,1,0:T(8,128)S(1)}, f32[4,16,128]{2,1,0:T(8,128)}, u32[]{:S(2)}) copy-start(f32[4,16,128]{2,1,0:T(8,128)} %param.10) | copy-start | bytes 98308
  0.0 12.8 %copy-start.8 = (f32[4,16]{1,0:T(4,128)S(1)}, f32[4,16]{1,0:T(4,128)}, u32[]{:S(2)}) copy-start(f32[4,16]{1,0:T(4,128)} %param.11) | copy-start | bytes 772
  0.0 12.9 %collective-permute-start.2 = (f32[4,16,128]{2,1,0:T(8,128)}, f32[4,16,128]{2,1,0:T(8,128)S(1)}, u32[]{:S(2)}, u32[]{:S(2)}) collective-permute-start(f32[4,16,128]{2,1,0:T(8,128)} %param.10), channel_id=1, source_target_pairs={{0,3},{1,0},{2,1},{3,2},{4,7},{5,4},{6,5},{7,6},{8,11},{9,8},{10,9... | collective-permute-start | bytes 98312 | tf_op jit(solution)/shard_map/ppermute | solution.py:30
  2.4 10.5 %collective-permute-start.1 = (f32[4,16,128]{2,1,0:T(8,128)}, f32[4,16,128]{2,1,0:T(8,128)S(1)}, u32[]{:S(2)}, u32[]{:S(2)}) collective-permute-start(f32[4,16,128]{2,1,0:T(8,128)} %param.10), channel_id=1, source_target_pairs={{0,2},{1,3},{2,0},{3,1},{4,6},{5,7},{6,4},{7,5},{8,10},{9,11},{10,... | collective-permute-start | bytes 98312 | tf_op jit(solution)/shard_map/ppermute | solution.py:30
  3.1 9.9 %collective-permute-start = (f32[4,16,128]{2,1,0:T(8,128)}, f32[4,16,128]{2,1,0:T(8,128)S(1)}, u32[]{:S(2)}, u32[]{:S(2)}) collective-permute-start(f32[4,16,128]{2,1,0:T(8,128)} %param.10), channel_id=1, source_target_pairs={{0,1},{1,2},{2,3},{3,0},{4,5},{5,6},{6,7},{7,4},{8,9},{9,10},{10,1... | collective-permute-start | bytes 98312 | tf_op jit(solution)/shard_map/ppermute | solution.py:30
  4.2 10.4 %collective-permute-start.3 = (f32[128,256]{1,0:T(8,128)S(1)}, f32[128,256]{1,0:T(8,128)S(1)}, u32[]{:S(2)}, u32[]{:S(2)}) collective-permute-start(f32[128,256]{1,0:T(8,128)S(1)} %get-tuple-element.18), channel_id=1, source_target_pairs={{0,4},{4,8},{8,12},{12,16},{16,20},{20,24},{24,28},{1,5},{5,9},{9,... | collective-permute-start | bytes 393224 | tf_op jit(solution)/shard_map/ppermute | solution.py:16
  7.7 8.2 %collective-permute-start.4 = (f32[128,256]{1,0:T(8,128)S(1)}, f32[128,256]{1,0:T(8,128)S(1)}, u32[]{:S(2)}, u32[]{:S(2)}) collective-permute-start(f32[128,256]{1,0:T(8,128)S(1)} %get-tuple-element.17), channel_id=1, source_target_pairs={{4,0},{8,4},{12,8},{16,12},{20,16},{24,20},{28,24},{5,1},{9,5},{13... | collective-permute-start | bytes 393224 | tf_op jit(solution)/shard_map/ppermute | solution.py:21
  13.0 1.6 %copy-start.4 = (f32[384,256]{1,0:T(8,128)S(1)}, f32[384,256]{1,0:T(8,128)}, u32[]{:S(2)}) copy-start(f32[384,256]{1,0:T(8,128)} %param.7) | copy-start | bytes 1179652
  13.7 2.2 %copy-start.1 = (f32[1024,640]{1,0:T(8,128)S(1)}, f32[1024,640]{1,0:T(8,128)}, u32[]{:S(2)}) copy-start(f32[1024,640]{1,0:T(8,128)} %fusion.2) | copy-start | bytes 7864324
  15.9 1.6 %copy-start.2 = (f32[640,256]{1,0:T(8,128)}, f32[640,256]{1,0:T(8,128)S(1)}, u32[]{:S(2)}) copy-start(f32[640,256]{1,0:T(8,128)S(1)} %constant_dynamic-update-slice_fusion) | copy-start | bytes 1966084
  22.0 10.8 %copy-start.7 = (s32[2,512]{1,0:T(2,128)S(1)}, s32[2,512]{1,0:T(2,128)}, u32[]{:S(2)}) copy-start(s32[2,512]{1,0:T(2,128)} %param.9) | copy-start | bytes 12292
  26.3 12.4 %collective-permute-start.6 = (f32[256,256]{1,0:T(8,128)S(1)}, f32[256,256]{1,0:T(8,128)S(1)}, u32[]{:S(2)}, u32[]{:S(2)}) collective-permute-start(f32[256,256]{1,0:T(8,128)S(1)} %get-tuple-element.16), channel_id=1, source_target_pairs={{4,0},{8,4},{12,8},{16,12},{20,16},{24,20},{28,24},{5,1},{9,5},{13... | collective-permute-start | bytes 786440 | tf_op jit(solution)/shard_map/ppermute | solution.py:21
  27.6 15.9 %collective-permute-start.5 = (f32[256,256]{1,0:T(8,128)S(1)}, f32[256,256]{1,0:T(8,128)S(1)}, u32[]{:S(2)}, u32[]{:S(2)}) collective-permute-start(f32[256,256]{1,0:T(8,128)S(1)} %get-tuple-element.15), channel_id=1, source_target_pairs={{0,4},{4,8},{8,12},{12,16},{16,20},{20,24},{24,28},{1,5},{5,9},{9,... | collective-permute-start | bytes 786440 | tf_op jit(solution)/shard_map/ppermute | solution.py:16
  36.3 7.2 %copy-start.3 = (f32[640,256]{1,0:T(8,128)S(1)}, f32[640,256]{1,0:T(8,128)}, u32[]{:S(2)}) copy-start(f32[640,256]{1,0:T(8,128)} %copy-done.2) | copy-start | bytes 1966084
  43.7 11.6 %copy-start.5 = (f32[384,256]{1,0:T(8,128)S(1)}, f32[384,256]{1,0:T(8,128)}, u32[]{:S(2)}) copy-start(f32[384,256]{1,0:T(8,128)} %param.7) | copy-start | bytes 1179652
  44.2 8.1 %collective-permute-start.8 = (f32[128,256]{1,0:T(8,128)S(1)}, f32[128,256]{1,0:T(8,128)S(1)}, u32[]{:S(2)}, u32[]{:S(2)}) collective-permute-start(f32[128,256]{1,0:T(8,128)S(1)} %get-tuple-element.20), channel_id=1, source_target_pairs={{4,0},{8,4},{12,8},{16,12},{20,16},{24,20},{28,24},{5,1},{9,5},{13... | collective-permute-start | bytes 393224 | tf_op jit(solution)/shard_map/ppermute | solution.py:21
  45.5 9.7 %collective-permute-start.7 = (f32[128,256]{1,0:T(8,128)S(1)}, f32[128,256]{1,0:T(8,128)S(1)}, u32[]{:S(2)}, u32[]{:S(2)}) collective-permute-start(f32[128,256]{1,0:T(8,128)S(1)} %get-tuple-element.19), channel_id=1, source_target_pairs={{0,4},{4,8},{8,12},{12,16},{16,20},{20,24},{24,28},{1,5},{5,9},{9,... | collective-permute-start | bytes 393224 | tf_op jit(solution)/shard_map/ppermute | solution.py:16

commit v19 on v16

--- a/solution.py
+++ b/solution.py
@@ -128,6 +128,7 @@
     owned = lax.optimization_barrier(
         jnp.dot(operator[g : g + own], step_ext, precision=lax.Precision.HIGH)
         - filter_center * step_one
+        - wavefunctions
     )
     zeros_own = jnp.zeros((own - g, owned.shape[1]), jnp.float32)
     second_image = (
@@ -135,8 +136,7 @@
         + jnp.concatenate([from_before, zeros_own], axis=0)
         + jnp.concatenate([zeros_own, from_after], axis=0)
     )
-    filtered = 2.0 * second_image / filter_half - wavefunctions
-    return filtered
+    return second_image
 
 
 def solution(mesh):

time: 47.6 us -> 47.6 us (level)
    sub x1 -> x0, other arithmetic: 0.83 us -> none  [on_device(): filtered = 2.0 * second_image / filter_half - wavefunctions]
    add x0 -> x1, other arithmetic: none -> 0.79 us  [on_device(): owned + jnp.concatenate([from_before, zeros_own], axis=0)]
where the time goes in v19:
time: 47.6 us; the launch traced here: 47.2 us
  starting transfers between devices  21.8 us (46%)
  matrix products  11.2 us (24%)
  waiting for transfers between devices  7.18 us (15%)
  other arithmetic  4.15 us (9%)
  local copies, waits for them, and re-layouts  1.85 us (4%)
  between operations  0.99 us (2%)
    ppermute x3, starting transfers between devices, from_left(): return lax.ppermute(x, axis, [(i, i + 1) for i in range(count - 1)])  13.3 us
    ppermute x3, starting transfers between devices, gather_band(): lax.ppermute(piece, 'band', [(i, (i + k) % count) for i in range(count)])  4.68 us
    ppermute x3, waiting for transfers between devices, from_right(): return lax.ppermute(x, axis, [(i + 1, i) for i in range(count - 1)])  4.37 us
    ppermute x3, starting transfers between devices, from_right(): return lax.ppermute(x, axis, [(i + 1, i) for i in range(count - 1)])  3.88 us
    dot_general x2, matrix products, scatter_rows(): lax.dot_general(onehot, values, (((0,), (0,)), ((), ())), precision=lax.P...  3.16 us
    ppermute x3, waiting for transfers between devices, from_left(): return lax.ppermute(x, axis, [(i, i + 1) for i in range(count - 1)])  2.8 us
    dot_general x1, matrix products, on_device(): jnp.einsum('cij,cjq->ciq', matrices, onehot.reshape(cells, nodes, ext), p...  1.95 us
    dot_general x1, matrix products, on_device(): jnp.dot((placed_late * weights_late[:, None]).T, placed_late, precision=h...  1.58 us
  transfers between devices with their start and end apart: 9, of which 3 were waited for; matrix products, arithmetic and copies ran while one was open for 24% of the time, Pallas kernels for 0%

profile of v19, /device:TPU:0, one launch (start us, length us, event | category | flops | bytes accessed | tf_op | source)
XLA Modules:
  0.0 47.2 jit_solution(12395706561871504889)
XLA Ops:
  0.0 0.5 collective-permute-start
  0.5 2.0 %collective-permute-start.2 = (f32[4,16,128]{2,1,0:T(8,128)}, f32[4,16,128]{2,1,0:T(8,128)S(1)}, u32[]{:S(2)}, u32[]{:S(2)}) collective-permute-start(f32[4,16,128]{2,1,0:T(8,128)} %param.10), channel_id=1, source_target_pairs={{0,3},{1,0},{2,1},{3,2},{4,7},{5,4},{6,5},{7,6},{8,11},{9,8},{10,9... | collective-permute-start | bytes 98312 | tf_op jit(solution)/shard_map/ppermute | solution.py:30
  2.4 2.2 %collective-permute-start.1 = (f32[4,16,128]{2,1,0:T(8,128)}, f32[4,16,128]{2,1,0:T(8,128)S(1)}, u32[]{:S(2)}, u32[]{:S(2)}) collective-permute-start(f32[4,16,128]{2,1,0:T(8,128)} %param.10), channel_id=1, source_target_pairs={{0,2},{1,3},{2,0},{3,1},{4,6},{5,7},{6,4},{7,5},{8,10},{9,11},{10,... | collective-permute-start | bytes 98312 | tf_op jit(solution)/shard_map/ppermute | solution.py:30
  4.7 1.0 %fusion.28 = (f32[128,256]{1,0:T(8,128)S(1)}, f32[128,256]{1,0:T(8,128)S(1)}) fusion(f32[384,256]{1,0:T(8,128)} %param.7), kind=kLoop, calls=%fused_computation.76 | loop fusion | bytes 524288 | tf_op jit(solution)/shard_map/slice | solution.py:84
  5.7 1.3 %collective-permute-start.4 = (f32[128,256]{1,0:T(8,128)S(1)}, f32[128,256]{1,0:T(8,128)S(1)}, u32[]{:S(2)}, u32[]{:S(2)}) collective-permute-start(f32[128,256]{1,0:T(8,128)S(1)} %get-tuple-element.17), channel_id=1, source_target_pairs={{4,0},{8,4},{12,8},{16,12},{20,16},{24,20},{28,24},{5,1},{9,5},{13... | collective-permute-start | bytes 393224 | tf_op jit(solution)/shard_map/ppermute | solution.py:21
  7.0 4.6 %collective-permute-start.3 = (f32[128,256]{1,0:T(8,128)S(1)}, f32[128,256]{1,0:T(8,128)S(1)}, u32[]{:S(2)}, u32[]{:S(2)}) collective-permute-start(f32[128,256]{1,0:T(8,128)S(1)} %get-tuple-element.18), channel_id=1, source_target_pairs={{0,4},{4,8},{8,12},{12,16},{16,20},{20,24},{24,28},{1,5},{5,9},{9,... | collective-permute-start | bytes 393224 | tf_op jit(solution)/shard_map/ppermute | solution.py:16
  12.2 0.7 %and_compare_fusion.7 = (pred[4]{0:T(512)(128)(4,1)S(1)}, pred[4]{0:T(512)(128)(4,1)S(1)}, pred[4]{0:T(512)(128)(4,1)S(1)}, pred[4]{0:T(512)(128)(4,1)S(1)}, pre...) fusion(s32[4]{0:T(128)} %param.12), kind=kLoop, calls=%fused_computation.71 | loop fusion | flops 100 | bytes 48 | tf_op jit(solution)/shard_map/eq | solution.py:45
  12.9 0.8 %broadcast_multiply_fusion = f32[4,16]{1,0:T(4,128)S(1)} fusion(f32[4,16]{1,0:T(4,128)} %param.11, f32[4]{0:T(128)S(1)} %compare_convert_fusion), kind=kLoop, calls=%fused_computation.60 | loop fusion | flops 64 | bytes 528 | tf_op jit(solution)/shard_map/mul | solution.py:57
  13.7 0.1 reshape.123
  13.8 0.0 collective-permute-done
  13.8 0.0 collective-permute-done.2
  13.8 0.0 collective-permute-done.1
  13.8 0.8 %pad_maximum_fusion = f32[4,4,16,128]{3,2,1,0:T(8,128)S(1)} fusion(f32[1,4,16,128]{3,2,1,0:T(8,128)S(1)} %bitcast.53, f32[1,4,16,128]{3,2,1,0:T(8,128)S(1)} %bitcast.54, f32[1,4,16,128]{3,2,1,0:T(8,128)S(1)} %bitcast.52, f32[1,4,16,128]{3,2,1,0:T(8,128)} %bitcast.51), kind=kLoop, calls=%fused_computation.38 | loop fusion | flops 98304 | bytes 262144 | tf_op jit(solution)/shard_map/stack | solution.py:32
  14.6 0.6 %gather_fusion = f32[4,4,16,128]{3,2,1,0:T(8,128)S(1)} fusion(f32[4,4,16,128]{3,2,1,0:T(8,128)S(1)} %pad_maximum_fusion, s32[1024]{0:T(1024)S(1)} %pad_clamp_fusion), kind=kCustom, calls=%fused_computation | custom fusion | bytes 262160 | tf_op jit(solution)/shard_map/jit(_take)/gather | solution.py:34
  15.1 0.1 copy_bitcast_fusion
  15.2 0.0 copy-start.1
  15.3 0.1 pad_select_fusion
  15.4 0.1 pad_select_fusion.7
  15.5 0.1 pad_select_fusion.6
  15.6 0.0 copy-start.2
  15.6 0.1 pad_select_fusion.5
  15.7 0.1 pad_select_fusion.4
  15.9 0.1 pad_select_fusion.3
  16.0 0.1 pad_select_fusion.2
  16.1 0.1 pad_select_fusion.1
  16.2 0.0 copy-done.1
  16.3 0.0 collective-permute-done.4
  16.3 0.0 copy-done.2
  16.3 1.6 %fusion.3 = f32[2,512,256]{2,1,0:T(8,128)S(1)} fusion(s32[2,512]{1,0:T(2,128)S(1)} %copy-done.2, f32[640,256]{1,0:T(8,128)S(1)} %constant_dynamic-update-slice_fusion), kind=kOutput, calls=%fused_computation.5 | convolution fusion | flops 1007288320 | bytes 1708032 | tf_op jit(solution)/shard_map/dot_general | solution.py:93
  17.9 1.0 %convolution_bitcast_fusion = f32[2,512,256]{2,1,0:T(8,128)S(1)} fusion(f32[2,512,256]{2,1,0:T(8,128)S(1)} %fusion.3, f32[2,512,512]{2,1,0:T(8,128)S(1)} %copy-done), kind=kOutput, calls=%fused_computation.7 | convolution fusion | flops 805306368 | bytes 4194304 | tf_op jit(solution)/shard_map/cij,cjb->cib/dot_general | solution.py:94
  18.9 0.9 %fusion.8 = f32[640,256]{1,0:T(8,128)S(1)} fusion(f32[2,512,256]{2,1,0:T(8,128)S(1)} %convolution_bitcast_fusion, s32[2,512]{1,0:T(2,128)S(1)} %copy-done.2), kind=kOutput, calls=%fused_computation.12 | convolution fusion | flops 1007288320 | bytes 1708032 | tf_op jit(solution)/shard_map/dot_general | solution.py:69
  19.8 0.3 convolution_multiply_fusion
  20.1 0.5 %convolution_add_fusion = f32[640,256]{1,0:T(8,128)S(1)} fusion(f32[640,256]{1,0:T(8,128)S(1)} %fusion.8, f32[64,640]{1,0:T(8,128)S(1)} %bitcast.43, f32[64,256]{1,0:T(8,128)S(1)} %convolution_multiply_fusion), kind=kOutput, calls=%fused_computation.13 | convolution fusion | flops 63078400 | bytes 1540096 | tf_op jit(solution)/shard_map/dot_general | solution.py:95
  20.6 4.3 %collective-permute-start.5 = (f32[256,256]{1,0:T(8,128)S(1)}, f32[256,256]{1,0:T(8,128)S(1)}, u32[]{:S(2)}, u32[]{:S(2)}) collective-permute-start(f32[256,256]{1,0:T(8,128)S(1)} %get-tuple-element.15), channel_id=1, source_target_pairs={{0,4},{4,8},{8,12},{12,16},{16,20},{20,24},{24,28},{1,5},{5,9},{9,... | collective-permute-start | bytes 786440 | tf_op jit(solution)/shard_map/ppermute | solution.py:16
  25.0 1.3 %collective-permute-start.6 = (f32[256,256]{1,0:T(8,128)S(1)}, f32[256,256]{1,0:T(8,128)S(1)}, u32[]{:S(2)}, u32[]{:S(2)}) collective-permute-start(f32[256,256]{1,0:T(8,128)S(1)} %get-tuple-element.16), channel_id=1, source_target_pairs={{4,0},{8,4},{12,8},{16,12},{20,16},{24,20},{28,24},{5,1},{9,5},{13... | collective-permute-start | bytes 786440 | tf_op jit(solution)/shard_map/ppermute | solution.py:21
  26.3 1.9 %fusion.1 = f32[2,512,640]{2,1,0:T(8,128)S(1)} fusion(f32[2,512,512]{2,1,0:T(8,128)S(1)} %copy-done, s32[2,512]{1,0:T(2,128)S(1)} %copy-done.2), kind=kOutput, calls=%fused_computation.3 | convolution fusion | flops 2013921280 | bytes 4722688 | tf_op jit(solution)/shard_map/cij,cjq->ciq/dot_general | solution.py:102
  28.2 1.6 %fusion.16 = f32[640,640]{1,0:T(8,128)S(1)} fusion(f32[64,640]{1,0:T(8,128)S(1)} %bitcast.44, f32[64]{0:T(128)S(1)} %reshape.123), kind=kOutput, calls=%fused_computation.26 | convolution fusion | flops 314613760 | bytes 1802496 | tf_op jit(solution)/shard_map/dot_general | solution.py:105
  29.8 2.3 %bitcast_add_fusion = f32[640,640]{1,0:T(8,128)S(1)} fusion(f32[640,640]{1,0:T(8,128)S(1)} %fusion.16, f32[2,512,640]{2,1,0:T(8,128)S(1)} %fusion.1, s32[2,512]{1,0:T(2,128)S(1)} %copy-done.2), kind=kOutput, calls=%fused_computation.6 | convolution fusion | flops 2517647360 | bytes 5902336 | tf_op jit(solution)/shard_map/dot_general | solution.py:69
  32.2 2.3 %collective-permute-done.5 = f32[256,256]{1,0:T(8,128)S(1)} collective-permute-done((f32[256,256]{1,0:T(8,128)S(1)}, f32[256,256]{1,0:T(8,128)S(1)}, u32[]{:S(2)}, u32[]{:S(2)}) %collective-permute-start.5) | collective-permute-done | bytes 262176 | tf_op jit(solution)/shard_map/ppermute | solution.py:16
  34.4 0.0 collective-permute-done.6
  34.4 0.2 multiply_select_fusion
  34.6 0.5 %fusion.11 = f32[256,256]{1,0:T(8,128)S(1)} fusion(f32[640,256]{1,0:T(8,128)S(1)} %multiply_select_fusion, f32[128,640]{1,0:T(8,128)S(1)} %get-tuple-element.14, f32[128,640]{1,0:T(8,128)S(1)} %get-tuple-element.13), kind=kOutput, calls=%fused_computation.18 | convolution fusion | flops 251822080 | bytes 1572864 | tf_op jit(solution)/shard_map/dot_general | solution.py:125
  35.2 4.4 %collective-permute-start.7 = (f32[128,256]{1,0:T(8,128)S(1)}, f32[128,256]{1,0:T(8,128)S(1)}, u32[]{:S(2)}, u32[]{:S(2)}) collective-permute-start(f32[128,256]{1,0:T(8,128)S(1)} %get-tuple-element.19), channel_id=1, source_target_pairs={{0,4},{4,8},{8,12},{12,16},{16,20},{20,24},{24,28},{1,5},{5,9},{9,... | collective-permute-start | bytes 393224 | tf_op jit(solution)/shard_map/ppermute | solution.py:16
  39.6 1.3 %collective-permute-start.8 = (f32[128,256]{1,0:T(8,128)S(1)}, f32[128,256]{1,0:T(8,128)S(1)}, u32[]{:S(2)}, u32[]{:S(2)}) collective-permute-start(f32[128,256]{1,0:T(8,128)S(1)} %get-tuple-element.20), channel_id=1, source_target_pairs={{4,0},{8,4},{12,8},{16,12},{20,16},{24,20},{28,24},{5,1},{9,5},{13... | collective-permute-start | bytes 393224 | tf_op jit(solution)/shard_map/ppermute | solution.py:21
  40.9 0.7 %fusion.9 = f32[384,256]{1,0:T(8,128)S(1)} fusion(f32[384,256]{1,0:T(8,128)S(1)} %copy-done.1, f32[640,256]{1,0:T(8,128)S(1)} %multiply_select_fusion, f32[640,640]{1,0:T(8,128)S(1)} %bitcast_add_fusion), kind=kOutput, calls=%fused_computation.15 | convolution fusion | flops 377782272 | bytes 2818048 | tf_op jit(solution)/shard_map/dot_general | solution.py:129
  41.5 0.5 %collective-permute-done.7 = f32[128,256]{1,0:T(8,128)S(1)} collective-permute-done((f32[128,256]{1,0:T(8,128)S(1)}, f32[128,256]{1,0:T(8,128)S(1)}, u32[]{:S(2)}, u32[]{:S(2)}) %collective-permute-start.7) | collective-permute-done | bytes 131104 | tf_op jit(solution)/shard_map/ppermute | solution.py:16
  42.1 4.4 %collective-permute-done.8 = f32[128,256]{1,0:T(8,128)S(1)} collective-permute-done((f32[128,256]{1,0:T(8,128)S(1)}, f32[128,256]{1,0:T(8,128)S(1)}, u32[]{:S(2)}, u32[]{:S(2)}) %collective-permute-start.8) | collective-permute-done | bytes 131104 | tf_op jit(solution)/shard_map/ppermute | solution.py:21
  46.4 0.8 %pad_add_fusion = f32[384,256]{1,0:T(8,128)} fusion(f32[128,256]{1,0:T(8,128)S(1)} %collective-permute-done.8, f32[384,256]{1,0:T(8,128)S(1)} %fusion.9, f32[128,256]{1,0:T(8,128)S(1)} %collective-permute-done.7), kind=kLoop, calls=%fused_computation.25 | loop fusion | flops 196608 | bytes 1048576 | tf_op jit(solution)/shard_map/add | solution.py:135
  (16 shorter events, 0.2 us)
Async XLA Ops:
  0.0 17.9 %copy-start = (f32[2,512,512]{2,1,0:T(8,128)S(1)}, f32[2,512,512]{2,1,0:T(8,128)}, u32[]{:S(2)}) copy-start(f32[2,512,512]{2,1,0:T(8,128)} %param.8) | copy-start | bytes 6291460
  0.0 13.8 %collective-permute-start = (f32[4,16,128]{2,1,0:T(8,128)}, f32[4,16,128]{2,1,0:T(8,128)S(1)}, u32[]{:S(2)}, u32[]{:S(2)}) collective-permute-start(f32[4,16,128]{2,1,0:T(8,128)} %param.10), channel_id=1, source_target_pairs={{0,1},{1,2},{2,3},{3,0},{4,5},{5,6},{6,7},{7,4},{8,9},{9,10},{10,1... | collective-permute-start | bytes 98312 | tf_op jit(solution)/shard_map/ppermute | solution.py:30
  0.5 13.3 %collective-permute-start.2 = (f32[4,16,128]{2,1,0:T(8,128)}, f32[4,16,128]{2,1,0:T(8,128)S(1)}, u32[]{:S(2)}, u32[]{:S(2)}) collective-permute-start(f32[4,16,128]{2,1,0:T(8,128)} %param.10), channel_id=1, source_target_pairs={{0,3},{1,0},{2,1},{3,2},{4,7},{5,4},{6,5},{7,6},{8,11},{9,8},{10,9... | collective-permute-start | bytes 98312 | tf_op jit(solution)/shard_map/ppermute | solution.py:30
  2.4 11.4 %collective-permute-start.1 = (f32[4,16,128]{2,1,0:T(8,128)}, f32[4,16,128]{2,1,0:T(8,128)S(1)}, u32[]{:S(2)}, u32[]{:S(2)}) collective-permute-start(f32[4,16,128]{2,1,0:T(8,128)} %param.10), channel_id=1, source_target_pairs={{0,2},{1,3},{2,0},{3,1},{4,6},{5,7},{6,4},{7,5},{8,10},{9,11},{10,... | collective-permute-start | bytes 98312 | tf_op jit(solution)/shard_map/ppermute | solution.py:30
  5.7 10.6 %collective-permute-start.4 = (f32[128,256]{1,0:T(8,128)S(1)}, f32[128,256]{1,0:T(8,128)S(1)}, u32[]{:S(2)}, u32[]{:S(2)}) collective-permute-start(f32[128,256]{1,0:T(8,128)S(1)} %get-tuple-element.17), channel_id=1, source_target_pairs={{4,0},{8,4},{12,8},{16,12},{20,16},{24,20},{28,24},{5,1},{9,5},{13... | collective-permute-start | bytes 393224 | tf_op jit(solution)/shard_map/ppermute | solution.py:21
  7.0 9.2 %collective-permute-start.3 = (f32[128,256]{1,0:T(8,128)S(1)}, f32[128,256]{1,0:T(8,128)S(1)}, u32[]{:S(2)}, u32[]{:S(2)}) collective-permute-start(f32[128,256]{1,0:T(8,128)S(1)} %get-tuple-element.18), channel_id=1, source_target_pairs={{0,4},{4,8},{8,12},{12,16},{16,20},{20,24},{24,28},{1,5},{5,9},{9,... | collective-permute-start | bytes 393224 | tf_op jit(solution)/shard_map/ppermute | solution.py:16
  15.2 1.0 %copy-start.1 = (f32[384,256]{1,0:T(8,128)S(1)}, f32[384,256]{1,0:T(8,128)}, u32[]{:S(2)}) copy-start(f32[384,256]{1,0:T(8,128)} %param.7) | copy-start | bytes 1179652
  15.6 0.7 %copy-start.2 = (s32[2,512]{1,0:T(2,128)S(1)}, s32[2,512]{1,0:T(2,128)}, u32[]{:S(2)}) copy-start(s32[2,512]{1,0:T(2,128)} %param.9) | copy-start | bytes 12292
  20.6 13.8 %collective-permute-start.5 = (f32[256,256]{1,0:T(8,128)S(1)}, f32[256,256]{1,0:T(8,128)S(1)}, u32[]{:S(2)}, u32[]{:S(2)}) collective-permute-start(f32[256,256]{1,0:T(8,128)S(1)} %get-tuple-element.15), channel_id=1, source_target_pairs={{0,4},{4,8},{8,12},{12,16},{16,20},{20,24},{24,28},{1,5},{5,9},{9,... | collective-permute-start | bytes 786440 | tf_op jit(solution)/shard_map/ppermute | solution.py:16
  25.0 9.5 %collective-permute-start.6 = (f32[256,256]{1,0:T(8,128)S(1)}, f32[256,256]{1,0:T(8,128)S(1)}, u32[]{:S(2)}, u32[]{:S(2)}) collective-permute-start(f32[256,256]{1,0:T(8,128)S(1)} %get-tuple-element.16), channel_id=1, source_target_pairs={{4,0},{8,4},{12,8},{16,12},{20,16},{24,20},{28,24},{5,1},{9,5},{13... | collective-permute-start | bytes 786440 | tf_op jit(solution)/shard_map/ppermute | solution.py:21
  35.2 6.9 %collective-permute-start.7 = (f32[128,256]{1,0:T(8,128)S(1)}, f32[128,256]{1,0:T(8,128)S(1)}, u32[]{:S(2)}, u32[]{:S(2)}) collective-permute-start(f32[128,256]{1,0:T(8,128)S(1)} %get-tuple-element.19), channel_id=1, source_target_pairs={{0,4},{4,8},{8,12},{12,16},{16,20},{20,24},{24,28},{1,5},{5,9},{9,... | collective-permute-start | bytes 393224 | tf_op jit(solution)/shard_map/ppermute | solution.py:16
  39.6 6.9 %collective-permute-start.8 = (f32[128,256]{1,0:T(8,128)S(1)}, f32[128,256]{1,0:T(8,128)S(1)}, u32[]{:S(2)}, u32[]{:S(2)}) collective-permute-start(f32[128,256]{1,0:T(8,128)S(1)} %get-tuple-element.20), channel_id=1, source_target_pairs={{4,0},{8,4},{12,8},{16,12},{20,16},{24,20},{28,24},{5,1},{9,5},{13... | collective-permute-start | bytes 393224 | tf_op jit(solution)/shard_map/ppermute | solution.py:21

commit v20 on v19

--- a/solution.py
+++ b/solution.py
@@ -108,12 +108,12 @@
     left_sums = from_left(first[ext - 2 * g :], "dom")
     right_sums = from_right(first[: 2 * g], "dom")
     zeros_side = jnp.zeros((ext - 2 * g, first.shape[1]), jnp.float32)
-    first_image = (
-        first
+    (pending,) = lax.optimization_barrier((first - filter_center * extended,))
+    step_ext = (
+        pending
         + jnp.concatenate([left_sums, zeros_side], axis=0)
         + jnp.concatenate([zeros_side, right_sums], axis=0)
-    )
-    step_ext = (first_image - filter_center * extended) / filter_half
+    ) / filter_half
     row = lax.broadcasted_iota(jnp.int32, (ext, 1), 0)
     keep = jnp.logical_and(
         jnp.logical_or(row >= g, me > 0), jnp.logical_or(row < ext - g, me < count - 1)

time: 47.6 us -> 47.6 us (level)
  no operation moved by 1% of the time
where the time goes in v20:
time: 47.6 us; the launch traced here: 47.2 us
  starting transfers between devices  21.8 us (46%)
  matrix products  11.2 us (24%)
  waiting for transfers between devices  7.08 us (15%)
  other arithmetic  4.25 us (9%)
  local copies, waits for them, and re-layouts  1.85 us (4%)
  between operations  1.01 us (2%)
    ppermute x3, starting transfers between devices, from_left(): return lax.ppermute(x, axis, [(i, i + 1) for i in range(count - 1)])  13.3 us
    ppermute x3, starting transfers between devices, gather_band(): lax.ppermute(piece, 'band', [(i, (i + k) % count) for i in range(count)])  4.68 us
    ppermute x3, waiting for transfers between devices, from_right(): return lax.ppermute(x, axis, [(i + 1, i) for i in range(count - 1)])  4.37 us
    ppermute x3, starting transfers between devices, from_right(): return lax.ppermute(x, axis, [(i + 1, i) for i in range(count - 1)])  3.88 us
    dot_general x2, matrix products, scatter_rows(): lax.dot_general(onehot, values, (((0,), (0,)), ((), ())), precision=lax.P...  3.16 us
    ppermute x3, waiting for transfers between devices, from_left(): return lax.ppermute(x, axis, [(i, i + 1) for i in range(count - 1)])  2.71 us
    dot_general x1, matrix products, on_device(): jnp.einsum('cij,cjq->ciq', matrices, onehot.reshape(cells, nodes, ext), p...  1.95 us
    dot_general x1, matrix products, on_device(): jnp.dot((placed_late * weights_late[:, None]).T, placed_late, precision=h...  1.58 us
  transfers between devices with their start and end apart: 9, of which 3 were waited for; matrix products, arithmetic and copies ran while one was open for 24% of the time, Pallas kernels for 0%

profile of v20, /device:TPU:0, one launch (start us, length us, event | category | flops | bytes accessed | tf_op | source)
XLA Modules:
  0.0 47.2 jit_solution(17954491047046604316)
XLA Ops:
  0.0 0.5 collective-permute-start
  0.5 2.0 %collective-permute-start.2 = (f32[4,16,128]{2,1,0:T(8,128)}, f32[4,16,128]{2,1,0:T(8,128)S(1)}, u32[]{:S(2)}, u32[]{:S(2)}) collective-permute-start(f32[4,16,128]{2,1,0:T(8,128)} %param.10), channel_id=1, source_target_pairs={{0,3},{1,0},{2,1},{3,2},{4,7},{5,4},{6,5},{7,6},{8,11},{9,8},{10,9... | collective-permute-start | bytes 98312 | tf_op jit(solution)/shard_map/ppermute | solution.py:30
  2.4 2.2 %collective-permute-start.1 = (f32[4,16,128]{2,1,0:T(8,128)}, f32[4,16,128]{2,1,0:T(8,128)S(1)}, u32[]{:S(2)}, u32[]{:S(2)}) collective-permute-start(f32[4,16,128]{2,1,0:T(8,128)} %param.10), channel_id=1, source_target_pairs={{0,2},{1,3},{2,0},{3,1},{4,6},{5,7},{6,4},{7,5},{8,10},{9,11},{10,... | collective-permute-start | bytes 98312 | tf_op jit(solution)/shard_map/ppermute | solution.py:30
  4.7 1.0 %fusion.28 = (f32[128,256]{1,0:T(8,128)S(1)}, f32[128,256]{1,0:T(8,128)S(1)}) fusion(f32[384,256]{1,0:T(8,128)} %param.7), kind=kLoop, calls=%fused_computation.77 | loop fusion | bytes 524288 | tf_op jit(solution)/shard_map/slice | solution.py:84
  5.7 1.3 %collective-permute-start.4 = (f32[128,256]{1,0:T(8,128)S(1)}, f32[128,256]{1,0:T(8,128)S(1)}, u32[]{:S(2)}, u32[]{:S(2)}) collective-permute-start(f32[128,256]{1,0:T(8,128)S(1)} %get-tuple-element.17), channel_id=1, source_target_pairs={{4,0},{8,4},{12,8},{16,12},{20,16},{24,20},{28,24},{5,1},{9,5},{13... | collective-permute-start | bytes 393224 | tf_op jit(solution)/shard_map/ppermute | solution.py:21
  7.0 4.6 %collective-permute-start.3 = (f32[128,256]{1,0:T(8,128)S(1)}, f32[128,256]{1,0:T(8,128)S(1)}, u32[]{:S(2)}, u32[]{:S(2)}) collective-permute-start(f32[128,256]{1,0:T(8,128)S(1)} %get-tuple-element.18), channel_id=1, source_target_pairs={{0,4},{4,8},{8,12},{12,16},{16,20},{20,24},{24,28},{1,5},{5,9},{9,... | collective-permute-start | bytes 393224 | tf_op jit(solution)/shard_map/ppermute | solution.py:16
  12.2 0.7 %and_compare_fusion.7 = (pred[4]{0:T(512)(128)(4,1)S(1)}, pred[4]{0:T(512)(128)(4,1)S(1)}, pred[4]{0:T(512)(128)(4,1)S(1)}, pred[4]{0:T(512)(128)(4,1)S(1)}, pre...) fusion(s32[4]{0:T(128)} %param.12), kind=kLoop, calls=%fused_computation.72 | loop fusion | flops 100 | bytes 48 | tf_op jit(solution)/shard_map/eq | solution.py:45
  12.9 0.8 %broadcast_multiply_fusion = f32[4,16]{1,0:T(4,128)S(1)} fusion(f32[4,16]{1,0:T(4,128)} %param.11, f32[4]{0:T(128)S(1)} %compare_convert_fusion), kind=kLoop, calls=%fused_computation.61 | loop fusion | flops 64 | bytes 528 | tf_op jit(solution)/shard_map/mul | solution.py:57
  13.7 0.1 reshape.123
  13.8 0.0 collective-permute-done
  13.8 0.0 collective-permute-done.2
  13.8 0.8 %pad_maximum_fusion = f32[4,4,16,128]{3,2,1,0:T(8,128)S(1)} fusion(f32[1,4,16,128]{3,2,1,0:T(8,128)S(1)} %bitcast.53, f32[1,4,16,128]{3,2,1,0:T(8,128)S(1)} %bitcast.54, f32[1,4,16,128]{3,2,1,0:T(8,128)S(1)} %bitcast.52, f32[1,4,16,128]{3,2,1,0:T(8,128)} %bitcast.51), kind=kLoop, calls=%fused_computation.39 | loop fusion | flops 98304 | bytes 262144 | tf_op jit(solution)/shard_map/stack | solution.py:32
  14.6 0.6 %gather_fusion = f32[4,4,16,128]{3,2,1,0:T(8,128)S(1)} fusion(f32[4,4,16,128]{3,2,1,0:T(8,128)S(1)} %pad_maximum_fusion, s32[1024]{0:T(1024)S(1)} %pad_clamp_fusion), kind=kCustom, calls=%fused_computation | custom fusion | bytes 262160 | tf_op jit(solution)/shard_map/jit(_take)/gather | solution.py:34
  15.1 0.1 copy_bitcast_fusion
  15.2 0.0 copy-start.1
  15.3 0.1 pad_select_fusion
  15.4 0.1 pad_select_fusion.7
  15.5 0.1 pad_select_fusion.6
  15.6 0.0 copy-start.2
  15.6 0.1 pad_select_fusion.5
  15.7 0.1 pad_select_fusion.4
  15.9 0.1 pad_select_fusion.3
  16.0 0.1 pad_select_fusion.2
  16.1 0.1 pad_select_fusion.1
  16.2 0.0 copy-done.1
  16.3 0.0 collective-permute-done.4
  16.3 0.0 copy-done.2
  16.3 1.6 %fusion.3 = f32[2,512,256]{2,1,0:T(8,128)S(1)} fusion(s32[2,512]{1,0:T(2,128)S(1)} %copy-done.2, f32[640,256]{1,0:T(8,128)S(1)} %constant_dynamic-update-slice_fusion), kind=kOutput, calls=%fused_computation.5 | convolution fusion | flops 1007288320 | bytes 1708032 | tf_op jit(solution)/shard_map/dot_general | solution.py:93
  17.9 1.0 %convolution_bitcast_fusion = f32[2,512,256]{2,1,0:T(8,128)S(1)} fusion(f32[2,512,256]{2,1,0:T(8,128)S(1)} %fusion.3, f32[2,512,512]{2,1,0:T(8,128)S(1)} %copy-done), kind=kOutput, calls=%fused_computation.7 | convolution fusion | flops 805306368 | bytes 4194304 | tf_op jit(solution)/shard_map/cij,cjb->cib/dot_general | solution.py:94
  18.9 0.9 %fusion.8 = f32[640,256]{1,0:T(8,128)S(1)} fusion(f32[2,512,256]{2,1,0:T(8,128)S(1)} %convolution_bitcast_fusion, s32[2,512]{1,0:T(2,128)S(1)} %copy-done.2), kind=kOutput, calls=%fused_computation.12 | convolution fusion | flops 1007288320 | bytes 1708032 | tf_op jit(solution)/shard_map/dot_general | solution.py:69
  19.8 0.3 convolution_multiply_fusion
  20.1 0.5 %convolution_add_fusion = f32[640,256]{1,0:T(8,128)S(1)} fusion(f32[640,256]{1,0:T(8,128)S(1)} %fusion.8, f32[64,640]{1,0:T(8,128)S(1)} %bitcast.43, f32[64,256]{1,0:T(8,128)S(1)} %convolution_multiply_fusion), kind=kOutput, calls=%fused_computation.13 | convolution fusion | flops 63078400 | bytes 1540096 | tf_op jit(solution)/shard_map/dot_general | solution.py:95
  20.6 4.3 %collective-permute-start.5 = (f32[256,256]{1,0:T(8,128)S(1)}, f32[256,256]{1,0:T(8,128)S(1)}, u32[]{:S(2)}, u32[]{:S(2)}) collective-permute-start(f32[256,256]{1,0:T(8,128)S(1)} %get-tuple-element.15), channel_id=1, source_target_pairs={{0,4},{4,8},{8,12},{12,16},{16,20},{20,24},{24,28},{1,5},{5,9},{9,... | collective-permute-start | bytes 786440 | tf_op jit(solution)/shard_map/ppermute | solution.py:16
  25.0 1.3 %collective-permute-start.6 = (f32[256,256]{1,0:T(8,128)S(1)}, f32[256,256]{1,0:T(8,128)S(1)}, u32[]{:S(2)}, u32[]{:S(2)}) collective-permute-start(f32[256,256]{1,0:T(8,128)S(1)} %get-tuple-element.16), channel_id=1, source_target_pairs={{4,0},{8,4},{12,8},{16,12},{20,16},{24,20},{28,24},{5,1},{9,5},{13... | collective-permute-start | bytes 786440 | tf_op jit(solution)/shard_map/ppermute | solution.py:21
  26.3 1.9 %fusion.1 = f32[2,512,640]{2,1,0:T(8,128)S(1)} fusion(f32[2,512,512]{2,1,0:T(8,128)S(1)} %copy-done, s32[2,512]{1,0:T(2,128)S(1)} %copy-done.2), kind=kOutput, calls=%fused_computation.3 | convolution fusion | flops 2013921280 | bytes 4722688 | tf_op jit(solution)/shard_map/cij,cjq->ciq/dot_general | solution.py:102
  28.2 1.6 %fusion.16 = f32[640,640]{1,0:T(8,128)S(1)} fusion(f32[64,640]{1,0:T(8,128)S(1)} %bitcast.44, f32[64]{0:T(128)S(1)} %reshape.123), kind=kOutput, calls=%fused_computation.27 | convolution fusion | flops 314613760 | bytes 1802496 | tf_op jit(solution)/shard_map/dot_general | solution.py:105
  29.8 2.3 %bitcast_add_fusion = f32[640,640]{1,0:T(8,128)S(1)} fusion(f32[640,640]{1,0:T(8,128)S(1)} %fusion.16, f32[2,512,640]{2,1,0:T(8,128)S(1)} %fusion.1, s32[2,512]{1,0:T(2,128)S(1)} %copy-done.2), kind=kOutput, calls=%fused_computation.6 | convolution fusion | flops 2517647360 | bytes 5902336 | tf_op jit(solution)/shard_map/dot_general | solution.py:69
  32.1 0.1 multiply_subtract_fusion
  32.3 2.2 %collective-permute-done.5 = f32[256,256]{1,0:T(8,128)S(1)} collective-permute-done((f32[256,256]{1,0:T(8,128)S(1)}, f32[256,256]{1,0:T(8,128)S(1)}, u32[]{:S(2)}, u32[]{:S(2)}) %collective-permute-start.5) | collective-permute-done | bytes 262176 | tf_op jit(solution)/shard_map/ppermute | solution.py:16
  34.4 0.0 collective-permute-done.6
  34.4 0.2 multiply_select_fusion
  34.6 0.5 %fusion.11 = f32[256,256]{1,0:T(8,128)S(1)} fusion(f32[640,256]{1,0:T(8,128)S(1)} %multiply_select_fusion, f32[128,640]{1,0:T(8,128)S(1)} %get-tuple-element.14, f32[128,640]{1,0:T(8,128)S(1)} %get-tuple-element.13), kind=kOutput, calls=%fused_computation.18 | convolution fusion | flops 251822080 | bytes 1572864 | tf_op jit(solution)/shard_map/dot_general | solution.py:125
  35.2 4.4 %collective-permute-start.7 = (f32[128,256]{1,0:T(8,128)S(1)}, f32[128,256]{1,0:T(8,128)S(1)}, u32[]{:S(2)}, u32[]{:S(2)}) collective-permute-start(f32[128,256]{1,0:T(8,128)S(1)} %get-tuple-element.19), channel_id=1, source_target_pairs={{0,4},{4,8},{8,12},{12,16},{16,20},{20,24},{24,28},{1,5},{5,9},{9,... | collective-permute-start | bytes 393224 | tf_op jit(solution)/shard_map/ppermute | solution.py:16
  39.6 1.3 %collective-permute-start.8 = (f32[128,256]{1,0:T(8,128)S(1)}, f32[128,256]{1,0:T(8,128)S(1)}, u32[]{:S(2)}, u32[]{:S(2)}) collective-permute-start(f32[128,256]{1,0:T(8,128)S(1)} %get-tuple-element.20), channel_id=1, source_target_pairs={{4,0},{8,4},{12,8},{16,12},{20,16},{24,20},{28,24},{5,1},{9,5},{13... | collective-permute-start | bytes 393224 | tf_op jit(solution)/shard_map/ppermute | solution.py:21
  40.9 0.7 %fusion.9 = f32[384,256]{1,0:T(8,128)S(1)} fusion(f32[384,256]{1,0:T(8,128)S(1)} %copy-done.1, f32[640,256]{1,0:T(8,128)S(1)} %multiply_select_fusion, f32[640,640]{1,0:T(8,128)S(1)} %bitcast_add_fusion), kind=kOutput, calls=%fused_computation.15 | convolution fusion | flops 377782272 | bytes 2818048 | tf_op jit(solution)/shard_map/dot_general | solution.py:129
  41.5 0.5 %collective-permute-done.7 = f32[128,256]{1,0:T(8,128)S(1)} collective-permute-done((f32[128,256]{1,0:T(8,128)S(1)}, f32[128,256]{1,0:T(8,128)S(1)}, u32[]{:S(2)}, u32[]{:S(2)}) %collective-permute-start.7) | collective-permute-done | bytes 131104 | tf_op jit(solution)/shard_map/ppermute | solution.py:16
  42.1 4.4 %collective-permute-done.8 = f32[128,256]{1,0:T(8,128)S(1)} collective-permute-done((f32[128,256]{1,0:T(8,128)S(1)}, f32[128,256]{1,0:T(8,128)S(1)}, u32[]{:S(2)}, u32[]{:S(2)}) %collective-permute-start.8) | collective-permute-done | bytes 131104 | tf_op jit(solution)/shard_map/ppermute | solution.py:21
  46.4 0.8 %pad_add_fusion = f32[384,256]{1,0:T(8,128)} fusion(f32[128,256]{1,0:T(8,128)S(1)} %collective-permute-done.8, f32[384,256]{1,0:T(8,128)S(1)} %fusion.9, f32[128,256]{1,0:T(8,128)S(1)} %collective-permute-done.7), kind=kLoop, calls=%fused_computation.26 | loop fusion | flops 196608 | bytes 1048576 | tf_op jit(solution)/shard_map/add | solution.py:135
  (17 shorter events, 0.2 us)
Async XLA Ops:
  0.0 17.9 %copy-start = (f32[2,512,512]{2,1,0:T(8,128)S(1)}, f32[2,512,512]{2,1,0:T(8,128)}, u32[]{:S(2)}) copy-start(f32[2,512,512]{2,1,0:T(8,128)} %param.8) | copy-start | bytes 6291460
  0.0 13.8 %collective-permute-start = (f32[4,16,128]{2,1,0:T(8,128)}, f32[4,16,128]{2,1,0:T(8,128)S(1)}, u32[]{:S(2)}, u32[]{:S(2)}) collective-permute-start(f32[4,16,128]{2,1,0:T(8,128)} %param.10), channel_id=1, source_target_pairs={{0,1},{1,2},{2,3},{3,0},{4,5},{5,6},{6,7},{7,4},{8,9},{9,10},{10,1... | collective-permute-start | bytes 98312 | tf_op jit(solution)/shard_map/ppermute | solution.py:30
  0.5 13.3 %collective-permute-start.2 = (f32[4,16,128]{2,1,0:T(8,128)}, f32[4,16,128]{2,1,0:T(8,128)S(1)}, u32[]{:S(2)}, u32[]{:S(2)}) collective-permute-start(f32[4,16,128]{2,1,0:T(8,128)} %param.10), channel_id=1, source_target_pairs={{0,3},{1,0},{2,1},{3,2},{4,7},{5,4},{6,5},{7,6},{8,11},{9,8},{10,9... | collective-permute-start | bytes 98312 | tf_op jit(solution)/shard_map/ppermute | solution.py:30
  2.4 11.4 %collective-permute-start.1 = (f32[4,16,128]{2,1,0:T(8,128)}, f32[4,16,128]{2,1,0:T(8,128)S(1)}, u32[]{:S(2)}, u32[]{:S(2)}) collective-permute-start(f32[4,16,128]{2,1,0:T(8,128)} %param.10), channel_id=1, source_target_pairs={{0,2},{1,3},{2,0},{3,1},{4,6},{5,7},{6,4},{7,5},{8,10},{9,11},{10,... | collective-permute-start | bytes 98312 | tf_op jit(solution)/shard_map/ppermute | solution.py:30
  5.7 10.6 %collective-permute-start.4 = (f32[128,256]{1,0:T(8,128)S(1)}, f32[128,256]{1,0:T(8,128)S(1)}, u32[]{:S(2)}, u32[]{:S(2)}) collective-permute-start(f32[128,256]{1,0:T(8,128)S(1)} %get-tuple-element.17), channel_id=1, source_target_pairs={{4,0},{8,4},{12,8},{16,12},{20,16},{24,20},{28,24},{5,1},{9,5},{13... | collective-permute-start | bytes 393224 | tf_op jit(solution)/shard_map/ppermute | solution.py:21
  7.0 9.2 %collective-permute-start.3 = (f32[128,256]{1,0:T(8,128)S(1)}, f32[128,256]{1,0:T(8,128)S(1)}, u32[]{:S(2)}, u32[]{:S(2)}) collective-permute-start(f32[128,256]{1,0:T(8,128)S(1)} %get-tuple-element.18), channel_id=1, source_target_pairs={{0,4},{4,8},{8,12},{12,16},{16,20},{20,24},{24,28},{1,5},{5,9},{9,... | collective-permute-start | bytes 393224 | tf_op jit(solution)/shard_map/ppermute | solution.py:16
  15.2 1.0 %copy-start.1 = (f32[384,256]{1,0:T(8,128)S(1)}, f32[384,256]{1,0:T(8,128)}, u32[]{:S(2)}) copy-start(f32[384,256]{1,0:T(8,128)} %param.7) | copy-start | bytes 1179652
  15.6 0.7 %copy-start.2 = (s32[2,512]{1,0:T(2,128)S(1)}, s32[2,512]{1,0:T(2,128)}, u32[]{:S(2)}) copy-start(s32[2,512]{1,0:T(2,128)} %param.9) | copy-start | bytes 12292
  20.6 13.8 %collective-permute-start.5 = (f32[256,256]{1,0:T(8,128)S(1)}, f32[256,256]{1,0:T(8,128)S(1)}, u32[]{:S(2)}, u32[]{:S(2)}) collective-permute-start(f32[256,256]{1,0:T(8,128)S(1)} %get-tuple-element.15), channel_id=1, source_target_pairs={{0,4},{4,8},{8,12},{12,16},{16,20},{20,24},{24,28},{1,5},{5,9},{9,... | collective-permute-start | bytes 786440 | tf_op jit(solution)/shard_map/ppermute | solution.py:16
  25.0 9.5 %collective-permute-start.6 = (f32[256,256]{1,0:T(8,128)S(1)}, f32[256,256]{1,0:T(8,128)S(1)}, u32[]{:S(2)}, u32[]{:S(2)}) collective-permute-start(f32[256,256]{1,0:T(8,128)S(1)} %get-tuple-element.16), channel_id=1, source_target_pairs={{4,0},{8,4},{12,8},{16,12},{20,16},{24,20},{28,24},{5,1},{9,5},{13... | collective-permute-start | bytes 786440 | tf_op jit(solution)/shard_map/ppermute | solution.py:21
  35.2 6.9 %collective-permute-start.7 = (f32[128,256]{1,0:T(8,128)S(1)}, f32[128,256]{1,0:T(8,128)S(1)}, u32[]{:S(2)}, u32[]{:S(2)}) collective-permute-start(f32[128,256]{1,0:T(8,128)S(1)} %get-tuple-element.19), channel_id=1, source_target_pairs={{0,4},{4,8},{8,12},{12,16},{16,20},{20,24},{24,28},{1,5},{5,9},{9,... | collective-permute-start | bytes 393224 | tf_op jit(solution)/shard_map/ppermute | solution.py:16
  39.6 6.9 %collective-permute-start.8 = (f32[128,256]{1,0:T(8,128)S(1)}, f32[128,256]{1,0:T(8,128)S(1)}, u32[]{:S(2)}, u32[]{:S(2)}) collective-permute-start(f32[128,256]{1,0:T(8,128)S(1)} %get-tuple-element.20), channel_id=1, source_target_pairs={{4,0},{8,4},{12,8},{16,12},{20,16},{24,20},{28,24},{5,1},{9,5},{13... | collective-permute-start | bytes 393224 | tf_op jit(solution)/shard_map/ppermute | solution.py:21
